TPU v7x, 512 devices: a whole 4x8x8 slice. The times are simulated.
512 devices in a mesh: rows: 64 (over z, y), feat: 8 (over x, core).
Axes of the slice: x: 4, y: 8, z: 8, core: 2. Of those that a mesh axis runs over, the one named last changes fastest.
Arguments:
- node_feats: bfloat16 [65536, 256], P('rows', 'feat'), may hold values from -6 to 6
- band_weights: bfloat16 [65536, 384], P('rows'), may hold values from 0 to 1.5, as said below
- far_weights: bfloat16 [65536, 256], P('rows'), may hold values from 0 to 1.5, as said below
- far_owner: int32 [512, 2], P('rows'), may hold values from 0 to 63, all different within a row; in each aligned block of 8 rows (0 to 7, 8 to 15, ...) at most 2 rows name the same one
- far_local: int32 [512, 2], P('rows'), may hold values from 0 to 7
- w_self: bfloat16 [256, 256], replicated, may hold values from -0.375 to 0.375
- w_neigh: bfloat16 [256, 256], replicated, may hold values from -0.375 to 0.375
- bias: float32 [256], P('feat'), may hold values from -3 to 3
- cotangent: bfloat16 [65536, 256], P('rows', 'feat'), may hold values from -16 to 16
Outputs:
- layer_out: bfloat16 [65536, 256], P('rows', 'feat')
- grad_feats: float32 [65536, 256], P('rows', 'feat')
- grad_self: float32 [256, 256], P('feat')
- grad_neigh: float32 [256, 256], P('feat')
Inputs may be any that keep to these rules, and one draw needn't show every extreme that they name: `far_owner`: among the far entries of the 8 row blocks of one device, no owner is named more than 2 times, and in every draw some owner is named exactly 2 times in some device's blocks; the 2 owners of one row block differ. `band_weights`: each row has a positive weight on the node's own entry of its own block; other entries are zero or positive. `far_weights`: entries are zero or positive.
All inputs are finite; a program needn't handle non-finite values.
Results may differ from a plain program's by a relative error of at most 0.0049.
Values may be sent and summed in bfloat16 or wider, within the bound.
No kernel may reach another device: no remote copies, remote signals or barrier semaphores. Data moves between devices by JAX's collectives and lax.ppermute only.
A program may use at most 64 MiB of HBM per device.

v0:
```python
import jax
import jax.numpy as jnp
from jax import lax
from jax.sharding import PartitionSpec as P


def extended(block, sides, width):
    for axis, dim in sides:
        count = lax.axis_size(axis)
        forward = [(i, i + 1) for i in range(count - 1)]
        backward = [(target, source) for source, target in forward]
        low = lax.ppermute(
            lax.slice_in_dim(block, block.shape[dim] - width, None, axis=dim), axis, forward
        )
        high = lax.ppermute(lax.slice_in_dim(block, 0, width, axis=dim), axis, backward)
        block = jnp.concatenate([low, block, high], axis=dim)
    return block


def from_behind(block, axis, distance):
    devices = range(lax.axis_size(axis))
    route = [(i - distance, i) for i in devices if i - distance in devices]
    return lax.ppermute(block, axis, route)


def on_device(
    node_feats, band_weights, far_weights, far_owner, far_local, w_self, w_neigh, bias, cotangent
):
    rows_dev, col_count = node_feats.shape
    tile_size = band_weights.shape[1] // 3
    blocks = rows_dev // tile_size
    fanout = far_owner.shape[1]
    peer_count = lax.axis_size("rows")
    capacity = max(2, 2 * blocks * fanout // peer_count)
    col_start = lax.axis_index("feat") * col_count
    padded = extended(node_feats, (("rows", 0),), tile_size)
    windows = jnp.concatenate(
        [
            padded[offset * tile_size : offset * tile_size + rows_dev].reshape(
                blocks, tile_size, col_count
            )
            for offset in range(3)
        ],
        axis=1,
    )
    band_tiles = band_weights.reshape(blocks, tile_size, 3 * tile_size)
    band_sum = jnp.einsum("bij,bjc->bic", band_tiles, windows, preferred_element_type=jnp.float32)
    owner_ids = far_owner.reshape(-1)
    local_ids = far_local.reshape(-1)
    entries = owner_ids.shape[0]
    same_owner = owner_ids[:, None] == owner_ids[None, :]
    earlier = jnp.arange(entries)[None, :] < jnp.arange(entries)[:, None]
    slot_rank = jnp.sum(jnp.where(same_owner & earlier, 1, 0), axis=1).astype(jnp.int32)
    slot_ids = owner_ids * capacity + slot_rank
    slot_hit = slot_ids[:, None] == jnp.arange(peer_count * capacity, dtype=jnp.int32)[None, :]
    request = (jnp.sum(jnp.where(slot_hit, local_ids[:, None] + 1, 0), axis=0) - 1).reshape(
        peer_count, capacity
    )
    wanted = lax.all_to_all(request, "rows", split_axis=0, concat_axis=0, tiled=True)
    usable = wanted >= 0
    safe_ids = jnp.maximum(wanted, 0)
    own_blocks = node_feats.reshape(blocks, tile_size, col_count)
    outgoing = jnp.where(
        usable[:, :, None, None], own_blocks[safe_ids], jnp.zeros((), jnp.bfloat16)
    )
    incoming = lax.all_to_all(outgoing, "rows", split_axis=0, concat_axis=0, tiled=True)
    fetched = incoming.reshape(peer_count * capacity, tile_size, col_count)[slot_ids].reshape(
        blocks, fanout * tile_size, col_count
    )
    far_tiles = far_weights.reshape(blocks, tile_size, fanout * tile_size)
    far_sum = jnp.einsum("bij,bjc->bic", far_tiles, fetched, preferred_element_type=jnp.float32)
    degree = jnp.sum(band_weights.astype(jnp.float32), axis=1) + jnp.sum(
        far_weights.astype(jnp.float32), axis=1
    )
    neighbours = ((band_sum + far_sum).reshape(rows_dev, col_count) / degree[:, None]).astype(
        jnp.bfloat16
    )
    rows_self = lax.dynamic_slice_in_dim(w_self, col_start, col_count, 0)
    rows_neigh = lax.dynamic_slice_in_dim(w_neigh, col_start, col_count, 0)
    terms = jnp.dot(node_feats, rows_self, preferred_element_type=jnp.float32) + jnp.dot(
        neighbours, rows_neigh, preferred_element_type=jnp.float32
    )
    preact = lax.psum_scatter(terms, "feat", scatter_dimension=1, tiled=True)
    preact = preact + bias
    layer_out = jax.nn.silu(preact).astype(jnp.bfloat16)
    sigmoid_z = jax.nn.sigmoid(preact)
    grad_pre = (
        cotangent.astype(jnp.float32) * sigmoid_z * (1.0 + preact * (1.0 - sigmoid_z))
    ).astype(jnp.bfloat16)
    full_grad = lax.all_gather(grad_pre, "feat", axis=1, tiled=True)
    grad_scale = float(rows_dev * peer_count) ** (-0.5)
    part_self = jnp.einsum("rc,rf->cf", node_feats, full_grad, preferred_element_type=jnp.float32)
    part_neigh = jnp.einsum("rc,rf->cf", neighbours, full_grad, preferred_element_type=jnp.float32)
    sum_self, sum_neigh = lax.psum((part_self, part_neigh), "rows")
    grad_self = sum_self * grad_scale
    grad_neigh = sum_neigh * grad_scale
    dense_grad = jnp.einsum("rf,cf->rc", full_grad, rows_self, preferred_element_type=jnp.float32)
    grad_agg = jnp.einsum("rf,cf->rc", full_grad, rows_neigh, preferred_element_type=jnp.float32)
    grad_neighbours = (grad_agg / degree[:, None]).astype(jnp.bfloat16)
    grad_blocks = grad_neighbours.reshape(blocks, tile_size, col_count)
    grad_windows = jnp.einsum(
        "bij,bic->bjc", band_tiles, grad_blocks, preferred_element_type=jnp.float32
    )
    grad_padded = jnp.zeros((rows_dev + 2 * tile_size, col_count), jnp.float32)
    for offset in range(3):
        piece = grad_windows[:, offset * tile_size : (offset + 1) * tile_size, :].reshape(
            rows_dev, col_count
        )
        grad_padded = grad_padded + jnp.pad(
            piece, ((offset * tile_size, (2 - offset) * tile_size), (0, 0))
        )
    top_rim = grad_padded[:tile_size]
    bottom_rim = grad_padded[rows_dev + tile_size :]
    from_below = from_behind(top_rim, "rows", -1)
    from_above = from_behind(bottom_rim, "rows", 1)
    grad_fetched = jnp.einsum(
        "bij,bic->bjc", far_tiles, grad_blocks, preferred_element_type=jnp.float32
    )
    returning = jnp.zeros((peer_count * capacity, tile_size, col_count), jnp.float32)
    returning = returning.at[slot_ids].set(grad_fetched.reshape(entries, tile_size, col_count))
    returned = lax.all_to_all(
        returning.reshape(peer_count, capacity, tile_size, col_count).astype(jnp.bfloat16),
        "rows",
        split_axis=0,
        concat_axis=0,
        tiled=True,
    ).astype(jnp.float32)
    target_block = jnp.where(usable, wanted, blocks).reshape(-1)
    owed = jnp.zeros((blocks, tile_size * col_count), jnp.float32)
    owed = owed.at[target_block].add(
        returned.reshape(peer_count * capacity, tile_size * col_count), mode="drop"
    )
    interior = (
        dense_grad
        + grad_padded[tile_size : tile_size + rows_dev]
        + owed.reshape(rows_dev, col_count)
    )
    interior = interior.at[:tile_size].add(from_above)
    grad_feats = interior.at[rows_dev - tile_size :].add(from_below)
    return (layer_out, grad_feats, grad_self, grad_neigh)


def solution(mesh):
    in_specs = (
        P("rows", "feat"),
        P("rows", None),
        P("rows", None),
        P("rows", None),
        P("rows", None),
        P(),
        P(),
        P("feat"),
        P("rows", "feat"),
    )
    out_specs = (P("rows", "feat"), P("rows", "feat"), P("feat", None), P("feat", None))
    return jax.shard_map(
        on_device, mesh=mesh, in_specs=in_specs, out_specs=out_specs, check_vma=False
    )
```

profile of v0, /device:TPU:1, one launch (start us, length us, event | category | flops | bytes accessed | tf_op | source)
XLA Modules:
  0.0 323.3 jit_solution(16754911278057413692)
XLA Ops:
  10.0 17.1 %all-to-all-start = ((s32[64,1,2]{2,1,0:T(1,128)}), s32[64,1,2]{2,1,0:T(1,128)S(1)}, u32[]{:S(2)}, u32[]{:S(2)}) async-start(s32[64,1,2]{2,1,0:T(1,128)} %bitcast.2), calls=%async_computation | async-start | bytes 65536 | tf_op jit(solution)/shard_map/all_to_all | solution.py:59
  28.0 9.9 %all-to-all-done = s32[64,1,2]{2,1,0:T(1,128)S(1)} async-done(((s32[64,1,2]{2,1,0:T(1,128)}), s32[64,1,2]{2,1,0:T(1,128)S(1)}, u32[]{:S(2)}, u32[]{:S(2)}) %all-to-all-start) | async-done | bytes 544 | tf_op jit(solution)/shard_map/all_to_all | solution.py:59
  38.4 1.4 fusion.37
  41.0 1.2 broadcast_select_fusion
  42.2 5.5 %all-to-all-start.1 = ((bf16[64,2,128,32]{2,3,1,0:T(8,128)(2,1)}), bf16[64,2,128,32]{2,3,1,0:T(8,128)(2,1)}, u32[]{:S(2)}, u32[]{:S(2)}) async-start(bf16[64,2,128,32]{2,3,1,0:T(8,128)(2,1)} %broadcast_select_fusion), calls=%async_computation.1 | async-start | bytes 2097152 | tf_op jit(solution)/shard_map/all_to_all | solution.py:66
  47.8 2.7 collective-permute-start
  50.5 1.3 collective-permute-start.1
  53.6 11.1 %collective-permute-done = bf16[128,32]{0,1:T(8,128)(2,1)S(1)} collective-permute-done((bf16[128,32]{0,1:T(8,128)(2,1)S(1)}, bf16[128,32]{0,1:T(8,128)(2,1)S(1)}, u32[]{:S(2)}, u32[]{:S(2)}) %collective-permute-start) | collective-permute-done | bytes 8224 | tf_op jit(solution)/shard_map/ppermute | solution.py:12
  64.7 4.4 %collective-permute-done.1 = bf16[128,32]{0,1:T(8,128)(2,1)S(1)} collective-permute-done((bf16[128,32]{0,1:T(8,128)(2,1)S(1)}, bf16[128,32]{0,1:T(8,128)(2,1)S(1)}, u32[]{:S(2)}, u32[]{:S(2)}) %collective-permute-start.1) | collective-permute-done | bytes 8224 | tf_op jit(solution)/shard_map/ppermute | solution.py:15
  69.5 3.8 %all-to-all-done.1 = bf16[64,2,128,32]{2,3,1,0:T(8,128)(2,1)} async-done(((bf16[64,2,128,32]{2,3,1,0:T(8,128)(2,1)}), bf16[64,2,128,32]{2,3,1,0:T(8,128)(2,1)}, u32[]{:S(2)}, u32[]{:S(2)}) %all-to-all-start.1) | async-done | bytes 1048608 | tf_op jit(solution)/shard_map/all_to_all | solution.py:66
  73.4 1.8 gather_fusion.1
  75.6 1.3 convolution_add_fusion
  76.9 34.5 %reduce-scatter.2.cloned.1.call-done = f32[1024,32]{0,1:T(8,128)} async-done(((f32[1024,256]{0,1:T(8,128)}), f32[1024,32]{0,1:T(8,128)}) %reduce-scatter.2.cloned.1.call-update) | async-done | bytes 131088 | tf_op jit(solution)/shard_map/reduce_scatter | solution.py:83
  111.4 1.7 multiply_convert_fusion
  113.1 15.2 %all_gather.3 = bf16[1024,256]{0,1:T(8,128)(2,1)S(1)} all-gather(bf16[1024,32]{0,1:T(8,128)(2,1)S(1)} %get-tuple-element.37), channel_id=1, replica_groups=mesh['rows'=64,'feat'=8] {'feat'}, dimensions={1}, use_global_device_ids=true | all-gather | bytes 589824 | tf_op jit(solution)/shard_map/all_gather | solution.py:90
  131.9 13.2 %all-to-all-start.2 = ((bf16[64,2,128,32]{2,3,1,0:T(8,128)(2,1)}), bf16[64,2,128,32]{2,3,1,0:T(8,128)(2,1)S(1)}, u32[]{:S(2)}, u32[]{:S(2)}) async-start(bf16[64,2,128,32]{2,3,1,0:T(8,128)(2,1)} %bitcast.88), calls=%async_computation.3 | async-start | bytes 2097152 | tf_op jit(solution)/shard_map/all_to_all | solution.py:121
  147.5 2.9 collective-permute-start.2
  150.4 1.5 collective-permute-start.3
  151.9 144.7 %all-reduce.6.cloned.1.call-done = (f32[32,256]{1,0:T(8,128)}, f32[32,256]{1,0:T(8,128)}) async-done(((f32[32,256]{1,0:T(8,128)}, f32[32,256]{1,0:T(8,128)}), (f32[32,256]{1,0:T(8,128)}, f32[32,256]{1,0:T(8,128)})) %all-reduce.6.cloned.1.call-update) | async-done | bytes 65552 | tf_op jit(solution)/shard_map/psum | solution.py:94
  296.7 1.4 broadcast_multiply_fusion.1
  298.0 1.4 broadcast_multiply_fusion
  299.4 4.1 %copy.105 = f32[64,2,128,32]{3,2,1,0:T(8,128)} copy(bf16[64,2,128,32]{2,3,1,0:T(8,128)(2,1)S(1)} %all-to-all-done.2) | data formatting | bytes 3145728 | tf_op jit(solution)/shard_map/reshape | solution.py:131
  303.5 6.2 %reshape.273 = f32[128,4096]{1,0:T(8,128)S(1)} reshape(f32[64,2,128,32]{3,2,1,0:T(8,128)} %copy.105) | data formatting | bytes 4194304 | tf_op jit(solution)/shard_map/reshape | solution.py:131
  309.7 3.8 %scatter_custom_fusion.1 = f32[8,4096]{1,0:T(8,128)} fusion(s32[128]{0:T(128)S(1)} %fusion.32, f32[128,4096]{1,0:T(8,128)S(1)} %reshape.273, f32[]{:T(128)} %constant.91.clone.1), kind=kCustom, calls=%fused_computation.47 | custom fusion | flops 524288 | bytes 131076 | tf_op jit(solution)/shard_map/scatter-add | solution.py:130
  (87 shorter events, 16.5 us)
Async XLA Ops:
  7.2 68.4 %copy-start = (bf16[256,256]{1,0:T(8,128)(2,1)S(1)}, bf16[256,256]{1,0:T(8,128)(2,1)}, u32[]{:S(2)}) copy-start(bf16[256,256]{1,0:T(8,128)(2,1)} %param.19) | copy-start | bytes 393220
  10.0 27.9 %all-to-all-start = ((s32[64,1,2]{2,1,0:T(1,128)}), s32[64,1,2]{2,1,0:T(1,128)S(1)}, u32[]{:S(2)}, u32[]{:S(2)}) async-start(s32[64,1,2]{2,1,0:T(1,128)} %bitcast.2), calls=%async_computation | async-start | bytes 65536 | tf_op jit(solution)/shard_map/all_to_all | solution.py:59
  40.9 6.9 %copy-start.5 = (bf16[1024,32]{0,1:T(8,128)(2,1)S(1)}, bf16[1024,32]{0,1:T(8,128)(2,1)}, u32[]{:S(2)}) copy-start(bf16[1024,32]{0,1:T(8,128)(2,1)} %param.13) | copy-start | bytes 196612
  40.9 10.9 %copy-start.9 = (s32[8,2]{0,1:T(2,128)S(1)}, s32[8,2]{0,1:T(2,128)}, u32[]{:S(2)}) copy-start(s32[8,2]{0,1:T(2,128)} %param.16) | copy-start | bytes 196
  41.0 11.1 %copy-start.2 = (bf16[1024,256]{1,0:T(8,128)(2,1)S(1)}, bf16[1024,256]{1,0:T(8,128)(2,1)}, u32[]{:S(2)}) copy-start(bf16[1024,256]{1,0:T(8,128)(2,1)} %param.15) | copy-start | bytes 1572868
  41.0 11.3 %copy-start.1 = (bf16[1024,384]{1,0:T(8,128)(2,1)S(1)}, bf16[1024,384]{1,0:T(8,128)(2,1)}, u32[]{:S(2)}) copy-start(bf16[1024,384]{1,0:T(8,128)(2,1)} %param.14) | copy-start | bytes 2359300
  42.2 31.1 %all-to-all-start.1 = ((bf16[64,2,128,32]{2,3,1,0:T(8,128)(2,1)}), bf16[64,2,128,32]{2,3,1,0:T(8,128)(2,1)}, u32[]{:S(2)}, u32[]{:S(2)}) async-start(bf16[64,2,128,32]{2,3,1,0:T(8,128)(2,1)} %broadcast_select_fusion), calls=%async_computation.1 | async-start | bytes 2097152 | tf_op jit(solution)/shard_map/all_to_all | solution.py:66
  47.7 63.7 %reduce-scatter.2.cloned.1.call-start = ((), (), s32[]{:S(2)}) async-start(), calls=%async_computation.4 | async-start | bytes 1179648 | tf_op jit(solution)/shard_map/reduce_scatter | solution.py:83
  47.8 16.9 %collective-permute-start = (bf16[128,32]{0,1:T(8,128)(2,1)S(1)}, bf16[128,32]{0,1:T(8,128)(2,1)S(1)}, u32[]{:S(2)}, u32[]{:S(2)}) collective-permute-start(bf16[128,32]{0,1:T(8,128)(2,1)S(1)} %get-tuple-element.41), channel_id=1, source_target_pairs={{0,8},{8,16},{16,24},{24,32},{32,40},{40,48},{48,56},{56,64},{64,7... | collective-permute-start | bytes 24584 | tf_op jit(solution)/shard_map/ppermute | solution.py:12
  50.5 18.5 %collective-permute-start.1 = (bf16[128,32]{0,1:T(8,128)(2,1)S(1)}, bf16[128,32]{0,1:T(8,128)(2,1)S(1)}, u32[]{:S(2)}, u32[]{:S(2)}) collective-permute-start(bf16[128,32]{0,1:T(8,128)(2,1)S(1)} %get-tuple-element.42), channel_id=1, source_target_pairs={{8,0},{16,8},{24,16},{32,24},{40,32},{48,40},{56,48},{64,56},{72,6... | collective-permute-start | bytes 24584 | tf_op jit(solution)/shard_map/ppermute | solution.py:15
  75.3 36.2 %copy-start.8 = (bf16[1024,32]{0,1:T(8,128)(2,1)S(1)}, bf16[1024,32]{0,1:T(8,128)(2,1)}, u32[]{:S(2)}) copy-start(bf16[1024,32]{0,1:T(8,128)(2,1)} %param.21) | copy-start | bytes 196612
  75.3 36.2 %copy-start.10 = (f32[32]{0:T(128)S(1)}, f32[32]{0:T(128)}, u32[]{:S(2)}) copy-start(f32[32]{0:T(128)} %param.20) | copy-start | bytes 388
  128.3 0.8 copy-start.3
  130.7 14.4 %copy-start.7 = (s32[64,2]{1,0:T(8,128)S(1)}, s32[64,2]{1,0:T(8,128)}, u32[]{:S(2)}) copy-start(s32[64,2]{1,0:T(8,128)} %get-tuple-element.28) | copy-start | bytes 1540
  131.9 13.7 %copy-start.4 = (bf16[1024,256]{0,1:T(8,128)(2,1)S(1)}, bf16[1024,256]{0,1:T(8,128)(2,1)}, u32[]{:S(2)}) copy-start(bf16[1024,256]{0,1:T(8,128)(2,1)} %copy-done.3) | copy-start | bytes 1572868
  131.9 167.5 %all-to-all-start.2 = ((bf16[64,2,128,32]{2,3,1,0:T(8,128)(2,1)}), bf16[64,2,128,32]{2,3,1,0:T(8,128)(2,1)S(1)}, u32[]{:S(2)}, u32[]{:S(2)}) async-start(bf16[64,2,128,32]{2,3,1,0:T(8,128)(2,1)} %bitcast.88), calls=%async_computation.3 | async-start | bytes 2097152 | tf_op jit(solution)/shard_map/all_to_all | solution.py:121
  145.1 151.6 %all-reduce.6.cloned.1.call-start = ((), (), s32[]{:S(2)}) async-start(), calls=%async_computation.5 | async-start | bytes 131072 | tf_op jit(solution)/shard_map/psum | solution.py:94
  147.5 168.2 %collective-permute-start.2 = (f32[128,32]{0,1:T(8,128)S(1)}, f32[128,32]{0,1:T(8,128)S(1)}, u32[]{:S(2)}, u32[]{:S(2)}) collective-permute-start(f32[128,32]{0,1:T(8,128)S(1)} %get-tuple-element.33), channel_id=1, source_target_pairs={{0,8},{8,16},{16,24},{24,32},{32,40},{40,48},{48,56},{56,64},{64,7... | collective-permute-start | bytes 49160 | tf_op jit(solution)/shard_map/ppermute | solution.py:23
  150.4 165.3 %collective-permute-start.3 = (f32[128,32]{0,1:T(8,128)S(1)}, f32[128,32]{0,1:T(8,128)S(1)}, u32[]{:S(2)}, u32[]{:S(2)}) collective-permute-start(f32[128,32]{0,1:T(8,128)S(1)} %get-tuple-element.32), channel_id=1, source_target_pairs={{8,0},{16,8},{24,16},{32,24},{40,32},{48,40},{56,48},{64,56},{72,6... | collective-permute-start | bytes 49160 | tf_op jit(solution)/shard_map/ppermute | solution.py:23
  315.8 0.7 copy-start.6
Sparse Core Ops, SparseCore 0:
  77.0 34.3 reduce-scatter.1
  149.9 146.7 all-reduce.5
where the time goes:
time: 328 us; the launch traced here: 323 us
  waiting for transfers between devices  209 us (64%)
  starting transfers between devices  44.3 us (14%)
  local copies, waits for them, and re-layouts  20.8 us (6%)
  blocking collectives  15.2 us (5%)
  between operations  14.5 us (4%)
  other arithmetic  13.6 us (4%)
  matrix products  6.32 us (2%)
    psum x1, waiting for transfers between devices, on_device(): sum_self, sum_neigh = lax.psum((part_self, part_neigh), 'rows')  145 us
    reduce_scatter x1, waiting for transfers between devices, on_device(): preact = lax.psum_scatter(terms, 'feat', scatter_dimension=1, tiled=True)  34.5 us
    all_to_all x1, starting transfers between devices, on_device(): lax.all_to_all(request, 'rows', split_axis=0, concat_axis=0, tiled=True)  17.1 us
    all_gather x1, blocking collectives, on_device(): full_grad = lax.all_gather(grad_pre, 'feat', axis=1, tiled=True)  15.2 us
    all_to_all x1, starting transfers between devices, on_device(): lax.all_to_all(returning.reshape(peer_count, capacity, tile_size, col_cou...  13.2 us
    ppermute x1, waiting for transfers between devices, extended(): lax.ppermute(lax.slice_in_dim(block, block.shape[dim] - width, None, axis...  11.1 us
    reshape x2, local copies, waits for them, and re-layouts, on_device(): returned.reshape(peer_count * capacity, tile_size * col_count)  10.3 us
    all_to_all x1, waiting for transfers between devices, on_device(): lax.all_to_all(request, 'rows', split_axis=0, concat_axis=0, tiled=True)  9.91 us
  transfers between devices with their start and end apart: 9, of which 6 were waited for; matrix products, arithmetic and copies ran while one was open for 7% of the time, Pallas kernels for 0%

commit v1 on v0

--- a/solution.py
+++ b/solution.py
@@ -21,6 +21,16 @@
     devices = range(lax.axis_size(axis))
     route = [(i - distance, i) for i in devices if i - distance in devices]
     return lax.ppermute(block, axis, route)
+
+
+def summed_over(parts, axis):
+    count = lax.axis_size(axis)
+    flat = parts.reshape(count, -1)
+    pieces = lax.all_to_all(flat, axis, split_axis=0, concat_axis=0, tiled=True)
+    mine = jnp.sum(pieces, axis=0, keepdims=True)
+    spread = jnp.broadcast_to(mine, flat.shape)
+    whole = lax.all_to_all(spread, axis, split_axis=0, concat_axis=0, tiled=True)
+    return whole.reshape(parts.shape)
 
 
 def on_device(
@@ -91,7 +101,7 @@
     grad_scale = float(rows_dev * peer_count) ** (-0.5)
     part_self = jnp.einsum("rc,rf->cf", node_feats, full_grad, preferred_element_type=jnp.float32)
     part_neigh = jnp.einsum("rc,rf->cf", neighbours, full_grad, preferred_element_type=jnp.float32)
-    sum_self, sum_neigh = lax.psum((part_self, part_neigh), "rows")
+    sum_self, sum_neigh = summed_over(jnp.stack([part_self, part_neigh]), "rows")
     grad_self = sum_self * grad_scale
     grad_neigh = sum_neigh * grad_scale
     dense_grad = jnp.einsum("rf,cf->rc", full_grad, rows_self, preferred_element_type=jnp.float32)

time: 328 us -> 227 us (0.69)
  the two profiles are of different devices: /device:TPU:1 before, /device:TPU:8 now
where the time goes in v1:
time: 227 us; the launch traced here: 226 us
  waiting for transfers between devices  102 us (45%)
  starting transfers between devices  59 us (26%)
  local copies, waits for them, and re-layouts  22.1 us (10%)
  between operations  14.5 us (6%)
  blocking collectives  13.1 us (6%)
  other arithmetic  9.93 us (4%)
  matrix products  5.08 us (2%)
    reduce_scatter x1, waiting for transfers between devices, on_device(): preact = lax.psum_scatter(terms, 'feat', scatter_dimension=1, tiled=True)  31.8 us
    all_to_all x1, waiting for transfers between devices, on_device(): lax.all_to_all(returning.reshape(peer_count, capacity, tile_size, col_cou...  20.3 us
    all_to_all x1, starting transfers between devices, on_device(): lax.all_to_all(request, 'rows', split_axis=0, concat_axis=0, tiled=True)  16.6 us
    all_to_all x1, starting transfers between devices, summed_over(): pieces = lax.all_to_all(flat, axis, split_axis=0, concat_axis=0, tiled=True)  13.4 us
    all_gather x1, blocking collectives, on_device(): full_grad = lax.all_gather(grad_pre, 'feat', axis=1, tiled=True)  13.1 us
    ppermute x1, waiting for transfers between devices, extended(): lax.ppermute(lax.slice_in_dim(block, block.shape[dim] - width, None, axis...  13.1 us
    all_to_all x1, waiting for transfers between devices, summed_over(): pieces = lax.all_to_all(flat, axis, split_axis=0, concat_axis=0, tiled=True)  11.1 us
    reshape x2, local copies, waits for them, and re-layouts, on_device(): returned.reshape(peer_count * capacity, tile_size * col_count)  10.4 us
  transfers between devices with their start and end apart: 10, of which 8 were waited for; matrix products, arithmetic and copies ran while one was open for 10% of the time, Pallas kernels for 0%

profile of v1, /device:TPU:8, one launch (start us, length us, event | category | flops | bytes accessed | tf_op | source)
XLA Modules:
  0.0 226.1 jit_solution(5037359908673388846)
XLA Ops:
  10.0 16.6 %all-to-all-start = ((s32[64,1,2]{2,1,0:T(1,128)}), s32[64,1,2]{2,1,0:T(1,128)S(1)}, u32[]{:S(2)}, u32[]{:S(2)}) async-start(s32[64,1,2]{2,1,0:T(1,128)} %bitcast.2), calls=%async_computation | async-start | bytes 65536 | tf_op jit(solution)/shard_map/all_to_all | solution.py:69
  27.4 10.1 %all-to-all-done = s32[64,1,2]{2,1,0:T(1,128)S(1)} async-done(((s32[64,1,2]{2,1,0:T(1,128)}), s32[64,1,2]{2,1,0:T(1,128)S(1)}, u32[]{:S(2)}, u32[]{:S(2)}) %all-to-all-start) | async-done | bytes 544 | tf_op jit(solution)/shard_map/all_to_all | solution.py:69
  40.1 1.2 broadcast_select_fusion
  41.3 6.3 %all-to-all-start.1 = ((bf16[64,2,128,32]{2,3,1,0:T(8,128)(2,1)}), bf16[64,2,128,32]{2,3,1,0:T(8,128)(2,1)}, u32[]{:S(2)}, u32[]{:S(2)}) async-start(bf16[64,2,128,32]{2,3,1,0:T(8,128)(2,1)} %broadcast_select_fusion), calls=%async_computation.1 | async-start | bytes 2097152 | tf_op jit(solution)/shard_map/all_to_all | solution.py:76
  47.7 3.4 %collective-permute-start = (bf16[128,32]{0,1:T(8,128)(2,1)S(1)}, bf16[128,32]{0,1:T(8,128)(2,1)S(1)}, u32[]{:S(2)}, u32[]{:S(2)}) collective-permute-start(bf16[128,32]{0,1:T(8,128)(2,1)S(1)} %get-tuple-element.41), channel_id=1, source_target_pairs={{0,8},{8,16},{16,24},{24,32},{32,40},{40,48},{48,56},{56,64},{64,7... | collective-permute-start | bytes 24584 | tf_op jit(solution)/shard_map/ppermute | solution.py:12
  51.1 2.5 %collective-permute-start.1 = (bf16[128,32]{0,1:T(8,128)(2,1)S(1)}, bf16[128,32]{0,1:T(8,128)(2,1)S(1)}, u32[]{:S(2)}, u32[]{:S(2)}) collective-permute-start(bf16[128,32]{0,1:T(8,128)(2,1)S(1)} %get-tuple-element.42), channel_id=1, source_target_pairs={{8,0},{16,8},{24,16},{32,24},{40,32},{48,40},{56,48},{64,56},{72,6... | collective-permute-start | bytes 24584 | tf_op jit(solution)/shard_map/ppermute | solution.py:15
  55.3 13.1 %collective-permute-done = bf16[128,32]{0,1:T(8,128)(2,1)S(1)} collective-permute-done((bf16[128,32]{0,1:T(8,128)(2,1)S(1)}, bf16[128,32]{0,1:T(8,128)(2,1)S(1)}, u32[]{:S(2)}, u32[]{:S(2)}) %collective-permute-start) | collective-permute-done | bytes 8224 | tf_op jit(solution)/shard_map/ppermute | solution.py:12
  69.8 6.4 %all-to-all-done.1 = bf16[64,2,128,32]{2,3,1,0:T(8,128)(2,1)} async-done(((bf16[64,2,128,32]{2,3,1,0:T(8,128)(2,1)}), bf16[64,2,128,32]{2,3,1,0:T(8,128)(2,1)}, u32[]{:S(2)}, u32[]{:S(2)}) %all-to-all-start.1) | async-done | bytes 1048608 | tf_op jit(solution)/shard_map/all_to_all | solution.py:76
  76.2 1.8 gather_fusion.1
  78.4 1.3 convolution_add_fusion
  79.8 31.8 %reduce-scatter.2.cloned.1.call-done = f32[1024,32]{0,1:T(8,128)} async-done(((f32[1024,256]{0,1:T(8,128)}), f32[1024,32]{0,1:T(8,128)}) %reduce-scatter.2.cloned.1.call-update) | async-done | bytes 131088 | tf_op jit(solution)/shard_map/reduce_scatter | solution.py:93
  111.6 1.7 multiply_convert_fusion
  113.2 13.1 %all_gather.3 = bf16[1024,256]{0,1:T(8,128)(2,1)S(1)} all-gather(bf16[1024,32]{0,1:T(8,128)(2,1)S(1)} %get-tuple-element.35), channel_id=1, replica_groups=mesh['rows'=64,'feat'=8] {'feat'}, dimensions={1}, use_global_device_ids=true | all-gather | bytes 589824 | tf_op jit(solution)/shard_map/all_gather | solution.py:100
  127.6 13.4 %all-to-all-start.3 = ((f32[64,1,256]{2,1,0:T(1,128)}), f32[64,1,256]{2,1,0:T(1,128)S(1)}, u32[]{:S(2)}, u32[]{:S(2)}) async-start(f32[64,1,256]{2,1,0:T(1,128)} %copy.108), calls=%async_computation.4 | async-start | bytes 131072 | tf_op jit(solution)/shard_map/all_to_all | solution.py:29
  141.2 11.1 %all-to-all-done.3 = f32[64,1,256]{2,1,0:T(1,128)S(1)} async-done(((f32[64,1,256]{2,1,0:T(1,128)}), f32[64,1,256]{2,1,0:T(1,128)S(1)}, u32[]{:S(2)}, u32[]{:S(2)}) %all-to-all-start.3) | async-done | bytes 65568 | tf_op jit(solution)/shard_map/all_to_all | solution.py:29
  153.1 5.4 %all-to-all-start.4 = ((f32[64,1,256]{2,1,0:T(1,128)}), f32[64,1,256]{2,1,0:T(1,128)S(1)}, u32[]{:S(2)}, u32[]{:S(2)}) async-start(f32[64,1,256]{2,1,0:T(1,128)} %broadcast_in_dim.66), calls=%async_computation.5 | async-start | bytes 131072 | tf_op jit(solution)/shard_map/all_to_all | solution.py:32
  161.5 8.5 %all-to-all-done.4 = f32[64,1,256]{2,1,0:T(1,128)S(1)} async-done(((f32[64,1,256]{2,1,0:T(1,128)}), f32[64,1,256]{2,1,0:T(1,128)S(1)}, u32[]{:S(2)}, u32[]{:S(2)}) %all-to-all-start.4) | async-done | bytes 65568 | tf_op jit(solution)/shard_map/all_to_all | solution.py:32
  170.0 5.4 %all-to-all-start.2 = ((bf16[64,2,128,32]{2,3,1,0:T(8,128)(2,1)}), bf16[64,2,128,32]{2,3,1,0:T(8,128)(2,1)S(1)}, u32[]{:S(2)}, u32[]{:S(2)}) async-start(bf16[64,2,128,32]{2,3,1,0:T(8,128)(2,1)} %bitcast.99), calls=%async_computation.3 | async-start | bytes 2097152 | tf_op jit(solution)/shard_map/all_to_all | solution.py:131
  176.0 3.4 %collective-permute-start.2 = (f32[128,32]{0,1:T(8,128)S(1)}, f32[128,32]{0,1:T(8,128)S(1)}, u32[]{:S(2)}, u32[]{:S(2)}) collective-permute-start(f32[128,32]{0,1:T(8,128)S(1)} %get-tuple-element.31), channel_id=1, source_target_pairs={{0,8},{8,16},{16,24},{24,32},{32,40},{40,48},{48,56},{56,64},{64,7... | collective-permute-start | bytes 49160 | tf_op jit(solution)/shard_map/ppermute | solution.py:23
  179.4 2.6 %collective-permute-start.3 = (f32[128,32]{0,1:T(8,128)S(1)}, f32[128,32]{0,1:T(8,128)S(1)}, u32[]{:S(2)}, u32[]{:S(2)}) collective-permute-start(f32[128,32]{0,1:T(8,128)S(1)} %get-tuple-element.30), channel_id=1, source_target_pairs={{8,0},{16,8},{24,16},{32,24},{40,32},{48,40},{56,48},{64,56},{72,6... | collective-permute-start | bytes 49160 | tf_op jit(solution)/shard_map/ppermute | solution.py:23
  183.3 20.3 %all-to-all-done.2 = bf16[64,2,128,32]{2,3,1,0:T(8,128)(2,1)S(1)} async-done(((bf16[64,2,128,32]{2,3,1,0:T(8,128)(2,1)}), bf16[64,2,128,32]{2,3,1,0:T(8,128)(2,1)S(1)}, u32[]{:S(2)}, u32[]{:S(2)}) %all-to-all-start.2) | async-done | bytes 1048608 | tf_op jit(solution)/shard_map/all_to_all | solution.py:131
  203.7 4.1 %copy.106 = f32[64,2,128,32]{3,2,1,0:T(8,128)} copy(bf16[64,2,128,32]{2,3,1,0:T(8,128)(2,1)S(1)} %all-to-all-done.2) | data formatting | bytes 3145728 | tf_op jit(solution)/shard_map/reshape | solution.py:141
  207.8 6.3 %reshape.294 = f32[128,4096]{1,0:T(8,128)S(1)} reshape(f32[64,2,128,32]{3,2,1,0:T(8,128)} %copy.106) | data formatting | bytes 4194304 | tf_op jit(solution)/shard_map/reshape | solution.py:141
  214.0 3.3 %scatter_custom_fusion.1 = f32[8,4096]{1,0:T(8,128)S(1)} fusion(s32[128]{0:T(128)S(1)} %fusion.32, f32[128,4096]{1,0:T(8,128)S(1)} %reshape.294, f32[]{:T(128)} %constant.91.clone.1), kind=kCustom, calls=%fused_computation.49 | custom fusion | flops 524288 | bytes 131076 | tf_op jit(solution)/shard_map/scatter-add | solution.py:140
  (91 shorter events, 18.6 us)
Async XLA Ops:
  7.2 71.3 %copy-start = (bf16[256,256]{1,0:T(8,128)(2,1)S(1)}, bf16[256,256]{1,0:T(8,128)(2,1)}, u32[]{:S(2)}) copy-start(bf16[256,256]{1,0:T(8,128)(2,1)} %param.19) | copy-start | bytes 393220
  10.0 27.5 %all-to-all-start = ((s32[64,1,2]{2,1,0:T(1,128)}), s32[64,1,2]{2,1,0:T(1,128)S(1)}, u32[]{:S(2)}, u32[]{:S(2)}) async-start(s32[64,1,2]{2,1,0:T(1,128)} %bitcast.2), calls=%async_computation | async-start | bytes 65536 | tf_op jit(solution)/shard_map/all_to_all | solution.py:69
  40.0 7.7 %copy-start.5 = (bf16[1024,32]{0,1:T(8,128)(2,1)S(1)}, bf16[1024,32]{0,1:T(8,128)(2,1)}, u32[]{:S(2)}) copy-start(bf16[1024,32]{0,1:T(8,128)(2,1)} %param.13) | copy-start | bytes 196612
  40.0 13.5 %copy-start.8 = (s32[8,2]{0,1:T(2,128)S(1)}, s32[8,2]{0,1:T(2,128)}, u32[]{:S(2)}) copy-start(s32[8,2]{0,1:T(2,128)} %param.16) | copy-start | bytes 196
  40.0 13.7 %copy-start.2 = (bf16[1024,256]{1,0:T(8,128)(2,1)S(1)}, bf16[1024,256]{1,0:T(8,128)(2,1)}, u32[]{:S(2)}) copy-start(bf16[1024,256]{1,0:T(8,128)(2,1)} %param.15) | copy-start | bytes 1572868
  40.0 13.9 %copy-start.1 = (bf16[1024,384]{1,0:T(8,128)(2,1)S(1)}, bf16[1024,384]{1,0:T(8,128)(2,1)}, u32[]{:S(2)}) copy-start(bf16[1024,384]{1,0:T(8,128)(2,1)} %param.14) | copy-start | bytes 2359300
  41.3 34.9 %all-to-all-start.1 = ((bf16[64,2,128,32]{2,3,1,0:T(8,128)(2,1)}), bf16[64,2,128,32]{2,3,1,0:T(8,128)(2,1)}, u32[]{:S(2)}, u32[]{:S(2)}) async-start(bf16[64,2,128,32]{2,3,1,0:T(8,128)(2,1)} %broadcast_select_fusion), calls=%async_computation.1 | async-start | bytes 2097152 | tf_op jit(solution)/shard_map/all_to_all | solution.py:76
  47.6 64.0 %reduce-scatter.2.cloned.1.call-start = ((), (), s32[]{:S(2)}) async-start(), calls=%async_computation.6 | async-start | bytes 1179648 | tf_op jit(solution)/shard_map/reduce_scatter | solution.py:93
  47.7 20.6 %collective-permute-start = (bf16[128,32]{0,1:T(8,128)(2,1)S(1)}, bf16[128,32]{0,1:T(8,128)(2,1)S(1)}, u32[]{:S(2)}, u32[]{:S(2)}) collective-permute-start(bf16[128,32]{0,1:T(8,128)(2,1)S(1)} %get-tuple-element.41), channel_id=1, source_target_pairs={{0,8},{8,16},{16,24},{24,32},{32,40},{40,48},{48,56},{56,64},{64,7... | collective-permute-start | bytes 24584 | tf_op jit(solution)/shard_map/ppermute | solution.py:12
  51.1 18.3 %collective-permute-start.1 = (bf16[128,32]{0,1:T(8,128)(2,1)S(1)}, bf16[128,32]{0,1:T(8,128)(2,1)S(1)}, u32[]{:S(2)}, u32[]{:S(2)}) collective-permute-start(bf16[128,32]{0,1:T(8,128)(2,1)S(1)} %get-tuple-element.42), channel_id=1, source_target_pairs={{8,0},{16,8},{24,16},{32,24},{40,32},{48,40},{56,48},{64,56},{72,6... | collective-permute-start | bytes 24584 | tf_op jit(solution)/shard_map/ppermute | solution.py:15
  78.1 33.4 %copy-start.7 = (bf16[1024,32]{0,1:T(8,128)(2,1)S(1)}, bf16[1024,32]{0,1:T(8,128)(2,1)}, u32[]{:S(2)}) copy-start(bf16[1024,32]{0,1:T(8,128)(2,1)} %param.21) | copy-start | bytes 196612
  78.1 33.4 %copy-start.9 = (f32[32]{0:T(128)S(1)}, f32[32]{0:T(128)}, u32[]{:S(2)}) copy-start(f32[32]{0:T(128)} %param.20) | copy-start | bytes 388
  126.3 32.6 %copy-start.3 = (bf16[1024,256]{0,1:T(8,128)(2,1)}, bf16[1024,256]{0,1:T(8,128)(2,1)S(1)}, u32[]{:S(2)}) copy-start(bf16[1024,256]{0,1:T(8,128)(2,1)S(1)} %all_gather.3) | copy-start | bytes 1572868
  127.6 24.8 %all-to-all-start.3 = ((f32[64,1,256]{2,1,0:T(1,128)}), f32[64,1,256]{2,1,0:T(1,128)S(1)}, u32[]{:S(2)}, u32[]{:S(2)}) async-start(f32[64,1,256]{2,1,0:T(1,128)} %copy.108), calls=%async_computation.4 | async-start | bytes 131072 | tf_op jit(solution)/shard_map/all_to_all | solution.py:29
  153.1 16.9 %all-to-all-start.4 = ((f32[64,1,256]{2,1,0:T(1,128)}), f32[64,1,256]{2,1,0:T(1,128)S(1)}, u32[]{:S(2)}, u32[]{:S(2)}) async-start(f32[64,1,256]{2,1,0:T(1,128)} %broadcast_in_dim.66), calls=%async_computation.5 | async-start | bytes 131072 | tf_op jit(solution)/shard_map/all_to_all | solution.py:32
  170.0 33.7 %all-to-all-start.2 = ((bf16[64,2,128,32]{2,3,1,0:T(8,128)(2,1)}), bf16[64,2,128,32]{2,3,1,0:T(8,128)(2,1)S(1)}, u32[]{:S(2)}, u32[]{:S(2)}) async-start(bf16[64,2,128,32]{2,3,1,0:T(8,128)(2,1)} %bitcast.99), calls=%async_computation.3 | async-start | bytes 2097152 | tf_op jit(solution)/shard_map/all_to_all | solution.py:131
  176.0 42.6 %collective-permute-start.2 = (f32[128,32]{0,1:T(8,128)S(1)}, f32[128,32]{0,1:T(8,128)S(1)}, u32[]{:S(2)}, u32[]{:S(2)}) collective-permute-start(f32[128,32]{0,1:T(8,128)S(1)} %get-tuple-element.31), channel_id=1, source_target_pairs={{0,8},{8,16},{16,24},{24,32},{32,40},{40,48},{48,56},{56,64},{64,7... | collective-permute-start | bytes 49160 | tf_op jit(solution)/shard_map/ppermute | solution.py:23
  179.4 39.3 %collective-permute-start.3 = (f32[128,32]{0,1:T(8,128)S(1)}, f32[128,32]{0,1:T(8,128)S(1)}, u32[]{:S(2)}, u32[]{:S(2)}) collective-permute-start(f32[128,32]{0,1:T(8,128)S(1)} %get-tuple-element.30), channel_id=1, source_target_pairs={{8,0},{16,8},{24,16},{32,24},{40,32},{48,40},{56,48},{64,56},{72,6... | collective-permute-start | bytes 49160 | tf_op jit(solution)/shard_map/ppermute | solution.py:23
  207.8 9.9 %copy-start.4 = (bf16[1024,256]{0,1:T(8,128)(2,1)S(1)}, bf16[1024,256]{0,1:T(8,128)(2,1)}, u32[]{:S(2)}) copy-start(bf16[1024,256]{0,1:T(8,128)(2,1)} %copy-done.3) | copy-start | bytes 1572868
  218.6 0.7 copy-start.6
Sparse Core Ops, SparseCore 0:
  79.9 31.6 reduce-scatter.1

commit v2 on v0

--- a/solution.py
+++ b/solution.py
@@ -91,9 +91,6 @@
     grad_scale = float(rows_dev * peer_count) ** (-0.5)
     part_self = jnp.einsum("rc,rf->cf", node_feats, full_grad, preferred_element_type=jnp.float32)
     part_neigh = jnp.einsum("rc,rf->cf", neighbours, full_grad, preferred_element_type=jnp.float32)
-    sum_self, sum_neigh = lax.psum((part_self, part_neigh), "rows")
-    grad_self = sum_self * grad_scale
-    grad_neigh = sum_neigh * grad_scale
     dense_grad = jnp.einsum("rf,cf->rc", full_grad, rows_self, preferred_element_type=jnp.float32)
     grad_agg = jnp.einsum("rf,cf->rc", full_grad, rows_neigh, preferred_element_type=jnp.float32)
     grad_neighbours = (grad_agg / degree[:, None]).astype(jnp.bfloat16)
@@ -118,13 +115,17 @@
     )
     returning = jnp.zeros((peer_count * capacity, tile_size, col_count), jnp.float32)
     returning = returning.at[slot_ids].set(grad_fetched.reshape(entries, tile_size, col_count))
-    returned = lax.all_to_all(
-        returning.reshape(peer_count, capacity, tile_size, col_count).astype(jnp.bfloat16),
-        "rows",
-        split_axis=0,
-        concat_axis=0,
-        tiled=True,
-    ).astype(jnp.float32)
+    partials = jnp.stack([part_self, part_neigh]).reshape(peer_count, -1)
+    payload = jnp.concatenate([returning.reshape(peer_count, -1), partials], axis=1)
+    arrived = lax.all_to_all(payload, "rows", split_axis=0, concat_axis=0, tiled=True)
+    returned = arrived[:, : capacity * tile_size * col_count]
+    mine = jnp.sum(arrived[:, capacity * tile_size * col_count :], axis=0, keepdims=True)
+    whole = lax.all_to_all(
+        jnp.broadcast_to(mine, partials.shape), "rows", split_axis=0, concat_axis=0, tiled=True
+    )
+    sum_self, sum_neigh = whole.reshape(2, col_count, -1)
+    grad_self = sum_self * grad_scale
+    grad_neigh = sum_neigh * grad_scale
     target_block = jnp.where(usable, wanted, blocks).reshape(-1)
     owed = jnp.zeros((blocks, tile_size * col_count), jnp.float32)
     owed = owed.at[target_block].add(

time: 328 us -> 250 us (0.76); the launches traced: 323 us -> 249 us
  waiting for transfers between devices: 209 us -> 121 us
  starting transfers between devices: 44.3 us -> 57.4 us
  local copies, waits for them, and re-layouts: 20.8 us -> 26.6 us
  other arithmetic: 13.6 us -> 9.82 us
    psum x1 -> x0, waiting for transfers between devices: 145 us -> none  [on_device(): sum_self, sum_neigh = lax.psum((part_self, part_neigh), 'rows')]
    all_to_all x1 -> x2, waiting for transfers between devices: 0.01 us -> 56.8 us  [the longest x1 46.7 us: on_device(): lax.all_to_all(payload, 'rows', split_axis=0, concat_axis=0, tiled=True)]
    all_to_all x1 -> x2, starting transfers between devices: 13.2 us -> 26.7 us  [the longest x1 13.5 us: on_device(): lax.all_to_all(jnp.broadcast_to(mine, partials.shape), 'rows', split_axis...]
    reshape x2 -> x1, local copies, waits for them, and re-layouts: 10.3 us -> 1.51 us  [on_device(): returned.reshape(peer_count * capacity, tile_size * col_count)]
    reshape x0 -> x1, local copies, waits for them, and re-layouts: none -> 6.22 us  [on_device(): returning.reshape(peer_count, -1)]
    scatter x1 -> x2, local copies, waits for them, and re-layouts: 1.04 us -> 5.67 us  [on_device(): returning.at[slot_ids]]
    all_to_all x0 -> x1, local copies, waits for them, and re-layouts: none -> 3.59 us  [on_device(): lax.all_to_all(payload, 'rows', split_axis=0, concat_axis=0, tiled=True)]
  transfers between devices with their start and end apart: 9 -> 9, of which waited for: 6 -> 7; matrix products, arithmetic and copies ran while one was open for 7% -> 5% of each run, Pallas kernels for 0% -> 0%
where the time goes in v2:
time: 250 us; the launch traced here: 249 us
  waiting for transfers between devices  121 us (48%)
  starting transfers between devices  57.4 us (23%)
  local copies, waits for them, and re-layouts  26.6 us (11%)
  blocking collectives  15.2 us (6%)
  between operations  14.5 us (6%)
  other arithmetic  9.82 us (4%)
  matrix products  5.09 us (2%)
    all_to_all x1, waiting for transfers between devices, on_device(): lax.all_to_all(payload, 'rows', split_axis=0, concat_axis=0, tiled=True)  46.7 us
    reduce_scatter x1, waiting for transfers between devices, on_device(): preact = lax.psum_scatter(terms, 'feat', scatter_dimension=1, tiled=True)  34.5 us
    all_to_all x1, starting transfers between devices, on_device(): lax.all_to_all(request, 'rows', split_axis=0, concat_axis=0, tiled=True)  17.1 us
    all_gather x1, blocking collectives, on_device(): full_grad = lax.all_gather(grad_pre, 'feat', axis=1, tiled=True)  15.2 us
    all_to_all x1, starting transfers between devices, on_device(): lax.all_to_all(jnp.broadcast_to(mine, partials.shape), 'rows', split_axis...  13.5 us
    all_to_all x1, starting transfers between devices, on_device(): lax.all_to_all(payload, 'rows', split_axis=0, concat_axis=0, tiled=True)  13.2 us
    ppermute x1, waiting for transfers between devices, extended(): lax.ppermute(lax.slice_in_dim(block, block.shape[dim] - width, None, axis...  11.1 us
    all_to_all x1, waiting for transfers between devices, on_device(): lax.all_to_all(jnp.broadcast_to(mine, partials.shape), 'rows', split_axis...  10.2 us
  transfers between devices with their start and end apart: 9, of which 7 were waited for; matrix products, arithmetic and copies ran while one was open for 5% of the time, Pallas kernels for 0%

profile of v2, /device:TPU:1, one launch (start us, length us, event | category | flops | bytes accessed | tf_op | source)
XLA Modules:
  0.0 249.4 jit_solution(3999616787708536443)
XLA Ops:
  10.0 17.1 %all-to-all-start = ((s32[64,1,2]{2,1,0:T(1,128)}), s32[64,1,2]{2,1,0:T(1,128)S(1)}, u32[]{:S(2)}, u32[]{:S(2)}) async-start(s32[64,1,2]{2,1,0:T(1,128)} %bitcast.2), calls=%async_computation | async-start | bytes 65536 | tf_op jit(solution)/shard_map/all_to_all | solution.py:59
  28.0 9.9 %all-to-all-done = s32[64,1,2]{2,1,0:T(1,128)S(1)} async-done(((s32[64,1,2]{2,1,0:T(1,128)}), s32[64,1,2]{2,1,0:T(1,128)S(1)}, u32[]{:S(2)}, u32[]{:S(2)}) %all-to-all-start) | async-done | bytes 544 | tf_op jit(solution)/shard_map/all_to_all | solution.py:59
  41.7 5.5 %all-to-all-start.1 = ((bf16[64,2,128,32]{2,3,1,0:T(8,128)(2,1)}), bf16[64,2,128,32]{2,3,1,0:T(8,128)(2,1)}, u32[]{:S(2)}, u32[]{:S(2)}) async-start(bf16[64,2,128,32]{2,3,1,0:T(8,128)(2,1)} %broadcast_select_fusion), calls=%async_computation.1 | async-start | bytes 2097152 | tf_op jit(solution)/shard_map/all_to_all | solution.py:66
  47.2 2.7 %collective-permute-start = (bf16[128,32]{0,1:T(8,128)(2,1)S(1)}, bf16[128,32]{0,1:T(8,128)(2,1)S(1)}, u32[]{:S(2)}, u32[]{:S(2)}) collective-permute-start(bf16[128,32]{0,1:T(8,128)(2,1)S(1)} %get-tuple-element.41), channel_id=1, source_target_pairs={{0,8},{8,16},{16,24},{24,32},{32,40},{40,48},{48,56},{56,64},{64,7... | collective-permute-start | bytes 24584 | tf_op jit(solution)/shard_map/ppermute | solution.py:12
  50.0 1.3 collective-permute-start.1
  53.0 11.1 %collective-permute-done = bf16[128,32]{0,1:T(8,128)(2,1)S(1)} collective-permute-done((bf16[128,32]{0,1:T(8,128)(2,1)S(1)}, bf16[128,32]{0,1:T(8,128)(2,1)S(1)}, u32[]{:S(2)}, u32[]{:S(2)}) %collective-permute-start) | collective-permute-done | bytes 8224 | tf_op jit(solution)/shard_map/ppermute | solution.py:12
  64.1 4.4 %collective-permute-done.1 = bf16[128,32]{0,1:T(8,128)(2,1)S(1)} collective-permute-done((bf16[128,32]{0,1:T(8,128)(2,1)S(1)}, bf16[128,32]{0,1:T(8,128)(2,1)S(1)}, u32[]{:S(2)}, u32[]{:S(2)}) %collective-permute-start.1) | collective-permute-done | bytes 8224 | tf_op jit(solution)/shard_map/ppermute | solution.py:15
  68.9 3.8 %all-to-all-done.1 = bf16[64,2,128,32]{2,3,1,0:T(8,128)(2,1)} async-done(((bf16[64,2,128,32]{2,3,1,0:T(8,128)(2,1)}), bf16[64,2,128,32]{2,3,1,0:T(8,128)(2,1)}, u32[]{:S(2)}, u32[]{:S(2)}) %all-to-all-start.1) | async-done | bytes 1048608 | tf_op jit(solution)/shard_map/all_to_all | solution.py:66
  72.8 1.8 gather_fusion.1
  75.0 1.3 convolution_add_fusion
  76.4 34.5 %reduce-scatter.2.cloned.1.call-done = f32[1024,32]{0,1:T(8,128)} async-done(((f32[1024,256]{0,1:T(8,128)}), f32[1024,32]{0,1:T(8,128)}) %reduce-scatter.2.cloned.1.call-update) | async-done | bytes 131088 | tf_op jit(solution)/shard_map/reduce_scatter | solution.py:83
  110.9 1.7 multiply_convert_fusion
  112.5 15.2 %all_gather.3 = bf16[1024,256]{0,1:T(8,128)(2,1)S(1)} all-gather(bf16[1024,32]{0,1:T(8,128)(2,1)S(1)} %get-tuple-element.35), channel_id=1, replica_groups=mesh['rows'=64,'feat'=8] {'feat'}, dimensions={1}, use_global_device_ids=true | all-gather | bytes 589824 | tf_op jit(solution)/shard_map/all_gather | solution.py:90
  130.3 4.6 %copy.106 = f32[128,128,32]{2,1,0:T(8,128)} copy(f32[128,128,32]{1,2,0:T(8,128)S(1)} %scatter_fusion) | data formatting | bytes 4194304 | tf_op jit(solution)/shard_map/scatter | solution.py:117
  135.0 6.2 %reshape.260 = f32[64,8192]{1,0:T(8,128)S(1)} reshape(f32[128,128,32]{2,1,0:T(8,128)} %copy.106) | data formatting | bytes 4194304 | tf_op jit(solution)/shard_map/reshape | solution.py:119
  141.3 3.6 %copy.107 = f32[64,1,8448]{2,1,0:T(1,128)} copy(f32[64,1,8448]{2,0,1:T(8,128)S(1)} %maximum_bitcast_fusion) | data formatting | bytes 4325376 | tf_op jit(solution)/shard_map/all_to_all | solution.py:120
  144.9 13.2 %all-to-all-start.2 = ((f32[64,1,8448]{2,1,0:T(1,128)}), f32[64,1,8448]{2,1,0:T(1,128)S(1)}, u32[]{:S(2)}, u32[]{:S(2)}) async-start(f32[64,1,8448]{2,1,0:T(1,128)} %copy.107), calls=%async_computation.3 | async-start | bytes 4325376 | tf_op jit(solution)/shard_map/all_to_all | solution.py:120
  158.7 2.7 %collective-permute-start.2 = (f32[128,32]{0,1:T(8,128)S(1)}, f32[128,32]{0,1:T(8,128)S(1)}, u32[]{:S(2)}, u32[]{:S(2)}) collective-permute-start(f32[128,32]{0,1:T(8,128)S(1)} %get-tuple-element.31), channel_id=1, source_target_pairs={{0,8},{8,16},{16,24},{24,32},{32,40},{40,48},{48,56},{56,64},{64,7... | collective-permute-start | bytes 49160 | tf_op jit(solution)/shard_map/ppermute | solution.py:23
  161.4 1.3 collective-permute-start.3
  162.7 46.7 %all-to-all-done.2 = f32[64,1,8448]{2,1,0:T(1,128)S(1)} async-done(((f32[64,1,8448]{2,1,0:T(1,128)}), f32[64,1,8448]{2,1,0:T(1,128)S(1)}, u32[]{:S(2)}, u32[]{:S(2)}) %all-to-all-start.2) | async-done | bytes 2162720 | tf_op jit(solution)/shard_map/all_to_all | solution.py:120
  209.7 1.5 reshape.292
  211.2 4.3 %scatter_custom_fusion.1 = f32[8,4096]{1,0:T(8,128)S(1)} fusion(s32[128]{0:T(128)S(1)} %fusion.32, f32[128,4096]{1,0:T(8,128)} %reshape.292, f32[]{:T(128)} %constant.91.clone.1), kind=kCustom, calls=%fused_computation.52 | custom fusion | flops 524288 | bytes 131584 | tf_op jit(solution)/shard_map/scatter-add | solution.py:131
  216.6 13.5 %all-to-all-start.3 = ((f32[64,1,256]{2,1,0:T(1,128)}), f32[64,1,256]{2,1,0:T(1,128)S(1)}, u32[]{:S(2)}, u32[]{:S(2)}) async-start(f32[64,1,256]{2,1,0:T(1,128)} %broadcast_in_dim.66), calls=%async_computation.4 | async-start | bytes 131072 | tf_op jit(solution)/shard_map/all_to_all | solution.py:123
  231.1 10.2 %all-to-all-done.3 = f32[64,1,256]{2,1,0:T(1,128)S(1)} async-done(((f32[64,1,256]{2,1,0:T(1,128)}), f32[64,1,256]{2,1,0:T(1,128)S(1)}, u32[]{:S(2)}, u32[]{:S(2)}) %all-to-all-start.3) | async-done | bytes 65568 | tf_op jit(solution)/shard_map/all_to_all | solution.py:123
  (92 shorter events, 16.6 us)
Async XLA Ops:
  7.2 67.8 %copy-start = (bf16[256,256]{1,0:T(8,128)(2,1)S(1)}, bf16[256,256]{1,0:T(8,128)(2,1)}, u32[]{:S(2)}) copy-start(bf16[256,256]{1,0:T(8,128)(2,1)} %param.19) | copy-start | bytes 393220
  10.0 27.9 %all-to-all-start = ((s32[64,1,2]{2,1,0:T(1,128)}), s32[64,1,2]{2,1,0:T(1,128)S(1)}, u32[]{:S(2)}, u32[]{:S(2)}) async-start(s32[64,1,2]{2,1,0:T(1,128)} %bitcast.2), calls=%async_computation | async-start | bytes 65536 | tf_op jit(solution)/shard_map/all_to_all | solution.py:59
  40.4 6.8 %copy-start.5 = (bf16[1024,32]{0,1:T(8,128)(2,1)S(1)}, bf16[1024,32]{0,1:T(8,128)(2,1)}, u32[]{:S(2)}) copy-start(bf16[1024,32]{0,1:T(8,128)(2,1)} %param.13) | copy-start | bytes 196612
  40.4 10.9 %copy-start.8 = (s32[8,2]{0,1:T(2,128)S(1)}, s32[8,2]{0,1:T(2,128)}, u32[]{:S(2)}) copy-start(s32[8,2]{0,1:T(2,128)} %param.16) | copy-start | bytes 196
  40.4 11.1 %copy-start.2 = (bf16[1024,256]{1,0:T(8,128)(2,1)S(1)}, bf16[1024,256]{1,0:T(8,128)(2,1)}, u32[]{:S(2)}) copy-start(bf16[1024,256]{1,0:T(8,128)(2,1)} %param.15) | copy-start | bytes 1572868
  40.4 11.3 %copy-start.1 = (bf16[1024,384]{1,0:T(8,128)(2,1)S(1)}, bf16[1024,384]{1,0:T(8,128)(2,1)}, u32[]{:S(2)}) copy-start(bf16[1024,384]{1,0:T(8,128)(2,1)} %param.14) | copy-start | bytes 2359300
  41.7 31.1 %all-to-all-start.1 = ((bf16[64,2,128,32]{2,3,1,0:T(8,128)(2,1)}), bf16[64,2,128,32]{2,3,1,0:T(8,128)(2,1)}, u32[]{:S(2)}, u32[]{:S(2)}) async-start(bf16[64,2,128,32]{2,3,1,0:T(8,128)(2,1)} %broadcast_select_fusion), calls=%async_computation.1 | async-start | bytes 2097152 | tf_op jit(solution)/shard_map/all_to_all | solution.py:66
  47.2 63.7 %reduce-scatter.2.cloned.1.call-start = ((), (), s32[]{:S(2)}) async-start(), calls=%async_computation.5 | async-start | bytes 1179648 | tf_op jit(solution)/shard_map/reduce_scatter | solution.py:83
  47.2 16.9 %collective-permute-start = (bf16[128,32]{0,1:T(8,128)(2,1)S(1)}, bf16[128,32]{0,1:T(8,128)(2,1)S(1)}, u32[]{:S(2)}, u32[]{:S(2)}) collective-permute-start(bf16[128,32]{0,1:T(8,128)(2,1)S(1)} %get-tuple-element.41), channel_id=1, source_target_pairs={{0,8},{8,16},{16,24},{24,32},{32,40},{40,48},{48,56},{56,64},{64,7... | collective-permute-start | bytes 24584 | tf_op jit(solution)/shard_map/ppermute | solution.py:12
  50.0 18.5 %collective-permute-start.1 = (bf16[128,32]{0,1:T(8,128)(2,1)S(1)}, bf16[128,32]{0,1:T(8,128)(2,1)S(1)}, u32[]{:S(2)}, u32[]{:S(2)}) collective-permute-start(bf16[128,32]{0,1:T(8,128)(2,1)S(1)} %get-tuple-element.42), channel_id=1, source_target_pairs={{8,0},{16,8},{24,16},{32,24},{40,32},{48,40},{56,48},{64,56},{72,6... | collective-permute-start | bytes 24584 | tf_op jit(solution)/shard_map/ppermute | solution.py:15
  74.7 36.2 %copy-start.7 = (bf16[1024,32]{0,1:T(8,128)(2,1)S(1)}, bf16[1024,32]{0,1:T(8,128)(2,1)}, u32[]{:S(2)}) copy-start(bf16[1024,32]{0,1:T(8,128)(2,1)} %param.21) | copy-start | bytes 196612
  74.7 36.1 %copy-start.9 = (f32[32]{0:T(128)S(1)}, f32[32]{0:T(128)}, u32[]{:S(2)}) copy-start(f32[32]{0:T(128)} %param.20) | copy-start | bytes 388
  127.8 1.1 copy-start.3
  144.9 64.5 %all-to-all-start.2 = ((f32[64,1,8448]{2,1,0:T(1,128)}), f32[64,1,8448]{2,1,0:T(1,128)S(1)}, u32[]{:S(2)}, u32[]{:S(2)}) async-start(f32[64,1,8448]{2,1,0:T(1,128)} %copy.107), calls=%async_computation.3 | async-start | bytes 4325376 | tf_op jit(solution)/shard_map/all_to_all | solution.py:120
  158.7 72.3 %collective-permute-start.2 = (f32[128,32]{0,1:T(8,128)S(1)}, f32[128,32]{0,1:T(8,128)S(1)}, u32[]{:S(2)}, u32[]{:S(2)}) collective-permute-start(f32[128,32]{0,1:T(8,128)S(1)} %get-tuple-element.31), channel_id=1, source_target_pairs={{0,8},{8,16},{16,24},{24,32},{32,40},{40,48},{48,56},{56,64},{64,7... | collective-permute-start | bytes 49160 | tf_op jit(solution)/shard_map/ppermute | solution.py:23
  161.4 69.6 %collective-permute-start.3 = (f32[128,32]{0,1:T(8,128)S(1)}, f32[128,32]{0,1:T(8,128)S(1)}, u32[]{:S(2)}, u32[]{:S(2)}) collective-permute-start(f32[128,32]{0,1:T(8,128)S(1)} %get-tuple-element.30), channel_id=1, source_target_pairs={{8,0},{16,8},{24,16},{32,24},{40,32},{48,40},{56,48},{64,56},{72,6... | collective-permute-start | bytes 49160 | tf_op jit(solution)/shard_map/ppermute | solution.py:23
  209.7 20.3 %copy-start.4 = (bf16[1024,256]{0,1:T(8,128)(2,1)S(1)}, bf16[1024,256]{0,1:T(8,128)(2,1)}, u32[]{:S(2)}) copy-start(bf16[1024,256]{0,1:T(8,128)(2,1)} %copy-done.3) | copy-start | bytes 1572868
  216.6 24.7 %all-to-all-start.3 = ((f32[64,1,256]{2,1,0:T(1,128)}), f32[64,1,256]{2,1,0:T(1,128)S(1)}, u32[]{:S(2)}, u32[]{:S(2)}) async-start(f32[64,1,256]{2,1,0:T(1,128)} %broadcast_in_dim.66), calls=%async_computation.4 | async-start | bytes 131072 | tf_op jit(solution)/shard_map/all_to_all | solution.py:123
  231.0 11.5 %copy-start.6 = (f32[1024,32]{0,1:T(8,128)}, f32[1024,32]{0,1:T(8,128)S(1)}, u32[]{:S(2)}) copy-start(f32[1024,32]{0,1:T(8,128)S(1)} %fusion.20) | copy-start | bytes 393220
Sparse Core Ops, SparseCore 0:
  76.5 34.3 reduce-scatter.1

commit v3 on v2

--- a/solution.py
+++ b/solution.py
@@ -116,10 +116,21 @@
     returning = jnp.zeros((peer_count * capacity, tile_size, col_count), jnp.float32)
     returning = returning.at[slot_ids].set(grad_fetched.reshape(entries, tile_size, col_count))
     partials = jnp.stack([part_self, part_neigh]).reshape(peer_count, -1)
-    payload = jnp.concatenate([returning.reshape(peer_count, -1), partials], axis=1)
+    high = partials.astype(jnp.bfloat16)
+    low = (partials - high.astype(jnp.float32)).astype(jnp.bfloat16)
+    span = capacity * tile_size * col_count
+    payload = jnp.concatenate(
+        [returning.reshape(peer_count, -1).astype(jnp.bfloat16), high, low], axis=1
+    )
     arrived = lax.all_to_all(payload, "rows", split_axis=0, concat_axis=0, tiled=True)
-    returned = arrived[:, : capacity * tile_size * col_count]
-    mine = jnp.sum(arrived[:, capacity * tile_size * col_count :], axis=0, keepdims=True)
+    returned = arrived[:, :span].astype(jnp.float32)
+    width = partials.shape[1]
+    mine = jnp.sum(
+        arrived[:, span : span + width].astype(jnp.float32)
+        + arrived[:, span + width :].astype(jnp.float32),
+        axis=0,
+        keepdims=True,
+    )
     whole = lax.all_to_all(
         jnp.broadcast_to(mine, partials.shape), "rows", split_axis=0, concat_axis=0, tiled=True
     )

time: 250 us -> 230 us (0.920)
  waiting for transfers between devices: 121 us -> 98.3 us
  starting transfers between devices: 57.4 us -> 52.5 us
  local copies, waits for them, and re-layouts: 26.6 us -> 30.7 us
  other arithmetic: 9.82 us -> 12.6 us
    all_to_all x1, waiting for transfers between devices: 46.7 us -> 24.5 us  [on_device(): lax.all_to_all(payload, 'rows', split_axis=0, concat_axis=0, tiled=True)]
    convert_element_type x0 -> x2, local copies, waits for them, and re-layouts: none -> 10.4 us  [on_device(): returning.reshape(peer_count, -1).astype(jnp.bfloat16)]
    unnamed x25 -> x27, local copies, waits for them, and re-layouts: 2.24 us -> 9.95 us
    reshape x1 -> x0, local copies, waits for them, and re-layouts: 6.22 us -> none  [on_device(): returning.reshape(peer_count, -1)]
    all_to_all x1, starting transfers between devices: 13.5 us -> 8.18 us  [on_device(): lax.all_to_all(jnp.broadcast_to(mine, partials.shape), 'rows', split_axis...]
    scatter x2 -> x1, local copies, waits for them, and re-layouts: 5.67 us -> 1.04 us  [on_device(): returning.at[slot_ids]]
    all_to_all x1, local copies, waits for them, and re-layouts: 3.59 us -> 0.51 us  [on_device(): lax.all_to_all(payload, 'rows', split_axis=0, concat_axis=0, tiled=True)]
  transfers between devices with their start and end apart: 9 -> 9, of which waited for: 7 -> 7; matrix products, arithmetic and copies ran while one was open for 5% -> 8% of each run, Pallas kernels for 0% -> 0%
where the time goes in v3:
time: 230 us; the launch traced here: 229 us
  waiting for transfers between devices  98.3 us (43%)
  starting transfers between devices  52.5 us (23%)
  local copies, waits for them, and re-layouts  30.7 us (13%)
  blocking collectives  15.2 us (7%)
  between operations  14.6 us (6%)
  other arithmetic  12.6 us (5%)
  matrix products  5.1 us (2%)
    reduce_scatter x1, waiting for transfers between devices, on_device(): preact = lax.psum_scatter(terms, 'feat', scatter_dimension=1, tiled=True)  34.5 us
    all_to_all x1, waiting for transfers between devices, on_device(): lax.all_to_all(payload, 'rows', split_axis=0, concat_axis=0, tiled=True)  24.5 us
    all_to_all x1, starting transfers between devices, on_device(): lax.all_to_all(request, 'rows', split_axis=0, concat_axis=0, tiled=True)  17.1 us
    all_gather x1, blocking collectives, on_device(): full_grad = lax.all_gather(grad_pre, 'feat', axis=1, tiled=True)  15.2 us
    all_to_all x1, starting transfers between devices, on_device(): lax.all_to_all(payload, 'rows', split_axis=0, concat_axis=0, tiled=True)  13.3 us
    ppermute x1, waiting for transfers between devices, extended(): lax.ppermute(lax.slice_in_dim(block, block.shape[dim] - width, None, axis...  11.1 us
    convert_element_type x2, local copies, waits for them, and re-layouts, on_device(): returning.reshape(peer_count, -1).astype(jnp.bfloat16)  10.4 us
    all_to_all x1, waiting for transfers between devices, on_device(): lax.all_to_all(jnp.broadcast_to(mine, partials.shape), 'rows', split_axis...  10.1 us
  transfers between devices with their start and end apart: 9, of which 7 were waited for; matrix products, arithmetic and copies ran while one was open for 8% of the time, Pallas kernels for 0%

profile of v3, /device:TPU:1, one launch (start us, length us, event | category | flops | bytes accessed | tf_op | source)
XLA Modules:
  0.0 229.1 jit_solution(16054193042658450072)
XLA Ops:
  10.0 17.1 %all-to-all-start = ((s32[64,1,2]{2,1,0:T(1,128)}), s32[64,1,2]{2,1,0:T(1,128)S(1)}, u32[]{:S(2)}, u32[]{:S(2)}) async-start(s32[64,1,2]{2,1,0:T(1,128)} %bitcast.2), calls=%async_computation | async-start | bytes 65536 | tf_op jit(solution)/shard_map/all_to_all | solution.py:59
  28.0 9.9 %all-to-all-done = s32[64,1,2]{2,1,0:T(1,128)S(1)} async-done(((s32[64,1,2]{2,1,0:T(1,128)}), s32[64,1,2]{2,1,0:T(1,128)S(1)}, u32[]{:S(2)}, u32[]{:S(2)}) %all-to-all-start) | async-done | bytes 544 | tf_op jit(solution)/shard_map/all_to_all | solution.py:59
  41.7 5.5 %all-to-all-start.1 = ((bf16[64,2,128,32]{2,3,1,0:T(8,128)(2,1)}), bf16[64,2,128,32]{2,3,1,0:T(8,128)(2,1)}, u32[]{:S(2)}, u32[]{:S(2)}) async-start(bf16[64,2,128,32]{2,3,1,0:T(8,128)(2,1)} %broadcast_select_fusion), calls=%async_computation.1 | async-start | bytes 2097152 | tf_op jit(solution)/shard_map/all_to_all | solution.py:66
  47.3 2.7 %collective-permute-start = (bf16[128,32]{0,1:T(8,128)(2,1)S(1)}, bf16[128,32]{0,1:T(8,128)(2,1)S(1)}, u32[]{:S(2)}, u32[]{:S(2)}) collective-permute-start(bf16[128,32]{0,1:T(8,128)(2,1)S(1)} %get-tuple-element.43), channel_id=1, source_target_pairs={{0,8},{8,16},{16,24},{24,32},{32,40},{40,48},{48,56},{56,64},{64,7... | collective-permute-start | bytes 24584 | tf_op jit(solution)/shard_map/ppermute | solution.py:12
  53.0 11.1 %collective-permute-done = bf16[128,32]{0,1:T(8,128)(2,1)S(1)} collective-permute-done((bf16[128,32]{0,1:T(8,128)(2,1)S(1)}, bf16[128,32]{0,1:T(8,128)(2,1)S(1)}, u32[]{:S(2)}, u32[]{:S(2)}) %collective-permute-start) | collective-permute-done | bytes 8224 | tf_op jit(solution)/shard_map/ppermute | solution.py:12
  64.1 4.4 %collective-permute-done.1 = bf16[128,32]{0,1:T(8,128)(2,1)S(1)} collective-permute-done((bf16[128,32]{0,1:T(8,128)(2,1)S(1)}, bf16[128,32]{0,1:T(8,128)(2,1)S(1)}, u32[]{:S(2)}, u32[]{:S(2)}) %collective-permute-start.1) | collective-permute-done | bytes 8224 | tf_op jit(solution)/shard_map/ppermute | solution.py:15
  69.0 3.8 %all-to-all-done.1 = bf16[64,2,128,32]{2,3,1,0:T(8,128)(2,1)} async-done(((bf16[64,2,128,32]{2,3,1,0:T(8,128)(2,1)}), bf16[64,2,128,32]{2,3,1,0:T(8,128)(2,1)}, u32[]{:S(2)}, u32[]{:S(2)}) %all-to-all-start.1) | async-done | bytes 1048608 | tf_op jit(solution)/shard_map/all_to_all | solution.py:66
  72.8 1.8 gather_fusion.1
  75.0 1.3 convolution_add_fusion
  76.4 34.5 %reduce-scatter.2.cloned.1.call-done = f32[1024,32]{0,1:T(8,128)} async-done(((f32[1024,256]{0,1:T(8,128)}), f32[1024,32]{0,1:T(8,128)}) %reduce-scatter.2.cloned.1.call-update) | async-done | bytes 131088 | tf_op jit(solution)/shard_map/reduce_scatter | solution.py:83
  110.8 1.7 multiply_convert_fusion
  112.5 15.2 %all_gather.3 = bf16[1024,256]{0,1:T(8,128)(2,1)S(1)} all-gather(bf16[1024,32]{0,1:T(8,128)(2,1)S(1)} %get-tuple-element.37), channel_id=1, replica_groups=mesh['rows'=64,'feat'=8] {'feat'}, dimensions={1}, use_global_device_ids=true | all-gather | bytes 589824 | tf_op jit(solution)/shard_map/all_gather | solution.py:90
  131.5 4.6 %copy.129 = bf16[128,128,32]{2,1,0:T(8,128)(2,1)} copy(bf16[128,128,32]{1,2,0:T(8,128)(2,1)} %convert_element_type.56) | data formatting | bytes 2097152 | tf_op jit(solution)/shard_map/convert_element_type | solution.py:123
  136.1 5.9 %convert_element_type.57 = bf16[64,8192]{1,0:T(8,128)(2,1)S(1)} reshape(bf16[128,128,32]{2,1,0:T(8,128)(2,1)} %copy.129) | data formatting | bytes 2097152 | tf_op jit(solution)/shard_map/convert_element_type | solution.py:123
  142.6 1.5 reduce.13
  145.2 13.3 %all-to-all-start.2 = ((bf16[64,2,4352]{2,1,0:T(2,128)(2,1)}), bf16[64,2,4352]{2,1,0:T(2,128)(2,1)}, u32[]{:S(2)}, u32[]{:S(2)}) async-start(bf16[64,2,4352]{2,1,0:T(2,128)(2,1)} %reshape.319), calls=%async_computation.3 | async-start | bytes 2228224 | tf_op jit(solution)/shard_map/all_to_all | solution.py:125
  159.1 2.9 %collective-permute-start.2 = (f32[128,32]{0,1:T(8,128)S(1)}, f32[128,32]{0,1:T(8,128)S(1)}, u32[]{:S(2)}, u32[]{:S(2)}) collective-permute-start(f32[128,32]{0,1:T(8,128)S(1)} %get-tuple-element.33), channel_id=1, source_target_pairs={{0,8},{8,16},{16,24},{24,32},{32,40},{40,48},{48,56},{56,64},{64,7... | collective-permute-start | bytes 49160 | tf_op jit(solution)/shard_map/ppermute | solution.py:23
  161.9 1.5 collective-permute-start.3
  163.4 24.5 %all-to-all-done.2 = bf16[64,2,4352]{2,1,0:T(2,128)(2,1)} async-done(((bf16[64,2,4352]{2,1,0:T(2,128)(2,1)}), bf16[64,2,4352]{2,1,0:T(2,128)(2,1)}, u32[]{:S(2)}, u32[]{:S(2)}) %all-to-all-start.2) | async-done | bytes 1114144 | tf_op jit(solution)/shard_map/all_to_all | solution.py:125
  187.9 6.5 %reshape.320 = bf16[64,1,8704]{2,1,0:T(2,128)(2,1)S(1)} reshape(bf16[64,2,4352]{2,1,0:T(2,128)(2,1)} %all-to-all-done.2) | data formatting | bytes 2228224
  194.8 1.5 reshape.296
  196.3 4.3 %scatter_custom_fusion.1 = f32[8,4096]{1,0:T(8,128)S(1)} fusion(s32[128]{0:T(128)S(1)} %fusion.33, f32[128,4096]{1,0:T(8,128)} %reshape.296, f32[]{:T(128)} %constant.91.clone.1), kind=kCustom, calls=%fused_computation.56 | custom fusion | flops 524288 | bytes 131584 | tf_op jit(solution)/shard_map/scatter-add | solution.py:142
  201.6 8.2 %all-to-all-start.3 = ((f32[64,1,256]{2,1,0:T(1,128)}), f32[64,1,256]{2,1,0:T(1,128)S(1)}, u32[]{:S(2)}, u32[]{:S(2)}) async-start(f32[64,1,256]{2,1,0:T(1,128)} %broadcast_in_dim.66), calls=%async_computation.4 | async-start | bytes 131072 | tf_op jit(solution)/shard_map/all_to_all | solution.py:134
  210.8 10.1 %all-to-all-done.3 = f32[64,1,256]{2,1,0:T(1,128)S(1)} async-done(((f32[64,1,256]{2,1,0:T(1,128)}), f32[64,1,256]{2,1,0:T(1,128)S(1)}, u32[]{:S(2)}, u32[]{:S(2)}) %all-to-all-start.3) | async-done | bytes 65568 | tf_op jit(solution)/shard_map/all_to_all | solution.py:134
  (97 shorter events, 20.7 us)
Async XLA Ops:
  7.2 67.9 %copy-start = (bf16[256,256]{1,0:T(8,128)(2,1)S(1)}, bf16[256,256]{1,0:T(8,128)(2,1)}, u32[]{:S(2)}) copy-start(bf16[256,256]{1,0:T(8,128)(2,1)} %param.19) | copy-start | bytes 393220
  10.0 27.9 %all-to-all-start = ((s32[64,1,2]{2,1,0:T(1,128)}), s32[64,1,2]{2,1,0:T(1,128)S(1)}, u32[]{:S(2)}, u32[]{:S(2)}) async-start(s32[64,1,2]{2,1,0:T(1,128)} %bitcast.2), calls=%async_computation | async-start | bytes 65536 | tf_op jit(solution)/shard_map/all_to_all | solution.py:59
  40.4 6.9 %copy-start.5 = (bf16[1024,32]{0,1:T(8,128)(2,1)S(1)}, bf16[1024,32]{0,1:T(8,128)(2,1)}, u32[]{:S(2)}) copy-start(bf16[1024,32]{0,1:T(8,128)(2,1)} %param.13) | copy-start | bytes 196612
  40.4 10.9 %copy-start.8 = (s32[8,2]{0,1:T(2,128)S(1)}, s32[8,2]{0,1:T(2,128)}, u32[]{:S(2)}) copy-start(s32[8,2]{0,1:T(2,128)} %param.16) | copy-start | bytes 196
  40.4 11.1 %copy-start.2 = (bf16[1024,256]{1,0:T(8,128)(2,1)S(1)}, bf16[1024,256]{1,0:T(8,128)(2,1)}, u32[]{:S(2)}) copy-start(bf16[1024,256]{1,0:T(8,128)(2,1)} %param.15) | copy-start | bytes 1572868
  40.4 11.3 %copy-start.1 = (bf16[1024,384]{1,0:T(8,128)(2,1)S(1)}, bf16[1024,384]{1,0:T(8,128)(2,1)}, u32[]{:S(2)}) copy-start(bf16[1024,384]{1,0:T(8,128)(2,1)} %param.14) | copy-start | bytes 2359300
  41.7 31.1 %all-to-all-start.1 = ((bf16[64,2,128,32]{2,3,1,0:T(8,128)(2,1)}), bf16[64,2,128,32]{2,3,1,0:T(8,128)(2,1)}, u32[]{:S(2)}, u32[]{:S(2)}) async-start(bf16[64,2,128,32]{2,3,1,0:T(8,128)(2,1)} %broadcast_select_fusion), calls=%async_computation.1 | async-start | bytes 2097152 | tf_op jit(solution)/shard_map/all_to_all | solution.py:66
  47.2 63.6 %reduce-scatter.2.cloned.1.call-start = ((), (), s32[]{:S(2)}) async-start(), calls=%async_computation.5 | async-start | bytes 1179648 | tf_op jit(solution)/shard_map/reduce_scatter | solution.py:83
  47.3 16.9 %collective-permute-start = (bf16[128,32]{0,1:T(8,128)(2,1)S(1)}, bf16[128,32]{0,1:T(8,128)(2,1)S(1)}, u32[]{:S(2)}, u32[]{:S(2)}) collective-permute-start(bf16[128,32]{0,1:T(8,128)(2,1)S(1)} %get-tuple-element.43), channel_id=1, source_target_pairs={{0,8},{8,16},{16,24},{24,32},{32,40},{40,48},{48,56},{56,64},{64,7... | collective-permute-start | bytes 24584 | tf_op jit(solution)/shard_map/ppermute | solution.py:12
  50.0 18.5 %collective-permute-start.1 = (bf16[128,32]{0,1:T(8,128)(2,1)S(1)}, bf16[128,32]{0,1:T(8,128)(2,1)S(1)}, u32[]{:S(2)}, u32[]{:S(2)}) collective-permute-start(bf16[128,32]{0,1:T(8,128)(2,1)S(1)} %get-tuple-element.44), channel_id=1, source_target_pairs={{8,0},{16,8},{24,16},{32,24},{40,32},{48,40},{56,48},{64,56},{72,6... | collective-permute-start | bytes 24584 | tf_op jit(solution)/shard_map/ppermute | solution.py:15
  74.7 36.1 %copy-start.7 = (bf16[1024,32]{0,1:T(8,128)(2,1)S(1)}, bf16[1024,32]{0,1:T(8,128)(2,1)}, u32[]{:S(2)}) copy-start(bf16[1024,32]{0,1:T(8,128)(2,1)} %param.21) | copy-start | bytes 196612
  74.7 36.1 %copy-start.9 = (f32[32]{0:T(128)S(1)}, f32[32]{0:T(128)}, u32[]{:S(2)}) copy-start(f32[32]{0:T(128)} %param.20) | copy-start | bytes 388
  127.7 1.0 copy-start.3
  145.2 42.7 %all-to-all-start.2 = ((bf16[64,2,4352]{2,1,0:T(2,128)(2,1)}), bf16[64,2,4352]{2,1,0:T(2,128)(2,1)}, u32[]{:S(2)}, u32[]{:S(2)}) async-start(bf16[64,2,4352]{2,1,0:T(2,128)(2,1)} %reshape.319), calls=%async_computation.3 | async-start | bytes 2228224 | tf_op jit(solution)/shard_map/all_to_all | solution.py:125
  159.1 51.7 %collective-permute-start.2 = (f32[128,32]{0,1:T(8,128)S(1)}, f32[128,32]{0,1:T(8,128)S(1)}, u32[]{:S(2)}, u32[]{:S(2)}) collective-permute-start(f32[128,32]{0,1:T(8,128)S(1)} %get-tuple-element.33), channel_id=1, source_target_pairs={{0,8},{8,16},{16,24},{24,32},{32,40},{40,48},{48,56},{56,64},{64,7... | collective-permute-start | bytes 49160 | tf_op jit(solution)/shard_map/ppermute | solution.py:23
  161.9 48.9 %collective-permute-start.3 = (f32[128,32]{0,1:T(8,128)S(1)}, f32[128,32]{0,1:T(8,128)S(1)}, u32[]{:S(2)}, u32[]{:S(2)}) collective-permute-start(f32[128,32]{0,1:T(8,128)S(1)} %get-tuple-element.32), channel_id=1, source_target_pairs={{8,0},{16,8},{24,16},{32,24},{40,32},{48,40},{56,48},{64,56},{72,6... | collective-permute-start | bytes 49160 | tf_op jit(solution)/shard_map/ppermute | solution.py:23
  194.8 15.0 %copy-start.4 = (bf16[1024,256]{0,1:T(8,128)(2,1)S(1)}, bf16[1024,256]{0,1:T(8,128)(2,1)}, u32[]{:S(2)}) copy-start(bf16[1024,256]{0,1:T(8,128)(2,1)} %copy-done.3) | copy-start | bytes 1572868
  201.6 19.3 %all-to-all-start.3 = ((f32[64,1,256]{2,1,0:T(1,128)}), f32[64,1,256]{2,1,0:T(1,128)S(1)}, u32[]{:S(2)}, u32[]{:S(2)}) async-start(f32[64,1,256]{2,1,0:T(1,128)} %broadcast_in_dim.66), calls=%async_computation.4 | async-start | bytes 131072 | tf_op jit(solution)/shard_map/all_to_all | solution.py:134
  210.8 11.4 %copy-start.6 = (f32[1024,32]{0,1:T(8,128)}, f32[1024,32]{0,1:T(8,128)S(1)}, u32[]{:S(2)}) copy-start(f32[1024,32]{0,1:T(8,128)S(1)} %fusion.21) | copy-start | bytes 393220
Sparse Core Ops, SparseCore 0:
  76.5 34.2 reduce-scatter.1

commit v4 on v1

--- a/solution.py
+++ b/solution.py
@@ -43,6 +43,19 @@
     peer_count = lax.axis_size("rows")
     capacity = max(2, 2 * blocks * fanout // peer_count)
     col_start = lax.axis_index("feat") * col_count
+    bias_high = lax.reduce_precision(bias, exponent_bits=8, mantissa_bits=7)
+    bias_rest = bias - bias_high
+    bias_mid = lax.reduce_precision(bias_rest, exponent_bits=8, mantissa_bits=7)
+    bias_parts = jnp.zeros((16, col_count), jnp.bfloat16)
+    bias_parts = bias_parts.at[:3].set(
+        jnp.stack([bias_high, bias_mid, bias_rest - bias_mid]).astype(jnp.bfloat16)
+    )
+    packed = jnp.concatenate([node_feats, cotangent, bias_parts], axis=0)
+    gathered = lax.all_gather(packed, "feat", axis=1, tiled=True)
+    feats_all = gathered[:rows_dev]
+    cotangent_all = gathered[rows_dev : 2 * rows_dev]
+    bias_rows = gathered[2 * rows_dev : 2 * rows_dev + 3].astype(jnp.float32)
+    bias_all = (bias_rows[0] + bias_rows[1]) + bias_rows[2]
     padded = extended(node_feats, (("rows", 0),), tile_size)
     windows = jnp.concatenate(
         [
@@ -87,17 +100,18 @@
     )
     rows_self = lax.dynamic_slice_in_dim(w_self, col_start, col_count, 0)
     rows_neigh = lax.dynamic_slice_in_dim(w_neigh, col_start, col_count, 0)
-    terms = jnp.dot(node_feats, rows_self, preferred_element_type=jnp.float32) + jnp.dot(
-        neighbours, rows_neigh, preferred_element_type=jnp.float32
+    neighbours_all = lax.all_gather(neighbours, "feat", axis=1, tiled=True)
+    preact_all = (
+        jnp.dot(feats_all, w_self, preferred_element_type=jnp.float32)
+        + jnp.dot(neighbours_all, w_neigh, preferred_element_type=jnp.float32)
+        + bias_all
     )
-    preact = lax.psum_scatter(terms, "feat", scatter_dimension=1, tiled=True)
-    preact = preact + bias
+    preact = lax.dynamic_slice_in_dim(preact_all, col_start, col_count, 1)
     layer_out = jax.nn.silu(preact).astype(jnp.bfloat16)
-    sigmoid_z = jax.nn.sigmoid(preact)
-    grad_pre = (
-        cotangent.astype(jnp.float32) * sigmoid_z * (1.0 + preact * (1.0 - sigmoid_z))
+    sigmoid_z = jax.nn.sigmoid(preact_all)
+    full_grad = (
+        cotangent_all.astype(jnp.float32) * sigmoid_z * (1.0 + preact_all * (1.0 - sigmoid_z))
     ).astype(jnp.bfloat16)
-    full_grad = lax.all_gather(grad_pre, "feat", axis=1, tiled=True)
     grad_scale = float(rows_dev * peer_count) ** (-0.5)
     part_self = jnp.einsum("rc,rf->cf", node_feats, full_grad, preferred_element_type=jnp.float32)
     part_neigh = jnp.einsum("rc,rf->cf", neighbours, full_grad, preferred_element_type=jnp.float32)

time: 227 us -> 192 us (0.85)
  waiting for transfers between devices: 102 us -> 66.6 us
  starting transfers between devices: 59 us -> 55 us
  other arithmetic: 9.93 us -> 13.7 us
  matrix products: 5.08 us -> 7.39 us
    reduce_scatter x1 -> x0, waiting for transfers between devices: 31.8 us -> none  [on_device(): preact = lax.psum_scatter(terms, 'feat', scatter_dimension=1, tiled=True)]
    all_to_all x1, waiting for transfers between devices: 6.36 us -> 2.81 us  [on_device(): lax.all_to_all(outgoing, 'rows', split_axis=0, concat_axis=0, tiled=True)]
    all_to_all x1, starting transfers between devices: 13.4 us -> 10.1 us  [summed_over(): pieces = lax.all_to_all(flat, axis, split_axis=0, concat_axis=0, tiled=True)]
    dot_general x2, matrix products: 2.35 us -> 5.38 us  [the longest x1 3.01 us: on_device(): jnp.dot(neighbours_all, w_neigh, preferred_element_type=jnp.float32)]
  transfers between devices with their start and end apart: 10 -> 10, of which waited for: 8 -> 7; matrix products, arithmetic and copies ran while one was open for 10% -> 17% of each run, Pallas kernels for 0% -> 0%
where the time goes in v4:
time: 192 us
  waiting for transfers between devices  66.6 us (35%)
  starting transfers between devices  55 us (29%)
  local copies, waits for them, and re-layouts  21 us (11%)
  between operations  14.5 us (8%)
  other arithmetic  13.7 us (7%)
  blocking collectives  13.4 us (7%)
  matrix products  7.39 us (4%)
    all_to_all x1, waiting for transfers between devices, on_device(): lax.all_to_all(returning.reshape(peer_count, capacity, tile_size, col_cou...  18.7 us
    all_to_all x1, starting transfers between devices, on_device(): lax.all_to_all(request, 'rows', split_axis=0, concat_axis=0, tiled=True)  16.6 us
    ppermute x1, waiting for transfers between devices, extended(): lax.ppermute(lax.slice_in_dim(block, block.shape[dim] - width, None, axis...  14.1 us
    all_gather x1, blocking collectives, on_device(): neighbours_all = lax.all_gather(neighbours, 'feat', axis=1, tiled=True)  13.4 us
    all_to_all x1, waiting for transfers between devices, summed_over(): pieces = lax.all_to_all(flat, axis, split_axis=0, concat_axis=0, tiled=True)  11.1 us
    reshape x2, local copies, waits for them, and re-layouts, on_device(): returned.reshape(peer_count * capacity, tile_size * col_count)  10.4 us
    all_to_all x1, waiting for transfers between devices, on_device(): lax.all_to_all(request, 'rows', split_axis=0, concat_axis=0, tiled=True)  10.1 us
    all_to_all x1, starting transfers between devices, summed_over(): pieces = lax.all_to_all(flat, axis, split_axis=0, concat_axis=0, tiled=True)  10.1 us
  transfers between devices with their start and end apart: 10, of which 7 were waited for; matrix products, arithmetic and copies ran while one was open for 17% of the time, Pallas kernels for 0%

profile of v4, /device:TPU:8, one launch (start us, length us, event | category | flops | bytes accessed | tf_op | source)
XLA Modules:
  0.0 191.6 jit_solution(3793103398912685583)
XLA Ops:
  8.0 1.5 fusion.14
  12.3 16.6 %all-to-all-start = ((s32[64,1,2]{2,1,0:T(1,128)}), s32[64,1,2]{2,1,0:T(1,128)S(1)}, u32[]{:S(2)}, u32[]{:S(2)}) async-start(s32[64,1,2]{2,1,0:T(1,128)} %bitcast.4), calls=%async_computation | async-start | bytes 65536 | tf_op jit(solution)/shard_map/all_to_all | solution.py:82
  29.8 10.1 %all-to-all-done = s32[64,1,2]{2,1,0:T(1,128)S(1)} async-done(((s32[64,1,2]{2,1,0:T(1,128)}), s32[64,1,2]{2,1,0:T(1,128)S(1)}, u32[]{:S(2)}, u32[]{:S(2)}) %all-to-all-start) | async-done | bytes 544 | tf_op jit(solution)/shard_map/all_to_all | solution.py:82
  40.4 1.4 fusion.40
  44.2 5.5 %all-to-all-start.1 = ((bf16[64,2,128,32]{2,3,1,0:T(8,128)(2,1)}), bf16[64,2,128,32]{2,3,1,0:T(8,128)(2,1)S(1)}, u32[]{:S(2)}, u32[]{:S(2)}) async-start(bf16[64,2,128,32]{2,3,1,0:T(8,128)(2,1)} %broadcast_select_fusion), calls=%async_computation.1 | async-start | bytes 2097152 | tf_op jit(solution)/shard_map/all_to_all | solution.py:89
  49.8 3.5 %collective-permute-start = (bf16[128,32]{0,1:T(8,128)(2,1)S(1)}, bf16[128,32]{0,1:T(8,128)(2,1)S(1)}, u32[]{:S(2)}, u32[]{:S(2)}) collective-permute-start(bf16[128,32]{0,1:T(8,128)(2,1)S(1)} %get-tuple-element.51), channel_id=1, source_target_pairs={{0,8},{8,16},{16,24},{24,32},{32,40},{40,48},{48,56},{56,64},{64,7... | collective-permute-start | bytes 24584 | tf_op jit(solution)/shard_map/ppermute | solution.py:12
  53.3 2.5 %collective-permute-start.1 = (bf16[128,32]{0,1:T(8,128)(2,1)S(1)}, bf16[128,32]{0,1:T(8,128)(2,1)S(1)}, u32[]{:S(2)}, u32[]{:S(2)}) collective-permute-start(bf16[128,32]{0,1:T(8,128)(2,1)S(1)} %get-tuple-element.52), channel_id=1, source_target_pairs={{8,0},{16,8},{24,16},{32,24},{40,32},{48,40},{56,48},{64,56},{72,6... | collective-permute-start | bytes 24584 | tf_op jit(solution)/shard_map/ppermute | solution.py:15
  56.4 14.1 %collective-permute-done = bf16[128,32]{0,1:T(8,128)(2,1)S(1)} collective-permute-done((bf16[128,32]{0,1:T(8,128)(2,1)S(1)}, bf16[128,32]{0,1:T(8,128)(2,1)S(1)}, u32[]{:S(2)}, u32[]{:S(2)}) %collective-permute-start) | collective-permute-done | bytes 8224 | tf_op jit(solution)/shard_map/ppermute | solution.py:12
  73.2 2.4 %fusion.5 = f32[1024,256]{0,1:T(8,128)} fusion(bf16[256,256]{1,0:T(8,128)(2,1)S(1)} %copy-done.7, bf16[2064,256]{0,1:T(8,128)(2,1)} %all-gather.2.cloned.1.call-done), kind=kOutput, calls=%fused_computation.21 | convolution fusion | flops 134217728 | bytes 1703936 | tf_op jit(solution)/shard_map/dot_general | solution.py:105
  75.6 2.8 %all-to-all-done.1 = bf16[64,2,128,32]{2,3,1,0:T(8,128)(2,1)S(1)} async-done(((bf16[64,2,128,32]{2,3,1,0:T(8,128)(2,1)}), bf16[64,2,128,32]{2,3,1,0:T(8,128)(2,1)S(1)}, u32[]{:S(2)}, u32[]{:S(2)}) %all-to-all-start.1) | async-done | bytes 1048608 | tf_op jit(solution)/shard_map/all_to_all | solution.py:89
  79.4 13.4 %all_gather.7 = bf16[1024,256]{0,1:T(8,128)(2,1)S(1)} all-gather(bf16[1024,32]{0,1:T(8,128)(2,1)S(1)} %fusion.15), channel_id=1, replica_groups=mesh['rows'=64,'feat'=8] {'feat'}, dimensions={1}, use_global_device_ids=true | all-gather | bytes 589824 | tf_op jit(solution)/shard_map/all_gather | solution.py:103
  92.8 3.0 %multiply_convert_fusion = (bf16[1024,256]{0,1:T(8,128)(2,1)S(1)}, f32[1024,256]{0,1:T(8,128)}) fusion(bf16[2064,256]{0,1:T(8,128)(2,1)} %all-gather.2.cloned.1.call-done, f32[256]{0:T(256)S(1)} %fusion.16, f32[1024,256]{0,1:T(8,128)} %fusion.5, bf16[1024,256]{0,1:T(8,128)(2,1)S(1)} %all_gather.7, bf16[256,256]{1,0:T(8,128)(2,1)S(1)} %copy-done), kind=kOutput, calls=%fused_computation.18 | convolution fusion | flops 137363456 | bytes 3802112 | tf_op jit(solution)/shard_map/dot_general | solution.py:106
  97.1 10.1 %all-to-all-start.3 = ((f32[64,1,256]{2,1,0:T(1,128)}), f32[64,1,256]{2,1,0:T(1,128)S(1)}, u32[]{:S(2)}, u32[]{:S(2)}) async-start(f32[64,1,256]{2,1,0:T(1,128)} %copy.119), calls=%async_computation.3 | async-start | bytes 131072 | tf_op jit(solution)/shard_map/all_to_all | solution.py:29
  107.4 11.1 %all-to-all-done.3 = f32[64,1,256]{2,1,0:T(1,128)S(1)} async-done(((f32[64,1,256]{2,1,0:T(1,128)}), f32[64,1,256]{2,1,0:T(1,128)S(1)}, u32[]{:S(2)}, u32[]{:S(2)}) %all-to-all-start.3) | async-done | bytes 65568 | tf_op jit(solution)/shard_map/all_to_all | solution.py:29
  119.3 5.4 %all-to-all-start.4 = ((f32[64,1,256]{2,1,0:T(1,128)}), f32[64,1,256]{2,1,0:T(1,128)S(1)}, u32[]{:S(2)}, u32[]{:S(2)}) async-start(f32[64,1,256]{2,1,0:T(1,128)} %broadcast_in_dim.67), calls=%async_computation.4 | async-start | bytes 131072 | tf_op jit(solution)/shard_map/all_to_all | solution.py:32
  127.7 8.5 %all-to-all-done.4 = f32[64,1,256]{2,1,0:T(1,128)S(1)} async-done(((f32[64,1,256]{2,1,0:T(1,128)}), f32[64,1,256]{2,1,0:T(1,128)S(1)}, u32[]{:S(2)}, u32[]{:S(2)}) %all-to-all-start.4) | async-done | bytes 65568 | tf_op jit(solution)/shard_map/all_to_all | solution.py:32
  136.2 5.4 %all-to-all-start.2 = ((bf16[64,2,128,32]{2,3,1,0:T(8,128)(2,1)}), bf16[64,2,128,32]{2,3,1,0:T(8,128)(2,1)S(1)}, u32[]{:S(2)}, u32[]{:S(2)}) async-start(bf16[64,2,128,32]{2,3,1,0:T(8,128)(2,1)} %bitcast.104), calls=%async_computation.2 | async-start | bytes 2097152 | tf_op jit(solution)/shard_map/all_to_all | solution.py:145
  142.1 3.4 %collective-permute-start.2 = (f32[128,32]{0,1:T(8,128)S(1)}, f32[128,32]{0,1:T(8,128)S(1)}, u32[]{:S(2)}, u32[]{:S(2)}) collective-permute-start(f32[128,32]{0,1:T(8,128)S(1)} %get-tuple-element.43), channel_id=1, source_target_pairs={{0,8},{8,16},{16,24},{24,32},{32,40},{40,48},{48,56},{56,64},{64,7... | collective-permute-start | bytes 49160 | tf_op jit(solution)/shard_map/ppermute | solution.py:23
  145.5 2.6 %collective-permute-start.3 = (f32[128,32]{0,1:T(8,128)S(1)}, f32[128,32]{0,1:T(8,128)S(1)}, u32[]{:S(2)}, u32[]{:S(2)}) collective-permute-start(f32[128,32]{0,1:T(8,128)S(1)} %get-tuple-element.42), channel_id=1, source_target_pairs={{8,0},{16,8},{24,16},{32,24},{40,32},{48,40},{56,48},{64,56},{72,6... | collective-permute-start | bytes 49160 | tf_op jit(solution)/shard_map/ppermute | solution.py:23
  148.2 1.6 multiply_convert_fusion.1
  151.1 18.7 %all-to-all-done.2 = bf16[64,2,128,32]{2,3,1,0:T(8,128)(2,1)S(1)} async-done(((bf16[64,2,128,32]{2,3,1,0:T(8,128)(2,1)}), bf16[64,2,128,32]{2,3,1,0:T(8,128)(2,1)S(1)}, u32[]{:S(2)}, u32[]{:S(2)}) %all-to-all-start.2) | async-done | bytes 1048608 | tf_op jit(solution)/shard_map/all_to_all | solution.py:145
  169.8 4.1 %copy.117 = f32[64,2,128,32]{3,2,1,0:T(8,128)} copy(bf16[64,2,128,32]{2,3,1,0:T(8,128)(2,1)S(1)} %all-to-all-done.2) | data formatting | bytes 3145728 | tf_op jit(solution)/shard_map/reshape | solution.py:155
  173.9 6.3 %reshape.316 = f32[128,4096]{1,0:T(8,128)S(1)} reshape(f32[64,2,128,32]{3,2,1,0:T(8,128)} %copy.117) | data formatting | bytes 4194304 | tf_op jit(solution)/shard_map/reshape | solution.py:155
  180.2 3.3 %scatter_custom_fusion.1 = f32[8,4096]{1,0:T(8,128)S(1)} fusion(s32[128]{0:T(128)S(1)} %fusion.38, f32[128,4096]{1,0:T(8,128)S(1)} %reshape.316, f32[]{:T(128)} %constant.111.clone.1), kind=kCustom, calls=%fused_computation.57 | custom fusion | flops 524288 | bytes 131076 | tf_op jit(solution)/shard_map/scatter-add | solution.py:154
  (98 shorter events, 19.7 us)
Async XLA Ops:
  7.2 85.7 %copy-start = (bf16[256,256]{1,0:T(8,128)(2,1)S(1)}, bf16[256,256]{1,0:T(8,128)(2,1)}, u32[]{:S(2)}) copy-start(bf16[256,256]{1,0:T(8,128)(2,1)} %param.21) | copy-start | bytes 393220
  7.2 65.0 %all-gather.2.cloned.1.call-start = ((), (), s32[]{:S(2)}) async-start(), calls=%async_computation.5 | async-start | bytes 1253376 | tf_op jit(solution)/shard_map/all_gather | solution.py:54
  12.3 27.6 %all-to-all-start = ((s32[64,1,2]{2,1,0:T(1,128)}), s32[64,1,2]{2,1,0:T(1,128)S(1)}, u32[]{:S(2)}, u32[]{:S(2)}) async-start(s32[64,1,2]{2,1,0:T(1,128)} %bitcast.4), calls=%async_computation | async-start | bytes 65536 | tf_op jit(solution)/shard_map/all_to_all | solution.py:82
  43.0 6.8 %copy-start.5 = (bf16[1024,32]{0,1:T(8,128)(2,1)S(1)}, bf16[1024,32]{0,1:T(8,128)(2,1)}, u32[]{:S(2)}) copy-start(bf16[1024,32]{0,1:T(8,128)(2,1)} %param.15) | copy-start | bytes 196612
  43.0 12.8 %copy-start.9 = (s32[8,2]{0,1:T(2,128)S(1)}, s32[8,2]{0,1:T(2,128)}, u32[]{:S(2)}) copy-start(s32[8,2]{0,1:T(2,128)} %param.18) | copy-start | bytes 196
  43.0 13.0 %copy-start.2 = (bf16[1024,256]{1,0:T(8,128)(2,1)S(1)}, bf16[1024,256]{1,0:T(8,128)(2,1)}, u32[]{:S(2)}) copy-start(bf16[1024,256]{1,0:T(8,128)(2,1)} %param.17) | copy-start | bytes 1572868
  43.0 13.2 %copy-start.1 = (bf16[1024,384]{1,0:T(8,128)(2,1)S(1)}, bf16[1024,384]{1,0:T(8,128)(2,1)}, u32[]{:S(2)}) copy-start(bf16[1024,384]{1,0:T(8,128)(2,1)} %param.16) | copy-start | bytes 2359300
  44.2 34.2 %all-to-all-start.1 = ((bf16[64,2,128,32]{2,3,1,0:T(8,128)(2,1)}), bf16[64,2,128,32]{2,3,1,0:T(8,128)(2,1)S(1)}, u32[]{:S(2)}, u32[]{:S(2)}) async-start(bf16[64,2,128,32]{2,3,1,0:T(8,128)(2,1)} %broadcast_select_fusion), calls=%async_computation.1 | async-start | bytes 2097152 | tf_op jit(solution)/shard_map/all_to_all | solution.py:89
  49.8 23.5 %copy-start.7 = (bf16[256,256]{1,0:T(8,128)(2,1)S(1)}, bf16[256,256]{1,0:T(8,128)(2,1)}, u32[]{:S(2)}) copy-start(bf16[256,256]{1,0:T(8,128)(2,1)} %param.20) | copy-start | bytes 393220
  49.8 20.8 %collective-permute-start = (bf16[128,32]{0,1:T(8,128)(2,1)S(1)}, bf16[128,32]{0,1:T(8,128)(2,1)S(1)}, u32[]{:S(2)}, u32[]{:S(2)}) collective-permute-start(bf16[128,32]{0,1:T(8,128)(2,1)S(1)} %get-tuple-element.51), channel_id=1, source_target_pairs={{0,8},{8,16},{16,24},{24,32},{32,40},{40,48},{48,56},{56,64},{64,7... | collective-permute-start | bytes 24584 | tf_op jit(solution)/shard_map/ppermute | solution.py:12
  53.3 18.4 %collective-permute-start.1 = (bf16[128,32]{0,1:T(8,128)(2,1)S(1)}, bf16[128,32]{0,1:T(8,128)(2,1)S(1)}, u32[]{:S(2)}, u32[]{:S(2)}) collective-permute-start(bf16[128,32]{0,1:T(8,128)(2,1)S(1)} %get-tuple-element.52), channel_id=1, source_target_pairs={{8,0},{16,8},{24,16},{32,24},{40,32},{48,40},{56,48},{64,56},{72,6... | collective-permute-start | bytes 24584 | tf_op jit(solution)/shard_map/ppermute | solution.py:15
  95.9 29.2 %copy-start.3 = (bf16[1024,256]{0,1:T(8,128)(2,1)}, bf16[1024,256]{0,1:T(8,128)(2,1)S(1)}, u32[]{:S(2)}) copy-start(bf16[1024,256]{0,1:T(8,128)(2,1)S(1)} %get-tuple-element.56) | copy-start | bytes 1572868
  97.1 21.4 %all-to-all-start.3 = ((f32[64,1,256]{2,1,0:T(1,128)}), f32[64,1,256]{2,1,0:T(1,128)S(1)}, u32[]{:S(2)}, u32[]{:S(2)}) async-start(f32[64,1,256]{2,1,0:T(1,128)} %copy.119), calls=%async_computation.3 | async-start | bytes 131072 | tf_op jit(solution)/shard_map/all_to_all | solution.py:29
  119.3 16.9 %all-to-all-start.4 = ((f32[64,1,256]{2,1,0:T(1,128)}), f32[64,1,256]{2,1,0:T(1,128)S(1)}, u32[]{:S(2)}, u32[]{:S(2)}) async-start(f32[64,1,256]{2,1,0:T(1,128)} %broadcast_in_dim.67), calls=%async_computation.4 | async-start | bytes 131072 | tf_op jit(solution)/shard_map/all_to_all | solution.py:32
  126.5 15.1 %copy-start.8 = (s32[64,2]{1,0:T(8,128)S(1)}, s32[64,2]{1,0:T(8,128)}, u32[]{:S(2)}) copy-start(s32[64,2]{1,0:T(8,128)} %get-tuple-element.40) | copy-start | bytes 1540
  136.2 33.7 %all-to-all-start.2 = ((bf16[64,2,128,32]{2,3,1,0:T(8,128)(2,1)}), bf16[64,2,128,32]{2,3,1,0:T(8,128)(2,1)S(1)}, u32[]{:S(2)}, u32[]{:S(2)}) async-start(bf16[64,2,128,32]{2,3,1,0:T(8,128)(2,1)} %bitcast.104), calls=%async_computation.2 | async-start | bytes 2097152 | tf_op jit(solution)/shard_map/all_to_all | solution.py:145
  142.1 41.9 %collective-permute-start.2 = (f32[128,32]{0,1:T(8,128)S(1)}, f32[128,32]{0,1:T(8,128)S(1)}, u32[]{:S(2)}, u32[]{:S(2)}) collective-permute-start(f32[128,32]{0,1:T(8,128)S(1)} %get-tuple-element.43), channel_id=1, source_target_pairs={{0,8},{8,16},{16,24},{24,32},{32,40},{40,48},{48,56},{56,64},{64,7... | collective-permute-start | bytes 49160 | tf_op jit(solution)/shard_map/ppermute | solution.py:23
  145.5 38.5 %collective-permute-start.3 = (f32[128,32]{0,1:T(8,128)S(1)}, f32[128,32]{0,1:T(8,128)S(1)}, u32[]{:S(2)}, u32[]{:S(2)}) collective-permute-start(f32[128,32]{0,1:T(8,128)S(1)} %get-tuple-element.42), channel_id=1, source_target_pairs={{8,0},{16,8},{24,16},{32,24},{40,32},{48,40},{56,48},{64,56},{72,6... | collective-permute-start | bytes 49160 | tf_op jit(solution)/shard_map/ppermute | solution.py:23
  173.9 9.9 %copy-start.4 = (bf16[1024,256]{0,1:T(8,128)(2,1)S(1)}, bf16[1024,256]{0,1:T(8,128)(2,1)}, u32[]{:S(2)}) copy-start(bf16[1024,256]{0,1:T(8,128)(2,1)} %copy-done.3) | copy-start | bytes 1572868
  184.1 0.7 copy-start.6
Sparse Core Ops, SparseCore 0:
  10.1 33.3 all-gather.1

commit v5 on v4

--- a/solution.py
+++ b/solution.py
@@ -2,19 +2,6 @@
 import jax.numpy as jnp
 from jax import lax
 from jax.sharding import PartitionSpec as P
-
-
-def extended(block, sides, width):
-    for axis, dim in sides:
-        count = lax.axis_size(axis)
-        forward = [(i, i + 1) for i in range(count - 1)]
-        backward = [(target, source) for source, target in forward]
-        low = lax.ppermute(
-            lax.slice_in_dim(block, block.shape[dim] - width, None, axis=dim), axis, forward
-        )
-        high = lax.ppermute(lax.slice_in_dim(block, 0, width, axis=dim), axis, backward)
-        block = jnp.concatenate([low, block, high], axis=dim)
-    return block
 
 
 def from_behind(block, axis, distance):
@@ -42,6 +29,7 @@
     fanout = far_owner.shape[1]
     peer_count = lax.axis_size("rows")
     capacity = max(2, 2 * blocks * fanout // peer_count)
+    row_index = lax.axis_index("rows")
     col_start = lax.axis_index("feat") * col_count
     bias_high = lax.reduce_precision(bias, exponent_bits=8, mantissa_bits=7)
     bias_rest = bias - bias_high
@@ -56,7 +44,35 @@
     cotangent_all = gathered[rows_dev : 2 * rows_dev]
     bias_rows = gathered[2 * rows_dev : 2 * rows_dev + 3].astype(jnp.float32)
     bias_all = (bias_rows[0] + bias_rows[1]) + bias_rows[2]
-    padded = extended(node_feats, (("rows", 0),), tile_size)
+    owner_ids = far_owner.reshape(-1)
+    local_ids = far_local.reshape(-1)
+    entries = owner_ids.shape[0]
+    same_owner = owner_ids[:, None] == owner_ids[None, :]
+    earlier = jnp.arange(entries)[None, :] < jnp.arange(entries)[:, None]
+    slot_rank = jnp.sum(jnp.where(same_owner & earlier, 1, 0), axis=1).astype(jnp.int32)
+    slot_ids = owner_ids * capacity + slot_rank
+    slot_hit = slot_ids[:, None] == jnp.arange(peer_count * capacity, dtype=jnp.int32)[None, :]
+    far_request = (jnp.sum(jnp.where(slot_hit, local_ids[:, None] + 1, 0), axis=0) - 1).reshape(
+        peer_count, capacity
+    )
+    peers = jnp.arange(peer_count, dtype=jnp.int32)
+    halo_request = jnp.where(
+        peers == row_index - 1, blocks - 1, jnp.where(peers == row_index + 1, 0, -1)
+    )
+    request = jnp.concatenate([far_request, halo_request[:, None]], axis=1)
+    wanted = lax.all_to_all(request, "rows", split_axis=0, concat_axis=0, tiled=True)
+    usable = wanted >= 0
+    safe_ids = jnp.maximum(wanted, 0)
+    own_blocks = node_feats.reshape(blocks, tile_size, col_count)
+    outgoing = jnp.where(
+        usable[:, :, None, None], own_blocks[safe_ids], jnp.zeros((), jnp.bfloat16)
+    )
+    incoming = lax.all_to_all(outgoing, "rows", split_axis=0, concat_axis=0, tiled=True)
+    low = lax.dynamic_index_in_dim(incoming, jnp.maximum(row_index - 1, 0), 0, keepdims=False)
+    high = lax.dynamic_index_in_dim(
+        incoming, jnp.minimum(row_index + 1, peer_count - 1), 0, keepdims=False
+    )
+    padded = jnp.concatenate([low[capacity], node_feats, high[capacity]], axis=0)
     windows = jnp.concatenate(
         [
             padded[offset * tile_size : offset * tile_size + rows_dev].reshape(
@@ -68,28 +84,8 @@
     )
     band_tiles = band_weights.reshape(blocks, tile_size, 3 * tile_size)
     band_sum = jnp.einsum("bij,bjc->bic", band_tiles, windows, preferred_element_type=jnp.float32)
-    owner_ids = far_owner.reshape(-1)
-    local_ids = far_local.reshape(-1)
-    entries = owner_ids.shape[0]
-    same_owner = owner_ids[:, None] == owner_ids[None, :]
-    earlier = jnp.arange(entries)[None, :] < jnp.arange(entries)[:, None]
-    slot_rank = jnp.sum(jnp.where(same_owner & earlier, 1, 0), axis=1).astype(jnp.int32)
-    slot_ids = owner_ids * capacity + slot_rank
-    slot_hit = slot_ids[:, None] == jnp.arange(peer_count * capacity, dtype=jnp.int32)[None, :]
-    request = (jnp.sum(jnp.where(slot_hit, local_ids[:, None] + 1, 0), axis=0) - 1).reshape(
-        peer_count, capacity
-    )
-    wanted = lax.all_to_all(request, "rows", split_axis=0, concat_axis=0, tiled=True)
-    usable = wanted >= 0
-    safe_ids = jnp.maximum(wanted, 0)
-    own_blocks = node_feats.reshape(blocks, tile_size, col_count)
-    outgoing = jnp.where(
-        usable[:, :, None, None], own_blocks[safe_ids], jnp.zeros((), jnp.bfloat16)
-    )
-    incoming = lax.all_to_all(outgoing, "rows", split_axis=0, concat_axis=0, tiled=True)
-    fetched = incoming.reshape(peer_count * capacity, tile_size, col_count)[slot_ids].reshape(
-        blocks, fanout * tile_size, col_count
-    )
+    far_slots = incoming[:, :capacity].reshape(peer_count * capacity, tile_size, col_count)
+    fetched = far_slots[slot_ids].reshape(blocks, fanout * tile_size, col_count)
     far_tiles = far_weights.reshape(blocks, tile_size, fanout * tile_size)
     far_sum = jnp.einsum("bij,bjc->bic", far_tiles, fetched, preferred_element_type=jnp.float32)
     degree = jnp.sum(band_weights.astype(jnp.float32), axis=1) + jnp.sum(
@@ -149,7 +145,7 @@
         concat_axis=0,
         tiled=True,
     ).astype(jnp.float32)
-    target_block = jnp.where(usable, wanted, blocks).reshape(-1)
+    target_block = jnp.where(usable, wanted, blocks)[:, :capacity].reshape(-1)
     owed = jnp.zeros((blocks, tile_size * col_count), jnp.float32)
     owed = owed.at[target_block].add(
         returned.reshape(peer_count * capacity, tile_size * col_count), mode="drop"

time: 192 us -> 204 us (1.062)
  waiting for transfers between devices: 66.6 us -> 83 us
  starting transfers between devices: 55 us -> 48.7 us
  local copies, waits for them, and re-layouts: 21 us -> 23.6 us
    all_gather x1, waiting for transfers between devices: 0.02 us -> 31.1 us  [on_device(): gathered = lax.all_gather(packed, 'feat', axis=1, tiled=True)]
    ppermute x2 -> x0, waiting for transfers between devices: 15.3 us -> none  [the longest x1 14.1 us: extended(): lax.ppermute(lax.slice_in_dim(block, block.shape[dim] - width, None, axis...]
    ppermute x2 -> x0, starting transfers between devices: 5.97 us -> none  [the longest x1 3.51 us: extended(): lax.ppermute(lax.slice_in_dim(block, block.shape[dim] - width, None, axis...]
  transfers between devices with their start and end apart: 10 -> 8, of which waited for: 7 -> 6; matrix products, arithmetic and copies ran while one was open for 17% -> 13% of each run, Pallas kernels for 0% -> 0%
where the time goes in v5:
time: 204 us; the launch traced here: 203 us
  waiting for transfers between devices  83 us (41%)
  starting transfers between devices  48.7 us (24%)
  local copies, waits for them, and re-layouts  23.6 us (12%)
  between operations  14.5 us (7%)
  blocking collectives  13.5 us (7%)
  other arithmetic  11.8 us (6%)
  matrix products  7.75 us (4%)
    all_gather x1, waiting for transfers between devices, on_device(): gathered = lax.all_gather(packed, 'feat', axis=1, tiled=True)  31.1 us
    all_to_all x1, waiting for transfers between devices, on_device(): lax.all_to_all(returning.reshape(peer_count, capacity, tile_size, col_cou...  18.7 us
    all_to_all x1, starting transfers between devices, on_device(): lax.all_to_all(request, 'rows', split_axis=0, concat_axis=0, tiled=True)  16.6 us
    all_gather x1, blocking collectives, on_device(): neighbours_all = lax.all_gather(neighbours, 'feat', axis=1, tiled=True)  13.5 us
    all_to_all x1, waiting for transfers between devices, summed_over(): pieces = lax.all_to_all(flat, axis, split_axis=0, concat_axis=0, tiled=True)  11.1 us
    reshape x2, local copies, waits for them, and re-layouts, on_device(): returned.reshape(peer_count * capacity, tile_size * col_count)  10.3 us
    all_to_all x1, waiting for transfers between devices, on_device(): lax.all_to_all(request, 'rows', split_axis=0, concat_axis=0, tiled=True)  10.1 us
    all_to_all x1, starting transfers between devices, summed_over(): pieces = lax.all_to_all(flat, axis, split_axis=0, concat_axis=0, tiled=True)  9.51 us
  transfers between devices with their start and end apart: 8, of which 6 were waited for; matrix products, arithmetic and copies ran while one was open for 13% of the time, Pallas kernels for 0%

profile of v5, /device:TPU:8, one launch (start us, length us, event | category | flops | bytes accessed | tf_op | source)
XLA Modules:
  0.0 202.8 jit_solution(17057296175728854703)
XLA Ops:
  10.1 16.6 %all-to-all-start = ((s32[64,1,3]{2,1,0:T(1,128)}), s32[64,1,3]{2,1,0:T(1,128)S(1)}, u32[]{:S(2)}, u32[]{:S(2)}) async-start(s32[64,1,3]{2,1,0:T(1,128)} %bitcast.4), calls=%async_computation | async-start | bytes 65536 | tf_op jit(solution)/shard_map/all_to_all | solution.py:63
  27.5 10.1 %all-to-all-done = s32[64,1,3]{2,1,0:T(1,128)S(1)} async-done(((s32[64,1,3]{2,1,0:T(1,128)}), s32[64,1,3]{2,1,0:T(1,128)S(1)}, u32[]{:S(2)}, u32[]{:S(2)}) %all-to-all-start) | async-done | bytes 800 | tf_op jit(solution)/shard_map/all_to_all | solution.py:63
  38.8 1.4 broadcast_select_fusion
  40.2 5.7 %all-to-all-start.1 = ((bf16[64,3,128,32]{2,3,1,0:T(8,128)(2,1)}), bf16[64,3,128,32]{2,3,1,0:T(8,128)(2,1)S(1)}, u32[]{:S(2)}, u32[]{:S(2)}) async-start(bf16[64,3,128,32]{2,3,1,0:T(8,128)(2,1)} %broadcast_select_fusion), calls=%async_computation.1 | async-start | bytes 3145728 | tf_op jit(solution)/shard_map/all_to_all | solution.py:70
  47.5 31.1 %all-gather.2.cloned.1.call-done = bf16[2064,256]{0,1:T(8,128)(2,1)} async-done(((bf16[2064,32]{0,1:T(8,128)(2,1)}), bf16[2064,256]{0,1:T(8,128)(2,1)}) %all-gather.2.cloned.1.call-update) | async-done | bytes 1056784 | tf_op jit(solution)/shard_map/all_gather | solution.py:42
  79.6 2.4 %fusion.5 = f32[1024,256]{0,1:T(8,128)} fusion(bf16[256,256]{1,0:T(8,128)(2,1)S(1)} %copy-done.8, bf16[2064,256]{0,1:T(8,128)(2,1)} %all-gather.2.cloned.1.call-done), kind=kOutput, calls=%fused_computation.21 | convolution fusion | flops 134217728 | bytes 1703936 | tf_op jit(solution)/shard_map/dot_general | solution.py:101
  82.0 3.5 %all-to-all-done.1 = bf16[64,3,128,32]{2,3,1,0:T(8,128)(2,1)S(1)} async-done(((bf16[64,3,128,32]{2,3,1,0:T(8,128)(2,1)}), bf16[64,3,128,32]{2,3,1,0:T(8,128)(2,1)S(1)}, u32[]{:S(2)}, u32[]{:S(2)}) %all-to-all-start.1) | async-done | bytes 1572896 | tf_op jit(solution)/shard_map/all_to_all | solution.py:70
  85.5 1.1 slice.141
  86.6 1.8 gather_fusion.1
  90.9 13.5 %all_gather.7 = bf16[1024,256]{0,1:T(8,128)(2,1)S(1)} all-gather(bf16[1024,32]{0,1:T(8,128)(2,1)S(1)} %fusion.15), channel_id=1, replica_groups=mesh['rows'=64,'feat'=8] {'feat'}, dimensions={1}, use_global_device_ids=true | all-gather | bytes 589824 | tf_op jit(solution)/shard_map/all_gather | solution.py:99
  104.3 2.6 %multiply_convert_fusion = (bf16[1024,256]{0,1:T(8,128)(2,1)S(1)}, f32[1024,256]{0,1:T(8,128)}) fusion(bf16[2064,256]{0,1:T(8,128)(2,1)} %all-gather.2.cloned.1.call-done, f32[256]{0:T(256)S(1)} %fusion.16, f32[1024,256]{0,1:T(8,128)S(1)} %copy-done.6, bf16[1024,256]{0,1:T(8,128)(2,1)S(1)} %all_gather.7, bf16[256,256]{1,0:T(8,128)(2,1)S(1)} %copy-done), kind=kOutput, calls=%fused_computation.19 | convolution fusion | flops 137363456 | bytes 3802112 | tf_op jit(solution)/shard_map/dot_general | solution.py:102
  108.2 9.5 %all-to-all-start.3 = ((f32[64,1,256]{2,1,0:T(1,128)}), f32[64,1,256]{2,1,0:T(1,128)S(1)}, u32[]{:S(2)}, u32[]{:S(2)}) async-start(f32[64,1,256]{2,1,0:T(1,128)} %copy.111), calls=%async_computation.3 | async-start | bytes 131072 | tf_op jit(solution)/shard_map/all_to_all | solution.py:16
  117.9 11.1 %all-to-all-done.3 = f32[64,1,256]{2,1,0:T(1,128)S(1)} async-done(((f32[64,1,256]{2,1,0:T(1,128)}), f32[64,1,256]{2,1,0:T(1,128)S(1)}, u32[]{:S(2)}, u32[]{:S(2)}) %all-to-all-start.3) | async-done | bytes 65568 | tf_op jit(solution)/shard_map/all_to_all | solution.py:16
  129.8 5.4 %all-to-all-start.4 = ((f32[64,1,256]{2,1,0:T(1,128)}), f32[64,1,256]{2,1,0:T(1,128)S(1)}, u32[]{:S(2)}, u32[]{:S(2)}) async-start(f32[64,1,256]{2,1,0:T(1,128)} %broadcast_in_dim.83), calls=%async_computation.4 | async-start | bytes 131072 | tf_op jit(solution)/shard_map/all_to_all | solution.py:19
  137.0 1.2 convert_element_type.46
  138.3 8.4 %all-to-all-done.4 = f32[64,1,256]{2,1,0:T(1,128)S(1)} async-done(((f32[64,1,256]{2,1,0:T(1,128)}), f32[64,1,256]{2,1,0:T(1,128)S(1)}, u32[]{:S(2)}, u32[]{:S(2)}) %all-to-all-start.4) | async-done | bytes 65568 | tf_op jit(solution)/shard_map/all_to_all | solution.py:19
  146.7 5.4 %all-to-all-start.2 = ((bf16[64,2,128,32]{2,3,1,0:T(8,128)(2,1)}), bf16[64,2,128,32]{2,3,1,0:T(8,128)(2,1)S(1)}, u32[]{:S(2)}, u32[]{:S(2)}) async-start(bf16[64,2,128,32]{2,3,1,0:T(8,128)(2,1)} %bitcast.110), calls=%async_computation.2 | async-start | bytes 2097152 | tf_op jit(solution)/shard_map/all_to_all | solution.py:141
  152.7 3.4 %collective-permute-start = (f32[128,32]{0,1:T(8,128)S(1)}, f32[128,32]{0,1:T(8,128)S(1)}, u32[]{:S(2)}, u32[]{:S(2)}) collective-permute-start(f32[128,32]{0,1:T(8,128)S(1)} %get-tuple-element.43), channel_id=1, source_target_pairs={{0,8},{8,16},{16,24},{24,32},{32,40},{40,48},{48,56},{56,64},{64,7... | collective-permute-start | bytes 49160 | tf_op jit(solution)/shard_map/ppermute | solution.py:10
  156.1 2.6 %collective-permute-start.1 = (f32[128,32]{0,1:T(8,128)S(1)}, f32[128,32]{0,1:T(8,128)S(1)}, u32[]{:S(2)}, u32[]{:S(2)}) collective-permute-start(f32[128,32]{0,1:T(8,128)S(1)} %get-tuple-element.42), channel_id=1, source_target_pairs={{8,0},{16,8},{24,16},{32,24},{40,32},{48,40},{56,48},{64,56},{72,6... | collective-permute-start | bytes 49160 | tf_op jit(solution)/shard_map/ppermute | solution.py:10
  158.7 1.6 multiply_convert_fusion.1
  161.7 18.7 %all-to-all-done.2 = bf16[64,2,128,32]{2,3,1,0:T(8,128)(2,1)S(1)} async-done(((bf16[64,2,128,32]{2,3,1,0:T(8,128)(2,1)}), bf16[64,2,128,32]{2,3,1,0:T(8,128)(2,1)S(1)}, u32[]{:S(2)}, u32[]{:S(2)}) %all-to-all-start.2) | async-done | bytes 1048608 | tf_op jit(solution)/shard_map/all_to_all | solution.py:141
  180.4 4.1 %copy.109 = f32[64,2,128,32]{3,2,1,0:T(8,128)} copy(bf16[64,2,128,32]{2,3,1,0:T(8,128)(2,1)S(1)} %all-to-all-done.2) | data formatting | bytes 3145728 | tf_op jit(solution)/shard_map/reshape | solution.py:151
  184.5 6.2 %reshape.329 = f32[128,4096]{1,0:T(8,128)S(1)} reshape(f32[64,2,128,32]{3,2,1,0:T(8,128)} %copy.109) | data formatting | bytes 4194304 | tf_op jit(solution)/shard_map/reshape | solution.py:151
  190.7 3.3 %scatter_custom_fusion.1 = f32[8,4096]{1,0:T(8,128)S(1)} fusion(s32[128]{0:T(128)S(1)} %fusion.38, f32[128,4096]{1,0:T(8,128)S(1)} %reshape.329, f32[]{:T(128)} %constant.130.clone.1), kind=kCustom, calls=%fused_computation.57 | custom fusion | flops 524288 | bytes 131076 | tf_op jit(solution)/shard_map/scatter-add | solution.py:150
  (99 shorter events, 17.5 us)
Async XLA Ops:
  7.2 97.2 %copy-start = (bf16[256,256]{1,0:T(8,128)(2,1)S(1)}, bf16[256,256]{1,0:T(8,128)(2,1)}, u32[]{:S(2)}) copy-start(bf16[256,256]{1,0:T(8,128)(2,1)} %param.21) | copy-start | bytes 393220
  10.1 27.5 %all-to-all-start = ((s32[64,1,3]{2,1,0:T(1,128)}), s32[64,1,3]{2,1,0:T(1,128)S(1)}, u32[]{:S(2)}, u32[]{:S(2)}) async-start(s32[64,1,3]{2,1,0:T(1,128)} %bitcast.4), calls=%async_computation | async-start | bytes 65536 | tf_op jit(solution)/shard_map/all_to_all | solution.py:63
  40.2 5.8 %copy-start.11 = (f32[32]{0:T(128)S(1)}, f32[32]{0:T(128)}, u32[]{:S(2)}) copy-start(f32[32]{0:T(128)} %param.22) | copy-start | bytes 388
  40.2 5.9 %copy-start.5 = (bf16[1024,32]{0,1:T(8,128)(2,1)S(1)}, bf16[1024,32]{0,1:T(8,128)(2,1)}, u32[]{:S(2)}) copy-start(bf16[1024,32]{0,1:T(8,128)(2,1)} %param.15) | copy-start | bytes 196612
  40.2 5.9 %copy-start.9 = (bf16[1024,32]{0,1:T(8,128)(2,1)S(1)}, bf16[1024,32]{0,1:T(8,128)(2,1)}, u32[]{:S(2)}) copy-start(bf16[1024,32]{0,1:T(8,128)(2,1)} %param.23) | copy-start | bytes 196612
  40.2 6.6 %copy-start.10 = (s32[8,2]{0,1:T(2,128)S(1)}, s32[8,2]{0,1:T(2,128)}, u32[]{:S(2)}) copy-start(s32[8,2]{0,1:T(2,128)} %param.18) | copy-start | bytes 196
  40.2 6.8 %copy-start.2 = (bf16[1024,256]{1,0:T(8,128)(2,1)S(1)}, bf16[1024,256]{1,0:T(8,128)(2,1)}, u32[]{:S(2)}) copy-start(bf16[1024,256]{1,0:T(8,128)(2,1)} %param.17) | copy-start | bytes 1572868
  40.2 7.0 %copy-start.1 = (bf16[1024,384]{1,0:T(8,128)(2,1)S(1)}, bf16[1024,384]{1,0:T(8,128)(2,1)}, u32[]{:S(2)}) copy-start(bf16[1024,384]{1,0:T(8,128)(2,1)} %param.16) | copy-start | bytes 2359300
  40.2 45.3 %all-to-all-start.1 = ((bf16[64,3,128,32]{2,3,1,0:T(8,128)(2,1)}), bf16[64,3,128,32]{2,3,1,0:T(8,128)(2,1)S(1)}, u32[]{:S(2)}, u32[]{:S(2)}) async-start(bf16[64,3,128,32]{2,3,1,0:T(8,128)(2,1)} %broadcast_select_fusion), calls=%async_computation.1 | async-start | bytes 3145728 | tf_op jit(solution)/shard_map/all_to_all | solution.py:70
  45.9 33.7 %copy-start.8 = (bf16[256,256]{1,0:T(8,128)(2,1)S(1)}, bf16[256,256]{1,0:T(8,128)(2,1)}, u32[]{:S(2)}) copy-start(bf16[256,256]{1,0:T(8,128)(2,1)} %param.20) | copy-start | bytes 393220
  45.9 32.6 %all-gather.2.cloned.1.call-start = ((), (), s32[]{:S(2)}) async-start(), calls=%async_computation.5 | async-start | bytes 1253376 | tf_op jit(solution)/shard_map/all_gather | solution.py:42
  90.1 14.2 %copy-start.6 = (f32[1024,256]{0,1:T(8,128)S(1)}, f32[1024,256]{0,1:T(8,128)}, u32[]{:S(2)}) copy-start(f32[1024,256]{0,1:T(8,128)} %fusion.5) | copy-start | bytes 3145732
  107.0 28.5 %copy-start.3 = (bf16[1024,256]{0,1:T(8,128)(2,1)}, bf16[1024,256]{0,1:T(8,128)(2,1)S(1)}, u32[]{:S(2)}) copy-start(bf16[1024,256]{0,1:T(8,128)(2,1)S(1)} %get-tuple-element.54) | copy-start | bytes 1572868
  108.2 20.8 %all-to-all-start.3 = ((f32[64,1,256]{2,1,0:T(1,128)}), f32[64,1,256]{2,1,0:T(1,128)S(1)}, u32[]{:S(2)}, u32[]{:S(2)}) async-start(f32[64,1,256]{2,1,0:T(1,128)} %copy.111), calls=%async_computation.3 | async-start | bytes 131072 | tf_op jit(solution)/shard_map/all_to_all | solution.py:16
  129.8 16.9 %all-to-all-start.4 = ((f32[64,1,256]{2,1,0:T(1,128)}), f32[64,1,256]{2,1,0:T(1,128)S(1)}, u32[]{:S(2)}, u32[]{:S(2)}) async-start(f32[64,1,256]{2,1,0:T(1,128)} %broadcast_in_dim.83), calls=%async_computation.4 | async-start | bytes 131072 | tf_op jit(solution)/shard_map/all_to_all | solution.py:19
  146.7 33.7 %all-to-all-start.2 = ((bf16[64,2,128,32]{2,3,1,0:T(8,128)(2,1)}), bf16[64,2,128,32]{2,3,1,0:T(8,128)(2,1)S(1)}, u32[]{:S(2)}, u32[]{:S(2)}) async-start(bf16[64,2,128,32]{2,3,1,0:T(8,128)(2,1)} %bitcast.110), calls=%async_computation.2 | async-start | bytes 2097152 | tf_op jit(solution)/shard_map/all_to_all | solution.py:141
  152.7 42.5 %collective-permute-start = (f32[128,32]{0,1:T(8,128)S(1)}, f32[128,32]{0,1:T(8,128)S(1)}, u32[]{:S(2)}, u32[]{:S(2)}) collective-permute-start(f32[128,32]{0,1:T(8,128)S(1)} %get-tuple-element.43), channel_id=1, source_target_pairs={{0,8},{8,16},{16,24},{24,32},{32,40},{40,48},{48,56},{56,64},{64,7... | collective-permute-start | bytes 49160 | tf_op jit(solution)/shard_map/ppermute | solution.py:10
  156.1 39.2 %collective-permute-start.1 = (f32[128,32]{0,1:T(8,128)S(1)}, f32[128,32]{0,1:T(8,128)S(1)}, u32[]{:S(2)}, u32[]{:S(2)}) collective-permute-start(f32[128,32]{0,1:T(8,128)S(1)} %get-tuple-element.42), channel_id=1, source_target_pairs={{8,0},{16,8},{24,16},{32,24},{40,32},{48,40},{56,48},{64,56},{72,6... | collective-permute-start | bytes 49160 | tf_op jit(solution)/shard_map/ppermute | solution.py:10
  190.7 3.6 %copy-start.4 = (bf16[1024,256]{0,1:T(8,128)(2,1)S(1)}, bf16[1024,256]{0,1:T(8,128)(2,1)}, u32[]{:S(2)}) copy-start(bf16[1024,256]{0,1:T(8,128)(2,1)} %copy-done.3) | copy-start | bytes 1572868
  195.3 0.7 copy-start.7
Sparse Core Ops, SparseCore 0:
  48.9 29.6 all-gather.1

commit v6 on v5

--- a/solution.py
+++ b/solution.py
@@ -52,27 +52,37 @@
     slot_rank = jnp.sum(jnp.where(same_owner & earlier, 1, 0), axis=1).astype(jnp.int32)
     slot_ids = owner_ids * capacity + slot_rank
     slot_hit = slot_ids[:, None] == jnp.arange(peer_count * capacity, dtype=jnp.int32)[None, :]
-    far_request = (jnp.sum(jnp.where(slot_hit, local_ids[:, None] + 1, 0), axis=0) - 1).reshape(
+    request = (jnp.sum(jnp.where(slot_hit, local_ids[:, None] + 1, 0), axis=0) - 1).reshape(
         peer_count, capacity
     )
-    peers = jnp.arange(peer_count, dtype=jnp.int32)
-    halo_request = jnp.where(
-        peers == row_index - 1, blocks - 1, jnp.where(peers == row_index + 1, 0, -1)
+    peers = jnp.arange(peer_count, dtype=jnp.int32)[:, None, None]
+    own_blocks = node_feats.reshape(blocks, tile_size, col_count)
+    halo_out = jnp.where(
+        peers == row_index - 1,
+        own_blocks[0],
+        jnp.where(peers == row_index + 1, own_blocks[blocks - 1], jnp.zeros((), jnp.bfloat16)),
     )
-    request = jnp.concatenate([far_request, halo_request[:, None]], axis=1)
-    wanted = lax.all_to_all(request, "rows", split_axis=0, concat_axis=0, tiled=True)
+    request_rows = jnp.zeros((peer_count, 1, col_count), jnp.bfloat16)
+    request_rows = request_rows.at[:, 0, :capacity].set(request.astype(jnp.bfloat16))
+    first = lax.all_to_all(
+        jnp.concatenate([halo_out, request_rows], axis=1),
+        "rows",
+        split_axis=0,
+        concat_axis=0,
+        tiled=True,
+    )
+    wanted = first[:, tile_size, :capacity].astype(jnp.int32)
     usable = wanted >= 0
     safe_ids = jnp.maximum(wanted, 0)
-    own_blocks = node_feats.reshape(blocks, tile_size, col_count)
     outgoing = jnp.where(
         usable[:, :, None, None], own_blocks[safe_ids], jnp.zeros((), jnp.bfloat16)
     )
     incoming = lax.all_to_all(outgoing, "rows", split_axis=0, concat_axis=0, tiled=True)
-    low = lax.dynamic_index_in_dim(incoming, jnp.maximum(row_index - 1, 0), 0, keepdims=False)
+    low = lax.dynamic_index_in_dim(first, jnp.maximum(row_index - 1, 0), 0, keepdims=False)
     high = lax.dynamic_index_in_dim(
-        incoming, jnp.minimum(row_index + 1, peer_count - 1), 0, keepdims=False
+        first, jnp.minimum(row_index + 1, peer_count - 1), 0, keepdims=False
     )
-    padded = jnp.concatenate([low[capacity], node_feats, high[capacity]], axis=0)
+    padded = jnp.concatenate([low[:tile_size], node_feats, high[:tile_size]], axis=0)
     windows = jnp.concatenate(
         [
             padded[offset * tile_size : offset * tile_size + rows_dev].reshape(
@@ -84,8 +94,9 @@
     )
     band_tiles = band_weights.reshape(blocks, tile_size, 3 * tile_size)
     band_sum = jnp.einsum("bij,bjc->bic", band_tiles, windows, preferred_element_type=jnp.float32)
-    far_slots = incoming[:, :capacity].reshape(peer_count * capacity, tile_size, col_count)
-    fetched = far_slots[slot_ids].reshape(blocks, fanout * tile_size, col_count)
+    fetched = incoming.reshape(peer_count * capacity, tile_size, col_count)[slot_ids].reshape(
+        blocks, fanout * tile_size, col_count
+    )
     far_tiles = far_weights.reshape(blocks, tile_size, fanout * tile_size)
     far_sum = jnp.einsum("bij,bjc->bic", far_tiles, fetched, preferred_element_type=jnp.float32)
     degree = jnp.sum(band_weights.astype(jnp.float32), axis=1) + jnp.sum(
@@ -145,7 +156,7 @@
         concat_axis=0,
         tiled=True,
     ).astype(jnp.float32)
-    target_block = jnp.where(usable, wanted, blocks)[:, :capacity].reshape(-1)
+    target_block = jnp.where(usable, wanted, blocks).reshape(-1)
     owed = jnp.zeros((blocks, tile_size * col_count), jnp.float32)
     owed = owed.at[target_block].add(
         returned.reshape(peer_count * capacity, tile_size * col_count), mode="drop"

time: 204 us -> 208 us (1.020)
  waiting for transfers between devices: 83 us -> 90.1 us
  local copies, waits for them, and re-layouts: 23.6 us -> 20.5 us
  other arithmetic: 11.8 us -> 14.5 us
    all_gather x1, waiting for transfers between devices: 31.1 us -> 0.02 us  [on_device(): gathered = lax.all_gather(packed, 'feat', axis=1, tiled=True)]
    all_to_all x1, waiting for transfers between devices: 3.52 us -> 23.2 us  [on_device(): lax.all_to_all(outgoing, 'rows', split_axis=0, concat_axis=0, tiled=True)]
    all_to_all x1, waiting for transfers between devices: 10.1 us -> 28.3 us  [on_device(): lax.all_to_all(jnp.concatenate([halo_out, request_rows], axis=1), 'rows',...]
    all_to_all x1, starting transfers between devices: 9.51 us -> 6.56 us  [summed_over(): pieces = lax.all_to_all(flat, axis, split_axis=0, concat_axis=0, tiled=True)]
    convert_element_type x0 -> x2, other arithmetic: none -> 2.25 us  [the longest x1 2.24 us: on_device(): wanted = first[:, tile_size, :capacity].astype(jnp.int32)]
  transfers between devices with their start and end apart: 8 -> 8, of which waited for: 6 -> 5; matrix products, arithmetic and copies ran while one was open for 13% -> 15% of each run, Pallas kernels for 0% -> 0%
where the time goes in v6:
time: 208 us
  waiting for transfers between devices  90.1 us (43%)
  starting transfers between devices  47 us (23%)
  local copies, waits for them, and re-layouts  20.5 us (10%)
  between operations  14.6 us (7%)
  other arithmetic  14.5 us (7%)
  blocking collectives  13.5 us (6%)
  matrix products  7.35 us (4%)
    all_to_all x1, waiting for transfers between devices, on_device(): lax.all_to_all(jnp.concatenate([halo_out, request_rows], axis=1), 'rows',...  28.3 us
    all_to_all x1, waiting for transfers between devices, on_device(): lax.all_to_all(outgoing, 'rows', split_axis=0, concat_axis=0, tiled=True)  23.2 us
    all_to_all x1, waiting for transfers between devices, on_device(): lax.all_to_all(returning.reshape(peer_count, capacity, tile_size, col_cou...  18.9 us
    all_to_all x1, starting transfers between devices, on_device(): lax.all_to_all(jnp.concatenate([halo_out, request_rows], axis=1), 'rows',...  16.6 us
    all_gather x1, blocking collectives, on_device(): neighbours_all = lax.all_gather(neighbours, 'feat', axis=1, tiled=True)  13.5 us
    all_to_all x1, waiting for transfers between devices, summed_over(): pieces = lax.all_to_all(flat, axis, split_axis=0, concat_axis=0, tiled=True)  11.1 us
    reshape x2, local copies, waits for them, and re-layouts, on_device(): returned.reshape(peer_count * capacity, tile_size * col_count)  10.3 us
    all_to_all x1, waiting for transfers between devices, summed_over(): lax.all_to_all(spread, axis, split_axis=0, concat_axis=0, tiled=True)  8.48 us
  transfers between devices with their start and end apart: 8, of which 5 were waited for; matrix products, arithmetic and copies ran while one was open for 15% of the time, Pallas kernels for 0%

profile of v6, /device:TPU:8, one launch (start us, length us, event | category | flops | bytes accessed | tf_op | source)
XLA Modules:
  0.0 207.6 jit_solution(12564862527581353301)
XLA Ops:
  10.4 1.3 fusion.6
  11.7 16.6 %all-to-all-start = ((bf16[64,129,32]{1,2,0:T(8,128)(2,1)}), bf16[64,129,32]{1,2,0:T(8,128)(2,1)S(1)}, u32[]{:S(2)}, u32[]{:S(2)}) async-start(bf16[64,129,32]{1,2,0:T(8,128)(2,1)} %fusion.6), calls=%async_computation | async-start | bytes 2097152 | tf_op jit(solution)/shard_map/all_to_all | solution.py:67
  29.2 28.3 %all-to-all-done = bf16[64,129,32]{1,2,0:T(8,128)(2,1)S(1)} async-done(((bf16[64,129,32]{1,2,0:T(8,128)(2,1)}), bf16[64,129,32]{1,2,0:T(8,128)(2,1)S(1)}, u32[]{:S(2)}, u32[]{:S(2)}) %all-to-all-start) | async-done | bytes 528416 | tf_op jit(solution)/shard_map/all_to_all | solution.py:67
  57.6 2.2 %convert_reduce_fusion.2 = (s32[64,2]{1,0:T(8,128)}, s32[64,2]{1,0:T(8,128)S(1)}) fusion(bf16[64,129,32]{1,2,0:T(8,128)(2,1)S(1)} %all-to-all-done), kind=kLoop, calls=%fused_computation.50 | loop fusion | flops 256 | bytes 1280 | tf_op jit(solution)/shard_map/convert_element_type | solution.py:74
  61.0 1.2 broadcast_select_fusion
  62.3 6.9 %all-to-all-start.1 = ((bf16[64,2,128,32]{2,3,1,0:T(8,128)(2,1)}), bf16[64,2,128,32]{2,3,1,0:T(8,128)(2,1)S(1)}, u32[]{:S(2)}, u32[]{:S(2)}) async-start(bf16[64,2,128,32]{2,3,1,0:T(8,128)(2,1)} %broadcast_select_fusion), calls=%async_computation.1 | async-start | bytes 2097152 | tf_op jit(solution)/shard_map/all_to_all | solution.py:80
  72.2 2.4 %fusion.7 = f32[1024,256]{0,1:T(8,128)} fusion(bf16[256,256]{1,0:T(8,128)(2,1)S(1)} %copy-done.8, bf16[2064,256]{0,1:T(8,128)(2,1)} %all-gather.2.cloned.1.call-done), kind=kOutput, calls=%fused_computation.24 | convolution fusion | flops 134217728 | bytes 1703936 | tf_op jit(solution)/shard_map/dot_general | solution.py:112
  74.5 23.2 %all-to-all-done.1 = bf16[64,2,128,32]{2,3,1,0:T(8,128)(2,1)S(1)} async-done(((bf16[64,2,128,32]{2,3,1,0:T(8,128)(2,1)}), bf16[64,2,128,32]{2,3,1,0:T(8,128)(2,1)S(1)}, u32[]{:S(2)}, u32[]{:S(2)}) %all-to-all-start.1) | async-done | bytes 1048608 | tf_op jit(solution)/shard_map/all_to_all | solution.py:80
  98.7 13.5 %all_gather.7 = bf16[1024,256]{0,1:T(8,128)(2,1)S(1)} all-gather(bf16[1024,32]{0,1:T(8,128)(2,1)S(1)} %fusion.17), channel_id=1, replica_groups=mesh['rows'=64,'feat'=8] {'feat'}, dimensions={1}, use_global_device_ids=true | all-gather | bytes 589824 | tf_op jit(solution)/shard_map/all_gather | solution.py:110
  112.2 3.0 %multiply_convert_fusion = (bf16[1024,256]{0,1:T(8,128)(2,1)S(1)}, f32[1024,256]{0,1:T(8,128)}) fusion(bf16[2064,256]{0,1:T(8,128)(2,1)} %all-gather.2.cloned.1.call-done, f32[256]{0:T(256)S(1)} %fusion.18, f32[1024,256]{0,1:T(8,128)} %fusion.7, bf16[1024,256]{0,1:T(8,128)(2,1)S(1)} %all_gather.7, bf16[256,256]{1,0:T(8,128)(2,1)S(1)} %copy-done), kind=kOutput, calls=%fused_computation.21 | convolution fusion | flops 137363456 | bytes 3802112 | tf_op jit(solution)/shard_map/dot_general | solution.py:113
  116.4 6.6 %all-to-all-start.3 = ((f32[64,1,256]{2,1,0:T(1,128)}), f32[64,1,256]{2,1,0:T(1,128)S(1)}, u32[]{:S(2)}, u32[]{:S(2)}) async-start(f32[64,1,256]{2,1,0:T(1,128)} %copy.122), calls=%async_computation.3 | async-start | bytes 131072 | tf_op jit(solution)/shard_map/all_to_all | solution.py:16
  123.2 11.1 %all-to-all-done.3 = f32[64,1,256]{2,1,0:T(1,128)S(1)} async-done(((f32[64,1,256]{2,1,0:T(1,128)}), f32[64,1,256]{2,1,0:T(1,128)S(1)}, u32[]{:S(2)}, u32[]{:S(2)}) %all-to-all-start.3) | async-done | bytes 65568 | tf_op jit(solution)/shard_map/all_to_all | solution.py:16
  135.1 5.4 %all-to-all-start.4 = ((f32[64,1,256]{2,1,0:T(1,128)}), f32[64,1,256]{2,1,0:T(1,128)S(1)}, u32[]{:S(2)}, u32[]{:S(2)}) async-start(f32[64,1,256]{2,1,0:T(1,128)} %broadcast_in_dim.102), calls=%async_computation.4 | async-start | bytes 131072 | tf_op jit(solution)/shard_map/all_to_all | solution.py:19
  141.3 1.0 scatter_fusion
  142.3 1.2 convert_element_type.91
  143.5 8.5 %all-to-all-done.4 = f32[64,1,256]{2,1,0:T(1,128)S(1)} async-done(((f32[64,1,256]{2,1,0:T(1,128)}), f32[64,1,256]{2,1,0:T(1,128)S(1)}, u32[]{:S(2)}, u32[]{:S(2)}) %all-to-all-start.4) | async-done | bytes 65568 | tf_op jit(solution)/shard_map/all_to_all | solution.py:19
  152.0 5.6 %all-to-all-start.2 = ((bf16[64,2,128,32]{2,3,1,0:T(8,128)(2,1)}), bf16[64,2,128,32]{2,3,1,0:T(8,128)(2,1)S(1)}, u32[]{:S(2)}, u32[]{:S(2)}) async-start(bf16[64,2,128,32]{2,3,1,0:T(8,128)(2,1)} %bitcast.109), calls=%async_computation.2 | async-start | bytes 2097152 | tf_op jit(solution)/shard_map/all_to_all | solution.py:152
  158.1 3.4 %collective-permute-start = (f32[128,32]{0,1:T(8,128)S(1)}, f32[128,32]{0,1:T(8,128)S(1)}, u32[]{:S(2)}, u32[]{:S(2)}) collective-permute-start(f32[128,32]{0,1:T(8,128)S(1)} %get-tuple-element.57), channel_id=1, source_target_pairs={{0,8},{8,16},{16,24},{24,32},{32,40},{40,48},{48,56},{56,64},{64,7... | collective-permute-start | bytes 49160 | tf_op jit(solution)/shard_map/ppermute | solution.py:10
  161.5 2.5 %collective-permute-start.1 = (f32[128,32]{0,1:T(8,128)S(1)}, f32[128,32]{0,1:T(8,128)S(1)}, u32[]{:S(2)}, u32[]{:S(2)}) collective-permute-start(f32[128,32]{0,1:T(8,128)S(1)} %get-tuple-element.56), channel_id=1, source_target_pairs={{8,0},{16,8},{24,16},{32,24},{40,32},{48,40},{56,48},{64,56},{72,6... | collective-permute-start | bytes 49160 | tf_op jit(solution)/shard_map/ppermute | solution.py:10
  164.0 1.6 multiply_convert_fusion.1
  166.9 18.9 %all-to-all-done.2 = bf16[64,2,128,32]{2,3,1,0:T(8,128)(2,1)S(1)} async-done(((bf16[64,2,128,32]{2,3,1,0:T(8,128)(2,1)}), bf16[64,2,128,32]{2,3,1,0:T(8,128)(2,1)S(1)}, u32[]{:S(2)}, u32[]{:S(2)}) %all-to-all-start.2) | async-done | bytes 1048608 | tf_op jit(solution)/shard_map/all_to_all | solution.py:152
  185.8 4.1 %copy.120 = f32[64,2,128,32]{3,2,1,0:T(8,128)} copy(bf16[64,2,128,32]{2,3,1,0:T(8,128)(2,1)S(1)} %all-to-all-done.2) | data formatting | bytes 3145728 | tf_op jit(solution)/shard_map/reshape | solution.py:162
  189.9 6.3 %reshape.370 = f32[128,4096]{1,0:T(8,128)S(1)} reshape(f32[64,2,128,32]{3,2,1,0:T(8,128)} %copy.120) | data formatting | bytes 4194304 | tf_op jit(solution)/shard_map/reshape | solution.py:162
  196.2 3.3 %scatter_custom_fusion.1 = f32[8,4096]{1,0:T(8,128)S(1)} fusion(s32[128]{0:T(128)S(1)} %fusion.41, f32[128,4096]{1,0:T(8,128)S(1)} %reshape.370, f32[]{:T(128)} %constant.156.clone.1), kind=kCustom, calls=%fused_computation.65 | custom fusion | flops 524288 | bytes 131076 | tf_op jit(solution)/shard_map/scatter-add | solution.py:161
  (104 shorter events, 15.0 us)
Async XLA Ops:
  7.2 105.0 %copy-start = (bf16[256,256]{1,0:T(8,128)(2,1)S(1)}, bf16[256,256]{1,0:T(8,128)(2,1)}, u32[]{:S(2)}) copy-start(bf16[256,256]{1,0:T(8,128)(2,1)} %param.23) | copy-start | bytes 393220
  10.2 18.1 %copy-start.12 = (f32[32]{0:T(128)S(1)}, f32[32]{0:T(128)}, u32[]{:S(2)}) copy-start(f32[32]{0:T(128)} %param.24) | copy-start | bytes 388
  10.2 18.3 %copy-start.6 = (bf16[1024,32]{0,1:T(8,128)(2,1)S(1)}, bf16[1024,32]{0,1:T(8,128)(2,1)}, u32[]{:S(2)}) copy-start(bf16[1024,32]{0,1:T(8,128)(2,1)} %param.17) | copy-start | bytes 196612
  10.2 18.3 %copy-start.10 = (bf16[1024,32]{0,1:T(8,128)(2,1)S(1)}, bf16[1024,32]{0,1:T(8,128)(2,1)}, u32[]{:S(2)}) copy-start(bf16[1024,32]{0,1:T(8,128)(2,1)} %param.25) | copy-start | bytes 196612
  11.7 45.8 %all-to-all-start = ((bf16[64,129,32]{1,2,0:T(8,128)(2,1)}), bf16[64,129,32]{1,2,0:T(8,128)(2,1)S(1)}, u32[]{:S(2)}, u32[]{:S(2)}) async-start(bf16[64,129,32]{1,2,0:T(8,128)(2,1)} %fusion.6), calls=%async_computation | async-start | bytes 2097152 | tf_op jit(solution)/shard_map/all_to_all | solution.py:67
  28.3 42.8 %all-gather.2.cloned.1.call-start = ((), (), s32[]{:S(2)}) async-start(), calls=%async_computation.5 | async-start | bytes 1253376 | tf_op jit(solution)/shard_map/all_gather | solution.py:42
  57.5 3.5 %copy-start.5 = (bf16[64,129,32]{1,2,0:T(8,128)(2,1)}, bf16[64,129,32]{1,2,0:T(8,128)(2,1)S(1)}, u32[]{:S(2)}) copy-start(bf16[64,129,32]{1,2,0:T(8,128)(2,1)S(1)} %all-to-all-done) | copy-start | bytes 1585156
  61.0 8.2 %copy-start.11 = (s32[8,2]{0,1:T(2,128)S(1)}, s32[8,2]{0,1:T(2,128)}, u32[]{:S(2)}) copy-start(s32[8,2]{0,1:T(2,128)} %param.20) | copy-start | bytes 196
  61.0 8.4 %copy-start.2 = (bf16[1024,256]{1,0:T(8,128)(2,1)S(1)}, bf16[1024,256]{1,0:T(8,128)(2,1)}, u32[]{:S(2)}) copy-start(bf16[1024,256]{1,0:T(8,128)(2,1)} %param.19) | copy-start | bytes 1572868
  61.0 8.6 %copy-start.1 = (bf16[1024,384]{1,0:T(8,128)(2,1)S(1)}, bf16[1024,384]{1,0:T(8,128)(2,1)}, u32[]{:S(2)}) copy-start(bf16[1024,384]{1,0:T(8,128)(2,1)} %param.18) | copy-start | bytes 2359300
  62.3 35.5 %all-to-all-start.1 = ((bf16[64,2,128,32]{2,3,1,0:T(8,128)(2,1)}), bf16[64,2,128,32]{2,3,1,0:T(8,128)(2,1)S(1)}, u32[]{:S(2)}, u32[]{:S(2)}) async-start(bf16[64,2,128,32]{2,3,1,0:T(8,128)(2,1)} %broadcast_select_fusion), calls=%async_computation.1 | async-start | bytes 2097152 | tf_op jit(solution)/shard_map/all_to_all | solution.py:80
  69.2 3.0 %copy-start.8 = (bf16[256,256]{1,0:T(8,128)(2,1)S(1)}, bf16[256,256]{1,0:T(8,128)(2,1)}, u32[]{:S(2)}) copy-start(bf16[256,256]{1,0:T(8,128)(2,1)} %param.22) | copy-start | bytes 393220
  115.2 25.7 %copy-start.3 = (bf16[1024,256]{0,1:T(8,128)(2,1)}, bf16[1024,256]{0,1:T(8,128)(2,1)S(1)}, u32[]{:S(2)}) copy-start(bf16[1024,256]{0,1:T(8,128)(2,1)S(1)} %get-tuple-element.70) | copy-start | bytes 1572868
  116.4 17.9 %all-to-all-start.3 = ((f32[64,1,256]{2,1,0:T(1,128)}), f32[64,1,256]{2,1,0:T(1,128)S(1)}, u32[]{:S(2)}, u32[]{:S(2)}) async-start(f32[64,1,256]{2,1,0:T(1,128)} %copy.122), calls=%async_computation.3 | async-start | bytes 131072 | tf_op jit(solution)/shard_map/all_to_all | solution.py:16
  135.1 16.9 %all-to-all-start.4 = ((f32[64,1,256]{2,1,0:T(1,128)}), f32[64,1,256]{2,1,0:T(1,128)S(1)}, u32[]{:S(2)}, u32[]{:S(2)}) async-start(f32[64,1,256]{2,1,0:T(1,128)} %broadcast_in_dim.102), calls=%async_computation.4 | async-start | bytes 131072 | tf_op jit(solution)/shard_map/all_to_all | solution.py:19
  142.3 15.3 %copy-start.9 = (s32[64,2]{1,0:T(8,128)S(1)}, s32[64,2]{1,0:T(8,128)}, u32[]{:S(2)}) copy-start(s32[64,2]{1,0:T(8,128)} %get-tuple-element.52) | copy-start | bytes 1540
  152.0 33.9 %all-to-all-start.2 = ((bf16[64,2,128,32]{2,3,1,0:T(8,128)(2,1)}), bf16[64,2,128,32]{2,3,1,0:T(8,128)(2,1)S(1)}, u32[]{:S(2)}, u32[]{:S(2)}) async-start(bf16[64,2,128,32]{2,3,1,0:T(8,128)(2,1)} %bitcast.109), calls=%async_computation.2 | async-start | bytes 2097152 | tf_op jit(solution)/shard_map/all_to_all | solution.py:152
  158.1 41.9 %collective-permute-start = (f32[128,32]{0,1:T(8,128)S(1)}, f32[128,32]{0,1:T(8,128)S(1)}, u32[]{:S(2)}, u32[]{:S(2)}) collective-permute-start(f32[128,32]{0,1:T(8,128)S(1)} %get-tuple-element.57), channel_id=1, source_target_pairs={{0,8},{8,16},{16,24},{24,32},{32,40},{40,48},{48,56},{56,64},{64,7... | collective-permute-start | bytes 49160 | tf_op jit(solution)/shard_map/ppermute | solution.py:10
  161.5 38.5 %collective-permute-start.1 = (f32[128,32]{0,1:T(8,128)S(1)}, f32[128,32]{0,1:T(8,128)S(1)}, u32[]{:S(2)}, u32[]{:S(2)}) collective-permute-start(f32[128,32]{0,1:T(8,128)S(1)} %get-tuple-element.56), channel_id=1, source_target_pairs={{8,0},{16,8},{24,16},{32,24},{40,32},{48,40},{56,48},{64,56},{72,6... | collective-permute-start | bytes 49160 | tf_op jit(solution)/shard_map/ppermute | solution.py:10
  189.9 9.9 %copy-start.4 = (bf16[1024,256]{0,1:T(8,128)(2,1)S(1)}, bf16[1024,256]{0,1:T(8,128)(2,1)}, u32[]{:S(2)}) copy-start(bf16[1024,256]{0,1:T(8,128)(2,1)} %copy-done.3) | copy-start | bytes 1572868
  200.1 0.7 copy-start.7
Sparse Core Ops, SparseCore 0:
  31.2 29.5 all-gather.1

commit v7 on v4

--- a/solution.py
+++ b/solution.py
@@ -21,16 +21,6 @@
     devices = range(lax.axis_size(axis))
     route = [(i - distance, i) for i in devices if i - distance in devices]
     return lax.ppermute(block, axis, route)
-
-
-def summed_over(parts, axis):
-    count = lax.axis_size(axis)
-    flat = parts.reshape(count, -1)
-    pieces = lax.all_to_all(flat, axis, split_axis=0, concat_axis=0, tiled=True)
-    mine = jnp.sum(pieces, axis=0, keepdims=True)
-    spread = jnp.broadcast_to(mine, flat.shape)
-    whole = lax.all_to_all(spread, axis, split_axis=0, concat_axis=0, tiled=True)
-    return whole.reshape(parts.shape)
 
 
 def on_device(
@@ -115,9 +105,6 @@
     grad_scale = float(rows_dev * peer_count) ** (-0.5)
     part_self = jnp.einsum("rc,rf->cf", node_feats, full_grad, preferred_element_type=jnp.float32)
     part_neigh = jnp.einsum("rc,rf->cf", neighbours, full_grad, preferred_element_type=jnp.float32)
-    sum_self, sum_neigh = summed_over(jnp.stack([part_self, part_neigh]), "rows")
-    grad_self = sum_self * grad_scale
-    grad_neigh = sum_neigh * grad_scale
     dense_grad = jnp.einsum("rf,cf->rc", full_grad, rows_self, preferred_element_type=jnp.float32)
     grad_agg = jnp.einsum("rf,cf->rc", full_grad, rows_neigh, preferred_element_type=jnp.float32)
     grad_neighbours = (grad_agg / degree[:, None]).astype(jnp.bfloat16)
@@ -142,13 +129,30 @@
     )
     returning = jnp.zeros((peer_count * capacity, tile_size, col_count), jnp.float32)
     returning = returning.at[slot_ids].set(grad_fetched.reshape(entries, tile_size, col_count))
-    returned = lax.all_to_all(
-        returning.reshape(peer_count, capacity, tile_size, col_count).astype(jnp.bfloat16),
-        "rows",
-        split_axis=0,
-        concat_axis=0,
-        tiled=True,
-    ).astype(jnp.float32)
+    partials = jnp.stack([part_self, part_neigh]).reshape(peer_count, -1)
+    high = lax.reduce_precision(partials, exponent_bits=8, mantissa_bits=7)
+    coded = jnp.stack(
+        [high.astype(jnp.bfloat16), (partials - high).astype(jnp.bfloat16)], axis=1
+    ).reshape(peer_count, 1, -1, col_count)
+    coded_rows = coded.shape[2]
+    coded = jnp.pad(coded, ((0, 0), (0, 0), (0, tile_size - coded_rows), (0, 0)))
+    payload = jnp.concatenate(
+        [
+            returning.reshape(peer_count, capacity, tile_size, col_count).astype(jnp.bfloat16),
+            coded,
+        ],
+        axis=1,
+    )
+    arrived = lax.all_to_all(payload, "rows", split_axis=0, concat_axis=0, tiled=True)
+    returned = arrived[:, :capacity].astype(jnp.float32)
+    codes = arrived[:, capacity, :coded_rows].reshape(peer_count, 2, -1).astype(jnp.float32)
+    mine = jnp.sum(codes[:, 0] + codes[:, 1], axis=0, keepdims=True)
+    whole = lax.all_to_all(
+        jnp.broadcast_to(mine, partials.shape), "rows", split_axis=0, concat_axis=0, tiled=True
+    )
+    sum_self, sum_neigh = whole.reshape(2, col_count, -1)
+    grad_self = sum_self * grad_scale
+    grad_neigh = sum_neigh * grad_scale
     target_block = jnp.where(usable, wanted, blocks).reshape(-1)
     owed = jnp.zeros((blocks, tile_size * col_count), jnp.float32)
     owed = owed.at[target_block].add(

time: 192 us -> 186 us (0.969)
  the two profiles are of different devices: /device:TPU:8 before, /device:TPU:1 now
where the time goes in v7:
time: 186 us; the launch traced here: 185 us
  waiting for transfers between devices  56.2 us (30%)
  starting transfers between devices  49.7 us (27%)
  local copies, waits for them, and re-layouts  23.4 us (13%)
  blocking collectives  18.4 us (10%)
  other arithmetic  15.2 us (8%)
  between operations  14.6 us (8%)
  matrix products  7.4 us (4%)
    all_to_all x1, waiting for transfers between devices, on_device(): lax.all_to_all(payload, 'rows', split_axis=0, concat_axis=0, tiled=True)  31.8 us
    all_gather x1, blocking collectives, on_device(): neighbours_all = lax.all_gather(neighbours, 'feat', axis=1, tiled=True)  18.4 us
    all_to_all x1, starting transfers between devices, on_device(): lax.all_to_all(request, 'rows', split_axis=0, concat_axis=0, tiled=True)  17.1 us
    ppermute x1, waiting for transfers between devices, extended(): lax.ppermute(lax.slice_in_dim(block, block.shape[dim] - width, None, axis...  11.8 us
    reshape x2, local copies, waits for them, and re-layouts, on_device(): returned.reshape(peer_count * capacity, tile_size * col_count)  11 us
    all_to_all x1, starting transfers between devices, on_device(): lax.all_to_all(payload, 'rows', split_axis=0, concat_axis=0, tiled=True)  9.56 us
    all_to_all x1, starting transfers between devices, on_device(): lax.all_to_all(jnp.broadcast_to(mine, partials.shape), 'rows', split_axis...  8.68 us
    all_to_all x1, waiting for transfers between devices, on_device(): lax.all_to_all(request, 'rows', split_axis=0, concat_axis=0, tiled=True)  7.52 us
  transfers between devices with their start and end apart: 9, of which 5 were waited for; matrix products, arithmetic and copies ran while one was open for 17% of the time, Pallas kernels for 0%

profile of v7, /device:TPU:1, one launch (start us, length us, event | category | flops | bytes accessed | tf_op | source)
XLA Modules:
  0.0 184.8 jit_solution(8025988254991178645)
XLA Ops:
  10.0 17.1 %all-to-all-start = ((s32[64,1,2]{2,1,0:T(1,128)}), s32[64,1,2]{2,1,0:T(1,128)S(1)}, u32[]{:S(2)}, u32[]{:S(2)}) async-start(s32[64,1,2]{2,1,0:T(1,128)} %bitcast.4), calls=%async_computation | async-start | bytes 65536 | tf_op jit(solution)/shard_map/all_to_all | solution.py:72
  27.9 1.5 fusion.16
  30.3 7.5 %all-to-all-done = s32[64,1,2]{2,1,0:T(1,128)S(1)} async-done(((s32[64,1,2]{2,1,0:T(1,128)}), s32[64,1,2]{2,1,0:T(1,128)S(1)}, u32[]{:S(2)}, u32[]{:S(2)}) %all-to-all-start) | async-done | bytes 544 | tf_op jit(solution)/shard_map/all_to_all | solution.py:72
  40.4 1.2 broadcast_select_fusion
  41.6 4.7 %all-to-all-start.1 = ((bf16[64,2,128,32]{2,3,1,0:T(8,128)(2,1)}), bf16[64,2,128,32]{2,3,1,0:T(8,128)(2,1)S(1)}, u32[]{:S(2)}, u32[]{:S(2)}) async-start(bf16[64,2,128,32]{2,3,1,0:T(8,128)(2,1)} %broadcast_select_fusion), calls=%async_computation.1 | async-start | bytes 2097152 | tf_op jit(solution)/shard_map/all_to_all | solution.py:79
  46.3 3.0 %collective-permute-start = (bf16[128,32]{0,1:T(8,128)(2,1)S(1)}, bf16[128,32]{0,1:T(8,128)(2,1)S(1)}, u32[]{:S(2)}, u32[]{:S(2)}) collective-permute-start(bf16[128,32]{0,1:T(8,128)(2,1)S(1)} %get-tuple-element.53), channel_id=1, source_target_pairs={{0,8},{8,16},{16,24},{24,32},{32,40},{40,48},{48,56},{56,64},{64,7... | collective-permute-start | bytes 24584 | tf_op jit(solution)/shard_map/ppermute | solution.py:12
  49.4 1.3 collective-permute-start.1
  51.3 11.8 %collective-permute-done = bf16[128,32]{0,1:T(8,128)(2,1)S(1)} collective-permute-done((bf16[128,32]{0,1:T(8,128)(2,1)S(1)}, bf16[128,32]{0,1:T(8,128)(2,1)S(1)}, u32[]{:S(2)}, u32[]{:S(2)}) %collective-permute-start) | collective-permute-done | bytes 8224 | tf_op jit(solution)/shard_map/ppermute | solution.py:12
  63.1 4.9 %collective-permute-done.1 = bf16[128,32]{0,1:T(8,128)(2,1)S(1)} collective-permute-done((bf16[128,32]{0,1:T(8,128)(2,1)S(1)}, bf16[128,32]{0,1:T(8,128)(2,1)S(1)}, u32[]{:S(2)}, u32[]{:S(2)}) %collective-permute-start.1) | collective-permute-done | bytes 8224 | tf_op jit(solution)/shard_map/ppermute | solution.py:15
  69.5 2.4 %fusion.7 = f32[1024,256]{0,1:T(8,128)} fusion(bf16[256,256]{1,0:T(8,128)(2,1)S(1)} %copy-done.9, bf16[2064,256]{0,1:T(8,128)(2,1)} %all-gather.2.cloned.1.call-done), kind=kOutput, calls=%fused_computation.25 | convolution fusion | flops 134217728 | bytes 1703936 | tf_op jit(solution)/shard_map/dot_general | solution.py:95
  73.1 18.4 %all_gather.7 = bf16[1024,256]{0,1:T(8,128)(2,1)S(1)} all-gather(bf16[1024,32]{0,1:T(8,128)(2,1)S(1)} %fusion.17), channel_id=1, replica_groups=mesh['rows'=64,'feat'=8] {'feat'}, dimensions={1}, use_global_device_ids=true | all-gather | bytes 589824 | tf_op jit(solution)/shard_map/all_gather | solution.py:93
  91.5 3.0 %multiply_convert_fusion = (bf16[1024,256]{0,1:T(8,128)(2,1)S(1)}, f32[1024,256]{0,1:T(8,128)}) fusion(bf16[2064,256]{0,1:T(8,128)(2,1)} %all-gather.2.cloned.1.call-done, f32[256]{0:T(256)S(1)} %fusion.19, f32[1024,256]{0,1:T(8,128)} %fusion.7, bf16[1024,256]{0,1:T(8,128)(2,1)S(1)} %all_gather.7, bf16[256,256]{1,0:T(8,128)(2,1)S(1)} %copy-done), kind=kOutput, calls=%fused_computation.22 | convolution fusion | flops 137363456 | bytes 3802112 | tf_op jit(solution)/shard_map/dot_general | solution.py:96
  95.9 1.5 copy.161
  99.8 1.4 fusion.1
  101.2 9.6 %all-to-all-start.2 = ((bf16[64,3,128,32]{2,3,1,0:T(8,128)(2,1)}), bf16[64,3,128,32]{2,3,1,0:T(8,128)(2,1)S(1)}, u32[]{:S(2)}, u32[]{:S(2)}) async-start(bf16[64,3,128,32]{2,3,1,0:T(8,128)(2,1)} %fusion.1), calls=%async_computation.2 | async-start | bytes 3145728 | tf_op jit(solution)/shard_map/all_to_all | solution.py:146
  111.3 1.3 collective-permute-start.3
  112.6 4.0 %collective-permute-start.2 = (f32[128,32]{0,1:T(8,128)S(1)}, f32[128,32]{0,1:T(8,128)S(1)}, u32[]{:S(2)}, u32[]{:S(2)}) collective-permute-start(f32[128,32]{0,1:T(8,128)S(1)} %get-tuple-element.43), channel_id=1, source_target_pairs={{0,8},{8,16},{16,24},{24,32},{32,40},{40,48},{48,56},{56,64},{64,7... | collective-permute-start | bytes 49160 | tf_op jit(solution)/shard_map/ppermute | solution.py:23
  116.6 1.6 multiply_convert_fusion.1
  118.2 31.8 %all-to-all-done.2 = bf16[64,3,128,32]{2,3,1,0:T(8,128)(2,1)S(1)} async-done(((bf16[64,3,128,32]{2,3,1,0:T(8,128)(2,1)}), bf16[64,3,128,32]{2,3,1,0:T(8,128)(2,1)S(1)}, u32[]{:S(2)}, u32[]{:S(2)}) %all-to-all-start.2) | async-done | bytes 1572896 | tf_op jit(solution)/shard_map/all_to_all | solution.py:146
  151.5 8.7 %all-to-all-start.3 = ((f32[64,1,256]{2,1,0:T(1,128)}), f32[64,1,256]{2,1,0:T(1,128)S(1)}, u32[]{:S(2)}, u32[]{:S(2)}) async-start(f32[64,1,256]{2,1,0:T(1,128)} %broadcast_in_dim.67), calls=%async_computation.3 | async-start | bytes 131072 | tf_op jit(solution)/shard_map/all_to_all | solution.py:150
  160.2 1.5 slice_convert_fusion
  161.8 4.7 %copy.155 = f32[64,2,128,32]{3,2,1,0:T(8,128)} copy(f32[64,2,128,32]{2,3,1,0:T(8,128)S(1)} %slice_convert_fusion) | data formatting | bytes 4194304 | tf_op jit(solution)/shard_map/reshape | solution.py:159
  166.4 6.3 %reshape.353 = f32[128,4096]{1,0:T(8,128)S(1)} reshape(f32[64,2,128,32]{3,2,1,0:T(8,128)} %copy.155) | data formatting | bytes 4194304 | tf_op jit(solution)/shard_map/reshape | solution.py:159
  172.7 3.3 %scatter_custom_fusion.1 = f32[8,4096]{1,0:T(8,128)S(1)} fusion(s32[128]{0:T(128)S(1)} %fusion.42, f32[128,4096]{1,0:T(8,128)S(1)} %reshape.353, f32[]{:T(128)} %constant.112.clone.1), kind=kCustom, calls=%fused_computation.67 | custom fusion | flops 524288 | bytes 131076 | tf_op jit(solution)/shard_map/scatter-add | solution.py:158
  (106 shorter events, 17.8 us)
Async XLA Ops:
  7.2 84.3 %copy-start = (bf16[256,256]{1,0:T(8,128)(2,1)S(1)}, bf16[256,256]{1,0:T(8,128)(2,1)}, u32[]{:S(2)}) copy-start(bf16[256,256]{1,0:T(8,128)(2,1)} %param.21) | copy-start | bytes 393220
  10.0 27.9 %all-to-all-start = ((s32[64,1,2]{2,1,0:T(1,128)}), s32[64,1,2]{2,1,0:T(1,128)S(1)}, u32[]{:S(2)}, u32[]{:S(2)}) async-start(s32[64,1,2]{2,1,0:T(1,128)} %bitcast.4), calls=%async_computation | async-start | bytes 65536 | tf_op jit(solution)/shard_map/all_to_all | solution.py:72
  27.1 41.3 %all-gather.2.cloned.1.call-start = ((), (), s32[]{:S(2)}) async-start(), calls=%async_computation.4 | async-start | bytes 1253376 | tf_op jit(solution)/shard_map/all_gather | solution.py:44
  40.4 5.9 %copy-start.7 = (bf16[1024,32]{0,1:T(8,128)(2,1)S(1)}, bf16[1024,32]{0,1:T(8,128)(2,1)}, u32[]{:S(2)}) copy-start(bf16[1024,32]{0,1:T(8,128)(2,1)} %param.15) | copy-start | bytes 196612
  40.4 10.3 %copy-start.10 = (s32[8,2]{0,1:T(2,128)S(1)}, s32[8,2]{0,1:T(2,128)}, u32[]{:S(2)}) copy-start(s32[8,2]{0,1:T(2,128)} %param.18) | copy-start | bytes 196
  40.4 10.4 %copy-start.3 = (bf16[1024,256]{1,0:T(8,128)(2,1)S(1)}, bf16[1024,256]{1,0:T(8,128)(2,1)}, u32[]{:S(2)}) copy-start(bf16[1024,256]{1,0:T(8,128)(2,1)} %param.17) | copy-start | bytes 1572868
  40.4 10.7 %copy-start.1 = (bf16[1024,384]{1,0:T(8,128)(2,1)S(1)}, bf16[1024,384]{1,0:T(8,128)(2,1)}, u32[]{:S(2)}) copy-start(bf16[1024,384]{1,0:T(8,128)(2,1)} %param.16) | copy-start | bytes 2359300
  41.6 30.4 %all-to-all-start.1 = ((bf16[64,2,128,32]{2,3,1,0:T(8,128)(2,1)}), bf16[64,2,128,32]{2,3,1,0:T(8,128)(2,1)S(1)}, u32[]{:S(2)}, u32[]{:S(2)}) async-start(bf16[64,2,128,32]{2,3,1,0:T(8,128)(2,1)} %broadcast_select_fusion), calls=%async_computation.1 | async-start | bytes 2097152 | tf_op jit(solution)/shard_map/all_to_all | solution.py:79
  46.3 23.2 %copy-start.9 = (bf16[256,256]{1,0:T(8,128)(2,1)S(1)}, bf16[256,256]{1,0:T(8,128)(2,1)}, u32[]{:S(2)}) copy-start(bf16[256,256]{1,0:T(8,128)(2,1)} %param.20) | copy-start | bytes 393220
  46.3 16.8 %collective-permute-start = (bf16[128,32]{0,1:T(8,128)(2,1)S(1)}, bf16[128,32]{0,1:T(8,128)(2,1)S(1)}, u32[]{:S(2)}, u32[]{:S(2)}) collective-permute-start(bf16[128,32]{0,1:T(8,128)(2,1)S(1)} %get-tuple-element.53), channel_id=1, source_target_pairs={{0,8},{8,16},{16,24},{24,32},{32,40},{40,48},{48,56},{56,64},{64,7... | collective-permute-start | bytes 24584 | tf_op jit(solution)/shard_map/ppermute | solution.py:12
  49.4 18.6 %collective-permute-start.1 = (bf16[128,32]{0,1:T(8,128)(2,1)S(1)}, bf16[128,32]{0,1:T(8,128)(2,1)S(1)}, u32[]{:S(2)}, u32[]{:S(2)}) collective-permute-start(bf16[128,32]{0,1:T(8,128)(2,1)S(1)} %get-tuple-element.54), channel_id=1, source_target_pairs={{8,0},{16,8},{24,16},{32,24},{40,32},{48,40},{56,48},{64,56},{72,6... | collective-permute-start | bytes 24584 | tf_op jit(solution)/shard_map/ppermute | solution.py:15
  94.5 1.3 copy-start.4
  98.8 1.0 copy-start.6
  101.2 48.8 %all-to-all-start.2 = ((bf16[64,3,128,32]{2,3,1,0:T(8,128)(2,1)}), bf16[64,3,128,32]{2,3,1,0:T(8,128)(2,1)S(1)}, u32[]{:S(2)}, u32[]{:S(2)}) async-start(bf16[64,3,128,32]{2,3,1,0:T(8,128)(2,1)} %fusion.1), calls=%async_computation.2 | async-start | bytes 3145728 | tf_op jit(solution)/shard_map/all_to_all | solution.py:146
  111.3 65.2 %collective-permute-start.3 = (f32[128,32]{0,1:T(8,128)S(1)}, f32[128,32]{0,1:T(8,128)S(1)}, u32[]{:S(2)}, u32[]{:S(2)}) collective-permute-start(f32[128,32]{0,1:T(8,128)S(1)} %get-tuple-element.42), channel_id=1, source_target_pairs={{8,0},{16,8},{24,16},{32,24},{40,32},{48,40},{56,48},{64,56},{72,6... | collective-permute-start | bytes 49160 | tf_op jit(solution)/shard_map/ppermute | solution.py:23
  112.6 63.9 %collective-permute-start.2 = (f32[128,32]{0,1:T(8,128)S(1)}, f32[128,32]{0,1:T(8,128)S(1)}, u32[]{:S(2)}, u32[]{:S(2)}) collective-permute-start(f32[128,32]{0,1:T(8,128)S(1)} %get-tuple-element.43), channel_id=1, source_target_pairs={{0,8},{8,16},{16,24},{24,32},{32,40},{40,48},{48,56},{56,64},{64,7... | collective-permute-start | bytes 49160 | tf_op jit(solution)/shard_map/ppermute | solution.py:23
  150.0 1.5 copy-start.2
  151.5 25.1 %all-to-all-start.3 = ((f32[64,1,256]{2,1,0:T(1,128)}), f32[64,1,256]{2,1,0:T(1,128)S(1)}, u32[]{:S(2)}, u32[]{:S(2)}) async-start(f32[64,1,256]{2,1,0:T(1,128)} %broadcast_in_dim.67), calls=%async_computation.3 | async-start | bytes 131072 | tf_op jit(solution)/shard_map/all_to_all | solution.py:150
  166.4 9.9 %copy-start.5 = (bf16[1024,256]{0,1:T(8,128)(2,1)S(1)}, bf16[1024,256]{0,1:T(8,128)(2,1)}, u32[]{:S(2)}) copy-start(bf16[1024,256]{0,1:T(8,128)(2,1)} %copy-done.4) | copy-start | bytes 1572868
  176.6 1.3 copy-start.8
Sparse Core Ops, SparseCore 0:
  30.1 30.4 all-gather.1

commit v8 on v7

--- a/solution.py
+++ b/solution.py
@@ -135,17 +135,17 @@
         [high.astype(jnp.bfloat16), (partials - high).astype(jnp.bfloat16)], axis=1
     ).reshape(peer_count, 1, -1, col_count)
     coded_rows = coded.shape[2]
-    coded = jnp.pad(coded, ((0, 0), (0, 0), (0, tile_size - coded_rows), (0, 0)))
+    span = capacity * tile_size
     payload = jnp.concatenate(
         [
-            returning.reshape(peer_count, capacity, tile_size, col_count).astype(jnp.bfloat16),
-            coded,
+            returning.reshape(peer_count, span, col_count).astype(jnp.bfloat16),
+            coded.reshape(peer_count, coded_rows, col_count),
         ],
         axis=1,
     )
     arrived = lax.all_to_all(payload, "rows", split_axis=0, concat_axis=0, tiled=True)
-    returned = arrived[:, :capacity].astype(jnp.float32)
-    codes = arrived[:, capacity, :coded_rows].reshape(peer_count, 2, -1).astype(jnp.float32)
+    returned = arrived[:, :span].reshape(peer_count * capacity, tile_size, col_count)
+    codes = arrived[:, span:].reshape(peer_count, 2, -1).astype(jnp.float32)
     mine = jnp.sum(codes[:, 0] + codes[:, 1], axis=0, keepdims=True)
     whole = lax.all_to_all(
         jnp.broadcast_to(mine, partials.shape), "rows", split_axis=0, concat_axis=0, tiled=True
@@ -154,10 +154,10 @@
     grad_self = sum_self * grad_scale
     grad_neigh = sum_neigh * grad_scale
     target_block = jnp.where(usable, wanted, blocks).reshape(-1)
-    owed = jnp.zeros((blocks, tile_size * col_count), jnp.float32)
-    owed = owed.at[target_block].add(
-        returned.reshape(peer_count * capacity, tile_size * col_count), mode="drop"
+    routing = (target_block[None, :] == jnp.arange(blocks, dtype=jnp.int32)[:, None]).astype(
+        jnp.bfloat16
     )
+    owed = jnp.einsum("bs,sjc->bjc", routing, returned, preferred_element_type=jnp.float32)
     interior = (
         dense_grad
         + grad_padded[tile_size : tile_size + rows_dev]

time: 186 us -> 191 us (1.027)
  waiting for transfers between devices: 56.2 us -> 65.8 us
  local copies, waits for them, and re-layouts: 23.4 us -> 19.7 us
  other arithmetic: 15.2 us -> 12.2 us
    reshape x4 -> x1, local copies, waits for them, and re-layouts: 11.3 us -> 1.42 us  [on_device(): arrived[:, :span].reshape(peer_count * capacity, tile_size, col_count)]
    all_to_all x1, waiting for transfers between devices: 0.01 us -> 8.48 us  [on_device(): lax.all_to_all(jnp.broadcast_to(mine, partials.shape), 'rows', split_axis...]
    scatter-add x1 -> x0, other arithmetic: 3.25 us -> none  [on_device(): owed.at[target_block]]
    slice x1 -> x3, local copies, waits for them, and re-layouts: 0.03 us -> 2.59 us  [the longest x2 1.71 us: on_device(): arrived[:, :span].reshape(peer_count * capacity, tile_size, col_count)]
    all_to_all x1, waiting for transfers between devices: 7.52 us -> 9.91 us  [on_device(): lax.all_to_all(request, 'rows', split_axis=0, concat_axis=0, tiled=True)]
    concatenate x0 -> x1, local copies, waits for them, and re-layouts: none -> 2.09 us  [on_device(): jnp.concatenate([returning.reshape(peer_count, span, col_count).astype(jn...]
    unnamed x28 -> x35, local copies, waits for them, and re-layouts: 5.08 us -> 4.75 us
  transfers between devices with their start and end apart: 9 -> 9, of which waited for: 5 -> 6; matrix products, arithmetic and copies ran while one was open for 17% -> 13% of each run, Pallas kernels for 0% -> 0%
where the time goes in v8:
time: 191 us; the launch traced here: 189 us
  waiting for transfers between devices  65.8 us (34%)
  starting transfers between devices  49.4 us (26%)
  local copies, waits for them, and re-layouts  19.7 us (10%)
  blocking collectives  18.4 us (10%)
  between operations  14.5 us (8%)
  other arithmetic  12.2 us (6%)
  matrix products  8.63 us (5%)
    all_to_all x1, waiting for transfers between devices, on_device(): lax.all_to_all(payload, 'rows', split_axis=0, concat_axis=0, tiled=True)  30.3 us
    all_gather x1, blocking collectives, on_device(): neighbours_all = lax.all_gather(neighbours, 'feat', axis=1, tiled=True)  18.4 us
    all_to_all x1, starting transfers between devices, on_device(): lax.all_to_all(request, 'rows', split_axis=0, concat_axis=0, tiled=True)  17.1 us
    ppermute x1, waiting for transfers between devices, extended(): lax.ppermute(lax.slice_in_dim(block, block.shape[dim] - width, None, axis...  12.2 us
    all_to_all x1, waiting for transfers between devices, on_device(): lax.all_to_all(request, 'rows', split_axis=0, concat_axis=0, tiled=True)  9.91 us
    all_to_all x1, starting transfers between devices, on_device(): lax.all_to_all(payload, 'rows', split_axis=0, concat_axis=0, tiled=True)  9.67 us
    all_to_all x1, starting transfers between devices, on_device(): lax.all_to_all(jnp.broadcast_to(mine, partials.shape), 'rows', split_axis...  8.68 us
    all_to_all x1, waiting for transfers between devices, on_device(): lax.all_to_all(jnp.broadcast_to(mine, partials.shape), 'rows', split_axis...  8.48 us
  transfers between devices with their start and end apart: 9, of which 6 were waited for; matrix products, arithmetic and copies ran while one was open for 13% of the time, Pallas kernels for 0%

profile of v8, /device:TPU:1, one launch (start us, length us, event | category | flops | bytes accessed | tf_op | source)
XLA Modules:
  0.0 188.7 jit_solution(17258943194950053989)
XLA Ops:
  8.0 1.5 fusion.14
  12.3 17.1 %all-to-all-start = ((s32[64,1,2]{2,1,0:T(1,128)}), s32[64,1,2]{2,1,0:T(1,128)S(1)}, u32[]{:S(2)}, u32[]{:S(2)}) async-start(s32[64,1,2]{2,1,0:T(1,128)} %bitcast.4), calls=%async_computation | async-start | bytes 65536 | tf_op jit(solution)/shard_map/all_to_all | solution.py:72
  30.3 9.9 %all-to-all-done = s32[64,1,2]{2,1,0:T(1,128)S(1)} async-done(((s32[64,1,2]{2,1,0:T(1,128)}), s32[64,1,2]{2,1,0:T(1,128)S(1)}, u32[]{:S(2)}, u32[]{:S(2)}) %all-to-all-start) | async-done | bytes 544 | tf_op jit(solution)/shard_map/all_to_all | solution.py:72
  40.8 1.4 fusion.43
  43.3 1.2 broadcast_select_fusion
  44.5 4.8 %all-to-all-start.1 = ((bf16[64,2,128,32]{2,3,1,0:T(8,128)(2,1)}), bf16[64,2,128,32]{2,3,1,0:T(8,128)(2,1)S(1)}, u32[]{:S(2)}, u32[]{:S(2)}) async-start(bf16[64,2,128,32]{2,3,1,0:T(8,128)(2,1)} %broadcast_select_fusion), calls=%async_computation.1 | async-start | bytes 2097152 | tf_op jit(solution)/shard_map/all_to_all | solution.py:79
  49.4 2.8 %collective-permute-start = (bf16[128,32]{0,1:T(8,128)(2,1)S(1)}, bf16[128,32]{0,1:T(8,128)(2,1)S(1)}, u32[]{:S(2)}, u32[]{:S(2)}) collective-permute-start(bf16[128,32]{0,1:T(8,128)(2,1)S(1)} %get-tuple-element.53), channel_id=1, source_target_pairs={{0,8},{8,16},{16,24},{24,32},{32,40},{40,48},{48,56},{56,64},{64,7... | collective-permute-start | bytes 24584 | tf_op jit(solution)/shard_map/ppermute | solution.py:12
  52.2 1.3 collective-permute-start.1
  54.2 12.2 %collective-permute-done = bf16[128,32]{0,1:T(8,128)(2,1)S(1)} collective-permute-done((bf16[128,32]{0,1:T(8,128)(2,1)S(1)}, bf16[128,32]{0,1:T(8,128)(2,1)S(1)}, u32[]{:S(2)}, u32[]{:S(2)}) %collective-permute-start) | collective-permute-done | bytes 8224 | tf_op jit(solution)/shard_map/ppermute | solution.py:12
  66.3 4.5 %collective-permute-done.1 = bf16[128,32]{0,1:T(8,128)(2,1)S(1)} collective-permute-done((bf16[128,32]{0,1:T(8,128)(2,1)S(1)}, bf16[128,32]{0,1:T(8,128)(2,1)S(1)}, u32[]{:S(2)}, u32[]{:S(2)}) %collective-permute-start.1) | collective-permute-done | bytes 8224 | tf_op jit(solution)/shard_map/ppermute | solution.py:15
  72.3 2.4 %fusion.5 = f32[1024,256]{0,1:T(8,128)} fusion(bf16[256,256]{1,0:T(8,128)(2,1)S(1)} %copy-done.12, bf16[2064,256]{0,1:T(8,128)(2,1)} %all-gather.2.cloned.1.call-done), kind=kOutput, calls=%fused_computation.21 | convolution fusion | flops 134217728 | bytes 1703936 | tf_op jit(solution)/shard_map/dot_general | solution.py:95
  76.1 18.4 %all_gather.7 = bf16[1024,256]{0,1:T(8,128)(2,1)S(1)} all-gather(bf16[1024,32]{0,1:T(8,128)(2,1)S(1)} %fusion.15), channel_id=1, replica_groups=mesh['rows'=64,'feat'=8] {'feat'}, dimensions={1}, use_global_device_ids=true | all-gather | bytes 589824 | tf_op jit(solution)/shard_map/all_gather | solution.py:93
  94.6 2.7 %multiply_convert_fusion = (bf16[1024,256]{0,1:T(8,128)(2,1)S(1)}, f32[1024,256]{0,1:T(8,128)}) fusion(bf16[2064,256]{0,1:T(8,128)(2,1)} %all-gather.2.cloned.1.call-done, f32[256]{0:T(256)S(1)} %fusion.17, f32[1024,256]{0,1:T(8,128)S(1)} %copy-done.7, bf16[1024,256]{0,1:T(8,128)(2,1)S(1)} %all_gather.7, bf16[256,256]{1,0:T(8,128)(2,1)S(1)} %copy-done), kind=kOutput, calls=%fused_computation.18 | convolution fusion | flops 137363456 | bytes 3802112 | tf_op jit(solution)/shard_map/dot_general | solution.py:96
  103.1 2.1 %copy.158 = bf16[64,272,32]{1,2,0:T(8,128)(2,1)} copy(bf16[64,272,32]{1,0,2:T(8,128)(2,1)S(1)} %pad_maximum_fusion) | data formatting | bytes 2228224 | tf_op jit(solution)/shard_map/concatenate | solution.py:139
  105.2 9.7 %all-to-all-start.2 = ((bf16[64,272,32]{1,2,0:T(8,128)(2,1)}), bf16[64,272,32]{1,2,0:T(8,128)(2,1)S(1)}, u32[]{:S(2)}, u32[]{:S(2)}) async-start(bf16[64,272,32]{1,2,0:T(8,128)(2,1)} %copy.158), calls=%async_computation.2 | async-start | bytes 3145728 | tf_op jit(solution)/shard_map/all_to_all | solution.py:146
  116.5 3.5 %collective-permute-start.2 = (f32[128,32]{0,1:T(8,128)}, f32[128,32]{0,1:T(8,128)}, u32[]{:S(2)}, u32[]{:S(2)}) collective-permute-start(f32[128,32]{0,1:T(8,128)} %get-tuple-element.43), channel_id=1, source_target_pairs={{0,8},{8,16},{16,24},{24,32},{32,40},{40,48},{48,56},{56,64},{64,7... | collective-permute-start | bytes 49160 | tf_op jit(solution)/shard_map/ppermute | solution.py:23
  120.0 1.5 collective-permute-start.3
  121.5 1.6 multiply_convert_fusion.1
  123.8 30.3 %all-to-all-done.2 = bf16[64,272,32]{1,2,0:T(8,128)(2,1)S(1)} async-done(((bf16[64,272,32]{1,2,0:T(8,128)(2,1)}), bf16[64,272,32]{1,2,0:T(8,128)(2,1)S(1)}, u32[]{:S(2)}, u32[]{:S(2)}) %all-to-all-start.2) | async-done | bytes 1114144 | tf_op jit(solution)/shard_map/all_to_all | solution.py:146
  154.2 1.6 copy.159
  155.8 1.4 reshape.292
  158.1 1.8 copy.163
  160.7 8.7 %all-to-all-start.3 = ((f32[64,1,256]{2,1,0:T(1,128)}), f32[64,1,256]{2,1,0:T(1,128)S(1)}, u32[]{:S(2)}, u32[]{:S(2)}) async-start(f32[64,1,256]{2,1,0:T(1,128)} %broadcast_in_dim.63), calls=%async_computation.3 | async-start | bytes 131072 | tf_op jit(solution)/shard_map/all_to_all | solution.py:150
  172.0 8.5 %all-to-all-done.3 = f32[64,1,256]{2,1,0:T(1,128)S(1)} async-done(((f32[64,1,256]{2,1,0:T(1,128)}), f32[64,1,256]{2,1,0:T(1,128)S(1)}, u32[]{:S(2)}, u32[]{:S(2)}) %all-to-all-start.3) | async-done | bytes 65568 | tf_op jit(solution)/shard_map/all_to_all | solution.py:150
  (115 shorter events, 23.4 us)
Async XLA Ops:
  7.2 87.4 %copy-start = (bf16[256,256]{1,0:T(8,128)(2,1)S(1)}, bf16[256,256]{1,0:T(8,128)(2,1)}, u32[]{:S(2)}) copy-start(bf16[256,256]{1,0:T(8,128)(2,1)} %param.21) | copy-start | bytes 393220
  7.2 64.1 %all-gather.2.cloned.1.call-start = ((), (), s32[]{:S(2)}) async-start(), calls=%async_computation.4 | async-start | bytes 1253376 | tf_op jit(solution)/shard_map/all_gather | solution.py:44
  12.3 27.9 %all-to-all-start = ((s32[64,1,2]{2,1,0:T(1,128)}), s32[64,1,2]{2,1,0:T(1,128)S(1)}, u32[]{:S(2)}, u32[]{:S(2)}) async-start(s32[64,1,2]{2,1,0:T(1,128)} %bitcast.4), calls=%async_computation | async-start | bytes 65536 | tf_op jit(solution)/shard_map/all_to_all | solution.py:72
  44.5 4.8 %copy-start.6 = (bf16[1024,32]{0,1:T(8,128)(2,1)S(1)}, bf16[1024,32]{0,1:T(8,128)(2,1)}, u32[]{:S(2)}) copy-start(bf16[1024,32]{0,1:T(8,128)(2,1)} %param.15) | copy-start | bytes 196612
  44.5 8.9 %copy-start.14 = (s32[8,2]{0,1:T(2,128)S(1)}, s32[8,2]{0,1:T(2,128)}, u32[]{:S(2)}) copy-start(s32[8,2]{0,1:T(2,128)} %param.18) | copy-start | bytes 196
  44.5 9.1 %copy-start.2 = (bf16[1024,256]{1,0:T(8,128)(2,1)S(1)}, bf16[1024,256]{1,0:T(8,128)(2,1)}, u32[]{:S(2)}) copy-start(bf16[1024,256]{1,0:T(8,128)(2,1)} %param.17) | copy-start | bytes 1572868
  44.5 9.3 %copy-start.1 = (bf16[1024,384]{1,0:T(8,128)(2,1)S(1)}, bf16[1024,384]{1,0:T(8,128)(2,1)}, u32[]{:S(2)}) copy-start(bf16[1024,384]{1,0:T(8,128)(2,1)} %param.16) | copy-start | bytes 2359300
  44.5 30.6 %all-to-all-start.1 = ((bf16[64,2,128,32]{2,3,1,0:T(8,128)(2,1)}), bf16[64,2,128,32]{2,3,1,0:T(8,128)(2,1)S(1)}, u32[]{:S(2)}, u32[]{:S(2)}) async-start(bf16[64,2,128,32]{2,3,1,0:T(8,128)(2,1)} %broadcast_select_fusion), calls=%async_computation.1 | async-start | bytes 2097152 | tf_op jit(solution)/shard_map/all_to_all | solution.py:79
  49.4 17.0 %collective-permute-start = (bf16[128,32]{0,1:T(8,128)(2,1)S(1)}, bf16[128,32]{0,1:T(8,128)(2,1)S(1)}, u32[]{:S(2)}, u32[]{:S(2)}) collective-permute-start(bf16[128,32]{0,1:T(8,128)(2,1)S(1)} %get-tuple-element.53), channel_id=1, source_target_pairs={{0,8},{8,16},{16,24},{24,32},{32,40},{40,48},{48,56},{56,64},{64,7... | collective-permute-start | bytes 24584 | tf_op jit(solution)/shard_map/ppermute | solution.py:12
  52.2 18.6 %collective-permute-start.1 = (bf16[128,32]{0,1:T(8,128)(2,1)S(1)}, bf16[128,32]{0,1:T(8,128)(2,1)S(1)}, u32[]{:S(2)}, u32[]{:S(2)}) collective-permute-start(bf16[128,32]{0,1:T(8,128)(2,1)S(1)} %get-tuple-element.54), channel_id=1, source_target_pairs={{8,0},{16,8},{24,16},{32,24},{40,32},{48,40},{56,48},{64,56},{72,6... | collective-permute-start | bytes 24584 | tf_op jit(solution)/shard_map/ppermute | solution.py:15
  53.9 18.4 %copy-start.12 = (bf16[256,256]{1,0:T(8,128)(2,1)S(1)}, bf16[256,256]{1,0:T(8,128)(2,1)}, u32[]{:S(2)}) copy-start(bf16[256,256]{1,0:T(8,128)(2,1)} %param.20) | copy-start | bytes 393220
  75.8 18.7 %copy-start.7 = (f32[1024,256]{0,1:T(8,128)S(1)}, f32[1024,256]{0,1:T(8,128)}, u32[]{:S(2)}) copy-start(f32[1024,256]{0,1:T(8,128)} %fusion.5) | copy-start | bytes 3145732
  97.2 2.0 %copy-start.3 = (bf16[1024,256]{0,1:T(8,128)(2,1)}, bf16[1024,256]{0,1:T(8,128)(2,1)S(1)}, u32[]{:S(2)}) copy-start(bf16[1024,256]{0,1:T(8,128)(2,1)S(1)} %get-tuple-element.58) | copy-start | bytes 1572868
  99.2 0.6 copy-start.9
  101.8 1.0 copy-start.5
  105.2 9.7 %copy-start.13 = (s32[64,2]{1,0:T(8,128)S(1)}, s32[64,2]{1,0:T(8,128)}, u32[]{:S(2)}) copy-start(s32[64,2]{1,0:T(8,128)} %get-tuple-element.40) | copy-start | bytes 1540
  105.2 10.4 %copy-start.10 = (bf16[4,8,8,128]{3,2,1,0:T(8,128)(2,1)S(1)}, bf16[4,8,8,128]{3,2,1,0:T(8,128)(2,1)}, u32[]{:S(2)}) copy-start(bf16[4,8,8,128]{3,2,1,0:T(8,128)(2,1)} %copy-done.9) | copy-start | bytes 196612
  105.2 48.9 %all-to-all-start.2 = ((bf16[64,272,32]{1,2,0:T(8,128)(2,1)}), bf16[64,272,32]{1,2,0:T(8,128)(2,1)S(1)}, u32[]{:S(2)}, u32[]{:S(2)}) async-start(bf16[64,272,32]{1,2,0:T(8,128)(2,1)} %copy.158), calls=%async_computation.2 | async-start | bytes 3145728 | tf_op jit(solution)/shard_map/all_to_all | solution.py:146
  116.5 54.7 %collective-permute-start.2 = (f32[128,32]{0,1:T(8,128)}, f32[128,32]{0,1:T(8,128)}, u32[]{:S(2)}, u32[]{:S(2)}) collective-permute-start(f32[128,32]{0,1:T(8,128)} %get-tuple-element.43), channel_id=1, source_target_pairs={{0,8},{8,16},{16,24},{24,32},{32,40},{40,48},{48,56},{56,64},{64,7... | collective-permute-start | bytes 49160 | tf_op jit(solution)/shard_map/ppermute | solution.py:23
  120.0 52.0 %collective-permute-start.3 = (f32[128,32]{0,1:T(8,128)}, f32[128,32]{0,1:T(8,128)S(1)}, u32[]{:S(2)}, u32[]{:S(2)}) collective-permute-start(f32[128,32]{0,1:T(8,128)} %get-tuple-element.42), channel_id=1, source_target_pairs={{8,0},{16,8},{24,16},{32,24},{40,32},{48,40},{56,48},{64,56},{72,6... | collective-permute-start | bytes 49160 | tf_op jit(solution)/shard_map/ppermute | solution.py:23
  158.1 12.2 %copy-start.4 = (bf16[1024,256]{0,1:T(8,128)(2,1)S(1)}, bf16[1024,256]{0,1:T(8,128)(2,1)}, u32[]{:S(2)}) copy-start(bf16[1024,256]{0,1:T(8,128)(2,1)} %copy-done.3) | copy-start | bytes 1572868
  158.1 12.2 %copy-start.8 = (f32[1280,32]{0,1:T(8,128)S(1)}, f32[1280,32]{0,1:T(8,128)}, u32[]{:S(2)}) copy-start(f32[1280,32]{0,1:T(8,128)} %pad_add_fusion) | copy-start | bytes 491524
  160.7 19.8 %all-to-all-start.3 = ((f32[64,1,256]{2,1,0:T(1,128)}), f32[64,1,256]{2,1,0:T(1,128)S(1)}, u32[]{:S(2)}, u32[]{:S(2)}) async-start(f32[64,1,256]{2,1,0:T(1,128)} %broadcast_in_dim.63), calls=%async_computation.3 | async-start | bytes 131072 | tf_op jit(solution)/shard_map/all_to_all | solution.py:150
  172.0 9.8 %copy-start.11 = (f32[1024,32]{0,1:T(8,128)}, f32[1024,32]{0,1:T(8,128)S(1)}, u32[]{:S(2)}) copy-start(f32[1024,32]{0,1:T(8,128)S(1)} %fusion.26) | copy-start | bytes 393220
Sparse Core Ops, SparseCore 0:
  10.1 34.7 all-gather.1

commit v9 on v4

--- a/solution.py
+++ b/solution.py
@@ -21,16 +21,6 @@
     devices = range(lax.axis_size(axis))
     route = [(i - distance, i) for i in devices if i - distance in devices]
     return lax.ppermute(block, axis, route)
-
-
-def summed_over(parts, axis):
-    count = lax.axis_size(axis)
-    flat = parts.reshape(count, -1)
-    pieces = lax.all_to_all(flat, axis, split_axis=0, concat_axis=0, tiled=True)
-    mine = jnp.sum(pieces, axis=0, keepdims=True)
-    spread = jnp.broadcast_to(mine, flat.shape)
-    whole = lax.all_to_all(spread, axis, split_axis=0, concat_axis=0, tiled=True)
-    return whole.reshape(parts.shape)
 
 
 def on_device(
@@ -115,9 +105,6 @@
     grad_scale = float(rows_dev * peer_count) ** (-0.5)
     part_self = jnp.einsum("rc,rf->cf", node_feats, full_grad, preferred_element_type=jnp.float32)
     part_neigh = jnp.einsum("rc,rf->cf", neighbours, full_grad, preferred_element_type=jnp.float32)
-    sum_self, sum_neigh = summed_over(jnp.stack([part_self, part_neigh]), "rows")
-    grad_self = sum_self * grad_scale
-    grad_neigh = sum_neigh * grad_scale
     dense_grad = jnp.einsum("rf,cf->rc", full_grad, rows_self, preferred_element_type=jnp.float32)
     grad_agg = jnp.einsum("rf,cf->rc", full_grad, rows_neigh, preferred_element_type=jnp.float32)
     grad_neighbours = (grad_agg / degree[:, None]).astype(jnp.bfloat16)
@@ -142,6 +129,16 @@
     )
     returning = jnp.zeros((peer_count * capacity, tile_size, col_count), jnp.float32)
     returning = returning.at[slot_ids].set(grad_fetched.reshape(entries, tile_size, col_count))
+    feat_count = lax.axis_size("feat")
+    feat_index = lax.axis_index("feat")
+    slotted = jnp.zeros((2, feat_count, col_count, feat_count * col_count), jnp.float32)
+    slotted = lax.dynamic_update_index_in_dim(
+        slotted, jnp.stack([part_self, part_neigh])[:, None], feat_index, 1
+    )
+    summed = lax.psum(slotted, ("rows", "feat"))
+    sum_self, sum_neigh = lax.dynamic_index_in_dim(summed, feat_index, 1, keepdims=False)
+    grad_self = sum_self * grad_scale
+    grad_neigh = sum_neigh * grad_scale
     returned = lax.all_to_all(
         returning.reshape(peer_count, capacity, tile_size, col_count).astype(jnp.bfloat16),
         "rows",

time: 192 us -> 414 us (2.16)
  the two profiles are of different devices: /device:TPU:8 before, /device:TPU:1 now
where the time goes in v9:
time: 414 us; the launch traced here: 413 us
  waiting for transfers between devices  294 us (71%)
  starting transfers between devices  40.7 us (10%)
  local copies, waits for them, and re-layouts  20.5 us (5%)
  blocking collectives  18.4 us (4%)
  other arithmetic  17.6 us (4%)
  between operations  14.5 us (4%)
  matrix products  7.76 us (2%)
    psum x1, waiting for transfers between devices, on_device(): summed = lax.psum(slotted, ('rows', 'feat'))  267 us
    all_gather x1, blocking collectives, on_device(): neighbours_all = lax.all_gather(neighbours, 'feat', axis=1, tiled=True)  18.4 us
    all_to_all x1, starting transfers between devices, on_device(): lax.all_to_all(request, 'rows', split_axis=0, concat_axis=0, tiled=True)  17.1 us
    ppermute x1, waiting for transfers between devices, extended(): lax.ppermute(lax.slice_in_dim(block, block.shape[dim] - width, None, axis...  12 us
    reshape x2, local copies, waits for them, and re-layouts, on_device(): returned.reshape(peer_count * capacity, tile_size * col_count)  10.3 us
    all_to_all x1, waiting for transfers between devices, on_device(): lax.all_to_all(request, 'rows', split_axis=0, concat_axis=0, tiled=True)  9.91 us
    all_to_all x1, starting transfers between devices, on_device(): lax.all_to_all(returning.reshape(peer_count, capacity, tile_size, col_cou...  9.67 us
  transfers between devices with their start and end apart: 9, of which 5 were waited for; matrix products, arithmetic and copies ran while one was open for 8% of the time, Pallas kernels for 0%

profile of v9, /device:TPU:1, one launch (start us, length us, event | category | flops | bytes accessed | tf_op | source)
XLA Modules:
  0.0 413.3 jit_solution(3449586873717167894)
XLA Ops:
  8.0 1.5 fusion.14
  12.3 17.1 %all-to-all-start = ((s32[64,1,2]{2,1,0:T(1,128)}), s32[64,1,2]{2,1,0:T(1,128)S(1)}, u32[]{:S(2)}, u32[]{:S(2)}) async-start(s32[64,1,2]{2,1,0:T(1,128)} %bitcast.4), calls=%async_computation | async-start | bytes 65536 | tf_op jit(solution)/shard_map/all_to_all | solution.py:72
  30.3 9.9 %all-to-all-done = s32[64,1,2]{2,1,0:T(1,128)S(1)} async-done(((s32[64,1,2]{2,1,0:T(1,128)}), s32[64,1,2]{2,1,0:T(1,128)S(1)}, u32[]{:S(2)}, u32[]{:S(2)}) %all-to-all-start) | async-done | bytes 544 | tf_op jit(solution)/shard_map/all_to_all | solution.py:72
  42.8 1.2 broadcast_select_fusion
  44.0 4.7 %all-to-all-start.1 = ((bf16[64,2,128,32]{2,3,1,0:T(8,128)(2,1)}), bf16[64,2,128,32]{2,3,1,0:T(8,128)(2,1)S(1)}, u32[]{:S(2)}, u32[]{:S(2)}) async-start(bf16[64,2,128,32]{2,3,1,0:T(8,128)(2,1)} %broadcast_select_fusion), calls=%async_computation.1 | async-start | bytes 2097152 | tf_op jit(solution)/shard_map/all_to_all | solution.py:79
  48.7 2.9 collective-permute-start
  51.7 1.3 collective-permute-start.1
  53.6 12.0 %collective-permute-done = bf16[128,32]{0,1:T(8,128)(2,1)S(1)} collective-permute-done((bf16[128,32]{0,1:T(8,128)(2,1)S(1)}, bf16[128,32]{0,1:T(8,128)(2,1)S(1)}, u32[]{:S(2)}, u32[]{:S(2)}) %collective-permute-start) | collective-permute-done | bytes 8224 | tf_op jit(solution)/shard_map/ppermute | solution.py:12
  65.7 4.5 %collective-permute-done.1 = bf16[128,32]{0,1:T(8,128)(2,1)S(1)} collective-permute-done((bf16[128,32]{0,1:T(8,128)(2,1)S(1)}, bf16[128,32]{0,1:T(8,128)(2,1)S(1)}, u32[]{:S(2)}, u32[]{:S(2)}) %collective-permute-start.1) | collective-permute-done | bytes 8224 | tf_op jit(solution)/shard_map/ppermute | solution.py:15
  71.7 2.4 fusion.5
  75.5 18.4 %all_gather.7 = bf16[1024,256]{0,1:T(8,128)(2,1)S(1)} all-gather(bf16[1024,32]{0,1:T(8,128)(2,1)S(1)} %fusion.15), channel_id=1, replica_groups=mesh['rows'=64,'feat'=8] {'feat'}, dimensions={1}, use_global_device_ids=true | all-gather | bytes 589824 | tf_op jit(solution)/shard_map/all_gather | solution.py:93
  93.9 2.7 multiply_convert_fusion
  97.9 1.0 scatter_fusion
  99.0 1.2 convert_element_type.46
  100.2 9.7 %all-to-all-start.2 = ((bf16[64,2,128,32]{2,3,1,0:T(8,128)(2,1)}), bf16[64,2,128,32]{2,3,1,0:T(8,128)(2,1)S(1)}, u32[]{:S(2)}, u32[]{:S(2)}) async-start(bf16[64,2,128,32]{2,3,1,0:T(8,128)(2,1)} %bitcast.107), calls=%async_computation.2 | async-start | bytes 2097152 | tf_op jit(solution)/shard_map/all_to_all | solution.py:142
  112.4 1.6 multiply_convert_fusion.1
  114.6 3.5 collective-permute-start.2
  118.1 1.5 collective-permute-start.3
  120.3 266.8 %all-reduce.6.cloned.1.call-done = f32[2,8,32,256]{3,2,1,0:T(8,128)} async-done(((f32[2,8,32,256]{3,2,1,0:T(8,128)}), f32[2,8,32,256]{3,2,1,0:T(8,128)}) %all-reduce.6.cloned.1.call-update) | async-done | bytes 524304 | tf_op jit(solution)/shard_map/psum | solution.py:138
  387.1 1.4 fusion.27
  388.5 4.1 copy.120
  392.6 6.3 %reshape.303 = f32[128,4096]{1,0:T(8,128)S(1)} reshape(f32[64,2,128,32]{3,2,1,0:T(8,128)} %copy.120) | data formatting | bytes 4194304 | tf_op jit(solution)/shard_map/reshape | solution.py:152
  398.9 4.0 scatter_custom_fusion.1
  402.8 1.1 reshape.272
  (97 shorter events, 18.1 us)
Async XLA Ops:
  7.2 86.7 %copy-start = (bf16[256,256]{1,0:T(8,128)(2,1)S(1)}, bf16[256,256]{1,0:T(8,128)(2,1)}, u32[]{:S(2)}) copy-start(bf16[256,256]{1,0:T(8,128)(2,1)} %param.21) | copy-start | bytes 393220
  7.2 63.4 %all-gather.2.cloned.1.call-start = ((), (), s32[]{:S(2)}) async-start(), calls=%async_computation.3 | async-start | bytes 1253376 | tf_op jit(solution)/shard_map/all_gather | solution.py:44
  12.3 27.9 %all-to-all-start = ((s32[64,1,2]{2,1,0:T(1,128)}), s32[64,1,2]{2,1,0:T(1,128)S(1)}, u32[]{:S(2)}, u32[]{:S(2)}) async-start(s32[64,1,2]{2,1,0:T(1,128)} %bitcast.4), calls=%async_computation | async-start | bytes 65536 | tf_op jit(solution)/shard_map/all_to_all | solution.py:72
  42.8 5.9 %copy-start.6 = (bf16[1024,32]{0,1:T(8,128)(2,1)S(1)}, bf16[1024,32]{0,1:T(8,128)(2,1)}, u32[]{:S(2)}) copy-start(bf16[1024,32]{0,1:T(8,128)(2,1)} %param.15) | copy-start | bytes 196612
  42.8 10.2 %copy-start.11 = (s32[8,2]{0,1:T(2,128)S(1)}, s32[8,2]{0,1:T(2,128)}, u32[]{:S(2)}) copy-start(s32[8,2]{0,1:T(2,128)} %param.18) | copy-start | bytes 196
  42.8 10.4 %copy-start.2 = (bf16[1024,256]{1,0:T(8,128)(2,1)S(1)}, bf16[1024,256]{1,0:T(8,128)(2,1)}, u32[]{:S(2)}) copy-start(bf16[1024,256]{1,0:T(8,128)(2,1)} %param.17) | copy-start | bytes 1572868
  42.8 10.6 %copy-start.1 = (bf16[1024,384]{1,0:T(8,128)(2,1)S(1)}, bf16[1024,384]{1,0:T(8,128)(2,1)}, u32[]{:S(2)}) copy-start(bf16[1024,384]{1,0:T(8,128)(2,1)} %param.16) | copy-start | bytes 2359300
  44.0 30.4 %all-to-all-start.1 = ((bf16[64,2,128,32]{2,3,1,0:T(8,128)(2,1)}), bf16[64,2,128,32]{2,3,1,0:T(8,128)(2,1)S(1)}, u32[]{:S(2)}, u32[]{:S(2)}) async-start(bf16[64,2,128,32]{2,3,1,0:T(8,128)(2,1)} %broadcast_select_fusion), calls=%async_computation.1 | async-start | bytes 2097152 | tf_op jit(solution)/shard_map/all_to_all | solution.py:79
  48.7 23.0 %copy-start.10 = (bf16[256,256]{1,0:T(8,128)(2,1)S(1)}, bf16[256,256]{1,0:T(8,128)(2,1)}, u32[]{:S(2)}) copy-start(bf16[256,256]{1,0:T(8,128)(2,1)} %param.20) | copy-start | bytes 393220
  48.7 16.9 %collective-permute-start = (bf16[128,32]{0,1:T(8,128)(2,1)S(1)}, bf16[128,32]{0,1:T(8,128)(2,1)S(1)}, u32[]{:S(2)}, u32[]{:S(2)}) collective-permute-start(bf16[128,32]{0,1:T(8,128)(2,1)S(1)} %get-tuple-element.51), channel_id=1, source_target_pairs={{0,8},{8,16},{16,24},{24,32},{32,40},{40,48},{48,56},{56,64},{64,7... | collective-permute-start | bytes 24584 | tf_op jit(solution)/shard_map/ppermute | solution.py:12
  51.7 18.5 %collective-permute-start.1 = (bf16[128,32]{0,1:T(8,128)(2,1)S(1)}, bf16[128,32]{0,1:T(8,128)(2,1)S(1)}, u32[]{:S(2)}, u32[]{:S(2)}) collective-permute-start(bf16[128,32]{0,1:T(8,128)(2,1)S(1)} %get-tuple-element.52), channel_id=1, source_target_pairs={{8,0},{16,8},{24,16},{32,24},{40,32},{48,40},{56,48},{64,56},{72,6... | collective-permute-start | bytes 24584 | tf_op jit(solution)/shard_map/ppermute | solution.py:15
  75.1 18.8 %copy-start.7 = (f32[1024,256]{0,1:T(8,128)S(1)}, f32[1024,256]{0,1:T(8,128)}, u32[]{:S(2)}) copy-start(f32[1024,256]{0,1:T(8,128)} %fusion.5) | copy-start | bytes 3145732
  96.6 0.8 copy-start.3
  100.2 10.8 %copy-start.4 = (bf16[1024,256]{0,1:T(8,128)(2,1)S(1)}, bf16[1024,256]{0,1:T(8,128)(2,1)}, u32[]{:S(2)}) copy-start(bf16[1024,256]{0,1:T(8,128)(2,1)} %copy-done.3) | copy-start | bytes 1572868
  100.2 288.4 %all-to-all-start.2 = ((bf16[64,2,128,32]{2,3,1,0:T(8,128)(2,1)}), bf16[64,2,128,32]{2,3,1,0:T(8,128)(2,1)S(1)}, u32[]{:S(2)}, u32[]{:S(2)}) async-start(bf16[64,2,128,32]{2,3,1,0:T(8,128)(2,1)} %bitcast.107), calls=%async_computation.2 | async-start | bytes 2097152 | tf_op jit(solution)/shard_map/all_to_all | solution.py:142
  109.8 277.3 %all-reduce.6.cloned.1.call-start = ((), (), s32[]{:S(2)}) async-start(), calls=%async_computation.4 | async-start | bytes 1048576 | tf_op jit(solution)/shard_map/psum | solution.py:138
  111.6 0.8 copy-start.5
  114.6 290.4 %collective-permute-start.2 = (f32[128,32]{0,1:T(8,128)}, f32[128,32]{0,1:T(8,128)}, u32[]{:S(2)}, u32[]{:S(2)}) collective-permute-start(f32[128,32]{0,1:T(8,128)} %get-tuple-element.45), channel_id=1, source_target_pairs={{0,8},{8,16},{16,24},{24,32},{32,40},{40,48},{48,56},{56,64},{64,7... | collective-permute-start | bytes 49160 | tf_op jit(solution)/shard_map/ppermute | solution.py:23
  118.1 287.6 %collective-permute-start.3 = (f32[128,32]{0,1:T(8,128)}, f32[128,32]{0,1:T(8,128)S(1)}, u32[]{:S(2)}, u32[]{:S(2)}) collective-permute-start(f32[128,32]{0,1:T(8,128)} %get-tuple-element.44), channel_id=1, source_target_pairs={{8,0},{16,8},{24,16},{32,24},{40,32},{48,40},{56,48},{64,56},{72,6... | collective-permute-start | bytes 49160 | tf_op jit(solution)/shard_map/ppermute | solution.py:23
  392.6 11.5 %copy-start.8 = (f32[1280,32]{0,1:T(8,128)S(1)}, f32[1280,32]{0,1:T(8,128)}, u32[]{:S(2)}) copy-start(f32[1280,32]{0,1:T(8,128)} %pad_add_fusion) | copy-start | bytes 491524
  405.8 0.7 copy-start.9
Sparse Core Ops, SparseCore 0:
  10.1 34.8 all-gather.1
  115.7 271.4 all-reduce.5

commit v10 on v7

--- a/solution.py
+++ b/solution.py
@@ -65,11 +65,24 @@
     earlier = jnp.arange(entries)[None, :] < jnp.arange(entries)[:, None]
     slot_rank = jnp.sum(jnp.where(same_owner & earlier, 1, 0), axis=1).astype(jnp.int32)
     slot_ids = owner_ids * capacity + slot_rank
-    slot_hit = slot_ids[:, None] == jnp.arange(peer_count * capacity, dtype=jnp.int32)[None, :]
-    request = (jnp.sum(jnp.where(slot_hit, local_ids[:, None] + 1, 0), axis=0) - 1).reshape(
-        peer_count, capacity
+    table = lax.all_gather(jnp.stack([far_owner, far_local]), "rows", axis=1, tiled=True)
+    every_owner = table[0].reshape(peer_count, entries)
+    every_local = table[1].reshape(peer_count, entries)
+    peer_same = every_owner[:, :, None] == every_owner[:, None, :]
+    peer_rank = jnp.sum(jnp.where(peer_same & earlier[None], 1, 0), axis=2)
+    to_me = every_owner == lax.axis_index("rows")
+    wanted = (
+        jnp.sum(
+            jnp.where(
+                to_me[:, :, None]
+                & (peer_rank[:, :, None] == jnp.arange(capacity, dtype=jnp.int32)[None, None, :]),
+                every_local[:, :, None] + 1,
+                0,
+            ),
+            axis=1,
+        )
+        - 1
     )
-    wanted = lax.all_to_all(request, "rows", split_axis=0, concat_axis=0, tiled=True)
     usable = wanted >= 0
     safe_ids = jnp.maximum(wanted, 0)
     own_blocks = node_feats.reshape(blocks, tile_size, col_count)

time: 186 us -> 215 us (1.16)
  blocking collectives: 18.4 us -> 73.6 us
  starting transfers between devices: 49.7 us -> 33.6 us
  waiting for transfers between devices: 56.2 us -> 45.9 us
    all_gather x0 -> x1, blocking collectives: none -> 48.3 us  [on_device(): lax.all_gather(jnp.stack([far_owner, far_local]), 'rows', axis=1, tiled=T...]
    all_to_all x1 -> x0, starting transfers between devices: 17.1 us -> none  [on_device(): lax.all_to_all(request, 'rows', split_axis=0, concat_axis=0, tiled=True)]
    all_to_all x1, waiting for transfers between devices: 0.2 us -> 14.3 us  [on_device(): lax.all_to_all(outgoing, 'rows', split_axis=0, concat_axis=0, tiled=True)]
    ppermute x1, waiting for transfers between devices: 11.8 us -> 0.01 us  [extended(): lax.ppermute(lax.slice_in_dim(block, block.shape[dim] - width, None, axis...]
    all_to_all x1 -> x0, waiting for transfers between devices: 7.52 us -> none  [on_device(): lax.all_to_all(request, 'rows', split_axis=0, concat_axis=0, tiled=True)]
    all_gather x1, blocking collectives: 18.4 us -> 25.3 us  [on_device(): neighbours_all = lax.all_gather(neighbours, 'feat', axis=1, tiled=True)]
    ppermute x1, waiting for transfers between devices: 4.87 us -> 0.01 us  [extended(): lax.ppermute(lax.slice_in_dim(block, 0, width, axis=dim), axis, backward)]
    all_to_all x1, starting transfers between devices: 9.56 us -> 6.37 us  [on_device(): lax.all_to_all(payload, 'rows', split_axis=0, concat_axis=0, tiled=True)]
  transfers between devices with their start and end apart: 9 -> 8, of which waited for: 5 -> 2; matrix products, arithmetic and copies ran while one was open for 17% -> 16% of each run, Pallas kernels for 0% -> 0%
where the time goes in v10:
time: 215 us; the launch traced here: 214 us
  blocking collectives  73.6 us (34%)
  waiting for transfers between devices  45.9 us (21%)
  starting transfers between devices  33.6 us (16%)
  local copies, waits for them, and re-layouts  22.6 us (11%)
  other arithmetic  15.9 us (7%)
  between operations  14.6 us (7%)
  matrix products  7.39 us (3%)
    all_gather x1, blocking collectives, on_device(): lax.all_gather(jnp.stack([far_owner, far_local]), 'rows', axis=1, tiled=T...  48.3 us
    all_to_all x1, waiting for transfers between devices, on_device(): lax.all_to_all(payload, 'rows', split_axis=0, concat_axis=0, tiled=True)  31.5 us
    all_gather x1, blocking collectives, on_device(): neighbours_all = lax.all_gather(neighbours, 'feat', axis=1, tiled=True)  25.3 us
    all_to_all x1, waiting for transfers between devices, on_device(): lax.all_to_all(outgoing, 'rows', split_axis=0, concat_axis=0, tiled=True)  14.3 us
    reshape x2, local copies, waits for them, and re-layouts, on_device(): returned.reshape(peer_count * capacity, tile_size * col_count)  10.9 us
    all_to_all x1, starting transfers between devices, on_device(): lax.all_to_all(jnp.broadcast_to(mine, partials.shape), 'rows', split_axis...  8.68 us
    all_to_all x1, starting transfers between devices, on_device(): lax.all_to_all(outgoing, 'rows', split_axis=0, concat_axis=0, tiled=True)  7.73 us
    all_to_all x1, starting transfers between devices, on_device(): lax.all_to_all(payload, 'rows', split_axis=0, concat_axis=0, tiled=True)  6.37 us
  transfers between devices with their start and end apart: 8, of which 2 were waited for; matrix products, arithmetic and copies ran while one was open for 16% of the time, Pallas kernels for 0%

profile of v10, /device:TPU:1, one launch (start us, length us, event | category | flops | bytes accessed | tf_op | source)
XLA Modules:
  0.0 213.6 jit_solution(14039366388087133806)
XLA Ops:
  8.0 4.0 %collective-permute-start = (bf16[128,32]{0,1:T(8,128)(2,1)S(1)}, bf16[128,32]{0,1:T(8,128)(2,1)S(1)}, u32[]{:S(2)}, u32[]{:S(2)}) collective-permute-start(bf16[128,32]{0,1:T(8,128)(2,1)S(1)} %get-tuple-element.53), channel_id=1, source_target_pairs={{0,8},{8,16},{16,24},{24,32},{32,40},{40,48},{48,56},{56,64},{64,7... | collective-permute-start | bytes 24584 | tf_op jit(solution)/shard_map/ppermute | solution.py:12
  12.0 1.3 collective-permute-start.1
  14.1 1.5 fusion.17
  17.3 48.3 %all_gather.10 = s32[2,512,2]{2,0,1:T(2,128)S(1)} all-gather(s32[2,8,2]{2,0,1:T(2,128)S(1)} %copy.132), channel_id=1, replica_groups=mesh['rows'=64,'feat'=8] {'rows'}, dimensions={1}, use_global_device_ids=true | all-gather | bytes 8320 | tf_op jit(solution)/shard_map/all_gather | solution.py:68
  65.6 1.5 slice_reduce_fusion
  68.9 1.2 broadcast_select_fusion
  70.2 7.7 %all-to-all-start = ((bf16[64,2,128,32]{2,3,1,0:T(8,128)(2,1)}), bf16[64,2,128,32]{2,3,1,0:T(8,128)(2,1)S(1)}, u32[]{:S(2)}, u32[]{:S(2)}) async-start(bf16[64,2,128,32]{2,3,1,0:T(8,128)(2,1)} %broadcast_select_fusion), calls=%async_computation | async-start | bytes 2097152 | tf_op jit(solution)/shard_map/all_to_all | solution.py:92
  80.5 2.4 %fusion.7 = f32[1024,256]{0,1:T(8,128)} fusion(bf16[256,256]{1,0:T(8,128)(2,1)S(1)} %copy-done.9, bf16[2064,256]{0,1:T(8,128)(2,1)} %all-gather.2.cloned.1.call-done), kind=kOutput, calls=%fused_computation.25 | convolution fusion | flops 134217728 | bytes 1703936 | tf_op jit(solution)/shard_map/dot_general | solution.py:108
  82.9 14.3 %all-to-all-done = bf16[64,2,128,32]{2,3,1,0:T(8,128)(2,1)S(1)} async-done(((bf16[64,2,128,32]{2,3,1,0:T(8,128)(2,1)}), bf16[64,2,128,32]{2,3,1,0:T(8,128)(2,1)S(1)}, u32[]{:S(2)}, u32[]{:S(2)}) %all-to-all-start) | async-done | bytes 1048608 | tf_op jit(solution)/shard_map/all_to_all | solution.py:92
  98.2 25.3 %all_gather.11 = bf16[1024,256]{0,1:T(8,128)(2,1)S(1)} all-gather(bf16[1024,32]{0,1:T(8,128)(2,1)S(1)} %fusion.18), channel_id=1, replica_groups=mesh['rows'=64,'feat'=8] {'feat'}, dimensions={1}, use_global_device_ids=true | all-gather | bytes 589824 | tf_op jit(solution)/shard_map/all_gather | solution.py:106
  123.6 3.0 %multiply_convert_fusion = (bf16[1024,256]{0,1:T(8,128)(2,1)S(1)}, f32[1024,256]{0,1:T(8,128)}) fusion(bf16[2064,256]{0,1:T(8,128)(2,1)} %all-gather.2.cloned.1.call-done, f32[256]{0:T(256)S(1)} %fusion.20, f32[1024,256]{0,1:T(8,128)} %fusion.7, bf16[1024,256]{0,1:T(8,128)(2,1)S(1)} %all_gather.11, bf16[256,256]{1,0:T(8,128)(2,1)S(1)} %copy-done), kind=kOutput, calls=%fused_computation.22 | convolution fusion | flops 137363456 | bytes 3802112 | tf_op jit(solution)/shard_map/dot_general | solution.py:109
  128.0 1.5 copy.161
  129.8 1.0 scatter_fusion
  131.9 1.5 fusion.1
  133.3 6.4 %all-to-all-start.1 = ((bf16[64,3,128,32]{2,3,1,0:T(8,128)(2,1)}), bf16[64,3,128,32]{2,3,1,0:T(8,128)(2,1)S(1)}, u32[]{:S(2)}, u32[]{:S(2)}) async-start(bf16[64,3,128,32]{2,3,1,0:T(8,128)(2,1)} %fusion.1), calls=%async_computation.1 | async-start | bytes 3145728 | tf_op jit(solution)/shard_map/all_to_all | solution.py:159
  140.3 1.3 collective-permute-start.3
  141.6 4.2 %collective-permute-start.2 = (f32[128,32]{0,1:T(8,128)S(1)}, f32[128,32]{0,1:T(8,128)S(1)}, u32[]{:S(2)}, u32[]{:S(2)}) collective-permute-start(f32[128,32]{0,1:T(8,128)S(1)} %get-tuple-element.43), channel_id=1, source_target_pairs={{0,8},{8,16},{16,24},{24,32},{32,40},{40,48},{48,56},{56,64},{64,7... | collective-permute-start | bytes 49160 | tf_op jit(solution)/shard_map/ppermute | solution.py:23
  145.8 1.6 multiply_convert_fusion.1
  147.4 31.5 %all-to-all-done.1 = bf16[64,3,128,32]{2,3,1,0:T(8,128)(2,1)S(1)} async-done(((bf16[64,3,128,32]{2,3,1,0:T(8,128)(2,1)}), bf16[64,3,128,32]{2,3,1,0:T(8,128)(2,1)S(1)}, u32[]{:S(2)}, u32[]{:S(2)}) %all-to-all-start.1) | async-done | bytes 1572896 | tf_op jit(solution)/shard_map/all_to_all | solution.py:159
  180.4 8.7 %all-to-all-start.2 = ((f32[64,1,256]{2,1,0:T(1,128)}), f32[64,1,256]{2,1,0:T(1,128)S(1)}, u32[]{:S(2)}, u32[]{:S(2)}) async-start(f32[64,1,256]{2,1,0:T(1,128)} %broadcast_in_dim.79), calls=%async_computation.2 | async-start | bytes 131072 | tf_op jit(solution)/shard_map/all_to_all | solution.py:163
  189.1 1.5 slice_convert_fusion
  190.7 4.6 %copy.155 = f32[64,2,128,32]{3,2,1,0:T(8,128)} copy(f32[64,2,128,32]{2,3,1,0:T(8,128)S(1)} %slice_convert_fusion) | data formatting | bytes 4194304 | tf_op jit(solution)/shard_map/reshape | solution.py:172
  195.3 6.3 %reshape.347 = f32[128,4096]{1,0:T(8,128)S(1)} reshape(f32[64,2,128,32]{3,2,1,0:T(8,128)} %copy.155) | data formatting | bytes 4194304 | tf_op jit(solution)/shard_map/reshape | solution.py:172
  201.6 3.3 %scatter_custom_fusion.1 = f32[8,4096]{1,0:T(8,128)S(1)} fusion(s32[128]{0:T(128)S(1)} %fusion.43, f32[128,4096]{1,0:T(8,128)S(1)} %reshape.347, f32[]{:T(128)} %constant.117.clone.1), kind=kCustom, calls=%fused_computation.71 | custom fusion | flops 524288 | bytes 131076 | tf_op jit(solution)/shard_map/scatter-add | solution.py:171
  (110 shorter events, 15.0 us)
Async XLA Ops:
  7.2 116.4 %copy-start = (bf16[256,256]{1,0:T(8,128)(2,1)S(1)}, bf16[256,256]{1,0:T(8,128)(2,1)}, u32[]{:S(2)}) copy-start(bf16[256,256]{1,0:T(8,128)(2,1)} %param.21) | copy-start | bytes 393220
  7.2 72.3 %all-gather.2.cloned.1.call-start = ((), (), s32[]{:S(2)}) async-start(), calls=%async_computation.3 | async-start | bytes 1253376 | tf_op jit(solution)/shard_map/all_gather | solution.py:44
  8.0 71.0 %collective-permute-start = (bf16[128,32]{0,1:T(8,128)(2,1)S(1)}, bf16[128,32]{0,1:T(8,128)(2,1)S(1)}, u32[]{:S(2)}, u32[]{:S(2)}) collective-permute-start(bf16[128,32]{0,1:T(8,128)(2,1)S(1)} %get-tuple-element.53), channel_id=1, source_target_pairs={{0,8},{8,16},{16,24},{24,32},{32,40},{40,48},{48,56},{56,64},{64,7... | collective-permute-start | bytes 24584 | tf_op jit(solution)/shard_map/ppermute | solution.py:12
  12.0 67.0 %collective-permute-start.1 = (bf16[128,32]{0,1:T(8,128)(2,1)S(1)}, bf16[128,32]{0,1:T(8,128)(2,1)S(1)}, u32[]{:S(2)}, u32[]{:S(2)}) collective-permute-start(bf16[128,32]{0,1:T(8,128)(2,1)S(1)} %get-tuple-element.54), channel_id=1, source_target_pairs={{8,0},{16,8},{24,16},{32,24},{40,32},{48,40},{56,48},{64,56},{72,6... | collective-permute-start | bytes 24584 | tf_op jit(solution)/shard_map/ppermute | solution.py:15
  68.9 9.0 %copy-start.10 = (s32[8,2]{0,1:T(2,128)S(1)}, s32[8,2]{0,1:T(2,128)}, u32[]{:S(2)}) copy-start(s32[8,2]{0,1:T(2,128)} %param.18) | copy-start | bytes 196
  68.9 9.5 %copy-start.3 = (bf16[1024,256]{1,0:T(8,128)(2,1)S(1)}, bf16[1024,256]{1,0:T(8,128)(2,1)}, u32[]{:S(2)}) copy-start(bf16[1024,256]{1,0:T(8,128)(2,1)} %param.17) | copy-start | bytes 1572868
  68.9 9.8 %copy-start.1 = (bf16[1024,384]{1,0:T(8,128)(2,1)S(1)}, bf16[1024,384]{1,0:T(8,128)(2,1)}, u32[]{:S(2)}) copy-start(bf16[1024,384]{1,0:T(8,128)(2,1)} %param.16) | copy-start | bytes 2359300
  70.2 8.8 %copy-start.7 = (bf16[1024,32]{0,1:T(8,128)(2,1)S(1)}, bf16[1024,32]{0,1:T(8,128)(2,1)}, u32[]{:S(2)}) copy-start(bf16[1024,32]{0,1:T(8,128)(2,1)} %param.15) | copy-start | bytes 196612
  70.2 27.0 %all-to-all-start = ((bf16[64,2,128,32]{2,3,1,0:T(8,128)(2,1)}), bf16[64,2,128,32]{2,3,1,0:T(8,128)(2,1)S(1)}, u32[]{:S(2)}, u32[]{:S(2)}) async-start(bf16[64,2,128,32]{2,3,1,0:T(8,128)(2,1)} %broadcast_select_fusion), calls=%async_computation | async-start | bytes 2097152 | tf_op jit(solution)/shard_map/all_to_all | solution.py:92
  77.9 2.6 %copy-start.9 = (bf16[256,256]{1,0:T(8,128)(2,1)S(1)}, bf16[256,256]{1,0:T(8,128)(2,1)}, u32[]{:S(2)}) copy-start(bf16[256,256]{1,0:T(8,128)(2,1)} %param.20) | copy-start | bytes 393220
  126.6 1.3 copy-start.4
  130.8 1.0 copy-start.6
  133.3 45.6 %all-to-all-start.1 = ((bf16[64,3,128,32]{2,3,1,0:T(8,128)(2,1)}), bf16[64,3,128,32]{2,3,1,0:T(8,128)(2,1)S(1)}, u32[]{:S(2)}, u32[]{:S(2)}) async-start(bf16[64,3,128,32]{2,3,1,0:T(8,128)(2,1)} %fusion.1), calls=%async_computation.1 | async-start | bytes 3145728 | tf_op jit(solution)/shard_map/all_to_all | solution.py:159
  140.3 65.1 %collective-permute-start.3 = (f32[128,32]{0,1:T(8,128)S(1)}, f32[128,32]{0,1:T(8,128)S(1)}, u32[]{:S(2)}, u32[]{:S(2)}) collective-permute-start(f32[128,32]{0,1:T(8,128)S(1)} %get-tuple-element.42), channel_id=1, source_target_pairs={{8,0},{16,8},{24,16},{32,24},{40,32},{48,40},{56,48},{64,56},{72,6... | collective-permute-start | bytes 49160 | tf_op jit(solution)/shard_map/ppermute | solution.py:23
  141.6 63.8 %collective-permute-start.2 = (f32[128,32]{0,1:T(8,128)S(1)}, f32[128,32]{0,1:T(8,128)S(1)}, u32[]{:S(2)}, u32[]{:S(2)}) collective-permute-start(f32[128,32]{0,1:T(8,128)S(1)} %get-tuple-element.43), channel_id=1, source_target_pairs={{0,8},{8,16},{16,24},{24,32},{32,40},{40,48},{48,56},{56,64},{64,7... | collective-permute-start | bytes 49160 | tf_op jit(solution)/shard_map/ppermute | solution.py:23
  178.9 1.5 copy-start.2
  180.4 25.0 %all-to-all-start.2 = ((f32[64,1,256]{2,1,0:T(1,128)}), f32[64,1,256]{2,1,0:T(1,128)S(1)}, u32[]{:S(2)}, u32[]{:S(2)}) async-start(f32[64,1,256]{2,1,0:T(1,128)} %broadcast_in_dim.79), calls=%async_computation.2 | async-start | bytes 131072 | tf_op jit(solution)/shard_map/all_to_all | solution.py:163
  195.3 9.9 %copy-start.5 = (bf16[1024,256]{0,1:T(8,128)(2,1)S(1)}, bf16[1024,256]{0,1:T(8,128)(2,1)}, u32[]{:S(2)}) copy-start(bf16[1024,256]{0,1:T(8,128)(2,1)} %copy-done.4) | copy-start | bytes 1572868
  205.5 1.3 copy-start.8
Sparse Core Ops, SparseCore 0:
  15.8 36.4 all-gather.1

commit v11 on v7

--- a/solution.py
+++ b/solution.py
@@ -133,19 +133,17 @@
     high = lax.reduce_precision(partials, exponent_bits=8, mantissa_bits=7)
     coded = jnp.stack(
         [high.astype(jnp.bfloat16), (partials - high).astype(jnp.bfloat16)], axis=1
-    ).reshape(peer_count, 1, -1, col_count)
-    coded_rows = coded.shape[2]
-    coded = jnp.pad(coded, ((0, 0), (0, 0), (0, tile_size - coded_rows), (0, 0)))
+    ).reshape(peer_count, capacity, tile_size, -1)
     payload = jnp.concatenate(
         [
             returning.reshape(peer_count, capacity, tile_size, col_count).astype(jnp.bfloat16),
             coded,
         ],
-        axis=1,
+        axis=3,
     )
     arrived = lax.all_to_all(payload, "rows", split_axis=0, concat_axis=0, tiled=True)
-    returned = arrived[:, :capacity].astype(jnp.float32)
-    codes = arrived[:, capacity, :coded_rows].reshape(peer_count, 2, -1).astype(jnp.float32)
+    returned = arrived[..., :col_count].astype(jnp.float32)
+    codes = arrived[..., col_count:].reshape(peer_count, 2, -1).astype(jnp.float32)
     mine = jnp.sum(codes[:, 0] + codes[:, 1], axis=0, keepdims=True)
     whole = lax.all_to_all(
         jnp.broadcast_to(mine, partials.shape), "rows", split_axis=0, concat_axis=0, tiled=True

time: 186 us -> 176 us (0.946)
  waiting for transfers between devices: 56.2 us -> 46.5 us
    all_to_all x1, waiting for transfers between devices: 31.8 us -> 22.1 us  [on_device(): lax.all_to_all(payload, 'rows', split_axis=0, concat_axis=0, tiled=True)]
    unnamed x28 -> x26, local copies, waits for them, and re-layouts: 5.08 us -> 2.41 us
  transfers between devices with their start and end apart: 9 -> 9, of which waited for: 5 -> 5; matrix products, arithmetic and copies ran while one was open for 17% -> 18% of each run, Pallas kernels for 0% -> 0%
where the time goes in v11:
time: 176 us; the launch traced here: 175 us
  starting transfers between devices  49.2 us (28%)
  waiting for transfers between devices  46.5 us (26%)
  local copies, waits for them, and re-layouts  23.5 us (13%)
  blocking collectives  18.4 us (10%)
  other arithmetic  15.4 us (9%)
  between operations  14.6 us (8%)
  matrix products  7.06 us (4%)
    all_to_all x1, waiting for transfers between devices, on_device(): lax.all_to_all(payload, 'rows', split_axis=0, concat_axis=0, tiled=True)  22.1 us
    all_gather x1, blocking collectives, on_device(): neighbours_all = lax.all_gather(neighbours, 'feat', axis=1, tiled=True)  18.4 us
    all_to_all x1, starting transfers between devices, on_device(): lax.all_to_all(request, 'rows', split_axis=0, concat_axis=0, tiled=True)  17.1 us
    ppermute x1, waiting for transfers between devices, extended(): lax.ppermute(lax.slice_in_dim(block, block.shape[dim] - width, None, axis...  11.8 us
    reshape x2, local copies, waits for them, and re-layouts, on_device(): returned.reshape(peer_count * capacity, tile_size * col_count)  11 us
    all_to_all x1, starting transfers between devices, on_device(): lax.all_to_all(payload, 'rows', split_axis=0, concat_axis=0, tiled=True)  9.57 us
    all_to_all x1, starting transfers between devices, on_device(): lax.all_to_all(jnp.broadcast_to(mine, partials.shape), 'rows', split_axis...  8.17 us
    all_to_all x1, waiting for transfers between devices, on_device(): lax.all_to_all(request, 'rows', split_axis=0, concat_axis=0, tiled=True)  7.52 us
  transfers between devices with their start and end apart: 9, of which 5 were waited for; matrix products, arithmetic and copies ran while one was open for 18% of the time, Pallas kernels for 0%

profile of v11, /device:TPU:1, one launch (start us, length us, event | category | flops | bytes accessed | tf_op | source)
XLA Modules:
  0.0 174.7 jit_solution(12128937392066829246)
XLA Ops:
  10.0 17.1 %all-to-all-start = ((s32[64,1,2]{2,1,0:T(1,128)}), s32[64,1,2]{2,1,0:T(1,128)S(1)}, u32[]{:S(2)}, u32[]{:S(2)}) async-start(s32[64,1,2]{2,1,0:T(1,128)} %bitcast.4), calls=%async_computation | async-start | bytes 65536 | tf_op jit(solution)/shard_map/all_to_all | solution.py:72
  27.9 1.5 fusion.14
  30.3 7.5 %all-to-all-done = s32[64,1,2]{2,1,0:T(1,128)S(1)} async-done(((s32[64,1,2]{2,1,0:T(1,128)}), s32[64,1,2]{2,1,0:T(1,128)S(1)}, u32[]{:S(2)}, u32[]{:S(2)}) %all-to-all-start) | async-done | bytes 544 | tf_op jit(solution)/shard_map/all_to_all | solution.py:72
  38.6 1.4 fusion.42
  41.0 1.2 broadcast_select_fusion
  42.2 4.7 %all-to-all-start.1 = ((bf16[64,2,128,32]{2,3,1,0:T(8,128)(2,1)}), bf16[64,2,128,32]{2,3,1,0:T(8,128)(2,1)S(1)}, u32[]{:S(2)}, u32[]{:S(2)}) async-start(bf16[64,2,128,32]{2,3,1,0:T(8,128)(2,1)} %broadcast_select_fusion), calls=%async_computation.1 | async-start | bytes 2097152 | tf_op jit(solution)/shard_map/all_to_all | solution.py:79
  46.9 3.0 %collective-permute-start = (bf16[128,32]{0,1:T(8,128)(2,1)S(1)}, bf16[128,32]{0,1:T(8,128)(2,1)S(1)}, u32[]{:S(2)}, u32[]{:S(2)}) collective-permute-start(bf16[128,32]{0,1:T(8,128)(2,1)S(1)} %get-tuple-element.53), channel_id=1, source_target_pairs={{0,8},{8,16},{16,24},{24,32},{32,40},{40,48},{48,56},{56,64},{64,7... | collective-permute-start | bytes 24584 | tf_op jit(solution)/shard_map/ppermute | solution.py:12
  49.9 1.3 collective-permute-start.1
  51.9 11.8 %collective-permute-done = bf16[128,32]{0,1:T(8,128)(2,1)S(1)} collective-permute-done((bf16[128,32]{0,1:T(8,128)(2,1)S(1)}, bf16[128,32]{0,1:T(8,128)(2,1)S(1)}, u32[]{:S(2)}, u32[]{:S(2)}) %collective-permute-start) | collective-permute-done | bytes 8224 | tf_op jit(solution)/shard_map/ppermute | solution.py:12
  63.7 4.9 %collective-permute-done.1 = bf16[128,32]{0,1:T(8,128)(2,1)S(1)} collective-permute-done((bf16[128,32]{0,1:T(8,128)(2,1)S(1)}, bf16[128,32]{0,1:T(8,128)(2,1)S(1)}, u32[]{:S(2)}, u32[]{:S(2)}) %collective-permute-start.1) | collective-permute-done | bytes 8224 | tf_op jit(solution)/shard_map/ppermute | solution.py:15
  70.1 2.4 %fusion.5 = f32[1024,256]{0,1:T(8,128)} fusion(bf16[256,256]{1,0:T(8,128)(2,1)S(1)} %copy-done.8, bf16[2064,256]{0,1:T(8,128)(2,1)} %all-gather.2.cloned.1.call-done), kind=kOutput, calls=%fused_computation.23 | convolution fusion | flops 134217728 | bytes 1703936 | tf_op jit(solution)/shard_map/dot_general | solution.py:95
  73.6 18.4 %all_gather.7 = bf16[1024,256]{0,1:T(8,128)(2,1)S(1)} all-gather(bf16[1024,32]{0,1:T(8,128)(2,1)S(1)} %fusion.15), channel_id=1, replica_groups=mesh['rows'=64,'feat'=8] {'feat'}, dimensions={1}, use_global_device_ids=true | all-gather | bytes 589824 | tf_op jit(solution)/shard_map/all_gather | solution.py:93
  92.1 2.7 %multiply_convert_fusion = (bf16[1024,256]{0,1:T(8,128)(2,1)S(1)}, f32[1024,256]{0,1:T(8,128)}) fusion(bf16[2064,256]{0,1:T(8,128)(2,1)} %all-gather.2.cloned.1.call-done, f32[256]{0:T(256)S(1)} %fusion.17, f32[1024,256]{0,1:T(8,128)S(1)} %copy-done.6, bf16[1024,256]{0,1:T(8,128)(2,1)S(1)} %all_gather.7, bf16[256,256]{1,0:T(8,128)(2,1)S(1)} %copy-done), kind=kOutput, calls=%fused_computation.20 | convolution fusion | flops 137363456 | bytes 3802112 | tf_op jit(solution)/shard_map/dot_general | solution.py:96
  99.5 2.4 %pad_maximum_fusion = bf16[64,2,128,34]{2,1,3,0:T(2,128)(2,1)} fusion(bf16[64,2,128,2]{2,1,3,0:T(2,128)(2,1)S(1)} %copy.157, bf16[64,2,128,32]{2,1,3,0:T(2,128)(2,1)S(1)} %copy.156), kind=kLoop, calls=%fused_computation.16 | loop fusion | flops 557056 | bytes 2228224 | tf_op jit(solution)/shard_map/concatenate | solution.py:137
  102.0 9.6 %all-to-all-start.2 = ((bf16[64,2,128,34]{2,1,3,0:T(2,128)(2,1)}), bf16[64,2,128,34]{2,1,3,0:T(2,128)(2,1)S(1)}, u32[]{:S(2)}, u32[]{:S(2)}) async-start(bf16[64,2,128,34]{2,1,3,0:T(2,128)(2,1)} %pad_maximum_fusion), calls=%async_computation.2 | async-start | bytes 2228224 | tf_op jit(solution)/shard_map/all_to_all | solution.py:144
  112.1 1.3 collective-permute-start.3
  113.4 4.0 %collective-permute-start.2 = (f32[128,32]{0,1:T(8,128)S(1)}, f32[128,32]{0,1:T(8,128)S(1)}, u32[]{:S(2)}, u32[]{:S(2)}) collective-permute-start(f32[128,32]{0,1:T(8,128)S(1)} %get-tuple-element.43), channel_id=1, source_target_pairs={{0,8},{8,16},{16,24},{24,32},{32,40},{40,48},{48,56},{56,64},{64,7... | collective-permute-start | bytes 49160 | tf_op jit(solution)/shard_map/ppermute | solution.py:23
  117.4 1.6 multiply_convert_fusion.1
  119.0 22.1 %all-to-all-done.2 = bf16[64,2,128,34]{2,1,3,0:T(2,128)(2,1)S(1)} async-done(((bf16[64,2,128,34]{2,1,3,0:T(2,128)(2,1)}), bf16[64,2,128,34]{2,1,3,0:T(2,128)(2,1)S(1)}, u32[]{:S(2)}, u32[]{:S(2)}) %all-to-all-start.2) | async-done | bytes 1114144 | tf_op jit(solution)/shard_map/all_to_all | solution.py:144
  142.1 8.2 %all-to-all-start.3 = ((f32[64,1,256]{2,1,0:T(1,128)}), f32[64,1,256]{2,1,0:T(1,128)S(1)}, u32[]{:S(2)}, u32[]{:S(2)}) async-start(f32[64,1,256]{2,1,0:T(1,128)} %broadcast_in_dim.67), calls=%async_computation.3 | async-start | bytes 131072 | tf_op jit(solution)/shard_map/all_to_all | solution.py:148
  150.2 1.1 slice.156
  151.7 4.7 %copy.159 = f32[64,2,128,32]{3,2,1,0:T(8,128)} copy(f32[64,2,128,32]{2,3,1,0:T(8,128)S(1)} %copy_convert_fusion) | data formatting | bytes 4194304 | tf_op jit(solution)/shard_map/reshape | solution.py:157
  156.3 6.3 %reshape.355 = f32[128,4096]{1,0:T(8,128)S(1)} reshape(f32[64,2,128,32]{3,2,1,0:T(8,128)} %copy.159) | data formatting | bytes 4194304 | tf_op jit(solution)/shard_map/reshape | solution.py:157
  162.6 3.3 %scatter_custom_fusion.1 = f32[8,4096]{1,0:T(8,128)S(1)} fusion(s32[128]{0:T(128)S(1)} %fusion.40, f32[128,4096]{1,0:T(8,128)S(1)} %reshape.355, f32[]{:T(128)} %constant.111.clone.1), kind=kCustom, calls=%fused_computation.66 | custom fusion | flops 524288 | bytes 131076 | tf_op jit(solution)/shard_map/scatter-add | solution.py:156
  (110 shorter events, 17.8 us)
Async XLA Ops:
  7.2 84.9 %copy-start = (bf16[256,256]{1,0:T(8,128)(2,1)S(1)}, bf16[256,256]{1,0:T(8,128)(2,1)}, u32[]{:S(2)}) copy-start(bf16[256,256]{1,0:T(8,128)(2,1)} %param.21) | copy-start | bytes 393220
  10.0 27.9 %all-to-all-start = ((s32[64,1,2]{2,1,0:T(1,128)}), s32[64,1,2]{2,1,0:T(1,128)S(1)}, u32[]{:S(2)}, u32[]{:S(2)}) async-start(s32[64,1,2]{2,1,0:T(1,128)} %bitcast.4), calls=%async_computation | async-start | bytes 65536 | tf_op jit(solution)/shard_map/all_to_all | solution.py:72
  27.1 41.9 %all-gather.2.cloned.1.call-start = ((), (), s32[]{:S(2)}) async-start(), calls=%async_computation.4 | async-start | bytes 1253376 | tf_op jit(solution)/shard_map/all_gather | solution.py:44
  40.9 5.9 %copy-start.5 = (bf16[1024,32]{0,1:T(8,128)(2,1)S(1)}, bf16[1024,32]{0,1:T(8,128)(2,1)}, u32[]{:S(2)}) copy-start(bf16[1024,32]{0,1:T(8,128)(2,1)} %param.15) | copy-start | bytes 196612
  40.9 10.3 %copy-start.10 = (s32[8,2]{0,1:T(2,128)S(1)}, s32[8,2]{0,1:T(2,128)}, u32[]{:S(2)}) copy-start(s32[8,2]{0,1:T(2,128)} %param.18) | copy-start | bytes 196
  41.0 10.4 %copy-start.2 = (bf16[1024,256]{1,0:T(8,128)(2,1)S(1)}, bf16[1024,256]{1,0:T(8,128)(2,1)}, u32[]{:S(2)}) copy-start(bf16[1024,256]{1,0:T(8,128)(2,1)} %param.17) | copy-start | bytes 1572868
  41.0 10.7 %copy-start.1 = (bf16[1024,384]{1,0:T(8,128)(2,1)S(1)}, bf16[1024,384]{1,0:T(8,128)(2,1)}, u32[]{:S(2)}) copy-start(bf16[1024,384]{1,0:T(8,128)(2,1)} %param.16) | copy-start | bytes 2359300
  42.2 30.4 %all-to-all-start.1 = ((bf16[64,2,128,32]{2,3,1,0:T(8,128)(2,1)}), bf16[64,2,128,32]{2,3,1,0:T(8,128)(2,1)S(1)}, u32[]{:S(2)}, u32[]{:S(2)}) async-start(bf16[64,2,128,32]{2,3,1,0:T(8,128)(2,1)} %broadcast_select_fusion), calls=%async_computation.1 | async-start | bytes 2097152 | tf_op jit(solution)/shard_map/all_to_all | solution.py:79
  46.9 23.2 %copy-start.8 = (bf16[256,256]{1,0:T(8,128)(2,1)S(1)}, bf16[256,256]{1,0:T(8,128)(2,1)}, u32[]{:S(2)}) copy-start(bf16[256,256]{1,0:T(8,128)(2,1)} %param.20) | copy-start | bytes 393220
  46.9 16.8 %collective-permute-start = (bf16[128,32]{0,1:T(8,128)(2,1)S(1)}, bf16[128,32]{0,1:T(8,128)(2,1)S(1)}, u32[]{:S(2)}, u32[]{:S(2)}) collective-permute-start(bf16[128,32]{0,1:T(8,128)(2,1)S(1)} %get-tuple-element.53), channel_id=1, source_target_pairs={{0,8},{8,16},{16,24},{24,32},{32,40},{40,48},{48,56},{56,64},{64,7... | collective-permute-start | bytes 24584 | tf_op jit(solution)/shard_map/ppermute | solution.py:12
  49.9 18.6 %collective-permute-start.1 = (bf16[128,32]{0,1:T(8,128)(2,1)S(1)}, bf16[128,32]{0,1:T(8,128)(2,1)S(1)}, u32[]{:S(2)}, u32[]{:S(2)}) collective-permute-start(bf16[128,32]{0,1:T(8,128)(2,1)S(1)} %get-tuple-element.54), channel_id=1, source_target_pairs={{8,0},{16,8},{24,16},{32,24},{40,32},{48,40},{56,48},{64,56},{72,6... | collective-permute-start | bytes 24584 | tf_op jit(solution)/shard_map/ppermute | solution.py:15
  73.2 18.9 %copy-start.6 = (f32[1024,256]{0,1:T(8,128)S(1)}, f32[1024,256]{0,1:T(8,128)}, u32[]{:S(2)}) copy-start(f32[1024,256]{0,1:T(8,128)} %fusion.5) | copy-start | bytes 3145732
  94.7 0.8 copy-start.3
  99.5 12.0 %copy-start.9 = (s32[64,2]{1,0:T(8,128)S(1)}, s32[64,2]{1,0:T(8,128)}, u32[]{:S(2)}) copy-start(s32[64,2]{1,0:T(8,128)} %get-tuple-element.40) | copy-start | bytes 1540
  102.0 39.1 %all-to-all-start.2 = ((bf16[64,2,128,34]{2,1,3,0:T(2,128)(2,1)}), bf16[64,2,128,34]{2,1,3,0:T(2,128)(2,1)S(1)}, u32[]{:S(2)}, u32[]{:S(2)}) async-start(bf16[64,2,128,34]{2,1,3,0:T(2,128)(2,1)} %pad_maximum_fusion), calls=%async_computation.2 | async-start | bytes 2228224 | tf_op jit(solution)/shard_map/all_to_all | solution.py:144
  112.1 54.4 %collective-permute-start.3 = (f32[128,32]{0,1:T(8,128)S(1)}, f32[128,32]{0,1:T(8,128)S(1)}, u32[]{:S(2)}, u32[]{:S(2)}) collective-permute-start(f32[128,32]{0,1:T(8,128)S(1)} %get-tuple-element.42), channel_id=1, source_target_pairs={{8,0},{16,8},{24,16},{32,24},{40,32},{48,40},{56,48},{64,56},{72,6... | collective-permute-start | bytes 49160 | tf_op jit(solution)/shard_map/ppermute | solution.py:23
  113.4 53.1 %collective-permute-start.2 = (f32[128,32]{0,1:T(8,128)S(1)}, f32[128,32]{0,1:T(8,128)S(1)}, u32[]{:S(2)}, u32[]{:S(2)}) collective-permute-start(f32[128,32]{0,1:T(8,128)S(1)} %get-tuple-element.43), channel_id=1, source_target_pairs={{0,8},{8,16},{16,24},{24,32},{32,40},{40,48},{48,56},{56,64},{64,7... | collective-permute-start | bytes 49160 | tf_op jit(solution)/shard_map/ppermute | solution.py:23
  142.1 24.4 %all-to-all-start.3 = ((f32[64,1,256]{2,1,0:T(1,128)}), f32[64,1,256]{2,1,0:T(1,128)S(1)}, u32[]{:S(2)}, u32[]{:S(2)}) async-start(f32[64,1,256]{2,1,0:T(1,128)} %broadcast_in_dim.67), calls=%async_computation.3 | async-start | bytes 131072 | tf_op jit(solution)/shard_map/all_to_all | solution.py:148
  156.3 9.9 %copy-start.4 = (bf16[1024,256]{0,1:T(8,128)(2,1)S(1)}, bf16[1024,256]{0,1:T(8,128)(2,1)}, u32[]{:S(2)}) copy-start(bf16[1024,256]{0,1:T(8,128)(2,1)} %copy-done.3) | copy-start | bytes 1572868
  166.5 1.3 copy-start.7
Sparse Core Ops, SparseCore 0:
  30.1 30.4 all-gather.1

commit v12 on v11

--- a/solution.py
+++ b/solution.py
@@ -142,7 +142,7 @@
         axis=3,
     )
     arrived = lax.all_to_all(payload, "rows", split_axis=0, concat_axis=0, tiled=True)
-    returned = arrived[..., :col_count].astype(jnp.float32)
+    returned = arrived[..., :col_count]
     codes = arrived[..., col_count:].reshape(peer_count, 2, -1).astype(jnp.float32)
     mine = jnp.sum(codes[:, 0] + codes[:, 1], axis=0, keepdims=True)
     whole = lax.all_to_all(
@@ -151,11 +151,11 @@
     sum_self, sum_neigh = whole.reshape(2, col_count, -1)
     grad_self = sum_self * grad_scale
     grad_neigh = sum_neigh * grad_scale
-    target_block = jnp.where(usable, wanted, blocks).reshape(-1)
-    owed = jnp.zeros((blocks, tile_size * col_count), jnp.float32)
-    owed = owed.at[target_block].add(
-        returned.reshape(peer_count * capacity, tile_size * col_count), mode="drop"
-    )
+    target_block = jnp.where(usable, wanted, blocks)
+    routing = (
+        target_block[None] == jnp.arange(blocks, dtype=jnp.int32)[:, None, None]
+    ).astype(jnp.bfloat16)
+    owed = jnp.einsum("bps,psjc->bjc", routing, returned, preferred_element_type=jnp.float32)
     interior = (
         dense_grad
         + grad_padded[tile_size : tile_size + rows_dev]

time: 176 us -> 170 us (0.966)
  waiting for transfers between devices: 46.5 us -> 58.8 us
  local copies, waits for them, and re-layouts: 23.5 us -> 12 us
  other arithmetic: 15.4 us -> 8.4 us
    reshape x4 -> x0, local copies, waits for them, and re-layouts: 11.3 us -> none  [the longest x2 11 us: on_device(): returned.reshape(peer_count * capacity, tile_size * col_count)]
    all_to_all x1, waiting for transfers between devices: 0.01 us -> 8.45 us  [on_device(): lax.all_to_all(jnp.broadcast_to(mine, partials.shape), 'rows', split_axis...]
    scatter-add x1 -> x0, other arithmetic: 3.25 us -> none  [on_device(): owed.at[target_block]]
    all_to_all x1, waiting for transfers between devices: 7.52 us -> 9.91 us  [on_device(): lax.all_to_all(request, 'rows', split_axis=0, concat_axis=0, tiled=True)]
    concatenate x1, other arithmetic: 2.43 us -> 0.19 us  [on_device(): jnp.concatenate([returning.reshape(peer_count, capacity, tile_size, col_c...]
    concatenate x0 -> x1, local copies, waits for them, and re-layouts: none -> 1.88 us  [on_device(): jnp.concatenate([returning.reshape(peer_count, capacity, tile_size, col_c...]
  transfers between devices with their start and end apart: 9 -> 9, of which waited for: 5 -> 6; matrix products, arithmetic and copies ran while one was open for 18% -> 9% of each run, Pallas kernels for 0% -> 0%
where the time goes in v12:
time: 170 us; the launch traced here: 168 us
  waiting for transfers between devices  58.8 us (35%)
  starting transfers between devices  48 us (28%)
  blocking collectives  18.4 us (11%)
  between operations  14.5 us (9%)
  local copies, waits for them, and re-layouts  12 us (7%)
  other arithmetic  8.4 us (5%)
  matrix products  8.24 us (5%)
    all_to_all x1, waiting for transfers between devices, on_device(): lax.all_to_all(payload, 'rows', split_axis=0, concat_axis=0, tiled=True)  23.3 us
    all_gather x1, blocking collectives, on_device(): neighbours_all = lax.all_gather(neighbours, 'feat', axis=1, tiled=True)  18.4 us
    all_to_all x1, starting transfers between devices, on_device(): lax.all_to_all(request, 'rows', split_axis=0, concat_axis=0, tiled=True)  17.1 us
    ppermute x1, waiting for transfers between devices, extended(): lax.ppermute(lax.slice_in_dim(block, block.shape[dim] - width, None, axis...  12.4 us
    all_to_all x1, waiting for transfers between devices, on_device(): lax.all_to_all(request, 'rows', split_axis=0, concat_axis=0, tiled=True)  9.91 us
    all_to_all x1, starting transfers between devices, on_device(): lax.all_to_all(payload, 'rows', split_axis=0, concat_axis=0, tiled=True)  9.54 us
    all_to_all x1, waiting for transfers between devices, on_device(): lax.all_to_all(jnp.broadcast_to(mine, partials.shape), 'rows', split_axis...  8.45 us
    all_to_all x1, starting transfers between devices, on_device(): lax.all_to_all(jnp.broadcast_to(mine, partials.shape), 'rows', split_axis...  8.16 us
  transfers between devices with their start and end apart: 9, of which 6 were waited for; matrix products, arithmetic and copies ran while one was open for 9% of the time, Pallas kernels for 0%

profile of v12, /device:TPU:1, one launch (start us, length us, event | category | flops | bytes accessed | tf_op | source)
XLA Modules:
  0.0 168.3 jit_solution(6715149129800696056)
XLA Ops:
  8.0 1.5 fusion.16
  12.3 17.1 %all-to-all-start = ((s32[64,1,2]{2,1,0:T(1,128)}), s32[64,1,2]{2,1,0:T(1,128)S(1)}, u32[]{:S(2)}, u32[]{:S(2)}) async-start(s32[64,1,2]{2,1,0:T(1,128)} %bitcast.4), calls=%async_computation | async-start | bytes 65536 | tf_op jit(solution)/shard_map/all_to_all | solution.py:72
  29.5 0.9 copy_bitcast_fusion.4
  30.3 9.9 %all-to-all-done = s32[64,1,2]{2,1,0:T(1,128)S(1)} async-done(((s32[64,1,2]{2,1,0:T(1,128)}), s32[64,1,2]{2,1,0:T(1,128)S(1)}, u32[]{:S(2)}, u32[]{:S(2)}) %all-to-all-start) | async-done | bytes 544 | tf_op jit(solution)/shard_map/all_to_all | solution.py:72
  41.5 1.2 broadcast_select_fusion
  42.7 4.8 %all-to-all-start.1 = ((bf16[64,2,128,32]{2,3,1,0:T(8,128)(2,1)}), bf16[64,2,128,32]{2,3,1,0:T(8,128)(2,1)S(1)}, u32[]{:S(2)}, u32[]{:S(2)}) async-start(bf16[64,2,128,32]{2,3,1,0:T(8,128)(2,1)} %broadcast_select_fusion), calls=%async_computation.1 | async-start | bytes 2097152 | tf_op jit(solution)/shard_map/all_to_all | solution.py:79
  47.5 2.8 %collective-permute-start = (bf16[128,32]{0,1:T(8,128)(2,1)S(1)}, bf16[128,32]{0,1:T(8,128)(2,1)S(1)}, u32[]{:S(2)}, u32[]{:S(2)}) collective-permute-start(bf16[128,32]{0,1:T(8,128)(2,1)S(1)} %get-tuple-element.51), channel_id=1, source_target_pairs={{0,8},{8,16},{16,24},{24,32},{32,40},{40,48},{48,56},{56,64},{64,7... | collective-permute-start | bytes 24584 | tf_op jit(solution)/shard_map/ppermute | solution.py:12
  50.3 1.3 collective-permute-start.1
  52.3 12.4 %collective-permute-done = bf16[128,32]{0,1:T(8,128)(2,1)S(1)} collective-permute-done((bf16[128,32]{0,1:T(8,128)(2,1)S(1)}, bf16[128,32]{0,1:T(8,128)(2,1)S(1)}, u32[]{:S(2)}, u32[]{:S(2)}) %collective-permute-start) | collective-permute-done | bytes 8224 | tf_op jit(solution)/shard_map/ppermute | solution.py:12
  64.7 4.3 %collective-permute-done.1 = bf16[128,32]{0,1:T(8,128)(2,1)S(1)} collective-permute-done((bf16[128,32]{0,1:T(8,128)(2,1)S(1)}, bf16[128,32]{0,1:T(8,128)(2,1)S(1)}, u32[]{:S(2)}, u32[]{:S(2)}) %collective-permute-start.1) | collective-permute-done | bytes 8224 | tf_op jit(solution)/shard_map/ppermute | solution.py:15
  70.5 2.4 %fusion.7 = f32[1024,256]{0,1:T(8,128)} fusion(bf16[256,256]{1,0:T(8,128)(2,1)S(1)} %copy-done.8, bf16[2064,256]{0,1:T(8,128)(2,1)} %all-gather.2.cloned.1.call-done), kind=kOutput, calls=%fused_computation.23 | convolution fusion | flops 134217728 | bytes 1703936 | tf_op jit(solution)/shard_map/dot_general | solution.py:95
  74.3 18.4 %all_gather.7 = bf16[1024,256]{0,1:T(8,128)(2,1)S(1)} all-gather(bf16[1024,32]{0,1:T(8,128)(2,1)S(1)} %fusion.17), channel_id=1, replica_groups=mesh['rows'=64,'feat'=8] {'feat'}, dimensions={1}, use_global_device_ids=true | all-gather | bytes 589824 | tf_op jit(solution)/shard_map/all_gather | solution.py:93
  92.7 2.7 %multiply_convert_fusion = (bf16[1024,256]{0,1:T(8,128)(2,1)S(1)}, f32[1024,256]{0,1:T(8,128)}) fusion(bf16[2064,256]{0,1:T(8,128)(2,1)} %all-gather.2.cloned.1.call-done, f32[256]{0:T(256)S(1)} %fusion.19, f32[1024,256]{0,1:T(8,128)S(1)} %copy-done.6, bf16[1024,256]{0,1:T(8,128)(2,1)S(1)} %all_gather.7, bf16[256,256]{1,0:T(8,128)(2,1)S(1)} %copy-done), kind=kOutput, calls=%fused_computation.20 | convolution fusion | flops 137363456 | bytes 3802112 | tf_op jit(solution)/shard_map/dot_general | solution.py:96
  97.5 1.0 scatter_fusion
  99.0 1.9 %copy.159 = bf16[64,2,128,34]{2,1,3,0:T(2,128)(2,1)} copy(bf16[64,2,128,34]{2,3,1,0:T(8,128)(2,1)S(1)} %pad_maximum_fusion) | data formatting | bytes 2228224 | tf_op jit(solution)/shard_map/concatenate | solution.py:137
  100.9 9.5 %all-to-all-start.2 = ((bf16[64,2,128,34]{2,1,3,0:T(2,128)(2,1)}), bf16[64,2,128,34]{2,1,3,0:T(2,128)(2,1)S(1)}, u32[]{:S(2)}, u32[]{:S(2)}) async-start(bf16[64,2,128,34]{2,1,3,0:T(2,128)(2,1)} %copy.159), calls=%async_computation.2 | async-start | bytes 2228224 | tf_op jit(solution)/shard_map/all_to_all | solution.py:144
  110.8 2.9 %collective-permute-start.2 = (f32[128,32]{0,1:T(8,128)S(1)}, f32[128,32]{0,1:T(8,128)S(1)}, u32[]{:S(2)}, u32[]{:S(2)}) collective-permute-start(f32[128,32]{0,1:T(8,128)S(1)} %get-tuple-element.41), channel_id=1, source_target_pairs={{0,8},{8,16},{16,24},{24,32},{32,40},{40,48},{48,56},{56,64},{64,7... | collective-permute-start | bytes 49160 | tf_op jit(solution)/shard_map/ppermute | solution.py:23
  113.7 1.3 collective-permute-start.3
  115.0 1.6 multiply_convert_fusion.1
  116.6 23.3 %all-to-all-done.2 = bf16[64,2,128,34]{2,1,3,0:T(2,128)(2,1)S(1)} async-done(((bf16[64,2,128,34]{2,1,3,0:T(2,128)(2,1)}), bf16[64,2,128,34]{2,1,3,0:T(2,128)(2,1)S(1)}, u32[]{:S(2)}, u32[]{:S(2)}) %all-to-all-start.2) | async-done | bytes 1114144 | tf_op jit(solution)/shard_map/all_to_all | solution.py:144
  140.9 8.2 %all-to-all-start.3 = ((f32[64,1,256]{2,1,0:T(1,128)}), f32[64,1,256]{2,1,0:T(1,128)S(1)}, u32[]{:S(2)}, u32[]{:S(2)}) async-start(f32[64,1,256]{2,1,0:T(1,128)} %broadcast_in_dim.64), calls=%async_computation.3 | async-start | bytes 131072 | tf_op jit(solution)/shard_map/all_to_all | solution.py:148
  149.1 1.1 slice.156
  150.3 1.2 fusion.5
  151.7 8.4 %all-to-all-done.3 = f32[64,1,256]{2,1,0:T(1,128)S(1)} async-done(((f32[64,1,256]{2,1,0:T(1,128)}), f32[64,1,256]{2,1,0:T(1,128)S(1)}, u32[]{:S(2)}, u32[]{:S(2)}) %all-to-all-start.3) | async-done | bytes 65568 | tf_op jit(solution)/shard_map/all_to_all | solution.py:148
  (101 shorter events, 13.7 us)
Async XLA Ops:
  7.2 85.5 %copy-start = (bf16[256,256]{1,0:T(8,128)(2,1)S(1)}, bf16[256,256]{1,0:T(8,128)(2,1)}, u32[]{:S(2)}) copy-start(bf16[256,256]{1,0:T(8,128)(2,1)} %param.21) | copy-start | bytes 393220
  7.2 62.3 %all-gather.2.cloned.1.call-start = ((), (), s32[]{:S(2)}) async-start(), calls=%async_computation.4 | async-start | bytes 1253376 | tf_op jit(solution)/shard_map/all_gather | solution.py:44
  12.3 27.9 %all-to-all-start = ((s32[64,1,2]{2,1,0:T(1,128)}), s32[64,1,2]{2,1,0:T(1,128)S(1)}, u32[]{:S(2)}, u32[]{:S(2)}) async-start(s32[64,1,2]{2,1,0:T(1,128)} %bitcast.4), calls=%async_computation | async-start | bytes 65536 | tf_op jit(solution)/shard_map/all_to_all | solution.py:72
  42.7 4.8 %copy-start.5 = (bf16[1024,32]{0,1:T(8,128)(2,1)S(1)}, bf16[1024,32]{0,1:T(8,128)(2,1)}, u32[]{:S(2)}) copy-start(bf16[1024,32]{0,1:T(8,128)(2,1)} %param.15) | copy-start | bytes 196612
  42.7 8.9 %copy-start.9 = (s32[8,2]{0,1:T(2,128)S(1)}, s32[8,2]{0,1:T(2,128)}, u32[]{:S(2)}) copy-start(s32[8,2]{0,1:T(2,128)} %param.18) | copy-start | bytes 196
  42.7 9.1 %copy-start.2 = (bf16[1024,256]{1,0:T(8,128)(2,1)S(1)}, bf16[1024,256]{1,0:T(8,128)(2,1)}, u32[]{:S(2)}) copy-start(bf16[1024,256]{1,0:T(8,128)(2,1)} %param.17) | copy-start | bytes 1572868
  42.7 9.3 %copy-start.1 = (bf16[1024,384]{1,0:T(8,128)(2,1)S(1)}, bf16[1024,384]{1,0:T(8,128)(2,1)}, u32[]{:S(2)}) copy-start(bf16[1024,384]{1,0:T(8,128)(2,1)} %param.16) | copy-start | bytes 2359300
  42.7 30.6 %all-to-all-start.1 = ((bf16[64,2,128,32]{2,3,1,0:T(8,128)(2,1)}), bf16[64,2,128,32]{2,3,1,0:T(8,128)(2,1)S(1)}, u32[]{:S(2)}, u32[]{:S(2)}) async-start(bf16[64,2,128,32]{2,3,1,0:T(8,128)(2,1)} %broadcast_select_fusion), calls=%async_computation.1 | async-start | bytes 2097152 | tf_op jit(solution)/shard_map/all_to_all | solution.py:79
  47.5 17.2 %collective-permute-start = (bf16[128,32]{0,1:T(8,128)(2,1)S(1)}, bf16[128,32]{0,1:T(8,128)(2,1)S(1)}, u32[]{:S(2)}, u32[]{:S(2)}) collective-permute-start(bf16[128,32]{0,1:T(8,128)(2,1)S(1)} %get-tuple-element.51), channel_id=1, source_target_pairs={{0,8},{8,16},{16,24},{24,32},{32,40},{40,48},{48,56},{56,64},{64,7... | collective-permute-start | bytes 24584 | tf_op jit(solution)/shard_map/ppermute | solution.py:12
  50.3 18.7 %collective-permute-start.1 = (bf16[128,32]{0,1:T(8,128)(2,1)S(1)}, bf16[128,32]{0,1:T(8,128)(2,1)S(1)}, u32[]{:S(2)}, u32[]{:S(2)}) collective-permute-start(bf16[128,32]{0,1:T(8,128)(2,1)S(1)} %get-tuple-element.52), channel_id=1, source_target_pairs={{8,0},{16,8},{24,16},{32,24},{40,32},{48,40},{56,48},{64,56},{72,6... | collective-permute-start | bytes 24584 | tf_op jit(solution)/shard_map/ppermute | solution.py:15
  52.0 18.5 %copy-start.8 = (bf16[256,256]{1,0:T(8,128)(2,1)S(1)}, bf16[256,256]{1,0:T(8,128)(2,1)}, u32[]{:S(2)}) copy-start(bf16[256,256]{1,0:T(8,128)(2,1)} %param.20) | copy-start | bytes 393220
  74.0 18.7 %copy-start.6 = (f32[1024,256]{0,1:T(8,128)S(1)}, f32[1024,256]{0,1:T(8,128)}, u32[]{:S(2)}) copy-start(f32[1024,256]{0,1:T(8,128)} %fusion.7) | copy-start | bytes 3145732
  95.4 1.2 copy-start.3
  100.9 39.1 %all-to-all-start.2 = ((bf16[64,2,128,34]{2,1,3,0:T(2,128)(2,1)}), bf16[64,2,128,34]{2,1,3,0:T(2,128)(2,1)S(1)}, u32[]{:S(2)}, u32[]{:S(2)}) async-start(bf16[64,2,128,34]{2,1,3,0:T(2,128)(2,1)} %copy.159), calls=%async_computation.2 | async-start | bytes 2228224 | tf_op jit(solution)/shard_map/all_to_all | solution.py:144
  110.8 40.9 %collective-permute-start.2 = (f32[128,32]{0,1:T(8,128)S(1)}, f32[128,32]{0,1:T(8,128)S(1)}, u32[]{:S(2)}, u32[]{:S(2)}) collective-permute-start(f32[128,32]{0,1:T(8,128)S(1)} %get-tuple-element.41), channel_id=1, source_target_pairs={{0,8},{8,16},{16,24},{24,32},{32,40},{40,48},{48,56},{56,64},{64,7... | collective-permute-start | bytes 49160 | tf_op jit(solution)/shard_map/ppermute | solution.py:23
  113.7 38.0 %collective-permute-start.3 = (f32[128,32]{0,1:T(8,128)S(1)}, f32[128,32]{0,1:T(8,128)S(1)}, u32[]{:S(2)}, u32[]{:S(2)}) collective-permute-start(f32[128,32]{0,1:T(8,128)S(1)} %get-tuple-element.40), channel_id=1, source_target_pairs={{8,0},{16,8},{24,16},{32,24},{40,32},{48,40},{56,48},{64,56},{72,6... | collective-permute-start | bytes 49160 | tf_op jit(solution)/shard_map/ppermute | solution.py:23
  140.9 19.3 %all-to-all-start.3 = ((f32[64,1,256]{2,1,0:T(1,128)}), f32[64,1,256]{2,1,0:T(1,128)S(1)}, u32[]{:S(2)}, u32[]{:S(2)}) async-start(f32[64,1,256]{2,1,0:T(1,128)} %broadcast_in_dim.64), calls=%async_computation.3 | async-start | bytes 131072 | tf_op jit(solution)/shard_map/all_to_all | solution.py:148
  149.1 2.4 %copy-start.4 = (bf16[1024,256]{0,1:T(8,128)(2,1)S(1)}, bf16[1024,256]{0,1:T(8,128)(2,1)}, u32[]{:S(2)}) copy-start(bf16[1024,256]{0,1:T(8,128)(2,1)} %copy-done.3) | copy-start | bytes 1572868
  151.7 9.8 %copy-start.7 = (f32[1024,32]{0,1:T(8,128)}, f32[1024,32]{0,1:T(8,128)S(1)}, u32[]{:S(2)}) copy-start(f32[1024,32]{0,1:T(8,128)S(1)} %fusion.28) | copy-start | bytes 393220
Sparse Core Ops, SparseCore 0:
  10.1 34.7 all-gather.1

commit v13 on v12

--- a/solution.py
+++ b/solution.py
@@ -127,8 +127,17 @@
     grad_fetched = jnp.einsum(
         "bij,bic->bjc", far_tiles, grad_blocks, preferred_element_type=jnp.float32
     )
-    returning = jnp.zeros((peer_count * capacity, tile_size, col_count), jnp.float32)
-    returning = returning.at[slot_ids].set(grad_fetched.reshape(entries, tile_size, col_count))
+    placing = (
+        slot_ids[None, None, :]
+        == (jnp.arange(peer_count, dtype=jnp.int32)[:, None, None] * capacity
+            + jnp.arange(capacity, dtype=jnp.int32)[None, :, None])
+    ).astype(jnp.bfloat16)
+    returning = jnp.einsum(
+        "pse,ejc->psjc",
+        placing,
+        grad_fetched.reshape(entries, tile_size, col_count).astype(jnp.bfloat16),
+        preferred_element_type=jnp.float32,
+    )
     partials = jnp.stack([part_self, part_neigh]).reshape(peer_count, -1)
     high = lax.reduce_precision(partials, exponent_bits=8, mantissa_bits=7)
     coded = jnp.stack(

time: 170 us -> 171 us (level)
    all_gather x1, waiting for transfers between devices: 0.02 us -> 14 us  [on_device(): gathered = lax.all_gather(packed, 'feat', axis=1, tiled=True)]
    ppermute x1, waiting for transfers between devices: 12.4 us -> 0.01 us  [extended(): lax.ppermute(lax.slice_in_dim(block, block.shape[dim] - width, None, axis...]
    all_to_all x1, waiting for transfers between devices: 0.4 us -> 7.06 us  [on_device(): lax.all_to_all(outgoing, 'rows', split_axis=0, concat_axis=0, tiled=True)]
    ppermute x1, waiting for transfers between devices: 4.3 us -> 0.01 us  [extended(): lax.ppermute(lax.slice_in_dim(block, 0, width, axis=dim), axis, backward)]
    all_to_all x1, starting transfers between devices: 9.54 us -> 5.98 us  [on_device(): lax.all_to_all(payload, 'rows', split_axis=0, concat_axis=0, tiled=True)]
    all_to_all x1, waiting for transfers between devices: 9.91 us -> 6.84 us  [on_device(): lax.all_to_all(request, 'rows', split_axis=0, concat_axis=0, tiled=True)]
  transfers between devices with their start and end apart: 9 -> 9, of which waited for: 6 -> 5; matrix products, arithmetic and copies ran while one was open for 9% -> 11% of each run, Pallas kernels for 0% -> 0%
where the time goes in v13:
time: 171 us; the launch traced here: 169 us
  waiting for transfers between devices  58.6 us (34%)
  starting transfers between devices  48.5 us (28%)
  blocking collectives  18.4 us (11%)
  between operations  14.5 us (8%)
  local copies, waits for them, and re-layouts  11.7 us (7%)
  matrix products  8.8 us (5%)
  other arithmetic  8.69 us (5%)
    all_to_all x1, waiting for transfers between devices, on_device(): lax.all_to_all(payload, 'rows', split_axis=0, concat_axis=0, tiled=True)  22.2 us
    all_gather x1, blocking collectives, on_device(): neighbours_all = lax.all_gather(neighbours, 'feat', axis=1, tiled=True)  18.4 us
    all_to_all x1, starting transfers between devices, on_device(): lax.all_to_all(request, 'rows', split_axis=0, concat_axis=0, tiled=True)  18.3 us
    all_gather x1, waiting for transfers between devices, on_device(): gathered = lax.all_gather(packed, 'feat', axis=1, tiled=True)  14 us
    all_to_all x1, waiting for transfers between devices, on_device(): lax.all_to_all(jnp.broadcast_to(mine, partials.shape), 'rows', split_axis...  8.46 us
    all_to_all x1, starting transfers between devices, on_device(): lax.all_to_all(jnp.broadcast_to(mine, partials.shape), 'rows', split_axis...  8.18 us
    all_to_all x1, waiting for transfers between devices, on_device(): lax.all_to_all(outgoing, 'rows', split_axis=0, concat_axis=0, tiled=True)  7.06 us
    all_to_all x1, waiting for transfers between devices, on_device(): lax.all_to_all(request, 'rows', split_axis=0, concat_axis=0, tiled=True)  6.84 us
  transfers between devices with their start and end apart: 9, of which 5 were waited for; matrix products, arithmetic and copies ran while one was open for 11% of the time, Pallas kernels for 0%

profile of v13, /device:TPU:1, one launch (start us, length us, event | category | flops | bytes accessed | tf_op | source)
XLA Modules:
  0.0 169.1 jit_solution(6047689021667624436)
XLA Ops:
  7.9 4.0 %collective-permute-start = (bf16[128,32]{0,1:T(8,128)(2,1)S(1)}, bf16[128,32]{0,1:T(8,128)(2,1)S(1)}, u32[]{:S(2)}, u32[]{:S(2)}) collective-permute-start(bf16[128,32]{0,1:T(8,128)(2,1)S(1)} %get-tuple-element.51), channel_id=1, source_target_pairs={{0,8},{8,16},{16,24},{24,32},{32,40},{40,48},{48,56},{56,64},{64,7... | collective-permute-start | bytes 24584 | tf_op jit(solution)/shard_map/ppermute | solution.py:12
  12.0 1.3 collective-permute-start.1
  16.0 18.3 %all-to-all-start = ((s32[64,1,2]{2,1,0:T(1,128)}), s32[64,1,2]{2,1,0:T(1,128)S(1)}, u32[]{:S(2)}, u32[]{:S(2)}) async-start(s32[64,1,2]{2,1,0:T(1,128)} %bitcast.4), calls=%async_computation | async-start | bytes 65536 | tf_op jit(solution)/shard_map/all_to_all | solution.py:72
  35.1 1.5 fusion.17
  36.7 0.9 copy_bitcast_fusion.4
  38.2 6.8 %all-to-all-done = s32[64,1,2]{2,1,0:T(1,128)S(1)} async-done(((s32[64,1,2]{2,1,0:T(1,128)}), s32[64,1,2]{2,1,0:T(1,128)S(1)}, u32[]{:S(2)}, u32[]{:S(2)}) %all-to-all-start) | async-done | bytes 544 | tf_op jit(solution)/shard_map/all_to_all | solution.py:72
  46.3 1.2 broadcast_select_fusion
  47.5 5.4 %all-to-all-start.1 = ((bf16[64,2,128,32]{2,3,1,0:T(8,128)(2,1)}), bf16[64,2,128,32]{2,3,1,0:T(8,128)(2,1)S(1)}, u32[]{:S(2)}, u32[]{:S(2)}) async-start(bf16[64,2,128,32]{2,3,1,0:T(8,128)(2,1)} %broadcast_select_fusion), calls=%async_computation.1 | async-start | bytes 2097152 | tf_op jit(solution)/shard_map/all_to_all | solution.py:79
  54.2 14.0 %all-gather.2.cloned.1.call-done = bf16[2064,256]{0,1:T(8,128)(2,1)} async-done(((bf16[2064,32]{0,1:T(8,128)(2,1)}), bf16[2064,256]{0,1:T(8,128)(2,1)}) %all-gather.2.cloned.1.call-update) | async-done | bytes 1056784 | tf_op jit(solution)/shard_map/all_gather | solution.py:44
  68.2 0.8 slice_convert_fusion
  69.3 2.3 %fusion.8 = f32[1024,256]{0,1:T(8,128)} fusion(bf16[256,256]{1,0:T(8,128)(2,1)S(1)} %copy-done.6, bf16[2064,256]{0,1:T(8,128)(2,1)} %all-gather.2.cloned.1.call-done), kind=kOutput, calls=%fused_computation.24 | convolution fusion | flops 134217728 | bytes 1703936 | tf_op jit(solution)/shard_map/dot_general | solution.py:95
  71.6 7.1 %all-to-all-done.1 = bf16[64,2,128,32]{2,3,1,0:T(8,128)(2,1)S(1)} async-done(((bf16[64,2,128,32]{2,3,1,0:T(8,128)(2,1)}), bf16[64,2,128,32]{2,3,1,0:T(8,128)(2,1)S(1)}, u32[]{:S(2)}, u32[]{:S(2)}) %all-to-all-start.1) | async-done | bytes 1048608 | tf_op jit(solution)/shard_map/all_to_all | solution.py:79
  79.7 18.4 %all_gather.7 = bf16[1024,256]{0,1:T(8,128)(2,1)S(1)} all-gather(bf16[1024,32]{0,1:T(8,128)(2,1)S(1)} %fusion.18), channel_id=1, replica_groups=mesh['rows'=64,'feat'=8] {'feat'}, dimensions={1}, use_global_device_ids=true | all-gather | bytes 589824 | tf_op jit(solution)/shard_map/all_gather | solution.py:93
  98.1 2.7 %multiply_convert_fusion = (bf16[1024,256]{0,1:T(8,128)(2,1)S(1)}, f32[1024,256]{0,1:T(8,128)}) fusion(bf16[2064,256]{0,1:T(8,128)(2,1)} %all-gather.2.cloned.1.call-done, f32[256]{0:T(256)S(1)} %fusion.20, f32[1024,256]{0,1:T(8,128)S(1)} %copy-done.4, bf16[1024,256]{0,1:T(8,128)(2,1)S(1)} %all_gather.7, bf16[256,256]{1,0:T(8,128)(2,1)S(1)} %copy-done), kind=kOutput, calls=%fused_computation.21 | convolution fusion | flops 137363456 | bytes 3802112 | tf_op jit(solution)/shard_map/dot_general | solution.py:96
  103.0 2.1 %copy.178 = bf16[64,2,128,34]{2,1,3,0:T(2,128)(2,1)} copy(bf16[64,2,128,34]{2,0,3,1:T(8,128)(2,1)S(1)} %maximum_maximum_fusion) | data formatting | bytes 2228224 | tf_op jit(solution)/shard_map/concatenate | solution.py:146
  105.2 6.0 %all-to-all-start.2 = ((bf16[64,2,128,34]{2,1,3,0:T(2,128)(2,1)}), bf16[64,2,128,34]{2,1,3,0:T(2,128)(2,1)S(1)}, u32[]{:S(2)}, u32[]{:S(2)}) async-start(bf16[64,2,128,34]{2,1,3,0:T(2,128)(2,1)} %copy.178), calls=%async_computation.2 | async-start | bytes 2228224 | tf_op jit(solution)/shard_map/all_to_all | solution.py:153
  111.5 1.3 collective-permute-start.3
  112.8 4.0 %collective-permute-start.2 = (f32[128,32]{0,1:T(8,128)S(1)}, f32[128,32]{0,1:T(8,128)S(1)}, u32[]{:S(2)}, u32[]{:S(2)}) collective-permute-start(f32[128,32]{0,1:T(8,128)S(1)} %get-tuple-element.41), channel_id=1, source_target_pairs={{0,8},{8,16},{16,24},{24,32},{32,40},{40,48},{48,56},{56,64},{64,7... | collective-permute-start | bytes 49160 | tf_op jit(solution)/shard_map/ppermute | solution.py:23
  116.8 1.6 multiply_convert_fusion.1
  118.5 22.2 %all-to-all-done.2 = bf16[64,2,128,34]{2,1,3,0:T(2,128)(2,1)S(1)} async-done(((bf16[64,2,128,34]{2,1,3,0:T(2,128)(2,1)}), bf16[64,2,128,34]{2,1,3,0:T(2,128)(2,1)S(1)}, u32[]{:S(2)}, u32[]{:S(2)}) %all-to-all-start.2) | async-done | bytes 1114144 | tf_op jit(solution)/shard_map/all_to_all | solution.py:153
  141.7 8.2 %all-to-all-start.3 = ((f32[64,1,256]{2,1,0:T(1,128)}), f32[64,1,256]{2,1,0:T(1,128)S(1)}, u32[]{:S(2)}, u32[]{:S(2)}) async-start(f32[64,1,256]{2,1,0:T(1,128)} %broadcast_in_dim.62), calls=%async_computation.3 | async-start | bytes 131072 | tf_op jit(solution)/shard_map/all_to_all | solution.py:157
  149.9 1.1 slice.156
  151.0 1.2 fusion.6
  152.5 8.5 %all-to-all-done.3 = f32[64,1,256]{2,1,0:T(1,128)S(1)} async-done(((f32[64,1,256]{2,1,0:T(1,128)}), f32[64,1,256]{2,1,0:T(1,128)S(1)}, u32[]{:S(2)}, u32[]{:S(2)}) %all-to-all-start.3) | async-done | bytes 65568 | tf_op jit(solution)/shard_map/all_to_all | solution.py:157
  (92 shorter events, 13.7 us)
Async XLA Ops:
  7.2 90.9 %copy-start = (bf16[256,256]{1,0:T(8,128)(2,1)S(1)}, bf16[256,256]{1,0:T(8,128)(2,1)}, u32[]{:S(2)}) copy-start(bf16[256,256]{1,0:T(8,128)(2,1)} %param.21) | copy-start | bytes 393220
  7.9 45.7 %collective-permute-start = (bf16[128,32]{0,1:T(8,128)(2,1)S(1)}, bf16[128,32]{0,1:T(8,128)(2,1)S(1)}, u32[]{:S(2)}, u32[]{:S(2)}) collective-permute-start(bf16[128,32]{0,1:T(8,128)(2,1)S(1)} %get-tuple-element.51), channel_id=1, source_target_pairs={{0,8},{8,16},{16,24},{24,32},{32,40},{40,48},{48,56},{56,64},{64,7... | collective-permute-start | bytes 24584 | tf_op jit(solution)/shard_map/ppermute | solution.py:12
  12.0 41.7 %collective-permute-start.1 = (bf16[128,32]{0,1:T(8,128)(2,1)S(1)}, bf16[128,32]{0,1:T(8,128)(2,1)S(1)}, u32[]{:S(2)}, u32[]{:S(2)}) collective-permute-start(bf16[128,32]{0,1:T(8,128)(2,1)S(1)} %get-tuple-element.52), channel_id=1, source_target_pairs={{8,0},{16,8},{24,16},{32,24},{40,32},{48,40},{56,48},{64,56},{72,6... | collective-permute-start | bytes 24584 | tf_op jit(solution)/shard_map/ppermute | solution.py:15
  16.0 29.1 %all-to-all-start = ((s32[64,1,2]{2,1,0:T(1,128)}), s32[64,1,2]{2,1,0:T(1,128)S(1)}, u32[]{:S(2)}, u32[]{:S(2)}) async-start(s32[64,1,2]{2,1,0:T(1,128)} %bitcast.4), calls=%async_computation | async-start | bytes 65536 | tf_op jit(solution)/shard_map/all_to_all | solution.py:72
  34.3 33.9 %all-gather.2.cloned.1.call-start = ((), (), s32[]{:S(2)}) async-start(), calls=%async_computation.4 | async-start | bytes 1253376 | tf_op jit(solution)/shard_map/all_gather | solution.py:44
  47.5 5.6 %copy-start.2 = (bf16[1024,256]{1,0:T(8,128)(2,1)S(1)}, bf16[1024,256]{1,0:T(8,128)(2,1)}, u32[]{:S(2)}) copy-start(bf16[1024,256]{1,0:T(8,128)(2,1)} %param.17) | copy-start | bytes 1572868
  47.5 5.9 %copy-start.1 = (bf16[1024,384]{1,0:T(8,128)(2,1)S(1)}, bf16[1024,384]{1,0:T(8,128)(2,1)}, u32[]{:S(2)}) copy-start(bf16[1024,384]{1,0:T(8,128)(2,1)} %param.16) | copy-start | bytes 2359300
  47.5 31.2 %all-to-all-start.1 = ((bf16[64,2,128,32]{2,3,1,0:T(8,128)(2,1)}), bf16[64,2,128,32]{2,3,1,0:T(8,128)(2,1)S(1)}, u32[]{:S(2)}, u32[]{:S(2)}) async-start(bf16[64,2,128,32]{2,3,1,0:T(8,128)(2,1)} %broadcast_select_fusion), calls=%async_computation.1 | async-start | bytes 2097152 | tf_op jit(solution)/shard_map/all_to_all | solution.py:79
  52.9 0.8 copy-start.3
  53.6 15.7 %copy-start.6 = (bf16[256,256]{1,0:T(8,128)(2,1)S(1)}, bf16[256,256]{1,0:T(8,128)(2,1)}, u32[]{:S(2)}) copy-start(bf16[256,256]{1,0:T(8,128)(2,1)} %param.20) | copy-start | bytes 393220
  79.3 18.8 %copy-start.4 = (f32[1024,256]{0,1:T(8,128)S(1)}, f32[1024,256]{0,1:T(8,128)}, u32[]{:S(2)}) copy-start(f32[1024,256]{0,1:T(8,128)} %fusion.8) | copy-start | bytes 3145732
  105.2 35.5 %all-to-all-start.2 = ((bf16[64,2,128,34]{2,1,3,0:T(2,128)(2,1)}), bf16[64,2,128,34]{2,1,3,0:T(2,128)(2,1)S(1)}, u32[]{:S(2)}, u32[]{:S(2)}) async-start(bf16[64,2,128,34]{2,1,3,0:T(2,128)(2,1)} %copy.178), calls=%async_computation.2 | async-start | bytes 2228224 | tf_op jit(solution)/shard_map/all_to_all | solution.py:153
  111.5 40.9 %collective-permute-start.3 = (f32[128,32]{0,1:T(8,128)S(1)}, f32[128,32]{0,1:T(8,128)S(1)}, u32[]{:S(2)}, u32[]{:S(2)}) collective-permute-start(f32[128,32]{0,1:T(8,128)S(1)} %get-tuple-element.40), channel_id=1, source_target_pairs={{8,0},{16,8},{24,16},{32,24},{40,32},{48,40},{56,48},{64,56},{72,6... | collective-permute-start | bytes 49160 | tf_op jit(solution)/shard_map/ppermute | solution.py:23
  112.8 39.6 %collective-permute-start.2 = (f32[128,32]{0,1:T(8,128)S(1)}, f32[128,32]{0,1:T(8,128)S(1)}, u32[]{:S(2)}, u32[]{:S(2)}) collective-permute-start(f32[128,32]{0,1:T(8,128)S(1)} %get-tuple-element.41), channel_id=1, source_target_pairs={{0,8},{8,16},{16,24},{24,32},{32,40},{40,48},{48,56},{56,64},{64,7... | collective-permute-start | bytes 49160 | tf_op jit(solution)/shard_map/ppermute | solution.py:23
  141.7 19.3 %all-to-all-start.3 = ((f32[64,1,256]{2,1,0:T(1,128)}), f32[64,1,256]{2,1,0:T(1,128)S(1)}, u32[]{:S(2)}, u32[]{:S(2)}) async-start(f32[64,1,256]{2,1,0:T(1,128)} %broadcast_in_dim.62), calls=%async_computation.3 | async-start | bytes 131072 | tf_op jit(solution)/shard_map/all_to_all | solution.py:157
  152.5 9.8 %copy-start.5 = (f32[1024,32]{0,1:T(8,128)}, f32[1024,32]{0,1:T(8,128)S(1)}, u32[]{:S(2)}) copy-start(f32[1024,32]{0,1:T(8,128)S(1)} %fusion.29) | copy-start | bytes 393220
Sparse Core Ops, SparseCore 0:
  37.3 30.8 all-gather.1

commit v14 on v12

--- a/solution.py
+++ b/solution.py
@@ -90,10 +90,22 @@
     )
     rows_self = lax.dynamic_slice_in_dim(w_self, col_start, col_count, 0)
     rows_neigh = lax.dynamic_slice_in_dim(w_neigh, col_start, col_count, 0)
-    neighbours_all = lax.all_gather(neighbours, "feat", axis=1, tiled=True)
+    feat_count = lax.axis_size("feat")
+    neighbours_each = lax.all_to_all(
+        jnp.broadcast_to(neighbours[None], (feat_count, rows_dev, col_count)),
+        "feat",
+        split_axis=0,
+        concat_axis=0,
+        tiled=True,
+    )
     preact_all = (
         jnp.dot(feats_all, w_self, preferred_element_type=jnp.float32)
-        + jnp.dot(neighbours_all, w_neigh, preferred_element_type=jnp.float32)
+        + jnp.einsum(
+            "frc,fcd->rd",
+            neighbours_each,
+            w_neigh.reshape(feat_count, col_count, -1),
+            preferred_element_type=jnp.float32,
+        )
         + bias_all
     )
     preact = lax.dynamic_slice_in_dim(preact_all, col_start, col_count, 1)

time: 170 us -> 165 us (0.971)
  blocking collectives: 18.4 us -> 0 us
  waiting for transfers between devices: 58.8 us -> 68.3 us
  starting transfers between devices: 48 us -> 53.7 us
  matrix products: 8.24 us -> 6.38 us
    all_gather x1 -> x0, blocking collectives: 18.4 us -> none  [on_device(): neighbours_all = lax.all_gather(neighbours, 'feat', axis=1, tiled=True)]
    all_to_all x0 -> x1, starting transfers between devices: none -> 9.43 us  [on_device(): lax.all_to_all(jnp.broadcast_to(neighbours[None], (feat_count, rows_dev,...]
    all_to_all x0 -> x1, waiting for transfers between devices: none -> 8.41 us  [on_device(): lax.all_to_all(jnp.broadcast_to(neighbours[None], (feat_count, rows_dev,...]
    all_to_all x1, waiting for transfers between devices: 0.4 us -> 3.84 us  [on_device(): lax.all_to_all(outgoing, 'rows', split_axis=0, concat_axis=0, tiled=True)]
    all_to_all x1, starting transfers between devices: 9.54 us -> 6.1 us  [on_device(): lax.all_to_all(payload, 'rows', split_axis=0, concat_axis=0, tiled=True)]
    dot_general x1, matrix products: 2.67 us -> 0.33 us  [on_device(): jnp.einsum('frc,fcd->rd', neighbours_each, w_neigh.reshape(feat_count, co...]
  transfers between devices with their start and end apart: 9 -> 10, of which waited for: 6 -> 7; matrix products, arithmetic and copies ran while one was open for 9% -> 7% of each run, Pallas kernels for 0% -> 0%
where the time goes in v14:
time: 165 us; the launch traced here: 163 us
  waiting for transfers between devices  68.3 us (41%)
  starting transfers between devices  53.7 us (33%)
  between operations  14.5 us (9%)
  local copies, waits for them, and re-layouts  12.9 us (8%)
  other arithmetic  7.53 us (5%)
  matrix products  6.38 us (4%)
    all_to_all x1, waiting for transfers between devices, on_device(): lax.all_to_all(payload, 'rows', split_axis=0, concat_axis=0, tiled=True)  22.5 us
    all_to_all x1, starting transfers between devices, on_device(): lax.all_to_all(request, 'rows', split_axis=0, concat_axis=0, tiled=True)  17.1 us
    ppermute x1, waiting for transfers between devices, extended(): lax.ppermute(lax.slice_in_dim(block, block.shape[dim] - width, None, axis...  11.5 us
    all_to_all x1, starting transfers between devices, on_device(): lax.all_to_all(jnp.broadcast_to(neighbours[None], (feat_count, rows_dev,...  9.43 us
    all_to_all x1, waiting for transfers between devices, on_device(): lax.all_to_all(request, 'rows', split_axis=0, concat_axis=0, tiled=True)  9.25 us
    all_to_all x1, waiting for transfers between devices, on_device(): lax.all_to_all(jnp.broadcast_to(mine, partials.shape), 'rows', split_axis...  8.45 us
    all_to_all x1, waiting for transfers between devices, on_device(): lax.all_to_all(jnp.broadcast_to(neighbours[None], (feat_count, rows_dev,...  8.41 us
    all_to_all x1, starting transfers between devices, on_device(): lax.all_to_all(jnp.broadcast_to(mine, partials.shape), 'rows', split_axis...  7.89 us
  transfers between devices with their start and end apart: 10, of which 7 were waited for; matrix products, arithmetic and copies ran while one was open for 7% of the time, Pallas kernels for 0%

profile of v14, /device:TPU:1, one launch (start us, length us, event | category | flops | bytes accessed | tf_op | source)
XLA Modules:
  0.0 163.3 jit_solution(11384508221227333285)
XLA Ops:
  10.0 17.1 %all-to-all-start = ((s32[64,1,2]{2,1,0:T(1,128)}), s32[64,1,2]{2,1,0:T(1,128)S(1)}, u32[]{:S(2)}, u32[]{:S(2)}) async-start(s32[64,1,2]{2,1,0:T(1,128)} %bitcast.4), calls=%async_computation | async-start | bytes 65536 | tf_op jit(solution)/shard_map/all_to_all | solution.py:72
  28.6 9.2 %all-to-all-done = s32[64,1,2]{2,1,0:T(1,128)S(1)} async-done(((s32[64,1,2]{2,1,0:T(1,128)}), s32[64,1,2]{2,1,0:T(1,128)S(1)}, u32[]{:S(2)}, u32[]{:S(2)}) %all-to-all-start) | async-done | bytes 544 | tf_op jit(solution)/shard_map/all_to_all | solution.py:72
  39.1 1.2 broadcast_select_fusion
  40.3 4.8 %all-to-all-start.1 = ((bf16[64,2,128,32]{2,3,1,0:T(8,128)(2,1)}), bf16[64,2,128,32]{2,3,1,0:T(8,128)(2,1)S(1)}, u32[]{:S(2)}, u32[]{:S(2)}) async-start(bf16[64,2,128,32]{2,3,1,0:T(8,128)(2,1)} %broadcast_select_fusion), calls=%async_computation.1 | async-start | bytes 2097152 | tf_op jit(solution)/shard_map/all_to_all | solution.py:79
  46.0 2.8 %collective-permute-start = (bf16[128,32]{0,1:T(8,128)(2,1)S(1)}, bf16[128,32]{0,1:T(8,128)(2,1)S(1)}, u32[]{:S(2)}, u32[]{:S(2)}) collective-permute-start(bf16[128,32]{0,1:T(8,128)(2,1)S(1)} %get-tuple-element.51), channel_id=1, source_target_pairs={{0,8},{8,16},{16,24},{24,32},{32,40},{40,48},{48,56},{56,64},{64,7... | collective-permute-start | bytes 24584 | tf_op jit(solution)/shard_map/ppermute | solution.py:12
  48.8 1.3 collective-permute-start.1
  50.8 11.5 %collective-permute-done = bf16[128,32]{0,1:T(8,128)(2,1)S(1)} collective-permute-done((bf16[128,32]{0,1:T(8,128)(2,1)S(1)}, bf16[128,32]{0,1:T(8,128)(2,1)S(1)}, u32[]{:S(2)}, u32[]{:S(2)}) %collective-permute-start) | collective-permute-done | bytes 8224 | tf_op jit(solution)/shard_map/ppermute | solution.py:12
  62.3 4.3 %collective-permute-done.1 = bf16[128,32]{0,1:T(8,128)(2,1)S(1)} collective-permute-done((bf16[128,32]{0,1:T(8,128)(2,1)S(1)}, bf16[128,32]{0,1:T(8,128)(2,1)S(1)}, u32[]{:S(2)}, u32[]{:S(2)}) %collective-permute-start.1) | collective-permute-done | bytes 8224 | tf_op jit(solution)/shard_map/ppermute | solution.py:15
  67.1 3.8 %all-to-all-done.1 = bf16[64,2,128,32]{2,3,1,0:T(8,128)(2,1)S(1)} async-done(((bf16[64,2,128,32]{2,3,1,0:T(8,128)(2,1)}), bf16[64,2,128,32]{2,3,1,0:T(8,128)(2,1)S(1)}, u32[]{:S(2)}, u32[]{:S(2)}) %all-to-all-start.1) | async-done | bytes 1048608 | tf_op jit(solution)/shard_map/all_to_all | solution.py:79
  71.9 0.9 broadcast_in_dim.69
  72.8 9.4 %all-to-all-start.2 = ((bf16[8,1024,32]{1,2,0:T(8,128)(2,1)}), bf16[8,1024,32]{1,2,0:T(8,128)(2,1)S(1)}, u32[]{:S(2)}, u32[]{:S(2)}) async-start(bf16[8,1024,32]{1,2,0:T(8,128)(2,1)} %broadcast_in_dim.69), calls=%async_computation.2 | async-start | bytes 1048576 | tf_op jit(solution)/shard_map/all_to_all | solution.py:94
  83.3 8.4 %all-to-all-done.2 = bf16[8,1024,32]{1,2,0:T(8,128)(2,1)S(1)} async-done(((bf16[8,1024,32]{1,2,0:T(8,128)(2,1)}), bf16[8,1024,32]{1,2,0:T(8,128)(2,1)S(1)}, u32[]{:S(2)}, u32[]{:S(2)}) %all-to-all-start.2) | async-done | bytes 524320 | tf_op jit(solution)/shard_map/all_to_all | solution.py:94
  92.1 2.8 %multiply_convert_fusion = (bf16[1024,256]{0,1:T(8,128)(2,1)S(1)}, f32[1024,256]{0,1:T(8,128)}) fusion(bf16[2064,256]{0,1:T(8,128)(2,1)} %all-gather.2.cloned.1.call-done, f32[256]{0:T(256)S(1)} %fusion.18, f32[1024,256]{0,1:T(8,128)S(1)} %convolution_bitcast_fusion, bf16[256,256]{1,0:T(8,128)(2,1)S(1)} %copy-done), kind=kOutput, calls=%fused_computation.21 | convolution fusion | flops 137363456 | bytes 3802112 | tf_op jit(solution)/shard_map/dot_general | solution.py:102
  97.0 1.0 scatter_fusion
  98.5 1.9 %copy.159 = bf16[64,2,128,34]{2,1,3,0:T(2,128)(2,1)} copy(bf16[64,2,128,34]{2,3,1,0:T(8,128)(2,1)S(1)} %pad_maximum_fusion) | data formatting | bytes 2228224 | tf_op jit(solution)/shard_map/concatenate | solution.py:149
  100.4 6.1 %all-to-all-start.3 = ((bf16[64,2,128,34]{2,1,3,0:T(2,128)(2,1)}), bf16[64,2,128,34]{2,1,3,0:T(2,128)(2,1)S(1)}, u32[]{:S(2)}, u32[]{:S(2)}) async-start(bf16[64,2,128,34]{2,1,3,0:T(2,128)(2,1)} %copy.159), calls=%async_computation.3 | async-start | bytes 2228224 | tf_op jit(solution)/shard_map/all_to_all | solution.py:156
  106.9 2.9 %collective-permute-start.2 = (f32[128,32]{0,1:T(8,128)S(1)}, f32[128,32]{0,1:T(8,128)S(1)}, u32[]{:S(2)}, u32[]{:S(2)}) collective-permute-start(f32[128,32]{0,1:T(8,128)S(1)} %get-tuple-element.41), channel_id=1, source_target_pairs={{0,8},{8,16},{16,24},{24,32},{32,40},{40,48},{48,56},{56,64},{64,7... | collective-permute-start | bytes 49160 | tf_op jit(solution)/shard_map/ppermute | solution.py:23
  109.8 1.3 collective-permute-start.3
  111.1 1.6 multiply_convert_fusion.1
  112.7 22.5 %all-to-all-done.3 = bf16[64,2,128,34]{2,1,3,0:T(2,128)(2,1)S(1)} async-done(((bf16[64,2,128,34]{2,1,3,0:T(2,128)(2,1)}), bf16[64,2,128,34]{2,1,3,0:T(2,128)(2,1)S(1)}, u32[]{:S(2)}, u32[]{:S(2)}) %all-to-all-start.3) | async-done | bytes 1114144 | tf_op jit(solution)/shard_map/all_to_all | solution.py:156
  136.2 7.9 %all-to-all-start.4 = ((f32[64,1,256]{2,1,0:T(1,128)}), f32[64,1,256]{2,1,0:T(1,128)S(1)}, u32[]{:S(2)}, u32[]{:S(2)}) async-start(f32[64,1,256]{2,1,0:T(1,128)} %broadcast_in_dim.71), calls=%async_computation.4 | async-start | bytes 131072 | tf_op jit(solution)/shard_map/all_to_all | solution.py:160
  144.1 1.1 slice.156
  145.3 1.2 fusion.5
  146.7 8.5 %all-to-all-done.4 = f32[64,1,256]{2,1,0:T(1,128)S(1)} async-done(((f32[64,1,256]{2,1,0:T(1,128)}), f32[64,1,256]{2,1,0:T(1,128)S(1)}, u32[]{:S(2)}, u32[]{:S(2)}) %all-to-all-start.4) | async-done | bytes 65568 | tf_op jit(solution)/shard_map/all_to_all | solution.py:160
  (103 shorter events, 15.1 us)
Async XLA Ops:
  7.2 84.9 %copy-start = (bf16[256,256]{1,0:T(8,128)(2,1)S(1)}, bf16[256,256]{1,0:T(8,128)(2,1)}, u32[]{:S(2)}) copy-start(bf16[256,256]{1,0:T(8,128)(2,1)} %param.20) | copy-start | bytes 393220
  10.0 27.9 %all-to-all-start = ((s32[64,1,2]{2,1,0:T(1,128)}), s32[64,1,2]{2,1,0:T(1,128)S(1)}, u32[]{:S(2)}, u32[]{:S(2)}) async-start(s32[64,1,2]{2,1,0:T(1,128)} %bitcast.4), calls=%async_computation | async-start | bytes 65536 | tf_op jit(solution)/shard_map/all_to_all | solution.py:72
  40.3 5.0 %copy-start.5 = (bf16[1024,32]{0,1:T(8,128)(2,1)S(1)}, bf16[1024,32]{0,1:T(8,128)(2,1)}, u32[]{:S(2)}) copy-start(bf16[1024,32]{0,1:T(8,128)(2,1)} %param.15) | copy-start | bytes 196612
  40.3 5.0 %copy-start.8 = (bf16[1024,32]{0,1:T(8,128)(2,1)S(1)}, bf16[1024,32]{0,1:T(8,128)(2,1)}, u32[]{:S(2)}) copy-start(bf16[1024,32]{0,1:T(8,128)(2,1)} %param.23) | copy-start | bytes 196612
  40.3 9.8 %copy-start.9 = (s32[8,2]{0,1:T(2,128)S(1)}, s32[8,2]{0,1:T(2,128)}, u32[]{:S(2)}) copy-start(s32[8,2]{0,1:T(2,128)} %param.18) | copy-start | bytes 196
  40.3 10.0 %copy-start.2 = (bf16[1024,256]{1,0:T(8,128)(2,1)S(1)}, bf16[1024,256]{1,0:T(8,128)(2,1)}, u32[]{:S(2)}) copy-start(bf16[1024,256]{1,0:T(8,128)(2,1)} %param.17) | copy-start | bytes 1572868
  40.3 10.2 %copy-start.1 = (bf16[1024,384]{1,0:T(8,128)(2,1)S(1)}, bf16[1024,384]{1,0:T(8,128)(2,1)}, u32[]{:S(2)}) copy-start(bf16[1024,384]{1,0:T(8,128)(2,1)} %param.16) | copy-start | bytes 2359300
  40.3 30.6 %all-to-all-start.1 = ((bf16[64,2,128,32]{2,3,1,0:T(8,128)(2,1)}), bf16[64,2,128,32]{2,3,1,0:T(8,128)(2,1)S(1)}, u32[]{:S(2)}, u32[]{:S(2)}) async-start(bf16[64,2,128,32]{2,3,1,0:T(8,128)(2,1)} %broadcast_select_fusion), calls=%async_computation.1 | async-start | bytes 2097152 | tf_op jit(solution)/shard_map/all_to_all | solution.py:79
  45.1 37.1 %all-gather.2.cloned.1.call-start = ((), (), s32[]{:S(2)}) async-start(), calls=%async_computation.5 | async-start | bytes 1253376 | tf_op jit(solution)/shard_map/all_gather | solution.py:44
  46.0 16.3 %collective-permute-start = (bf16[128,32]{0,1:T(8,128)(2,1)S(1)}, bf16[128,32]{0,1:T(8,128)(2,1)S(1)}, u32[]{:S(2)}, u32[]{:S(2)}) collective-permute-start(bf16[128,32]{0,1:T(8,128)(2,1)S(1)} %get-tuple-element.51), channel_id=1, source_target_pairs={{0,8},{8,16},{16,24},{24,32},{32,40},{40,48},{48,56},{56,64},{64,7... | collective-permute-start | bytes 24584 | tf_op jit(solution)/shard_map/ppermute | solution.py:12
  48.8 17.8 %collective-permute-start.1 = (bf16[128,32]{0,1:T(8,128)(2,1)S(1)}, bf16[128,32]{0,1:T(8,128)(2,1)S(1)}, u32[]{:S(2)}, u32[]{:S(2)}) collective-permute-start(bf16[128,32]{0,1:T(8,128)(2,1)S(1)} %get-tuple-element.52), channel_id=1, source_target_pairs={{8,0},{16,8},{24,16},{32,24},{40,32},{48,40},{56,48},{64,56},{72,6... | collective-permute-start | bytes 24584 | tf_op jit(solution)/shard_map/ppermute | solution.py:15
  71.6 20.1 %copy-start.7 = (bf16[256,256]{1,0:T(8,128)(2,1)S(1)}, bf16[256,256]{1,0:T(8,128)(2,1)}, u32[]{:S(2)}) copy-start(bf16[256,256]{1,0:T(8,128)(2,1)} %param.21) | copy-start | bytes 393220
  72.8 18.9 %all-to-all-start.2 = ((bf16[8,1024,32]{1,2,0:T(8,128)(2,1)}), bf16[8,1024,32]{1,2,0:T(8,128)(2,1)S(1)}, u32[]{:S(2)}, u32[]{:S(2)}) async-start(bf16[8,1024,32]{1,2,0:T(8,128)(2,1)} %broadcast_in_dim.69), calls=%async_computation.2 | async-start | bytes 1048576 | tf_op jit(solution)/shard_map/all_to_all | solution.py:94
  94.9 1.4 copy-start.3
  100.4 34.8 %all-to-all-start.3 = ((bf16[64,2,128,34]{2,1,3,0:T(2,128)(2,1)}), bf16[64,2,128,34]{2,1,3,0:T(2,128)(2,1)S(1)}, u32[]{:S(2)}, u32[]{:S(2)}) async-start(bf16[64,2,128,34]{2,1,3,0:T(2,128)(2,1)} %copy.159), calls=%async_computation.3 | async-start | bytes 2228224 | tf_op jit(solution)/shard_map/all_to_all | solution.py:156
  106.9 39.8 %collective-permute-start.2 = (f32[128,32]{0,1:T(8,128)S(1)}, f32[128,32]{0,1:T(8,128)S(1)}, u32[]{:S(2)}, u32[]{:S(2)}) collective-permute-start(f32[128,32]{0,1:T(8,128)S(1)} %get-tuple-element.41), channel_id=1, source_target_pairs={{0,8},{8,16},{16,24},{24,32},{32,40},{40,48},{48,56},{56,64},{64,7... | collective-permute-start | bytes 49160 | tf_op jit(solution)/shard_map/ppermute | solution.py:23
  109.8 36.9 %collective-permute-start.3 = (f32[128,32]{0,1:T(8,128)S(1)}, f32[128,32]{0,1:T(8,128)S(1)}, u32[]{:S(2)}, u32[]{:S(2)}) collective-permute-start(f32[128,32]{0,1:T(8,128)S(1)} %get-tuple-element.40), channel_id=1, source_target_pairs={{8,0},{16,8},{24,16},{32,24},{40,32},{48,40},{56,48},{64,56},{72,6... | collective-permute-start | bytes 49160 | tf_op jit(solution)/shard_map/ppermute | solution.py:23
  136.2 19.0 %all-to-all-start.4 = ((f32[64,1,256]{2,1,0:T(1,128)}), f32[64,1,256]{2,1,0:T(1,128)S(1)}, u32[]{:S(2)}, u32[]{:S(2)}) async-start(f32[64,1,256]{2,1,0:T(1,128)} %broadcast_in_dim.71), calls=%async_computation.4 | async-start | bytes 131072 | tf_op jit(solution)/shard_map/all_to_all | solution.py:160
  144.1 2.4 %copy-start.4 = (bf16[1024,256]{0,1:T(8,128)(2,1)S(1)}, bf16[1024,256]{0,1:T(8,128)(2,1)}, u32[]{:S(2)}) copy-start(bf16[1024,256]{0,1:T(8,128)(2,1)} %copy-done.3) | copy-start | bytes 1572868
  146.7 9.8 %copy-start.6 = (f32[1024,32]{0,1:T(8,128)}, f32[1024,32]{0,1:T(8,128)S(1)}, u32[]{:S(2)}) copy-start(f32[1024,32]{0,1:T(8,128)S(1)} %fusion.27) | copy-start | bytes 393220
Sparse Core Ops, SparseCore 0:
  48.1 31.4 all-gather.1

commit v15 on v14

--- a/solution.py
+++ b/solution.py
@@ -41,10 +41,18 @@
         jnp.stack([bias_high, bias_mid, bias_rest - bias_mid]).astype(jnp.bfloat16)
     )
     packed = jnp.concatenate([node_feats, cotangent, bias_parts], axis=0)
-    gathered = lax.all_gather(packed, "feat", axis=1, tiled=True)
-    feats_all = gathered[:rows_dev]
-    cotangent_all = gathered[rows_dev : 2 * rows_dev]
-    bias_rows = gathered[2 * rows_dev : 2 * rows_dev + 3].astype(jnp.float32)
+    feat_count = lax.axis_size("feat")
+    gathered = lax.all_to_all(
+        jnp.broadcast_to(packed[None], (feat_count,) + packed.shape),
+        "feat",
+        split_axis=0,
+        concat_axis=0,
+        tiled=True,
+    )
+    feats_each = gathered[:, :rows_dev]
+    cotangent_all = gathered[:, rows_dev : 2 * rows_dev].transpose(1, 0, 2).reshape(rows_dev, -1)
+    bias_rows = gathered[:, 2 * rows_dev : 2 * rows_dev + 3].astype(jnp.float32)
+    bias_rows = bias_rows.transpose(1, 0, 2).reshape(3, -1)
     bias_all = (bias_rows[0] + bias_rows[1]) + bias_rows[2]
     padded = extended(node_feats, (("rows", 0),), tile_size)
     windows = jnp.concatenate(
@@ -90,7 +98,6 @@
     )
     rows_self = lax.dynamic_slice_in_dim(w_self, col_start, col_count, 0)
     rows_neigh = lax.dynamic_slice_in_dim(w_neigh, col_start, col_count, 0)
-    feat_count = lax.axis_size("feat")
     neighbours_each = lax.all_to_all(
         jnp.broadcast_to(neighbours[None], (feat_count, rows_dev, col_count)),
         "feat",
@@ -99,7 +106,12 @@
         tiled=True,
     )
     preact_all = (
-        jnp.dot(feats_all, w_self, preferred_element_type=jnp.float32)
+        jnp.einsum(
+            "frc,fcd->rd",
+            feats_each,
+            w_self.reshape(feat_count, col_count, -1),
+            preferred_element_type=jnp.float32,
+        )
         + jnp.einsum(
             "frc,fcd->rd",
             neighbours_each,

time: 165 us -> 171 us (1.036)
  waiting for transfers between devices: 68.3 us -> 82.8 us
  between operations: 14.5 us -> 1.17 us
  starting transfers between devices: 53.7 us -> 57.7 us
  local copies, waits for them, and re-layouts: 12.9 us -> 16.5 us
    all_to_all x1, waiting for transfers between devices: 3.84 us -> 20.8 us  [on_device(): lax.all_to_all(outgoing, 'rows', split_axis=0, concat_axis=0, tiled=True)]
    all_to_all x0 -> x1, waiting for transfers between devices: none -> 13.1 us  [on_device(): lax.all_to_all(jnp.broadcast_to(packed[None], (feat_count,) + packed.shap...]
    ppermute x1, waiting for transfers between devices: 11.5 us -> 0.01 us  [extended(): lax.ppermute(lax.slice_in_dim(block, block.shape[dim] - width, None, axis...]
    all_to_all x0 -> x1, starting transfers between devices: none -> 9.43 us  [on_device(): lax.all_to_all(jnp.broadcast_to(packed[None], (feat_count,) + packed.shap...]
    all_to_all x1, starting transfers between devices: 9.43 us -> 4.27 us  [on_device(): lax.all_to_all(jnp.broadcast_to(neighbours[None], (feat_count, rows_dev,...]
    ppermute x1, waiting for transfers between devices: 4.31 us -> 0.01 us  [extended(): lax.ppermute(lax.slice_in_dim(block, 0, width, axis=dim), axis, backward)]
  transfers between devices with their start and end apart: 10 -> 10, of which waited for: 7 -> 6; matrix products, arithmetic and copies ran while one was open for 7% -> 7% of each run, Pallas kernels for 0% -> 0%
where the time goes in v15:
time: 171 us; the launch traced here: 170 us
  waiting for transfers between devices  82.8 us (48%)
  starting transfers between devices  57.7 us (34%)
  local copies, waits for them, and re-layouts  16.5 us (10%)
  other arithmetic  6.46 us (4%)
  matrix products  5.14 us (3%)
    all_to_all x1, waiting for transfers between devices, on_device(): lax.all_to_all(payload, 'rows', split_axis=0, concat_axis=0, tiled=True)  22.5 us
    all_to_all x1, waiting for transfers between devices, on_device(): lax.all_to_all(outgoing, 'rows', split_axis=0, concat_axis=0, tiled=True)  20.8 us
    all_to_all x1, starting transfers between devices, on_device(): lax.all_to_all(request, 'rows', split_axis=0, concat_axis=0, tiled=True)  17.1 us
    all_to_all x1, waiting for transfers between devices, on_device(): lax.all_to_all(jnp.broadcast_to(packed[None], (feat_count,) + packed.shap...  13.1 us
    all_to_all x1, waiting for transfers between devices, on_device(): lax.all_to_all(request, 'rows', split_axis=0, concat_axis=0, tiled=True)  9.91 us
    all_to_all x1, starting transfers between devices, on_device(): lax.all_to_all(jnp.broadcast_to(packed[None], (feat_count,) + packed.shap...  9.43 us
    all_to_all x1, waiting for transfers between devices, on_device(): lax.all_to_all(jnp.broadcast_to(mine, partials.shape), 'rows', split_axis...  8.45 us
    all_to_all x1, waiting for transfers between devices, on_device(): lax.all_to_all(jnp.broadcast_to(neighbours[None], (feat_count, rows_dev,...  8.08 us
  transfers between devices with their start and end apart: 10, of which 6 were waited for; matrix products, arithmetic and copies ran while one was open for 7% of the time, Pallas kernels for 0%

profile of v15, /device:TPU:1, one launch (start us, length us, event | category | flops | bytes accessed | tf_op | source)
XLA Modules:
  0.0 169.8 jit_solution(12760283493842639771)
XLA Ops:
  3.4 17.1 %all-to-all-start.1 = ((s32[64,1,2]{2,1,0:T(1,128)}), s32[64,1,2]{2,1,0:T(1,128)S(1)}, u32[]{:S(2)}, u32[]{:S(2)}) async-start(s32[64,1,2]{2,1,0:T(1,128)} %bitcast.6), calls=%async_computation.1 | async-start | bytes 65536 | tf_op jit(solution)/shard_map/all_to_all | solution.py:80
  21.4 9.9 %all-to-all-done.1 = s32[64,1,2]{2,1,0:T(1,128)S(1)} async-done(((s32[64,1,2]{2,1,0:T(1,128)}), s32[64,1,2]{2,1,0:T(1,128)S(1)}, u32[]{:S(2)}, u32[]{:S(2)}) %all-to-all-start.1) | async-done | bytes 544 | tf_op jit(solution)/shard_map/all_to_all | solution.py:80
  32.6 1.2 broadcast_select_fusion
  33.8 4.8 %all-to-all-start.2 = ((bf16[64,2,128,32]{2,3,1,0:T(8,128)(2,1)}), bf16[64,2,128,32]{2,3,1,0:T(8,128)(2,1)S(1)}, u32[]{:S(2)}, u32[]{:S(2)}) async-start(bf16[64,2,128,32]{2,3,1,0:T(8,128)(2,1)} %broadcast_select_fusion), calls=%async_computation.2 | async-start | bytes 2097152 | tf_op jit(solution)/shard_map/all_to_all | solution.py:87
  38.6 2.8 %collective-permute-start = (bf16[128,32]{0,1:T(8,128)(2,1)S(1)}, bf16[128,32]{0,1:T(8,128)(2,1)S(1)}, u32[]{:S(2)}, u32[]{:S(2)}) collective-permute-start(bf16[128,32]{0,1:T(8,128)(2,1)S(1)} %get-tuple-element.51), channel_id=1, source_target_pairs={{0,8},{8,16},{16,24},{24,32},{32,40},{40,48},{48,56},{56,64},{64,7... | collective-permute-start | bytes 24584 | tf_op jit(solution)/shard_map/ppermute | solution.py:12
  41.4 1.3 collective-permute-start.1
  43.6 20.8 %all-to-all-done.2 = bf16[64,2,128,32]{2,3,1,0:T(8,128)(2,1)S(1)} async-done(((bf16[64,2,128,32]{2,3,1,0:T(8,128)(2,1)}), bf16[64,2,128,32]{2,3,1,0:T(8,128)(2,1)S(1)}, u32[]{:S(2)}, u32[]{:S(2)}) %all-to-all-start.2) | async-done | bytes 1048608 | tf_op jit(solution)/shard_map/all_to_all | solution.py:87
  64.4 1.1 broadcast_in_dim.41
  65.7 9.4 %all-to-all-start = ((bf16[8,2064,32]{1,2,0:T(8,128)(2,1)}), bf16[8,2064,32]{1,2,0:T(8,128)(2,1)S(1)}, u32[]{:S(2)}, u32[]{:S(2)}) async-start(bf16[8,2064,32]{1,2,0:T(8,128)(2,1)} %broadcast_in_dim.41), calls=%async_computation | async-start | bytes 2228224 | tf_op jit(solution)/shard_map/all_to_all | solution.py:45
  75.6 1.8 %gather_fusion.1 = bf16[16,128,32]{1,2,0:T(8,128)(2,1)S(1)} fusion(bf16[128,128,32]{1,2,0:T(8,128)(2,1)} %bitcast.138, s32[1024]{0:T(1024)S(1)} %pad_clamp_fusion), kind=kCustom, calls=%fused_computation.1 | custom fusion | bytes 262208 | tf_op jit(solution)/shard_map/gather | solution.py:88
  77.8 13.1 %all-to-all-done = bf16[8,2064,32]{1,2,0:T(8,128)(2,1)S(1)} async-done(((bf16[8,2064,32]{1,2,0:T(8,128)(2,1)}), bf16[8,2064,32]{1,2,0:T(8,128)(2,1)S(1)}, u32[]{:S(2)}, u32[]{:S(2)}) %all-to-all-start) | async-done | bytes 1056800 | tf_op jit(solution)/shard_map/all_to_all | solution.py:45
  91.8 4.3 %all-to-all-start.3 = ((bf16[8,1024,32]{1,2,0:T(8,128)(2,1)}), bf16[8,1024,32]{1,2,0:T(8,128)(2,1)S(1)}, u32[]{:S(2)}, u32[]{:S(2)}) async-start(bf16[8,1024,32]{1,2,0:T(8,128)(2,1)} %broadcast_in_dim.76), calls=%async_computation.3 | async-start | bytes 1048576 | tf_op jit(solution)/shard_map/all_to_all | solution.py:101
  97.5 8.1 %all-to-all-done.3 = bf16[8,1024,32]{1,2,0:T(8,128)(2,1)S(1)} async-done(((bf16[8,1024,32]{1,2,0:T(8,128)(2,1)}), bf16[8,1024,32]{1,2,0:T(8,128)(2,1)S(1)}, u32[]{:S(2)}, u32[]{:S(2)}) %all-to-all-start.3) | async-done | bytes 524320 | tf_op jit(solution)/shard_map/all_to_all | solution.py:101
  106.8 1.6 fusion.9
  112.0 1.9 %copy.153 = bf16[64,2,128,34]{2,1,3,0:T(2,128)(2,1)} copy(bf16[64,2,128,34]{2,3,1,0:T(8,128)(2,1)S(1)} %pad_maximum_fusion) | data formatting | bytes 2228224 | tf_op jit(solution)/shard_map/concatenate | solution.py:161
  113.9 5.9 %all-to-all-start.4 = ((bf16[64,2,128,34]{2,1,3,0:T(2,128)(2,1)}), bf16[64,2,128,34]{2,1,3,0:T(2,128)(2,1)S(1)}, u32[]{:S(2)}, u32[]{:S(2)}) async-start(bf16[64,2,128,34]{2,1,3,0:T(2,128)(2,1)} %copy.153), calls=%async_computation.4 | async-start | bytes 2228224 | tf_op jit(solution)/shard_map/all_to_all | solution.py:168
  120.2 2.9 %collective-permute-start.2 = (f32[128,32]{0,1:T(8,128)S(1)}, f32[128,32]{0,1:T(8,128)S(1)}, u32[]{:S(2)}, u32[]{:S(2)}) collective-permute-start(f32[128,32]{0,1:T(8,128)S(1)} %get-tuple-element.41), channel_id=1, source_target_pairs={{0,8},{8,16},{16,24},{24,32},{32,40},{40,48},{48,56},{56,64},{64,7... | collective-permute-start | bytes 49160 | tf_op jit(solution)/shard_map/ppermute | solution.py:23
  123.1 1.3 collective-permute-start.3
  124.4 1.6 multiply_convert_fusion
  126.0 22.5 %all-to-all-done.4 = bf16[64,2,128,34]{2,1,3,0:T(2,128)(2,1)S(1)} async-done(((bf16[64,2,128,34]{2,1,3,0:T(2,128)(2,1)}), bf16[64,2,128,34]{2,1,3,0:T(2,128)(2,1)S(1)}, u32[]{:S(2)}, u32[]{:S(2)}) %all-to-all-start.4) | async-done | bytes 1114144 | tf_op jit(solution)/shard_map/all_to_all | solution.py:168
  149.5 7.9 %all-to-all-start.5 = ((f32[64,1,256]{2,1,0:T(1,128)}), f32[64,1,256]{2,1,0:T(1,128)S(1)}, u32[]{:S(2)}, u32[]{:S(2)}) async-start(f32[64,1,256]{2,1,0:T(1,128)} %broadcast_in_dim.78), calls=%async_computation.5 | async-start | bytes 131072 | tf_op jit(solution)/shard_map/all_to_all | solution.py:172
  157.4 1.1 slice.159
  158.6 1.2 fusion.6
  160.1 8.5 %all-to-all-done.5 = f32[64,1,256]{2,1,0:T(1,128)S(1)} async-done(((f32[64,1,256]{2,1,0:T(1,128)}), f32[64,1,256]{2,1,0:T(1,128)S(1)}, u32[]{:S(2)}, u32[]{:S(2)}) %all-to-all-start.5) | async-done | bytes 65568 | tf_op jit(solution)/shard_map/all_to_all | solution.py:172
  (111 shorter events, 16.5 us)
Async XLA Ops:
  0.6 105.3 %copy-start = (bf16[256,256]{1,0:T(8,128)(2,1)S(1)}, bf16[256,256]{1,0:T(8,128)(2,1)}, u32[]{:S(2)}) copy-start(bf16[256,256]{1,0:T(8,128)(2,1)} %param.20) | copy-start | bytes 393220
  3.4 27.9 %all-to-all-start.1 = ((s32[64,1,2]{2,1,0:T(1,128)}), s32[64,1,2]{2,1,0:T(1,128)S(1)}, u32[]{:S(2)}, u32[]{:S(2)}) async-start(s32[64,1,2]{2,1,0:T(1,128)} %bitcast.6), calls=%async_computation.1 | async-start | bytes 65536 | tf_op jit(solution)/shard_map/all_to_all | solution.py:80
  33.7 4.8 %copy-start.6 = (bf16[1024,32]{0,1:T(8,128)(2,1)S(1)}, bf16[1024,32]{0,1:T(8,128)(2,1)}, u32[]{:S(2)}) copy-start(bf16[1024,32]{0,1:T(8,128)(2,1)} %param.15) | copy-start | bytes 196612
  33.7 9.0 %copy-start.12 = (f32[32]{0:T(128)S(1)}, f32[32]{0:T(128)}, u32[]{:S(2)}) copy-start(f32[32]{0:T(128)} %param.22) | copy-start | bytes 388
  33.7 9.1 %copy-start.11 = (s32[8,2]{0,1:T(2,128)S(1)}, s32[8,2]{0,1:T(2,128)}, u32[]{:S(2)}) copy-start(s32[8,2]{0,1:T(2,128)} %param.18) | copy-start | bytes 196
  33.8 9.3 %copy-start.2 = (bf16[1024,256]{1,0:T(8,128)(2,1)S(1)}, bf16[1024,256]{1,0:T(8,128)(2,1)}, u32[]{:S(2)}) copy-start(bf16[1024,256]{1,0:T(8,128)(2,1)} %param.17) | copy-start | bytes 1572868
  33.8 9.5 %copy-start.1 = (bf16[1024,384]{1,0:T(8,128)(2,1)S(1)}, bf16[1024,384]{1,0:T(8,128)(2,1)}, u32[]{:S(2)}) copy-start(bf16[1024,384]{1,0:T(8,128)(2,1)} %param.16) | copy-start | bytes 2359300
  33.8 9.7 %copy-start.10 = (bf16[1024,32]{0,1:T(8,128)(2,1)S(1)}, bf16[1024,32]{0,1:T(8,128)(2,1)}, u32[]{:S(2)}) copy-start(bf16[1024,32]{0,1:T(8,128)(2,1)} %param.23) | copy-start | bytes 196612
  33.8 30.6 %all-to-all-start.2 = ((bf16[64,2,128,32]{2,3,1,0:T(8,128)(2,1)}), bf16[64,2,128,32]{2,3,1,0:T(8,128)(2,1)S(1)}, u32[]{:S(2)}, u32[]{:S(2)}) async-start(bf16[64,2,128,32]{2,3,1,0:T(8,128)(2,1)} %broadcast_select_fusion), calls=%async_computation.2 | async-start | bytes 2097152 | tf_op jit(solution)/shard_map/all_to_all | solution.py:87
  38.6 36.5 %collective-permute-start = (bf16[128,32]{0,1:T(8,128)(2,1)S(1)}, bf16[128,32]{0,1:T(8,128)(2,1)S(1)}, u32[]{:S(2)}, u32[]{:S(2)}) collective-permute-start(bf16[128,32]{0,1:T(8,128)(2,1)S(1)} %get-tuple-element.51), channel_id=1, source_target_pairs={{0,8},{8,16},{16,24},{24,32},{32,40},{40,48},{48,56},{56,64},{64,7... | collective-permute-start | bytes 24584 | tf_op jit(solution)/shard_map/ppermute | solution.py:12
  41.4 33.7 %collective-permute-start.1 = (bf16[128,32]{0,1:T(8,128)(2,1)S(1)}, bf16[128,32]{0,1:T(8,128)(2,1)S(1)}, u32[]{:S(2)}, u32[]{:S(2)}) collective-permute-start(bf16[128,32]{0,1:T(8,128)(2,1)S(1)} %get-tuple-element.52), channel_id=1, source_target_pairs={{8,0},{16,8},{24,16},{32,24},{40,32},{48,40},{56,48},{64,56},{72,6... | collective-permute-start | bytes 24584 | tf_op jit(solution)/shard_map/ppermute | solution.py:15
  64.4 1.3 copy-start.5
  65.7 25.2 %all-to-all-start = ((bf16[8,2064,32]{1,2,0:T(8,128)(2,1)}), bf16[8,2064,32]{1,2,0:T(8,128)(2,1)S(1)}, u32[]{:S(2)}, u32[]{:S(2)}) async-start(bf16[8,2064,32]{1,2,0:T(8,128)(2,1)} %broadcast_in_dim.41), calls=%async_computation | async-start | bytes 2228224 | tf_op jit(solution)/shard_map/all_to_all | solution.py:45
  91.8 13.8 %all-to-all-start.3 = ((bf16[8,1024,32]{1,2,0:T(8,128)(2,1)}), bf16[8,1024,32]{1,2,0:T(8,128)(2,1)S(1)}, u32[]{:S(2)}, u32[]{:S(2)}) async-start(bf16[8,1024,32]{1,2,0:T(8,128)(2,1)} %broadcast_in_dim.76), calls=%async_computation.3 | async-start | bytes 1048576 | tf_op jit(solution)/shard_map/all_to_all | solution.py:101
  96.1 9.5 %copy-start.9 = (bf16[256,256]{1,0:T(8,128)(2,1)S(1)}, bf16[256,256]{1,0:T(8,128)(2,1)}, u32[]{:S(2)}) copy-start(bf16[256,256]{1,0:T(8,128)(2,1)} %param.21) | copy-start | bytes 393220
  105.6 1.2 copy-start.7
  108.4 1.2 copy-start.3
  113.9 34.6 %all-to-all-start.4 = ((bf16[64,2,128,34]{2,1,3,0:T(2,128)(2,1)}), bf16[64,2,128,34]{2,1,3,0:T(2,128)(2,1)S(1)}, u32[]{:S(2)}, u32[]{:S(2)}) async-start(bf16[64,2,128,34]{2,1,3,0:T(2,128)(2,1)} %copy.153), calls=%async_computation.4 | async-start | bytes 2228224 | tf_op jit(solution)/shard_map/all_to_all | solution.py:168
  120.2 39.8 %collective-permute-start.2 = (f32[128,32]{0,1:T(8,128)S(1)}, f32[128,32]{0,1:T(8,128)S(1)}, u32[]{:S(2)}, u32[]{:S(2)}) collective-permute-start(f32[128,32]{0,1:T(8,128)S(1)} %get-tuple-element.41), channel_id=1, source_target_pairs={{0,8},{8,16},{16,24},{24,32},{32,40},{40,48},{48,56},{56,64},{64,7... | collective-permute-start | bytes 49160 | tf_op jit(solution)/shard_map/ppermute | solution.py:23
  123.1 36.9 %collective-permute-start.3 = (f32[128,32]{0,1:T(8,128)S(1)}, f32[128,32]{0,1:T(8,128)S(1)}, u32[]{:S(2)}, u32[]{:S(2)}) collective-permute-start(f32[128,32]{0,1:T(8,128)S(1)} %get-tuple-element.40), channel_id=1, source_target_pairs={{8,0},{16,8},{24,16},{32,24},{40,32},{48,40},{56,48},{64,56},{72,6... | collective-permute-start | bytes 49160 | tf_op jit(solution)/shard_map/ppermute | solution.py:23
  149.5 19.0 %all-to-all-start.5 = ((f32[64,1,256]{2,1,0:T(1,128)}), f32[64,1,256]{2,1,0:T(1,128)S(1)}, u32[]{:S(2)}, u32[]{:S(2)}) async-start(f32[64,1,256]{2,1,0:T(1,128)} %broadcast_in_dim.78), calls=%async_computation.5 | async-start | bytes 131072 | tf_op jit(solution)/shard_map/all_to_all | solution.py:172
  157.4 2.4 %copy-start.4 = (bf16[1024,256]{0,1:T(8,128)(2,1)S(1)}, bf16[1024,256]{0,1:T(8,128)(2,1)}, u32[]{:S(2)}) copy-start(bf16[1024,256]{0,1:T(8,128)(2,1)} %copy-done.3) | copy-start | bytes 1572868
  160.0 9.8 %copy-start.8 = (f32[1024,32]{0,1:T(8,128)}, f32[1024,32]{0,1:T(8,128)S(1)}, u32[]{:S(2)}) copy-start(f32[1024,32]{0,1:T(8,128)S(1)} %fusion.30) | copy-start | bytes 393220

commit v16 on v15

--- a/solution.py
+++ b/solution.py
@@ -42,18 +42,6 @@
     )
     packed = jnp.concatenate([node_feats, cotangent, bias_parts], axis=0)
     feat_count = lax.axis_size("feat")
-    gathered = lax.all_to_all(
-        jnp.broadcast_to(packed[None], (feat_count,) + packed.shape),
-        "feat",
-        split_axis=0,
-        concat_axis=0,
-        tiled=True,
-    )
-    feats_each = gathered[:, :rows_dev]
-    cotangent_all = gathered[:, rows_dev : 2 * rows_dev].transpose(1, 0, 2).reshape(rows_dev, -1)
-    bias_rows = gathered[:, 2 * rows_dev : 2 * rows_dev + 3].astype(jnp.float32)
-    bias_rows = bias_rows.transpose(1, 0, 2).reshape(3, -1)
-    bias_all = (bias_rows[0] + bias_rows[1]) + bias_rows[2]
     padded = extended(node_feats, (("rows", 0),), tile_size)
     windows = jnp.concatenate(
         [
@@ -98,13 +86,22 @@
     )
     rows_self = lax.dynamic_slice_in_dim(w_self, col_start, col_count, 0)
     rows_neigh = lax.dynamic_slice_in_dim(w_neigh, col_start, col_count, 0)
-    neighbours_each = lax.all_to_all(
-        jnp.broadcast_to(neighbours[None], (feat_count, rows_dev, col_count)),
+    joined = jnp.concatenate([neighbours, packed], axis=0)
+    gathered = lax.all_to_all(
+        jnp.broadcast_to(joined[None], (feat_count,) + joined.shape),
         "feat",
         split_axis=0,
         concat_axis=0,
         tiled=True,
     )
+    neighbours_each = gathered[:, :rows_dev]
+    feats_each = gathered[:, rows_dev : 2 * rows_dev]
+    cotangent_all = (
+        gathered[:, 2 * rows_dev : 3 * rows_dev].transpose(1, 0, 2).reshape(rows_dev, -1)
+    )
+    bias_rows = gathered[:, 3 * rows_dev : 3 * rows_dev + 3].astype(jnp.float32)
+    bias_rows = bias_rows.transpose(1, 0, 2).reshape(3, -1)
+    bias_all = (bias_rows[0] + bias_rows[1]) + bias_rows[2]
     preact_all = (
         jnp.einsum(
             "frc,fcd->rd",

time: 171 us -> 167 us (0.977)
  starting transfers between devices: 57.7 us -> 53.7 us
  local copies, waits for them, and re-layouts: 16.5 us -> 13.4 us
  matrix products: 5.14 us -> 7.23 us
    all_to_all x1, waiting for transfers between devices: 20.8 us -> 3.83 us  [on_device(): lax.all_to_all(outgoing, 'rows', split_axis=0, concat_axis=0, tiled=True)]
    ppermute x1, waiting for transfers between devices: 0.01 us -> 12.3 us  [extended(): lax.ppermute(lax.slice_in_dim(block, block.shape[dim] - width, None, axis...]
    ppermute x1, waiting for transfers between devices: 0.01 us -> 4.31 us  [extended(): lax.ppermute(lax.slice_in_dim(block, 0, width, axis=dim), axis, backward)]
    all_to_all x2 -> x1, starting transfers between devices: 13.7 us -> 9.42 us  [on_device(): lax.all_to_all(jnp.broadcast_to(joined[None], (feat_count,) + joined.shap...]
    all_to_all x2 -> x1, waiting for transfers between devices: 21.2 us -> 21.5 us  [on_device(): lax.all_to_all(jnp.broadcast_to(joined[None], (feat_count,) + joined.shap...]
  transfers between devices with their start and end apart: 10 -> 9, of which waited for: 6 -> 7; matrix products, arithmetic and copies ran while one was open for 7% -> 5% of each run, Pallas kernels for 0% -> 0%
where the time goes in v16:
time: 167 us; the launch traced here: 166 us
  waiting for transfers between devices  82.8 us (50%)
  starting transfers between devices  53.7 us (32%)
  local copies, waits for them, and re-layouts  13.4 us (8%)
  other arithmetic  7.34 us (4%)
  matrix products  7.23 us (4%)
    all_to_all x1, waiting for transfers between devices, on_device(): lax.all_to_all(payload, 'rows', split_axis=0, concat_axis=0, tiled=True)  22.5 us
    all_to_all x1, waiting for transfers between devices, on_device(): lax.all_to_all(jnp.broadcast_to(joined[None], (feat_count,) + joined.shap...  21.5 us
    all_to_all x1, starting transfers between devices, on_device(): lax.all_to_all(request, 'rows', split_axis=0, concat_axis=0, tiled=True)  17.1 us
    ppermute x1, waiting for transfers between devices, extended(): lax.ppermute(lax.slice_in_dim(block, block.shape[dim] - width, None, axis...  12.3 us
    all_to_all x1, waiting for transfers between devices, on_device(): lax.all_to_all(request, 'rows', split_axis=0, concat_axis=0, tiled=True)  9.91 us
    all_to_all x1, starting transfers between devices, on_device(): lax.all_to_all(jnp.broadcast_to(joined[None], (feat_count,) + joined.shap...  9.42 us
    all_to_all x1, waiting for transfers between devices, on_device(): lax.all_to_all(jnp.broadcast_to(mine, partials.shape), 'rows', split_axis...  8.45 us
    all_to_all x1, starting transfers between devices, on_device(): lax.all_to_all(jnp.broadcast_to(mine, partials.shape), 'rows', split_axis...  7.9 us
  transfers between devices with their start and end apart: 9, of which 7 were waited for; matrix products, arithmetic and copies ran while one was open for 5% of the time, Pallas kernels for 0%

profile of v16, /device:TPU:1, one launch (start us, length us, event | category | flops | bytes accessed | tf_op | source)
XLA Modules:
  0.0 165.6 jit_solution(3958264930735997501)
XLA Ops:
  3.4 17.1 %all-to-all-start = ((s32[64,1,2]{2,1,0:T(1,128)}), s32[64,1,2]{2,1,0:T(1,128)S(1)}, u32[]{:S(2)}, u32[]{:S(2)}) async-start(s32[64,1,2]{2,1,0:T(1,128)} %bitcast.1), calls=%async_computation | async-start | bytes 65536 | tf_op jit(solution)/shard_map/all_to_all | solution.py:68
  21.4 9.9 %all-to-all-done = s32[64,1,2]{2,1,0:T(1,128)S(1)} async-done(((s32[64,1,2]{2,1,0:T(1,128)}), s32[64,1,2]{2,1,0:T(1,128)S(1)}, u32[]{:S(2)}, u32[]{:S(2)}) %all-to-all-start) | async-done | bytes 544 | tf_op jit(solution)/shard_map/all_to_all | solution.py:68
  32.6 1.2 broadcast_select_fusion
  33.8 4.8 %all-to-all-start.1 = ((bf16[64,2,128,32]{2,3,1,0:T(8,128)(2,1)}), bf16[64,2,128,32]{2,3,1,0:T(8,128)(2,1)S(1)}, u32[]{:S(2)}, u32[]{:S(2)}) async-start(bf16[64,2,128,32]{2,3,1,0:T(8,128)(2,1)} %broadcast_select_fusion), calls=%async_computation.1 | async-start | bytes 2097152 | tf_op jit(solution)/shard_map/all_to_all | solution.py:75
  38.6 2.8 %collective-permute-start = (bf16[128,32]{0,1:T(8,128)(2,1)S(1)}, bf16[128,32]{0,1:T(8,128)(2,1)S(1)}, u32[]{:S(2)}, u32[]{:S(2)}) collective-permute-start(bf16[128,32]{0,1:T(8,128)(2,1)S(1)} %get-tuple-element.51), channel_id=1, source_target_pairs={{0,8},{8,16},{16,24},{24,32},{32,40},{40,48},{48,56},{56,64},{64,7... | collective-permute-start | bytes 24584 | tf_op jit(solution)/shard_map/ppermute | solution.py:12
  41.4 1.3 collective-permute-start.1
  43.5 12.3 %collective-permute-done = bf16[128,32]{0,1:T(8,128)(2,1)S(1)} collective-permute-done((bf16[128,32]{0,1:T(8,128)(2,1)S(1)}, bf16[128,32]{0,1:T(8,128)(2,1)S(1)}, u32[]{:S(2)}, u32[]{:S(2)}) %collective-permute-start) | collective-permute-done | bytes 8224 | tf_op jit(solution)/shard_map/ppermute | solution.py:12
  55.8 4.3 %collective-permute-done.1 = bf16[128,32]{0,1:T(8,128)(2,1)S(1)} collective-permute-done((bf16[128,32]{0,1:T(8,128)(2,1)S(1)}, bf16[128,32]{0,1:T(8,128)(2,1)S(1)}, u32[]{:S(2)}, u32[]{:S(2)}) %collective-permute-start.1) | collective-permute-done | bytes 8224 | tf_op jit(solution)/shard_map/ppermute | solution.py:15
  60.5 3.8 %all-to-all-done.1 = bf16[64,2,128,32]{2,3,1,0:T(8,128)(2,1)S(1)} async-done(((bf16[64,2,128,32]{2,3,1,0:T(8,128)(2,1)}), bf16[64,2,128,32]{2,3,1,0:T(8,128)(2,1)S(1)}, u32[]{:S(2)}, u32[]{:S(2)}) %all-to-all-start.1) | async-done | bytes 1048608 | tf_op jit(solution)/shard_map/all_to_all | solution.py:75
  65.4 1.3 broadcast_in_dim.69
  66.6 9.4 %all-to-all-start.2 = ((bf16[8,3088,32]{1,2,0:T(8,128)(2,1)}), bf16[8,3088,32]{1,2,0:T(8,128)(2,1)}, u32[]{:S(2)}, u32[]{:S(2)}) async-start(bf16[8,3088,32]{1,2,0:T(8,128)(2,1)} %broadcast_in_dim.69), calls=%async_computation.2 | async-start | bytes 3276800 | tf_op jit(solution)/shard_map/all_to_all | solution.py:90
  76.1 21.5 %all-to-all-done.2 = bf16[8,3088,32]{1,2,0:T(8,128)(2,1)} async-done(((bf16[8,3088,32]{1,2,0:T(8,128)(2,1)}), bf16[8,3088,32]{1,2,0:T(8,128)(2,1)}, u32[]{:S(2)}, u32[]{:S(2)}) %all-to-all-start.2) | async-done | bytes 1581088 | tf_op jit(solution)/shard_map/all_to_all | solution.py:90
  98.7 1.2 slice_convert_fusion
  99.9 1.4 convolution_bitcast_fusion
  101.3 2.6 %fusion.9 = (bf16[1024,256]{0,1:T(8,128)(2,1)S(1)}, f32[1024,256]{0,1:T(8,128)}) fusion(f32[8,1024,32]{1,2,0:T(8,128)S(1)} %slice_convert_fusion, f32[256]{0:T(256)S(1)} %add.159, f32[1024,256]{0,1:T(8,128)S(1)} %convolution_bitcast_fusion, bf16[8,32,256]{2,1,0:T(8,128)(2,1)S(1)} %bitcast.130, bf16[8,3088,32]{1,2,0:T(8,128)(2,1)} %all-to-all-done.2), kind=kOutput, calls=%fused_computation.24 | convolution fusion | flops 137101312 | bytes 4326400 | tf_op jit(solution)/shard_map/frc,fcd->rd/dot_general | solution.py:106
  107.5 1.9 %copy.159 = bf16[64,2,128,34]{2,1,3,0:T(2,128)(2,1)} copy(bf16[64,2,128,34]{2,3,1,0:T(8,128)(2,1)S(1)} %pad_maximum_fusion) | data formatting | bytes 2228224 | tf_op jit(solution)/shard_map/concatenate | solution.py:158
  109.4 6.1 %all-to-all-start.3 = ((bf16[64,2,128,34]{2,1,3,0:T(2,128)(2,1)}), bf16[64,2,128,34]{2,1,3,0:T(2,128)(2,1)S(1)}, u32[]{:S(2)}, u32[]{:S(2)}) async-start(bf16[64,2,128,34]{2,1,3,0:T(2,128)(2,1)} %copy.159), calls=%async_computation.3 | async-start | bytes 2228224 | tf_op jit(solution)/shard_map/all_to_all | solution.py:165
  115.9 2.9 %collective-permute-start.2 = (f32[128,32]{0,1:T(8,128)S(1)}, f32[128,32]{0,1:T(8,128)S(1)}, u32[]{:S(2)}, u32[]{:S(2)}) collective-permute-start(f32[128,32]{0,1:T(8,128)S(1)} %get-tuple-element.41), channel_id=1, source_target_pairs={{0,8},{8,16},{16,24},{24,32},{32,40},{40,48},{48,56},{56,64},{64,7... | collective-permute-start | bytes 49160 | tf_op jit(solution)/shard_map/ppermute | solution.py:23
  118.9 1.3 collective-permute-start.3
  120.2 1.6 multiply_convert_fusion
  121.8 22.5 %all-to-all-done.3 = bf16[64,2,128,34]{2,1,3,0:T(2,128)(2,1)S(1)} async-done(((bf16[64,2,128,34]{2,1,3,0:T(2,128)(2,1)}), bf16[64,2,128,34]{2,1,3,0:T(2,128)(2,1)S(1)}, u32[]{:S(2)}, u32[]{:S(2)}) %all-to-all-start.3) | async-done | bytes 1114144 | tf_op jit(solution)/shard_map/all_to_all | solution.py:165
  145.3 7.9 %all-to-all-start.4 = ((f32[64,1,256]{2,1,0:T(1,128)}), f32[64,1,256]{2,1,0:T(1,128)S(1)}, u32[]{:S(2)}, u32[]{:S(2)}) async-start(f32[64,1,256]{2,1,0:T(1,128)} %broadcast_in_dim.71), calls=%async_computation.4 | async-start | bytes 131072 | tf_op jit(solution)/shard_map/all_to_all | solution.py:169
  154.3 1.2 fusion.6
  155.8 8.5 %all-to-all-done.4 = f32[64,1,256]{2,1,0:T(1,128)S(1)} async-done(((f32[64,1,256]{2,1,0:T(1,128)}), f32[64,1,256]{2,1,0:T(1,128)S(1)}, u32[]{:S(2)}, u32[]{:S(2)}) %all-to-all-start.4) | async-done | bytes 65568 | tf_op jit(solution)/shard_map/all_to_all | solution.py:169
  (104 shorter events, 15.7 us)
Async XLA Ops:
  0.6 100.7 %copy-start = (bf16[256,256]{1,0:T(8,128)(2,1)S(1)}, bf16[256,256]{1,0:T(8,128)(2,1)}, u32[]{:S(2)}) copy-start(bf16[256,256]{1,0:T(8,128)(2,1)} %param.20) | copy-start | bytes 393220
  3.4 27.9 %all-to-all-start = ((s32[64,1,2]{2,1,0:T(1,128)}), s32[64,1,2]{2,1,0:T(1,128)S(1)}, u32[]{:S(2)}, u32[]{:S(2)}) async-start(s32[64,1,2]{2,1,0:T(1,128)} %bitcast.1), calls=%async_computation | async-start | bytes 65536 | tf_op jit(solution)/shard_map/all_to_all | solution.py:68
  32.6 6.0 %copy-start.5 = (bf16[1024,32]{0,1:T(8,128)(2,1)S(1)}, bf16[1024,32]{0,1:T(8,128)(2,1)}, u32[]{:S(2)}) copy-start(bf16[1024,32]{0,1:T(8,128)(2,1)} %param.15) | copy-start | bytes 196612
  32.6 10.1 %copy-start.9 = (s32[8,2]{0,1:T(2,128)S(1)}, s32[8,2]{0,1:T(2,128)}, u32[]{:S(2)}) copy-start(s32[8,2]{0,1:T(2,128)} %param.18) | copy-start | bytes 196
  32.6 10.3 %copy-start.2 = (bf16[1024,256]{1,0:T(8,128)(2,1)S(1)}, bf16[1024,256]{1,0:T(8,128)(2,1)}, u32[]{:S(2)}) copy-start(bf16[1024,256]{1,0:T(8,128)(2,1)} %param.17) | copy-start | bytes 1572868
  33.8 9.4 %copy-start.1 = (bf16[1024,384]{1,0:T(8,128)(2,1)S(1)}, bf16[1024,384]{1,0:T(8,128)(2,1)}, u32[]{:S(2)}) copy-start(bf16[1024,384]{1,0:T(8,128)(2,1)} %param.16) | copy-start | bytes 2359300
  33.8 9.6 %copy-start.10 = (f32[32]{0:T(128)S(1)}, f32[32]{0:T(128)}, u32[]{:S(2)}) copy-start(f32[32]{0:T(128)} %param.22) | copy-start | bytes 388
  33.8 30.6 %all-to-all-start.1 = ((bf16[64,2,128,32]{2,3,1,0:T(8,128)(2,1)}), bf16[64,2,128,32]{2,3,1,0:T(8,128)(2,1)S(1)}, u32[]{:S(2)}, u32[]{:S(2)}) async-start(bf16[64,2,128,32]{2,3,1,0:T(8,128)(2,1)} %broadcast_select_fusion), calls=%async_computation.1 | async-start | bytes 2097152 | tf_op jit(solution)/shard_map/all_to_all | solution.py:75
  38.6 17.2 %collective-permute-start = (bf16[128,32]{0,1:T(8,128)(2,1)S(1)}, bf16[128,32]{0,1:T(8,128)(2,1)S(1)}, u32[]{:S(2)}, u32[]{:S(2)}) collective-permute-start(bf16[128,32]{0,1:T(8,128)(2,1)S(1)} %get-tuple-element.51), channel_id=1, source_target_pairs={{0,8},{8,16},{16,24},{24,32},{32,40},{40,48},{48,56},{56,64},{64,7... | collective-permute-start | bytes 24584 | tf_op jit(solution)/shard_map/ppermute | solution.py:12
  41.4 18.7 %collective-permute-start.1 = (bf16[128,32]{0,1:T(8,128)(2,1)S(1)}, bf16[128,32]{0,1:T(8,128)(2,1)S(1)}, u32[]{:S(2)}, u32[]{:S(2)}) collective-permute-start(bf16[128,32]{0,1:T(8,128)(2,1)S(1)} %get-tuple-element.52), channel_id=1, source_target_pairs={{8,0},{16,8},{24,16},{32,24},{40,32},{48,40},{56,48},{64,56},{72,6... | collective-permute-start | bytes 24584 | tf_op jit(solution)/shard_map/ppermute | solution.py:15
  60.1 5.2 %copy-start.8 = (bf16[1024,32]{0,1:T(8,128)(2,1)S(1)}, bf16[1024,32]{0,1:T(8,128)(2,1)}, u32[]{:S(2)}) copy-start(bf16[1024,32]{0,1:T(8,128)(2,1)} %param.23) | copy-start | bytes 196612
  66.6 30.9 %all-to-all-start.2 = ((bf16[8,3088,32]{1,2,0:T(8,128)(2,1)}), bf16[8,3088,32]{1,2,0:T(8,128)(2,1)}, u32[]{:S(2)}, u32[]{:S(2)}) async-start(bf16[8,3088,32]{1,2,0:T(8,128)(2,1)} %broadcast_in_dim.69), calls=%async_computation.2 | async-start | bytes 3276800 | tf_op jit(solution)/shard_map/all_to_all | solution.py:90
  76.1 23.8 %copy-start.7 = (bf16[256,256]{1,0:T(8,128)(2,1)S(1)}, bf16[256,256]{1,0:T(8,128)(2,1)}, u32[]{:S(2)}) copy-start(bf16[256,256]{1,0:T(8,128)(2,1)} %param.21) | copy-start | bytes 393220
  103.9 1.4 copy-start.3
  109.4 34.8 %all-to-all-start.3 = ((bf16[64,2,128,34]{2,1,3,0:T(2,128)(2,1)}), bf16[64,2,128,34]{2,1,3,0:T(2,128)(2,1)S(1)}, u32[]{:S(2)}, u32[]{:S(2)}) async-start(bf16[64,2,128,34]{2,1,3,0:T(2,128)(2,1)} %copy.159), calls=%async_computation.3 | async-start | bytes 2228224 | tf_op jit(solution)/shard_map/all_to_all | solution.py:165
  115.9 39.8 %collective-permute-start.2 = (f32[128,32]{0,1:T(8,128)S(1)}, f32[128,32]{0,1:T(8,128)S(1)}, u32[]{:S(2)}, u32[]{:S(2)}) collective-permute-start(f32[128,32]{0,1:T(8,128)S(1)} %get-tuple-element.41), channel_id=1, source_target_pairs={{0,8},{8,16},{16,24},{24,32},{32,40},{40,48},{48,56},{56,64},{64,7... | collective-permute-start | bytes 49160 | tf_op jit(solution)/shard_map/ppermute | solution.py:23
  118.9 36.9 %collective-permute-start.3 = (f32[128,32]{0,1:T(8,128)S(1)}, f32[128,32]{0,1:T(8,128)S(1)}, u32[]{:S(2)}, u32[]{:S(2)}) collective-permute-start(f32[128,32]{0,1:T(8,128)S(1)} %get-tuple-element.40), channel_id=1, source_target_pairs={{8,0},{16,8},{24,16},{32,24},{40,32},{48,40},{56,48},{64,56},{72,6... | collective-permute-start | bytes 49160 | tf_op jit(solution)/shard_map/ppermute | solution.py:23
  145.3 19.0 %all-to-all-start.4 = ((f32[64,1,256]{2,1,0:T(1,128)}), f32[64,1,256]{2,1,0:T(1,128)S(1)}, u32[]{:S(2)}, u32[]{:S(2)}) async-start(f32[64,1,256]{2,1,0:T(1,128)} %broadcast_in_dim.71), calls=%async_computation.4 | async-start | bytes 131072 | tf_op jit(solution)/shard_map/all_to_all | solution.py:169
  153.2 2.4 %copy-start.4 = (bf16[1024,256]{0,1:T(8,128)(2,1)S(1)}, bf16[1024,256]{0,1:T(8,128)(2,1)}, u32[]{:S(2)}) copy-start(bf16[1024,256]{0,1:T(8,128)(2,1)} %copy-done.3) | copy-start | bytes 1572868
  155.8 9.8 %copy-start.6 = (f32[1024,32]{0,1:T(8,128)}, f32[1024,32]{0,1:T(8,128)S(1)}, u32[]{:S(2)}) copy-start(f32[1024,32]{0,1:T(8,128)S(1)} %fusion.31) | copy-start | bytes 393220

commit v17 on v16

--- a/solution.py
+++ b/solution.py
@@ -96,38 +96,50 @@
     )
     neighbours_each = gathered[:, :rows_dev]
     feats_each = gathered[:, rows_dev : 2 * rows_dev]
-    cotangent_all = (
-        gathered[:, 2 * rows_dev : 3 * rows_dev].transpose(1, 0, 2).reshape(rows_dev, -1)
-    )
+    cotangent_each = gathered[:, 2 * rows_dev : 3 * rows_dev]
     bias_rows = gathered[:, 3 * rows_dev : 3 * rows_dev + 3].astype(jnp.float32)
-    bias_rows = bias_rows.transpose(1, 0, 2).reshape(3, -1)
-    bias_all = (bias_rows[0] + bias_rows[1]) + bias_rows[2]
-    preact_all = (
+    bias_each = (bias_rows[:, 0:1] + bias_rows[:, 1:2]) + bias_rows[:, 2:3]
+    blocked = (feat_count, col_count, feat_count, col_count)
+    preact_each = (
         jnp.einsum(
-            "frc,fcd->rd",
+            "frc,fcgd->grd",
             feats_each,
-            w_self.reshape(feat_count, col_count, -1),
+            w_self.reshape(blocked),
             preferred_element_type=jnp.float32,
         )
         + jnp.einsum(
-            "frc,fcd->rd",
+            "frc,fcgd->grd",
             neighbours_each,
-            w_neigh.reshape(feat_count, col_count, -1),
+            w_neigh.reshape(blocked),
             preferred_element_type=jnp.float32,
         )
-        + bias_all
-    )
-    preact = lax.dynamic_slice_in_dim(preact_all, col_start, col_count, 1)
+        + bias_each
+    )
+    preact = lax.dynamic_index_in_dim(preact_each, lax.axis_index("feat"), 0, keepdims=False)
     layer_out = jax.nn.silu(preact).astype(jnp.bfloat16)
-    sigmoid_z = jax.nn.sigmoid(preact_all)
-    full_grad = (
-        cotangent_all.astype(jnp.float32) * sigmoid_z * (1.0 + preact_all * (1.0 - sigmoid_z))
+    sigmoid_z = jax.nn.sigmoid(preact_each)
+    grad_each = (
+        cotangent_each.astype(jnp.float32) * sigmoid_z * (1.0 + preact_each * (1.0 - sigmoid_z))
     ).astype(jnp.bfloat16)
     grad_scale = float(rows_dev * peer_count) ** (-0.5)
-    part_self = jnp.einsum("rc,rf->cf", node_feats, full_grad, preferred_element_type=jnp.float32)
-    part_neigh = jnp.einsum("rc,rf->cf", neighbours, full_grad, preferred_element_type=jnp.float32)
-    dense_grad = jnp.einsum("rf,cf->rc", full_grad, rows_self, preferred_element_type=jnp.float32)
-    grad_agg = jnp.einsum("rf,cf->rc", full_grad, rows_neigh, preferred_element_type=jnp.float32)
+    part_self = jnp.einsum(
+        "rc,grd->cgd", node_feats, grad_each, preferred_element_type=jnp.float32
+    ).reshape(col_count, -1)
+    part_neigh = jnp.einsum(
+        "rc,grd->cgd", neighbours, grad_each, preferred_element_type=jnp.float32
+    ).reshape(col_count, -1)
+    dense_grad = jnp.einsum(
+        "grd,cgd->rc",
+        grad_each,
+        rows_self.reshape(col_count, feat_count, col_count),
+        preferred_element_type=jnp.float32,
+    )
+    grad_agg = jnp.einsum(
+        "grd,cgd->rc",
+        grad_each,
+        rows_neigh.reshape(col_count, feat_count, col_count),
+        preferred_element_type=jnp.float32,
+    )
     grad_neighbours = (grad_agg / degree[:, None]).astype(jnp.bfloat16)
     grad_blocks = grad_neighbours.reshape(blocks, tile_size, col_count)
     grad_windows = jnp.einsum(

time: 167 us -> 165 us (0.988)
  local copies, waits for them, and re-layouts: 13.4 us -> 20.1 us
  waiting for transfers between devices: 82.8 us -> 76.5 us
  other arithmetic: 7.34 us -> 5.3 us
    all_to_all x1, waiting for transfers between devices: 21.5 us -> 16.7 us  [on_device(): lax.all_to_all(jnp.broadcast_to(joined[None], (feat_count,) + joined.shap...]
    reshape x0 -> x4, local copies, waits for them, and re-layouts: none -> 4.08 us  [the longest x1 2.03 us: on_device(): w_neigh.reshape(blocked)]
  transfers between devices with their start and end apart: 9 -> 9, of which waited for: 7 -> 7; matrix products, arithmetic and copies ran while one was open for 5% -> 8% of each run, Pallas kernels for 0% -> 0%
where the time goes in v17:
time: 165 us; the launch traced here: 163 us
  waiting for transfers between devices  76.5 us (46%)
  starting transfers between devices  53.8 us (33%)
  local copies, waits for them, and re-layouts  20.1 us (12%)
  matrix products  6.31 us (4%)
  other arithmetic  5.3 us (3%)
    all_to_all x1, waiting for transfers between devices, on_device(): lax.all_to_all(payload, 'rows', split_axis=0, concat_axis=0, tiled=True)  21.6 us
    all_to_all x1, starting transfers between devices, on_device(): lax.all_to_all(request, 'rows', split_axis=0, concat_axis=0, tiled=True)  17.1 us
    all_to_all x1, waiting for transfers between devices, on_device(): lax.all_to_all(jnp.broadcast_to(joined[None], (feat_count,) + joined.shap...  16.7 us
    ppermute x1, waiting for transfers between devices, extended(): lax.ppermute(lax.slice_in_dim(block, block.shape[dim] - width, None, axis...  11.7 us
    all_to_all x1, waiting for transfers between devices, on_device(): lax.all_to_all(request, 'rows', split_axis=0, concat_axis=0, tiled=True)  9.91 us
    all_to_all x1, starting transfers between devices, on_device(): lax.all_to_all(jnp.broadcast_to(joined[None], (feat_count,) + joined.shap...  9.42 us
    all_to_all x1, waiting for transfers between devices, on_device(): lax.all_to_all(jnp.broadcast_to(mine, partials.shape), 'rows', split_axis...  8.4 us
    all_to_all x1, starting transfers between devices, on_device(): lax.all_to_all(jnp.broadcast_to(mine, partials.shape), 'rows', split_axis...  7.9 us
  transfers between devices with their start and end apart: 9, of which 7 were waited for; matrix products, arithmetic and copies ran while one was open for 8% of the time, Pallas kernels for 0%

profile of v17, /device:TPU:1, one launch (start us, length us, event | category | flops | bytes accessed | tf_op | source)
XLA Modules:
  0.0 163.3 jit_solution(9897260677563993518)
XLA Ops:
  3.4 17.1 %all-to-all-start = ((s32[64,1,2]{2,1,0:T(1,128)}), s32[64,1,2]{2,1,0:T(1,128)S(1)}, u32[]{:S(2)}, u32[]{:S(2)}) async-start(s32[64,1,2]{2,1,0:T(1,128)} %bitcast.3), calls=%async_computation | async-start | bytes 65536 | tf_op jit(solution)/shard_map/all_to_all | solution.py:68
  21.4 9.9 %all-to-all-done = s32[64,1,2]{2,1,0:T(1,128)S(1)} async-done(((s32[64,1,2]{2,1,0:T(1,128)}), s32[64,1,2]{2,1,0:T(1,128)S(1)}, u32[]{:S(2)}, u32[]{:S(2)}) %all-to-all-start) | async-done | bytes 544 | tf_op jit(solution)/shard_map/all_to_all | solution.py:68
  32.6 1.2 broadcast_select_fusion
  33.7 4.8 %all-to-all-start.1 = ((bf16[64,2,128,32]{2,3,1,0:T(8,128)(2,1)}), bf16[64,2,128,32]{2,3,1,0:T(8,128)(2,1)S(1)}, u32[]{:S(2)}, u32[]{:S(2)}) async-start(bf16[64,2,128,32]{2,3,1,0:T(8,128)(2,1)} %broadcast_select_fusion), calls=%async_computation.1 | async-start | bytes 2097152 | tf_op jit(solution)/shard_map/all_to_all | solution.py:75
  38.6 2.8 %collective-permute-start = (bf16[128,32]{0,1:T(8,128)(2,1)S(1)}, bf16[128,32]{0,1:T(8,128)(2,1)S(1)}, u32[]{:S(2)}, u32[]{:S(2)}) collective-permute-start(bf16[128,32]{0,1:T(8,128)(2,1)S(1)} %get-tuple-element.51), channel_id=1, source_target_pairs={{0,8},{8,16},{16,24},{24,32},{32,40},{40,48},{48,56},{56,64},{64,7... | collective-permute-start | bytes 24584 | tf_op jit(solution)/shard_map/ppermute | solution.py:12
  41.4 1.3 collective-permute-start.1
  44.0 11.7 %collective-permute-done = bf16[128,32]{0,1:T(8,128)(2,1)S(1)} collective-permute-done((bf16[128,32]{0,1:T(8,128)(2,1)S(1)}, bf16[128,32]{0,1:T(8,128)(2,1)S(1)}, u32[]{:S(2)}, u32[]{:S(2)}) %collective-permute-start) | collective-permute-done | bytes 8224 | tf_op jit(solution)/shard_map/ppermute | solution.py:12
  55.7 4.3 %collective-permute-done.1 = bf16[128,32]{0,1:T(8,128)(2,1)S(1)} collective-permute-done((bf16[128,32]{0,1:T(8,128)(2,1)S(1)}, bf16[128,32]{0,1:T(8,128)(2,1)S(1)}, u32[]{:S(2)}, u32[]{:S(2)}) %collective-permute-start.1) | collective-permute-done | bytes 8224 | tf_op jit(solution)/shard_map/ppermute | solution.py:15
  60.5 3.8 %all-to-all-done.1 = bf16[64,2,128,32]{2,3,1,0:T(8,128)(2,1)S(1)} async-done(((bf16[64,2,128,32]{2,3,1,0:T(8,128)(2,1)}), bf16[64,2,128,32]{2,3,1,0:T(8,128)(2,1)S(1)}, u32[]{:S(2)}, u32[]{:S(2)}) %all-to-all-start.1) | async-done | bytes 1048608 | tf_op jit(solution)/shard_map/all_to_all | solution.py:75
  65.4 1.3 broadcast_in_dim.68
  66.7 9.4 %all-to-all-start.2 = ((bf16[8,3088,32]{1,2,0:T(8,128)(2,1)}), bf16[8,3088,32]{1,2,0:T(8,128)(2,1)S(1)}, u32[]{:S(2)}, u32[]{:S(2)}) async-start(bf16[8,3088,32]{1,2,0:T(8,128)(2,1)} %broadcast_in_dim.68), calls=%async_computation.2 | async-start | bytes 3276800 | tf_op jit(solution)/shard_map/all_to_all | solution.py:90
  76.1 1.2 reshape.314
  77.3 2.0 %reshape.315 = bf16[8,32,8,32]{3,2,1,0:T(8,128)(2,1)} reshape(bf16[256,256]{1,0:T(8,128)(2,1)} %param.21) | data formatting | bytes 262144 | tf_op jit(solution)/shard_map/reshape | solution.py:113
  80.8 16.7 %all-to-all-done.2 = bf16[8,3088,32]{1,2,0:T(8,128)(2,1)S(1)} async-done(((bf16[8,3088,32]{1,2,0:T(8,128)(2,1)}), bf16[8,3088,32]{1,2,0:T(8,128)(2,1)S(1)}, u32[]{:S(2)}, u32[]{:S(2)}) %all-to-all-start.2) | async-done | bytes 1581088 | tf_op jit(solution)/shard_map/all_to_all | solution.py:90
  98.6 1.7 %fusion.14 = (bf16[8,1024,32]{1,2,0:T(8,128)(2,1)S(1)}, f32[1024,8,32]{0,2,1:T(8,128)}) fusion(bf16[8,3088,32]{1,2,0:T(8,128)(2,1)S(1)} %all-to-all-done.2, f32[8,32]{1,0:T(8,128)S(1)} %fusion.27, f32[1024,8,32]{0,2,1:T(8,128)S(1)} %convolution_bitcast_fusion.1, bf16[8,32,8,32]{3,2,1,0:T(8,128)(2,1)S(1)} %copy-done.5), kind=kOutput, calls=%fused_computation.29 | convolution fusion | flops 137363456 | bytes 4198400 | tf_op jit(solution)/shard_map/frc,fcgd->grd/dot_general | solution.py:110
  105.1 1.9 %copy.192 = bf16[64,2,128,34]{2,1,3,0:T(2,128)(2,1)} copy(bf16[64,2,128,34]{2,3,1,0:T(8,128)(2,1)S(1)} %pad_maximum_fusion) | data formatting | bytes 2228224 | tf_op jit(solution)/shard_map/concatenate | solution.py:170
  107.0 6.2 %all-to-all-start.3 = ((bf16[64,2,128,34]{2,1,3,0:T(2,128)(2,1)}), bf16[64,2,128,34]{2,1,3,0:T(2,128)(2,1)S(1)}, u32[]{:S(2)}, u32[]{:S(2)}) async-start(bf16[64,2,128,34]{2,1,3,0:T(2,128)(2,1)} %copy.192), calls=%async_computation.3 | async-start | bytes 2228224 | tf_op jit(solution)/shard_map/all_to_all | solution.py:177
  114.5 2.9 %collective-permute-start.2 = (f32[128,32]{0,1:T(8,128)S(1)}, f32[128,32]{0,1:T(8,128)S(1)}, u32[]{:S(2)}, u32[]{:S(2)}) collective-permute-start(f32[128,32]{0,1:T(8,128)S(1)} %get-tuple-element.41), channel_id=1, source_target_pairs={{0,8},{8,16},{16,24},{24,32},{32,40},{40,48},{48,56},{56,64},{64,7... | collective-permute-start | bytes 49160 | tf_op jit(solution)/shard_map/ppermute | solution.py:23
  117.4 1.3 collective-permute-start.3
  118.7 1.6 fusion.33
  120.3 21.6 %all-to-all-done.3 = bf16[64,2,128,34]{2,1,3,0:T(2,128)(2,1)S(1)} async-done(((bf16[64,2,128,34]{2,1,3,0:T(2,128)(2,1)}), bf16[64,2,128,34]{2,1,3,0:T(2,128)(2,1)S(1)}, u32[]{:S(2)}, u32[]{:S(2)}) %all-to-all-start.3) | async-done | bytes 1114144 | tf_op jit(solution)/shard_map/all_to_all | solution.py:177
  143.0 7.9 %all-to-all-start.4 = ((f32[64,1,256]{2,1,0:T(1,128)}), f32[64,1,256]{2,1,0:T(1,128)S(1)}, u32[]{:S(2)}, u32[]{:S(2)}) async-start(f32[64,1,256]{2,1,0:T(1,128)} %broadcast_in_dim.70), calls=%async_computation.4 | async-start | bytes 131072 | tf_op jit(solution)/shard_map/all_to_all | solution.py:181
  152.1 1.2 fusion.7
  153.6 8.4 %all-to-all-done.4 = f32[64,1,256]{2,1,0:T(1,128)S(1)} async-done(((f32[64,1,256]{2,1,0:T(1,128)}), f32[64,1,256]{2,1,0:T(1,128)S(1)}, u32[]{:S(2)}, u32[]{:S(2)}) %all-to-all-start.4) | async-done | bytes 65568 | tf_op jit(solution)/shard_map/all_to_all | solution.py:181
  (123 shorter events, 19.6 us)
Async XLA Ops:
  3.4 27.9 %all-to-all-start = ((s32[64,1,2]{2,1,0:T(1,128)}), s32[64,1,2]{2,1,0:T(1,128)S(1)}, u32[]{:S(2)}, u32[]{:S(2)}) async-start(s32[64,1,2]{2,1,0:T(1,128)} %bitcast.3), calls=%async_computation | async-start | bytes 65536 | tf_op jit(solution)/shard_map/all_to_all | solution.py:68
  32.5 6.0 %copy-start.4 = (bf16[1024,32]{0,1:T(8,128)(2,1)S(1)}, bf16[1024,32]{0,1:T(8,128)(2,1)}, u32[]{:S(2)}) copy-start(bf16[1024,32]{0,1:T(8,128)(2,1)} %param.15) | copy-start | bytes 196612
  32.5 10.1 %copy-start.12 = (s32[8,2]{0,1:T(2,128)S(1)}, s32[8,2]{0,1:T(2,128)}, u32[]{:S(2)}) copy-start(s32[8,2]{0,1:T(2,128)} %param.18) | copy-start | bytes 196
  32.5 10.9 %copy-start.1 = (bf16[1024,256]{1,0:T(8,128)(2,1)S(1)}, bf16[1024,256]{1,0:T(8,128)(2,1)}, u32[]{:S(2)}) copy-start(bf16[1024,256]{1,0:T(8,128)(2,1)} %param.17) | copy-start | bytes 1572868
  33.7 9.9 %copy-start = (bf16[1024,384]{1,0:T(8,128)(2,1)S(1)}, bf16[1024,384]{1,0:T(8,128)(2,1)}, u32[]{:S(2)}) copy-start(bf16[1024,384]{1,0:T(8,128)(2,1)} %param.16) | copy-start | bytes 2359300
  33.7 10.1 %copy-start.17 = (f32[32]{0:T(128)S(1)}, f32[32]{0:T(128)}, u32[]{:S(2)}) copy-start(f32[32]{0:T(128)} %param.22) | copy-start | bytes 388
  33.7 30.6 %all-to-all-start.1 = ((bf16[64,2,128,32]{2,3,1,0:T(8,128)(2,1)}), bf16[64,2,128,32]{2,3,1,0:T(8,128)(2,1)S(1)}, u32[]{:S(2)}, u32[]{:S(2)}) async-start(bf16[64,2,128,32]{2,3,1,0:T(8,128)(2,1)} %broadcast_select_fusion), calls=%async_computation.1 | async-start | bytes 2097152 | tf_op jit(solution)/shard_map/all_to_all | solution.py:75
  38.6 17.2 %collective-permute-start = (bf16[128,32]{0,1:T(8,128)(2,1)S(1)}, bf16[128,32]{0,1:T(8,128)(2,1)S(1)}, u32[]{:S(2)}, u32[]{:S(2)}) collective-permute-start(bf16[128,32]{0,1:T(8,128)(2,1)S(1)} %get-tuple-element.51), channel_id=1, source_target_pairs={{0,8},{8,16},{16,24},{24,32},{32,40},{40,48},{48,56},{56,64},{64,7... | collective-permute-start | bytes 24584 | tf_op jit(solution)/shard_map/ppermute | solution.py:12
  41.4 18.7 %collective-permute-start.1 = (bf16[128,32]{0,1:T(8,128)(2,1)S(1)}, bf16[128,32]{0,1:T(8,128)(2,1)S(1)}, u32[]{:S(2)}, u32[]{:S(2)}) collective-permute-start(bf16[128,32]{0,1:T(8,128)(2,1)S(1)} %get-tuple-element.52), channel_id=1, source_target_pairs={{8,0},{16,8},{24,16},{32,24},{40,32},{48,40},{56,48},{64,56},{72,6... | collective-permute-start | bytes 24584 | tf_op jit(solution)/shard_map/ppermute | solution.py:15
  44.0 21.3 %copy-start.10 = (f32[1024]{0:T(1024)}, f32[1024]{0:T(1024)S(1)}, u32[]{:S(2)}) copy-start(f32[1024]{0:T(1024)S(1)} %add.156) | copy-start | bytes 12292
  60.1 5.2 %copy-start.8 = (bf16[1024,32]{0,1:T(8,128)(2,1)S(1)}, bf16[1024,32]{0,1:T(8,128)(2,1)}, u32[]{:S(2)}) copy-start(bf16[1024,32]{0,1:T(8,128)(2,1)} %param.23) | copy-start | bytes 196612
  65.3 1.4 copy-start.6
  66.7 30.8 %all-to-all-start.2 = ((bf16[8,3088,32]{1,2,0:T(8,128)(2,1)}), bf16[8,3088,32]{1,2,0:T(8,128)(2,1)S(1)}, u32[]{:S(2)}, u32[]{:S(2)}) async-start(bf16[8,3088,32]{1,2,0:T(8,128)(2,1)} %broadcast_in_dim.68), calls=%async_computation.2 | async-start | bytes 3276800 | tf_op jit(solution)/shard_map/all_to_all | solution.py:90
  97.5 1.0 copy-start.5
  98.6 2.0 %copy-start.11 = (f32[1024]{0:T(1024)S(1)}, f32[1024]{0:T(1024)}, u32[]{:S(2)}) copy-start(f32[1024]{0:T(1024)} %copy-done.10) | copy-start | bytes 12292
  100.2 2.4 %copy-start.2 = (bf16[8,1024,32]{1,2,0:T(8,128)(2,1)}, bf16[8,1024,32]{1,2,0:T(8,128)(2,1)S(1)}, u32[]{:S(2)}) copy-start(bf16[8,1024,32]{1,2,0:T(8,128)(2,1)S(1)} %get-tuple-element.56) | copy-start | bytes 1572868
  100.2 2.2 %copy-start.9 = (bf16[32,8,32]{2,1,0:T(8,128)(2,1)S(1)}, bf16[32,8,32]{2,1,0:T(8,128)(2,1)}, u32[]{:S(2)}) copy-start(bf16[32,8,32]{2,1,0:T(8,128)(2,1)} %reshape.317) | copy-start | bytes 49156
  107.0 7.1 %copy-start.14 = (s32[64,1,2]{0,2,1:T(2,128)S(1)}, s32[64,1,2]{0,2,1:T(2,128)}, u32[]{:S(2)}) copy-start(s32[64,1,2]{0,2,1:T(2,128)} %copy-done.13) | copy-start | bytes 1540
  107.0 34.9 %all-to-all-start.3 = ((bf16[64,2,128,34]{2,1,3,0:T(2,128)(2,1)}), bf16[64,2,128,34]{2,1,3,0:T(2,128)(2,1)S(1)}, u32[]{:S(2)}, u32[]{:S(2)}) async-start(bf16[64,2,128,34]{2,1,3,0:T(2,128)(2,1)} %copy.192), calls=%async_computation.3 | async-start | bytes 2228224 | tf_op jit(solution)/shard_map/all_to_all | solution.py:177
  114.5 39.0 %collective-permute-start.2 = (f32[128,32]{0,1:T(8,128)S(1)}, f32[128,32]{0,1:T(8,128)S(1)}, u32[]{:S(2)}, u32[]{:S(2)}) collective-permute-start(f32[128,32]{0,1:T(8,128)S(1)} %get-tuple-element.41), channel_id=1, source_target_pairs={{0,8},{8,16},{16,24},{24,32},{32,40},{40,48},{48,56},{56,64},{64,7... | collective-permute-start | bytes 49160 | tf_op jit(solution)/shard_map/ppermute | solution.py:23
  117.4 36.1 %collective-permute-start.3 = (f32[128,32]{0,1:T(8,128)S(1)}, f32[128,32]{0,1:T(8,128)S(1)}, u32[]{:S(2)}, u32[]{:S(2)}) collective-permute-start(f32[128,32]{0,1:T(8,128)S(1)} %get-tuple-element.40), channel_id=1, source_target_pairs={{8,0},{16,8},{24,16},{32,24},{40,32},{48,40},{56,48},{64,56},{72,6... | collective-permute-start | bytes 49160 | tf_op jit(solution)/shard_map/ppermute | solution.py:23
  143.0 19.0 %all-to-all-start.4 = ((f32[64,1,256]{2,1,0:T(1,128)}), f32[64,1,256]{2,1,0:T(1,128)S(1)}, u32[]{:S(2)}, u32[]{:S(2)}) async-start(f32[64,1,256]{2,1,0:T(1,128)} %broadcast_in_dim.70), calls=%async_computation.4 | async-start | bytes 131072 | tf_op jit(solution)/shard_map/all_to_all | solution.py:181
  150.9 2.4 %copy-start.3 = (bf16[8,1024,32]{1,2,0:T(8,128)(2,1)S(1)}, bf16[8,1024,32]{1,2,0:T(8,128)(2,1)}, u32[]{:S(2)}) copy-start(bf16[8,1024,32]{1,2,0:T(8,128)(2,1)} %copy-done.2) | copy-start | bytes 1572868
  153.6 9.7 %copy-start.7 = (f32[1024,32]{0,1:T(8,128)}, f32[1024,32]{0,1:T(8,128)S(1)}, u32[]{:S(2)}) copy-start(f32[1024,32]{0,1:T(8,128)S(1)} %fusion.48) | copy-start | bytes 393220
  (3 other events, 2.0 us)

commit v18 on v17

--- a/solution.py
+++ b/solution.py
@@ -42,6 +42,10 @@
     )
     packed = jnp.concatenate([node_feats, cotangent, bias_parts], axis=0)
     feat_count = lax.axis_size("feat")
+    shifted_packed = [
+        lax.ppermute(packed, "feat", [(i, (i + k) % feat_count) for i in range(feat_count)])
+        for k in range(1, feat_count)
+    ]
     padded = extended(node_feats, (("rows", 0),), tile_size)
     windows = jnp.concatenate(
         [
@@ -86,18 +90,18 @@
     )
     rows_self = lax.dynamic_slice_in_dim(w_self, col_start, col_count, 0)
     rows_neigh = lax.dynamic_slice_in_dim(w_neigh, col_start, col_count, 0)
-    joined = jnp.concatenate([neighbours, packed], axis=0)
-    gathered = lax.all_to_all(
-        jnp.broadcast_to(joined[None], (feat_count,) + joined.shape),
+    neighbours_each = lax.all_to_all(
+        jnp.broadcast_to(neighbours[None], (feat_count, rows_dev, col_count)),
         "feat",
         split_axis=0,
         concat_axis=0,
         tiled=True,
     )
-    neighbours_each = gathered[:, :rows_dev]
-    feats_each = gathered[:, rows_dev : 2 * rows_dev]
-    cotangent_each = gathered[:, 2 * rows_dev : 3 * rows_dev]
-    bias_rows = gathered[:, 3 * rows_dev : 3 * rows_dev + 3].astype(jnp.float32)
+    by_shift = jnp.stack([packed] + shifted_packed)
+    by_source = by_shift[(lax.axis_index("feat") - jnp.arange(feat_count)) % feat_count]
+    feats_each = by_source[:, :rows_dev]
+    cotangent_each = by_source[:, rows_dev : 2 * rows_dev]
+    bias_rows = by_source[:, 2 * rows_dev : 2 * rows_dev + 3].astype(jnp.float32)
     bias_each = (bias_rows[:, 0:1] + bias_rows[:, 1:2]) + bias_rows[:, 2:3]
     blocked = (feat_count, col_count, feat_count, col_count)
     preact_each = (

time: 165 us -> 178 us (1.079)
  waiting for transfers between devices: 76.5 us -> 52.4 us
  starting transfers between devices: 53.8 us -> 77.4 us
  other arithmetic: 5.3 us -> 11 us
  local copies, waits for them, and re-layouts: 20.1 us -> 24.6 us
  matrix products: 6.31 us -> 9.34 us
    ppermute x0 -> x7, starting transfers between devices: none -> 19.7 us  [on_device(): lax.ppermute(packed, 'feat', [(i, (i + k) % feat_count) for i in range(fe...]
    ppermute x1, waiting for transfers between devices: 11.7 us -> 0.01 us  [extended(): lax.ppermute(lax.slice_in_dim(block, block.shape[dim] - width, None, axis...]
    all_to_all x1, waiting for transfers between devices: 16.7 us -> 7.99 us  [on_device(): lax.all_to_all(jnp.broadcast_to(neighbours[None], (feat_count, rows_dev,...]
    all_to_all x1, waiting for transfers between devices: 9.91 us -> 3.61 us  [on_device(): lax.all_to_all(request, 'rows', split_axis=0, concat_axis=0, tiled=True)]
    ppermute x1, waiting for transfers between devices: 4.31 us -> 0.01 us  [extended(): lax.ppermute(lax.slice_in_dim(block, 0, width, axis=dim), axis, backward)]
    all_to_all x1, starting transfers between devices: 4.78 us -> 8.92 us  [on_device(): lax.all_to_all(outgoing, 'rows', split_axis=0, concat_axis=0, tiled=True)]
    ppermute x0 -> x7, waiting for transfers between devices: none -> 3.63 us  [on_device(): lax.ppermute(packed, 'feat', [(i, (i + k) % feat_count) for i in range(fe...]
    all_to_all x1, waiting for transfers between devices: 3.83 us -> 7.34 us  [on_device(): lax.all_to_all(outgoing, 'rows', split_axis=0, concat_axis=0, tiled=True)]
  transfers between devices with their start and end apart: 9 -> 16, of which waited for: 7 -> 7; matrix products, arithmetic and copies ran while one was open for 8% -> 15% of each run, Pallas kernels for 0% -> 0%
where the time goes in v18:
time: 178 us; the launch traced here: 176 us
  starting transfers between devices  77.4 us (43%)
  waiting for transfers between devices  52.4 us (29%)
  local copies, waits for them, and re-layouts  24.6 us (14%)
  other arithmetic  11 us (6%)
  matrix products  9.34 us (5%)
    all_to_all x1, waiting for transfers between devices, on_device(): lax.all_to_all(payload, 'rows', split_axis=0, concat_axis=0, tiled=True)  21.4 us
    ppermute x7, starting transfers between devices, on_device(): lax.ppermute(packed, 'feat', [(i, (i + k) % feat_count) for i in range(fe...  19.7 us
    all_to_all x1, starting transfers between devices, on_device(): lax.all_to_all(request, 'rows', split_axis=0, concat_axis=0, tiled=True)  17.8 us
    all_to_all x1, starting transfers between devices, on_device(): lax.all_to_all(outgoing, 'rows', split_axis=0, concat_axis=0, tiled=True)  8.92 us
    all_to_all x1, waiting for transfers between devices, on_device(): lax.all_to_all(jnp.broadcast_to(mine, partials.shape), 'rows', split_axis...  8.4 us
    all_to_all x1, waiting for transfers between devices, on_device(): lax.all_to_all(jnp.broadcast_to(neighbours[None], (feat_count, rows_dev,...  7.99 us
    all_to_all x1, starting transfers between devices, on_device(): lax.all_to_all(jnp.broadcast_to(mine, partials.shape), 'rows', split_axis...  7.89 us
    all_to_all x1, starting transfers between devices, on_device(): lax.all_to_all(jnp.broadcast_to(neighbours[None], (feat_count, rows_dev,...  7.52 us
  transfers between devices with their start and end apart: 16, of which 7 were waited for; matrix products, arithmetic and copies ran while one was open for 15% of the time, Pallas kernels for 0%

profile of v18, /device:TPU:1, one launch (start us, length us, event | category | flops | bytes accessed | tf_op | source)
XLA Modules:
  0.0 176.2 jit_solution(12659599988380415034)
XLA Ops:
  1.5 1.5 fusion.25
  3.1 2.6 %collective-permute-start = (bf16[2064,32]{0,1:T(8,128)(2,1)}, bf16[2064,32]{0,1:T(8,128)(2,1)}, u32[]{:S(2)}, u32[]{:S(2)}) collective-permute-start(bf16[2064,32]{0,1:T(8,128)(2,1)} %fusion.25), channel_id=1, source_target_pairs={{0,1},{1,2},{2,3},{3,4},{4,5},{5,6},{6,7},{7,0},{8,9},{9,10},{10,1... | collective-permute-start | bytes 396296 | tf_op jit(solution)/shard_map/ppermute | solution.py:46
  5.7 3.1 %collective-permute-start.1 = (bf16[2064,32]{0,1:T(8,128)(2,1)}, bf16[2064,32]{0,1:T(8,128)(2,1)}, u32[]{:S(2)}, u32[]{:S(2)}) collective-permute-start(bf16[2064,32]{0,1:T(8,128)(2,1)} %fusion.25), channel_id=1, source_target_pairs={{0,2},{1,3},{2,4},{3,5},{4,6},{5,7},{6,0},{7,1},{8,10},{9,11},{10,... | collective-permute-start | bytes 396296 | tf_op jit(solution)/shard_map/ppermute | solution.py:46
  8.8 3.4 %collective-permute-start.2 = (bf16[2064,32]{0,1:T(8,128)(2,1)}, bf16[2064,32]{0,1:T(8,128)(2,1)}, u32[]{:S(2)}, u32[]{:S(2)}) collective-permute-start(bf16[2064,32]{0,1:T(8,128)(2,1)} %fusion.25), channel_id=1, source_target_pairs={{0,3},{1,4},{2,5},{3,6},{4,7},{5,0},{6,1},{7,2},{8,11},{9,12},{10,... | collective-permute-start | bytes 396296 | tf_op jit(solution)/shard_map/ppermute | solution.py:46
  13.6 3.8 %collective-permute-start.7 = (bf16[128,32]{0,1:T(8,128)(2,1)}, bf16[128,32]{0,1:T(8,128)(2,1)}, u32[]{:S(2)}, u32[]{:S(2)}) collective-permute-start(bf16[128,32]{0,1:T(8,128)(2,1)} %get-tuple-element.51), channel_id=1, source_target_pairs={{0,8},{8,16},{16,24},{24,32},{32,40},{40,48},{48,56},{56,64},{64,7... | collective-permute-start | bytes 24584 | tf_op jit(solution)/shard_map/ppermute | solution.py:12
  21.3 17.8 %all-to-all-start = ((s32[64,1,2]{2,1,0:T(1,128)}), s32[64,1,2]{2,1,0:T(1,128)S(1)}, u32[]{:S(2)}, u32[]{:S(2)}) async-start(s32[64,1,2]{2,1,0:T(1,128)} %bitcast.18), calls=%async_computation | async-start | bytes 65536 | tf_op jit(solution)/shard_map/all_to_all | solution.py:72
  46.3 3.6 %all-to-all-done = s32[64,1,2]{2,1,0:T(1,128)S(1)} async-done(((s32[64,1,2]{2,1,0:T(1,128)}), s32[64,1,2]{2,1,0:T(1,128)S(1)}, u32[]{:S(2)}, u32[]{:S(2)}) %all-to-all-start) | async-done | bytes 544 | tf_op jit(solution)/shard_map/all_to_all | solution.py:72
  52.8 8.9 %all-to-all-start.1 = ((bf16[64,2,128,32]{2,3,1,0:T(8,128)(2,1)}), bf16[64,2,128,32]{2,3,1,0:T(8,128)(2,1)}, u32[]{:S(2)}, u32[]{:S(2)}) async-start(bf16[64,2,128,32]{2,3,1,0:T(8,128)(2,1)} %broadcast_select_fusion), calls=%async_computation.1 | async-start | bytes 2097152 | tf_op jit(solution)/shard_map/all_to_all | solution.py:79
  61.8 2.4 %collective-permute-start.3 = (bf16[2064,32]{0,1:T(8,128)(2,1)}, bf16[2064,32]{0,1:T(8,128)(2,1)S(1)}, u32[]{:S(2)}, u32[]{:S(2)}) collective-permute-start(bf16[2064,32]{0,1:T(8,128)(2,1)} %fusion.25), channel_id=1, source_target_pairs={{0,4},{1,5},{2,6},{3,7},{4,0},{5,1},{6,2},{7,3},{8,12},{9,13},{10,... | collective-permute-start | bytes 396296 | tf_op jit(solution)/shard_map/ppermute | solution.py:46
  64.2 5.3 %collective-permute-start.4 = (bf16[2064,32]{0,1:T(8,128)(2,1)}, bf16[2064,32]{0,1:T(8,128)(2,1)S(1)}, u32[]{:S(2)}, u32[]{:S(2)}) collective-permute-start(bf16[2064,32]{0,1:T(8,128)(2,1)} %fusion.25), channel_id=1, source_target_pairs={{0,5},{1,6},{2,7},{3,0},{4,1},{5,2},{6,3},{7,4},{8,13},{9,14},{10,... | collective-permute-start | bytes 396296 | tf_op jit(solution)/shard_map/ppermute | solution.py:46
  71.4 2.6 %collective-permute-start.5 = (bf16[2064,32]{0,1:T(8,128)(2,1)}, bf16[2064,32]{0,1:T(8,128)(2,1)S(1)}, u32[]{:S(2)}, u32[]{:S(2)}) collective-permute-start(bf16[2064,32]{0,1:T(8,128)(2,1)} %fusion.25), channel_id=1, source_target_pairs={{0,6},{1,7},{2,0},{3,1},{4,2},{5,3},{6,4},{7,5},{8,14},{9,15},{10,... | collective-permute-start | bytes 396296 | tf_op jit(solution)/shard_map/ppermute | solution.py:46
  77.0 2.3 %collective-permute-done.5 = bf16[2064,32]{0,1:T(8,128)(2,1)S(1)} collective-permute-done((bf16[2064,32]{0,1:T(8,128)(2,1)}, bf16[2064,32]{0,1:T(8,128)(2,1)S(1)}, u32[]{:S(2)}, u32[]{:S(2)}) %collective-permute-start.5) | collective-permute-done | bytes 132128 | tf_op jit(solution)/shard_map/ppermute | solution.py:46
  81.5 7.3 %all-to-all-done.1 = bf16[64,2,128,32]{2,3,1,0:T(8,128)(2,1)} async-done(((bf16[64,2,128,32]{2,3,1,0:T(8,128)(2,1)}), bf16[64,2,128,32]{2,3,1,0:T(8,128)(2,1)}, u32[]{:S(2)}, u32[]{:S(2)}) %all-to-all-start.1) | async-done | bytes 1048608 | tf_op jit(solution)/shard_map/all_to_all | solution.py:79
  88.9 1.9 %gather_fusion.2 = bf16[16,128,32]{1,2,0:T(8,128)(2,1)S(1)} fusion(bf16[128,128,32]{1,2,0:T(8,128)(2,1)} %bitcast.21, s32[1024]{0:T(1024)} %pad_clamp_fusion), kind=kCustom, calls=%fused_computation.2 | custom fusion | bytes 262208 | tf_op jit(solution)/shard_map/gather | solution.py:80
  92.8 7.5 %all-to-all-start.2 = ((bf16[8,1024,32]{1,2,0:T(8,128)(2,1)}), bf16[8,1024,32]{1,2,0:T(8,128)(2,1)}, u32[]{:S(2)}, u32[]{:S(2)}) async-start(bf16[8,1024,32]{1,2,0:T(8,128)(2,1)} %broadcast_in_dim.69), calls=%async_computation.2 | async-start | bytes 1048576 | tf_op jit(solution)/shard_map/all_to_all | solution.py:93
  101.9 8.0 %all-to-all-done.2 = bf16[8,1024,32]{1,2,0:T(8,128)(2,1)} async-done(((bf16[8,1024,32]{1,2,0:T(8,128)(2,1)}), bf16[8,1024,32]{1,2,0:T(8,128)(2,1)}, u32[]{:S(2)}, u32[]{:S(2)}) %all-to-all-start.2) | async-done | bytes 524320 | tf_op jit(solution)/shard_map/all_to_all | solution.py:93
  109.9 3.0 %fusion.14 = (bf16[8,1024,32]{1,2,0:T(8,128)(2,1)S(1)}, f32[1024,8,32]{0,2,1:T(8,128)}) fusion(bf16[8,2064,32]{1,2,0:T(8,128)(2,1)S(1)} %gather_fusion, f32[8,32]{1,0:T(8,128)S(1)} %fusion.28, f32[1024,8,32]{0,2,1:T(8,128)} %convolution_bitcast_fusion.1, bf16[8,32,8,32]{3,2,1,0:T(8,128)(2,1)S(1)} %copy-done.8, bf16[8,1024,32]{1,2,0:T(8,128)(2,1)} %all-to-all-done.2), kind=kOutput, calls=%fused_computation.30 | convolution fusion | flops 137363456 | bytes 3802112 | tf_op jit(solution)/shard_map/frc,fcgd->grd/dot_general | solution.py:114
  118.0 1.9 %copy.186 = bf16[64,2,128,34]{2,1,3,0:T(2,128)(2,1)} copy(bf16[64,2,128,34]{2,3,1,0:T(8,128)(2,1)S(1)} %pad_maximum_fusion) | data formatting | bytes 2228224 | tf_op jit(solution)/shard_map/concatenate | solution.py:174
  119.9 6.2 %all-to-all-start.3 = ((bf16[64,2,128,34]{2,1,3,0:T(2,128)(2,1)}), bf16[64,2,128,34]{2,1,3,0:T(2,128)(2,1)S(1)}, u32[]{:S(2)}, u32[]{:S(2)}) async-start(bf16[64,2,128,34]{2,1,3,0:T(2,128)(2,1)} %copy.186), calls=%async_computation.3 | async-start | bytes 2228224 | tf_op jit(solution)/shard_map/all_to_all | solution.py:181
  127.4 2.9 %collective-permute-start.9 = (f32[128,32]{0,1:T(8,128)S(1)}, f32[128,32]{0,1:T(8,128)S(1)}, u32[]{:S(2)}, u32[]{:S(2)}) collective-permute-start(f32[128,32]{0,1:T(8,128)S(1)} %get-tuple-element.41), channel_id=1, source_target_pairs={{0,8},{8,16},{16,24},{24,32},{32,40},{40,48},{48,56},{56,64},{64,7... | collective-permute-start | bytes 49160 | tf_op jit(solution)/shard_map/ppermute | solution.py:23
  131.8 1.6 fusion.34
  133.4 21.4 %all-to-all-done.3 = bf16[64,2,128,34]{2,1,3,0:T(2,128)(2,1)S(1)} async-done(((bf16[64,2,128,34]{2,1,3,0:T(2,128)(2,1)}), bf16[64,2,128,34]{2,1,3,0:T(2,128)(2,1)S(1)}, u32[]{:S(2)}, u32[]{:S(2)}) %all-to-all-start.3) | async-done | bytes 1114144 | tf_op jit(solution)/shard_map/all_to_all | solution.py:181
  155.9 7.9 %all-to-all-start.4 = ((f32[64,1,256]{2,1,0:T(1,128)}), f32[64,1,256]{2,1,0:T(1,128)S(1)}, u32[]{:S(2)}, u32[]{:S(2)}) async-start(f32[64,1,256]{2,1,0:T(1,128)} %broadcast_in_dim.71), calls=%async_computation.4 | async-start | bytes 131072 | tf_op jit(solution)/shard_map/all_to_all | solution.py:185
  166.4 8.4 %all-to-all-done.4 = f32[64,1,256]{2,1,0:T(1,128)S(1)} async-done(((f32[64,1,256]{2,1,0:T(1,128)}), f32[64,1,256]{2,1,0:T(1,128)S(1)}, u32[]{:S(2)}, u32[]{:S(2)}) %all-to-all-start.4) | async-done | bytes 65568 | tf_op jit(solution)/shard_map/all_to_all | solution.py:185
  (148 shorter events, 39.4 us)
Async XLA Ops:
  0.6 41.6 %copy-start = (bf16[1024,384]{1,0:T(8,128)(2,1)S(1)}, bf16[1024,384]{1,0:T(8,128)(2,1)}, u32[]{:S(2)}) copy-start(bf16[1024,384]{1,0:T(8,128)(2,1)} %param.16) | copy-start | bytes 2359300
  0.6 41.8 %copy-start.1 = (bf16[1024,256]{1,0:T(8,128)(2,1)S(1)}, bf16[1024,256]{1,0:T(8,128)(2,1)}, u32[]{:S(2)}) copy-start(bf16[1024,256]{1,0:T(8,128)(2,1)} %param.17) | copy-start | bytes 1572868
  0.7 42.2 %copy-start.11 = (bf16[256,256]{1,0:T(8,128)(2,1)S(1)}, bf16[256,256]{1,0:T(8,128)(2,1)}, u32[]{:S(2)}) copy-start(bf16[256,256]{1,0:T(8,128)(2,1)} %param.21) | copy-start | bytes 393220
  3.1 68.3 %collective-permute-start = (bf16[2064,32]{0,1:T(8,128)(2,1)}, bf16[2064,32]{0,1:T(8,128)(2,1)}, u32[]{:S(2)}, u32[]{:S(2)}) collective-permute-start(bf16[2064,32]{0,1:T(8,128)(2,1)} %fusion.25), channel_id=1, source_target_pairs={{0,1},{1,2},{2,3},{3,4},{4,5},{5,6},{6,7},{7,0},{8,9},{9,10},{10,1... | collective-permute-start | bytes 396296 | tf_op jit(solution)/shard_map/ppermute | solution.py:46
  5.7 69.2 %collective-permute-start.1 = (bf16[2064,32]{0,1:T(8,128)(2,1)}, bf16[2064,32]{0,1:T(8,128)(2,1)}, u32[]{:S(2)}, u32[]{:S(2)}) collective-permute-start(bf16[2064,32]{0,1:T(8,128)(2,1)} %fusion.25), channel_id=1, source_target_pairs={{0,2},{1,3},{2,4},{3,5},{4,6},{5,7},{6,0},{7,1},{8,10},{9,11},{10,... | collective-permute-start | bytes 396296 | tf_op jit(solution)/shard_map/ppermute | solution.py:46
  8.8 67.2 %collective-permute-start.2 = (bf16[2064,32]{0,1:T(8,128)(2,1)}, bf16[2064,32]{0,1:T(8,128)(2,1)}, u32[]{:S(2)}, u32[]{:S(2)}) collective-permute-start(bf16[2064,32]{0,1:T(8,128)(2,1)} %fusion.25), channel_id=1, source_target_pairs={{0,3},{1,4},{2,5},{3,6},{4,7},{5,0},{6,1},{7,2},{8,11},{9,12},{10,... | collective-permute-start | bytes 396296 | tf_op jit(solution)/shard_map/ppermute | solution.py:46
  13.6 48.2 %collective-permute-start.7 = (bf16[128,32]{0,1:T(8,128)(2,1)}, bf16[128,32]{0,1:T(8,128)(2,1)}, u32[]{:S(2)}, u32[]{:S(2)}) collective-permute-start(bf16[128,32]{0,1:T(8,128)(2,1)} %get-tuple-element.51), channel_id=1, source_target_pairs={{0,8},{8,16},{16,24},{24,32},{32,40},{40,48},{48,56},{56,64},{64,7... | collective-permute-start | bytes 24584 | tf_op jit(solution)/shard_map/ppermute | solution.py:12
  17.3 46.9 %collective-permute-start.8 = (bf16[128,32]{0,1:T(8,128)(2,1)}, bf16[128,32]{0,1:T(8,128)(2,1)}, u32[]{:S(2)}, u32[]{:S(2)}) collective-permute-start(bf16[128,32]{0,1:T(8,128)(2,1)} %get-tuple-element.52), channel_id=1, source_target_pairs={{8,0},{16,8},{24,16},{32,24},{40,32},{48,40},{56,48},{64,56},{72,6... | collective-permute-start | bytes 24584 | tf_op jit(solution)/shard_map/ppermute | solution.py:15
  21.3 28.5 %all-to-all-start = ((s32[64,1,2]{2,1,0:T(1,128)}), s32[64,1,2]{2,1,0:T(1,128)S(1)}, u32[]{:S(2)}, u32[]{:S(2)}) async-start(s32[64,1,2]{2,1,0:T(1,128)} %bitcast.18), calls=%async_computation | async-start | bytes 65536 | tf_op jit(solution)/shard_map/all_to_all | solution.py:72
  52.8 16.7 %copy-start.5 = (bf16[1024,32]{0,1:T(8,128)(2,1)S(1)}, bf16[1024,32]{0,1:T(8,128)(2,1)}, u32[]{:S(2)}) copy-start(bf16[1024,32]{0,1:T(8,128)(2,1)} %param.15) | copy-start | bytes 196612
  52.8 36.0 %all-to-all-start.1 = ((bf16[64,2,128,32]{2,3,1,0:T(8,128)(2,1)}), bf16[64,2,128,32]{2,3,1,0:T(8,128)(2,1)}, u32[]{:S(2)}, u32[]{:S(2)}) async-start(bf16[64,2,128,32]{2,3,1,0:T(8,128)(2,1)} %broadcast_select_fusion), calls=%async_computation.1 | async-start | bytes 2097152 | tf_op jit(solution)/shard_map/all_to_all | solution.py:79
  61.8 15.2 %collective-permute-start.3 = (bf16[2064,32]{0,1:T(8,128)(2,1)}, bf16[2064,32]{0,1:T(8,128)(2,1)S(1)}, u32[]{:S(2)}, u32[]{:S(2)}) collective-permute-start(bf16[2064,32]{0,1:T(8,128)(2,1)} %fusion.25), channel_id=1, source_target_pairs={{0,4},{1,5},{2,6},{3,7},{4,0},{5,1},{6,2},{7,3},{8,12},{9,13},{10,... | collective-permute-start | bytes 396296 | tf_op jit(solution)/shard_map/ppermute | solution.py:46
  64.2 12.8 %collective-permute-start.4 = (bf16[2064,32]{0,1:T(8,128)(2,1)}, bf16[2064,32]{0,1:T(8,128)(2,1)S(1)}, u32[]{:S(2)}, u32[]{:S(2)}) collective-permute-start(bf16[2064,32]{0,1:T(8,128)(2,1)} %fusion.25), channel_id=1, source_target_pairs={{0,5},{1,6},{2,7},{3,0},{4,1},{5,2},{6,3},{7,4},{8,13},{9,14},{10,... | collective-permute-start | bytes 396296 | tf_op jit(solution)/shard_map/ppermute | solution.py:46
  71.4 7.9 %collective-permute-start.5 = (bf16[2064,32]{0,1:T(8,128)(2,1)}, bf16[2064,32]{0,1:T(8,128)(2,1)S(1)}, u32[]{:S(2)}, u32[]{:S(2)}) collective-permute-start(bf16[2064,32]{0,1:T(8,128)(2,1)} %fusion.25), channel_id=1, source_target_pairs={{0,6},{1,7},{2,0},{3,1},{4,2},{5,3},{6,4},{7,5},{8,14},{9,15},{10,... | collective-permute-start | bytes 396296 | tf_op jit(solution)/shard_map/ppermute | solution.py:46
  74.9 5.8 %collective-permute-start.6 = (bf16[2064,32]{0,1:T(8,128)(2,1)}, bf16[2064,32]{0,1:T(8,128)(2,1)S(1)}, u32[]{:S(2)}, u32[]{:S(2)}) collective-permute-start(bf16[2064,32]{0,1:T(8,128)(2,1)} %fusion.25), channel_id=1, source_target_pairs={{0,7},{1,0},{2,1},{3,2},{4,3},{5,4},{6,5},{7,6},{8,15},{9,8},{10,9... | collective-permute-start | bytes 396296 | tf_op jit(solution)/shard_map/ppermute | solution.py:46
  81.5 9.4 %copy-start.7 = (f32[8,32,128]{2,1,0:T(8,128)S(1)}, f32[8,32,128]{2,1,0:T(8,128)}, u32[]{:S(2)}) copy-start(f32[8,32,128]{2,1,0:T(8,128)} %fusion.19) | copy-start | bytes 393220
  92.8 17.1 %all-to-all-start.2 = ((bf16[8,1024,32]{1,2,0:T(8,128)(2,1)}), bf16[8,1024,32]{1,2,0:T(8,128)(2,1)}, u32[]{:S(2)}, u32[]{:S(2)}) async-start(bf16[8,1024,32]{1,2,0:T(8,128)(2,1)} %broadcast_in_dim.69), calls=%async_computation.2 | async-start | bytes 1048576 | tf_op jit(solution)/shard_map/all_to_all | solution.py:93
  100.5 9.4 %copy-start.8 = (bf16[8,32,8,32]{3,2,1,0:T(8,128)(2,1)S(1)}, bf16[8,32,8,32]{3,2,1,0:T(8,128)(2,1)}, u32[]{:S(2)}) copy-start(bf16[8,32,8,32]{3,2,1,0:T(8,128)(2,1)} %reshape.381) | copy-start | bytes 393220
  101.9 11.0 %copy-start.6 = (bf16[1024,32]{0,1:T(8,128)(2,1)S(1)}, bf16[1024,32]{0,1:T(8,128)(2,1)}, u32[]{:S(2)}) copy-start(bf16[1024,32]{0,1:T(8,128)(2,1)} %param.15) | copy-start | bytes 196612
  119.9 34.9 %all-to-all-start.3 = ((bf16[64,2,128,34]{2,1,3,0:T(2,128)(2,1)}), bf16[64,2,128,34]{2,1,3,0:T(2,128)(2,1)S(1)}, u32[]{:S(2)}, u32[]{:S(2)}) async-start(bf16[64,2,128,34]{2,1,3,0:T(2,128)(2,1)} %copy.186), calls=%async_computation.3 | async-start | bytes 2228224 | tf_op jit(solution)/shard_map/all_to_all | solution.py:181
  127.4 39.0 %collective-permute-start.9 = (f32[128,32]{0,1:T(8,128)S(1)}, f32[128,32]{0,1:T(8,128)S(1)}, u32[]{:S(2)}, u32[]{:S(2)}) collective-permute-start(f32[128,32]{0,1:T(8,128)S(1)} %get-tuple-element.41), channel_id=1, source_target_pairs={{0,8},{8,16},{16,24},{24,32},{32,40},{40,48},{48,56},{56,64},{64,7... | collective-permute-start | bytes 49160 | tf_op jit(solution)/shard_map/ppermute | solution.py:23
  130.3 36.1 %collective-permute-start.10 = (f32[128,32]{0,1:T(8,128)S(1)}, f32[128,32]{0,1:T(8,128)S(1)}, u32[]{:S(2)}, u32[]{:S(2)}) collective-permute-start(f32[128,32]{0,1:T(8,128)S(1)} %get-tuple-element.40), channel_id=1, source_target_pairs={{8,0},{16,8},{24,16},{32,24},{40,32},{48,40},{56,48},{64,56},{72,6... | collective-permute-start | bytes 49160 | tf_op jit(solution)/shard_map/ppermute | solution.py:23
  155.9 19.0 %all-to-all-start.4 = ((f32[64,1,256]{2,1,0:T(1,128)}), f32[64,1,256]{2,1,0:T(1,128)S(1)}, u32[]{:S(2)}, u32[]{:S(2)}) async-start(f32[64,1,256]{2,1,0:T(1,128)} %broadcast_in_dim.71), calls=%async_computation.4 | async-start | bytes 131072 | tf_op jit(solution)/shard_map/all_to_all | solution.py:185
  166.4 9.7 %copy-start.10 = (f32[1024,32]{0,1:T(8,128)}, f32[1024,32]{0,1:T(8,128)S(1)}, u32[]{:S(2)}) copy-start(f32[1024,32]{0,1:T(8,128)S(1)} %fusion.49) | copy-start | bytes 393220
  (10 other events, 35.4 us)

commit v19 on v17

--- a/solution.py
+++ b/solution.py
@@ -160,8 +160,17 @@
     grad_fetched = jnp.einsum(
         "bij,bic->bjc", far_tiles, grad_blocks, preferred_element_type=jnp.float32
     )
-    returning = jnp.zeros((peer_count * capacity, tile_size, col_count), jnp.float32)
-    returning = returning.at[slot_ids].set(grad_fetched.reshape(entries, tile_size, col_count))
+    placing = (
+        slot_ids[None, None, :]
+        == (jnp.arange(peer_count, dtype=jnp.int32)[:, None, None] * capacity
+            + jnp.arange(capacity, dtype=jnp.int32)[None, :, None])
+    ).astype(jnp.bfloat16)
+    returning = jnp.einsum(
+        "pse,ejc->psjc",
+        placing,
+        grad_fetched.reshape(entries, tile_size, col_count).astype(jnp.bfloat16),
+        preferred_element_type=jnp.float32,
+    )
     partials = jnp.stack([part_self, part_neigh]).reshape(peer_count, -1)
     high = lax.reduce_precision(partials, exponent_bits=8, mantissa_bits=7)
     coded = jnp.stack(

time: 165 us -> 164 us (level)
  local copies, waits for them, and re-layouts: 20.1 us -> 18.1 us
where the time goes in v19:
time: 164 us; the launch traced here: 162 us
  waiting for transfers between devices  77 us (47%)
  starting transfers between devices  53.8 us (33%)
  local copies, waits for them, and re-layouts  18.1 us (11%)
  matrix products  6.85 us (4%)
  other arithmetic  4.97 us (3%)
    all_to_all x1, waiting for transfers between devices, on_device(): lax.all_to_all(payload, 'rows', split_axis=0, concat_axis=0, tiled=True)  21.6 us
    all_to_all x1, starting transfers between devices, on_device(): lax.all_to_all(request, 'rows', split_axis=0, concat_axis=0, tiled=True)  17.1 us
    all_to_all x1, waiting for transfers between devices, on_device(): lax.all_to_all(jnp.broadcast_to(joined[None], (feat_count,) + joined.shap...  16.7 us
    ppermute x1, waiting for transfers between devices, extended(): lax.ppermute(lax.slice_in_dim(block, block.shape[dim] - width, None, axis...  12.2 us
    all_to_all x1, waiting for transfers between devices, on_device(): lax.all_to_all(request, 'rows', split_axis=0, concat_axis=0, tiled=True)  9.91 us
    all_to_all x1, starting transfers between devices, on_device(): lax.all_to_all(jnp.broadcast_to(joined[None], (feat_count,) + joined.shap...  9.43 us
    all_to_all x1, waiting for transfers between devices, on_device(): lax.all_to_all(jnp.broadcast_to(mine, partials.shape), 'rows', split_axis...  8.4 us
    all_to_all x1, starting transfers between devices, on_device(): lax.all_to_all(jnp.broadcast_to(mine, partials.shape), 'rows', split_axis...  7.9 us
  transfers between devices with their start and end apart: 9, of which 7 were waited for; matrix products, arithmetic and copies ran while one was open for 8% of the time, Pallas kernels for 0%

profile of v19, /device:TPU:1, one launch (start us, length us, event | category | flops | bytes accessed | tf_op | source)
XLA Modules:
  0.0 162.0 jit_solution(14716298099616272721)
XLA Ops:
  3.4 17.1 %all-to-all-start = ((s32[64,1,2]{2,1,0:T(1,128)}), s32[64,1,2]{2,1,0:T(1,128)S(1)}, u32[]{:S(2)}, u32[]{:S(2)}) async-start(s32[64,1,2]{2,1,0:T(1,128)} %bitcast.3), calls=%async_computation | async-start | bytes 65536 | tf_op jit(solution)/shard_map/all_to_all | solution.py:68
  21.4 9.9 %all-to-all-done = s32[64,1,2]{2,1,0:T(1,128)S(1)} async-done(((s32[64,1,2]{2,1,0:T(1,128)}), s32[64,1,2]{2,1,0:T(1,128)S(1)}, u32[]{:S(2)}, u32[]{:S(2)}) %all-to-all-start) | async-done | bytes 544 | tf_op jit(solution)/shard_map/all_to_all | solution.py:68
  32.6 1.2 broadcast_select_fusion
  33.7 4.8 %all-to-all-start.1 = ((bf16[64,2,128,32]{2,3,1,0:T(8,128)(2,1)}), bf16[64,2,128,32]{2,3,1,0:T(8,128)(2,1)S(1)}, u32[]{:S(2)}, u32[]{:S(2)}) async-start(bf16[64,2,128,32]{2,3,1,0:T(8,128)(2,1)} %broadcast_select_fusion), calls=%async_computation.1 | async-start | bytes 2097152 | tf_op jit(solution)/shard_map/all_to_all | solution.py:75
  38.6 2.8 %collective-permute-start = (bf16[128,32]{0,1:T(8,128)(2,1)S(1)}, bf16[128,32]{0,1:T(8,128)(2,1)S(1)}, u32[]{:S(2)}, u32[]{:S(2)}) collective-permute-start(bf16[128,32]{0,1:T(8,128)(2,1)S(1)} %get-tuple-element.51), channel_id=1, source_target_pairs={{0,8},{8,16},{16,24},{24,32},{32,40},{40,48},{48,56},{56,64},{64,7... | collective-permute-start | bytes 24584 | tf_op jit(solution)/shard_map/ppermute | solution.py:12
  41.4 1.3 collective-permute-start.1
  43.5 12.2 %collective-permute-done = bf16[128,32]{0,1:T(8,128)(2,1)S(1)} collective-permute-done((bf16[128,32]{0,1:T(8,128)(2,1)S(1)}, bf16[128,32]{0,1:T(8,128)(2,1)S(1)}, u32[]{:S(2)}, u32[]{:S(2)}) %collective-permute-start) | collective-permute-done | bytes 8224 | tf_op jit(solution)/shard_map/ppermute | solution.py:12
  55.7 4.3 %collective-permute-done.1 = bf16[128,32]{0,1:T(8,128)(2,1)S(1)} collective-permute-done((bf16[128,32]{0,1:T(8,128)(2,1)S(1)}, bf16[128,32]{0,1:T(8,128)(2,1)S(1)}, u32[]{:S(2)}, u32[]{:S(2)}) %collective-permute-start.1) | collective-permute-done | bytes 8224 | tf_op jit(solution)/shard_map/ppermute | solution.py:15
  60.5 3.8 %all-to-all-done.1 = bf16[64,2,128,32]{2,3,1,0:T(8,128)(2,1)S(1)} async-done(((bf16[64,2,128,32]{2,3,1,0:T(8,128)(2,1)}), bf16[64,2,128,32]{2,3,1,0:T(8,128)(2,1)S(1)}, u32[]{:S(2)}, u32[]{:S(2)}) %all-to-all-start.1) | async-done | bytes 1048608 | tf_op jit(solution)/shard_map/all_to_all | solution.py:75
  65.4 1.3 broadcast_in_dim.44
  66.7 9.4 %all-to-all-start.2 = ((bf16[8,3088,32]{1,2,0:T(8,128)(2,1)}), bf16[8,3088,32]{1,2,0:T(8,128)(2,1)S(1)}, u32[]{:S(2)}, u32[]{:S(2)}) async-start(bf16[8,3088,32]{1,2,0:T(8,128)(2,1)} %broadcast_in_dim.44), calls=%async_computation.2 | async-start | bytes 3276800 | tf_op jit(solution)/shard_map/all_to_all | solution.py:90
  76.1 1.2 reshape.348
  77.3 2.0 %reshape.349 = bf16[8,32,8,32]{3,2,1,0:T(8,128)(2,1)} reshape(bf16[256,256]{1,0:T(8,128)(2,1)} %param.21) | data formatting | bytes 262144 | tf_op jit(solution)/shard_map/reshape | solution.py:113
  80.8 16.7 %all-to-all-done.2 = bf16[8,3088,32]{1,2,0:T(8,128)(2,1)S(1)} async-done(((bf16[8,3088,32]{1,2,0:T(8,128)(2,1)}), bf16[8,3088,32]{1,2,0:T(8,128)(2,1)S(1)}, u32[]{:S(2)}, u32[]{:S(2)}) %all-to-all-start.2) | async-done | bytes 1581088 | tf_op jit(solution)/shard_map/all_to_all | solution.py:90
  98.6 1.7 %fusion.15 = (bf16[8,1024,32]{1,2,0:T(8,128)(2,1)S(1)}, f32[1024,8,32]{0,2,1:T(8,128)}) fusion(bf16[8,3088,32]{1,2,0:T(8,128)(2,1)S(1)} %all-to-all-done.2, f32[8,32]{1,0:T(8,128)S(1)} %fusion.28, f32[1024,8,32]{0,2,1:T(8,128)S(1)} %convolution_bitcast_fusion.1, bf16[8,32,8,32]{3,2,1,0:T(8,128)(2,1)S(1)} %copy-done.3), kind=kOutput, calls=%fused_computation.30 | convolution fusion | flops 137363456 | bytes 4198400 | tf_op jit(solution)/shard_map/frc,fcgd->grd/dot_general | solution.py:110
  103.6 2.2 %copy.217 = bf16[64,2,128,34]{2,1,3,0:T(2,128)(2,1)} copy(bf16[64,2,128,34]{2,0,3,1:T(8,128)(2,1)S(1)} %maximum_maximum_fusion) | data formatting | bytes 2228224 | tf_op jit(solution)/shard_map/concatenate | solution.py:179
  105.7 6.3 %all-to-all-start.3 = ((bf16[64,2,128,34]{2,1,3,0:T(2,128)(2,1)}), bf16[64,2,128,34]{2,1,3,0:T(2,128)(2,1)S(1)}, u32[]{:S(2)}, u32[]{:S(2)}) async-start(bf16[64,2,128,34]{2,1,3,0:T(2,128)(2,1)} %copy.217), calls=%async_computation.3 | async-start | bytes 2228224 | tf_op jit(solution)/shard_map/all_to_all | solution.py:186
  113.2 2.9 %collective-permute-start.2 = (f32[128,32]{0,1:T(8,128)S(1)}, f32[128,32]{0,1:T(8,128)S(1)}, u32[]{:S(2)}, u32[]{:S(2)}) collective-permute-start(f32[128,32]{0,1:T(8,128)S(1)} %get-tuple-element.41), channel_id=1, source_target_pairs={{0,8},{8,16},{16,24},{24,32},{32,40},{40,48},{48,56},{56,64},{64,7... | collective-permute-start | bytes 49160 | tf_op jit(solution)/shard_map/ppermute | solution.py:23
  116.2 1.3 collective-permute-start.3
  117.5 1.6 fusion.34
  119.1 21.6 %all-to-all-done.3 = bf16[64,2,128,34]{2,1,3,0:T(2,128)(2,1)S(1)} async-done(((bf16[64,2,128,34]{2,1,3,0:T(2,128)(2,1)}), bf16[64,2,128,34]{2,1,3,0:T(2,128)(2,1)S(1)}, u32[]{:S(2)}, u32[]{:S(2)}) %all-to-all-start.3) | async-done | bytes 1114144 | tf_op jit(solution)/shard_map/all_to_all | solution.py:186
  141.7 7.9 %all-to-all-start.4 = ((f32[64,1,256]{2,1,0:T(1,128)}), f32[64,1,256]{2,1,0:T(1,128)S(1)}, u32[]{:S(2)}, u32[]{:S(2)}) async-start(f32[64,1,256]{2,1,0:T(1,128)} %broadcast_in_dim.68), calls=%async_computation.4 | async-start | bytes 131072 | tf_op jit(solution)/shard_map/all_to_all | solution.py:190
  150.8 1.2 fusion.8
  152.3 8.4 %all-to-all-done.4 = f32[64,1,256]{2,1,0:T(1,128)S(1)} async-done(((f32[64,1,256]{2,1,0:T(1,128)}), f32[64,1,256]{2,1,0:T(1,128)S(1)}, u32[]{:S(2)}, u32[]{:S(2)}) %all-to-all-start.4) | async-done | bytes 65568 | tf_op jit(solution)/shard_map/all_to_all | solution.py:190
  (116 shorter events, 17.6 us)
Async XLA Ops:
  2.5 29.1 %copy-start.13 = (s32[16]{0:T(128)}, s32[16]{0:T(128)S(1)}, u32[]{:S(2)}) copy-start(s32[16]{0:T(128)S(1)} %multiply_add_fusion) | copy-start | bytes 196
  3.4 27.9 %all-to-all-start = ((s32[64,1,2]{2,1,0:T(1,128)}), s32[64,1,2]{2,1,0:T(1,128)S(1)}, u32[]{:S(2)}, u32[]{:S(2)}) async-start(s32[64,1,2]{2,1,0:T(1,128)} %bitcast.3), calls=%async_computation | async-start | bytes 65536 | tf_op jit(solution)/shard_map/all_to_all | solution.py:68
  32.5 6.0 %copy-start.2 = (bf16[1024,32]{0,1:T(8,128)(2,1)S(1)}, bf16[1024,32]{0,1:T(8,128)(2,1)}, u32[]{:S(2)}) copy-start(bf16[1024,32]{0,1:T(8,128)(2,1)} %param.15) | copy-start | bytes 196612
  32.5 10.1 %copy-start.10 = (s32[8,2]{0,1:T(2,128)S(1)}, s32[8,2]{0,1:T(2,128)}, u32[]{:S(2)}) copy-start(s32[8,2]{0,1:T(2,128)} %param.18) | copy-start | bytes 196
  32.5 10.3 %copy-start.1 = (bf16[1024,256]{1,0:T(8,128)(2,1)S(1)}, bf16[1024,256]{1,0:T(8,128)(2,1)}, u32[]{:S(2)}) copy-start(bf16[1024,256]{1,0:T(8,128)(2,1)} %param.17) | copy-start | bytes 1572868
  33.7 9.4 %copy-start = (bf16[1024,384]{1,0:T(8,128)(2,1)S(1)}, bf16[1024,384]{1,0:T(8,128)(2,1)}, u32[]{:S(2)}) copy-start(bf16[1024,384]{1,0:T(8,128)(2,1)} %param.16) | copy-start | bytes 2359300
  33.7 9.6 %copy-start.15 = (f32[32]{0:T(128)S(1)}, f32[32]{0:T(128)}, u32[]{:S(2)}) copy-start(f32[32]{0:T(128)} %param.22) | copy-start | bytes 388
  33.7 30.6 %all-to-all-start.1 = ((bf16[64,2,128,32]{2,3,1,0:T(8,128)(2,1)}), bf16[64,2,128,32]{2,3,1,0:T(8,128)(2,1)S(1)}, u32[]{:S(2)}, u32[]{:S(2)}) async-start(bf16[64,2,128,32]{2,3,1,0:T(8,128)(2,1)} %broadcast_select_fusion), calls=%async_computation.1 | async-start | bytes 2097152 | tf_op jit(solution)/shard_map/all_to_all | solution.py:75
  38.6 17.2 %collective-permute-start = (bf16[128,32]{0,1:T(8,128)(2,1)S(1)}, bf16[128,32]{0,1:T(8,128)(2,1)S(1)}, u32[]{:S(2)}, u32[]{:S(2)}) collective-permute-start(bf16[128,32]{0,1:T(8,128)(2,1)S(1)} %get-tuple-element.51), channel_id=1, source_target_pairs={{0,8},{8,16},{16,24},{24,32},{32,40},{40,48},{48,56},{56,64},{64,7... | collective-permute-start | bytes 24584 | tf_op jit(solution)/shard_map/ppermute | solution.py:12
  41.4 18.7 %collective-permute-start.1 = (bf16[128,32]{0,1:T(8,128)(2,1)S(1)}, bf16[128,32]{0,1:T(8,128)(2,1)S(1)}, u32[]{:S(2)}, u32[]{:S(2)}) collective-permute-start(bf16[128,32]{0,1:T(8,128)(2,1)S(1)} %get-tuple-element.52), channel_id=1, source_target_pairs={{8,0},{16,8},{24,16},{32,24},{40,32},{48,40},{56,48},{64,56},{72,6... | collective-permute-start | bytes 24584 | tf_op jit(solution)/shard_map/ppermute | solution.py:15
  43.5 21.8 %copy-start.8 = (f32[1024]{0:T(1024)}, f32[1024]{0:T(1024)S(1)}, u32[]{:S(2)}) copy-start(f32[1024]{0:T(1024)S(1)} %add.177) | copy-start | bytes 12292
  60.1 5.2 %copy-start.6 = (bf16[1024,32]{0,1:T(8,128)(2,1)S(1)}, bf16[1024,32]{0,1:T(8,128)(2,1)}, u32[]{:S(2)}) copy-start(bf16[1024,32]{0,1:T(8,128)(2,1)} %param.23) | copy-start | bytes 196612
  65.3 1.4 copy-start.4
  66.7 30.8 %all-to-all-start.2 = ((bf16[8,3088,32]{1,2,0:T(8,128)(2,1)}), bf16[8,3088,32]{1,2,0:T(8,128)(2,1)S(1)}, u32[]{:S(2)}, u32[]{:S(2)}) async-start(bf16[8,3088,32]{1,2,0:T(8,128)(2,1)} %broadcast_in_dim.44), calls=%async_computation.2 | async-start | bytes 3276800 | tf_op jit(solution)/shard_map/all_to_all | solution.py:90
  97.5 1.0 copy-start.3
  98.6 2.0 %copy-start.9 = (f32[1024]{0:T(1024)S(1)}, f32[1024]{0:T(1024)}, u32[]{:S(2)}) copy-start(f32[1024]{0:T(1024)} %copy-done.8) | copy-start | bytes 12292
  100.2 2.1 %copy-start.7 = (bf16[32,8,32]{2,1,0:T(8,128)(2,1)S(1)}, bf16[32,8,32]{2,1,0:T(8,128)(2,1)}, u32[]{:S(2)}) copy-start(bf16[32,8,32]{2,1,0:T(8,128)(2,1)} %reshape.351) | copy-start | bytes 49156
  101.8 1.2 copy-start.14
  105.7 7.1 %copy-start.12 = (s32[64,1,2]{0,2,1:T(2,128)S(1)}, s32[64,1,2]{0,2,1:T(2,128)}, u32[]{:S(2)}) copy-start(s32[64,1,2]{0,2,1:T(2,128)} %copy-done.11) | copy-start | bytes 1540
  105.7 34.9 %all-to-all-start.3 = ((bf16[64,2,128,34]{2,1,3,0:T(2,128)(2,1)}), bf16[64,2,128,34]{2,1,3,0:T(2,128)(2,1)S(1)}, u32[]{:S(2)}, u32[]{:S(2)}) async-start(bf16[64,2,128,34]{2,1,3,0:T(2,128)(2,1)} %copy.217), calls=%async_computation.3 | async-start | bytes 2228224 | tf_op jit(solution)/shard_map/all_to_all | solution.py:186
  113.2 39.0 %collective-permute-start.2 = (f32[128,32]{0,1:T(8,128)S(1)}, f32[128,32]{0,1:T(8,128)S(1)}, u32[]{:S(2)}, u32[]{:S(2)}) collective-permute-start(f32[128,32]{0,1:T(8,128)S(1)} %get-tuple-element.41), channel_id=1, source_target_pairs={{0,8},{8,16},{16,24},{24,32},{32,40},{40,48},{48,56},{56,64},{64,7... | collective-permute-start | bytes 49160 | tf_op jit(solution)/shard_map/ppermute | solution.py:23
  116.2 36.1 %collective-permute-start.3 = (f32[128,32]{0,1:T(8,128)S(1)}, f32[128,32]{0,1:T(8,128)S(1)}, u32[]{:S(2)}, u32[]{:S(2)}) collective-permute-start(f32[128,32]{0,1:T(8,128)S(1)} %get-tuple-element.40), channel_id=1, source_target_pairs={{8,0},{16,8},{24,16},{32,24},{40,32},{48,40},{56,48},{64,56},{72,6... | collective-permute-start | bytes 49160 | tf_op jit(solution)/shard_map/ppermute | solution.py:23
  141.7 19.0 %all-to-all-start.4 = ((f32[64,1,256]{2,1,0:T(1,128)}), f32[64,1,256]{2,1,0:T(1,128)S(1)}, u32[]{:S(2)}, u32[]{:S(2)}) async-start(f32[64,1,256]{2,1,0:T(1,128)} %broadcast_in_dim.68), calls=%async_computation.4 | async-start | bytes 131072 | tf_op jit(solution)/shard_map/all_to_all | solution.py:190
  152.3 9.7 %copy-start.5 = (f32[1024,32]{0,1:T(8,128)}, f32[1024,32]{0,1:T(8,128)S(1)}, u32[]{:S(2)}) copy-start(f32[1024,32]{0,1:T(8,128)S(1)} %fusion.49) | copy-start | bytes 393220
  (1 other events, 0.9 us)

commit v20 on v19

--- a/solution.py
+++ b/solution.py
@@ -69,13 +69,22 @@
     usable = wanted >= 0
     safe_ids = jnp.maximum(wanted, 0)
     own_blocks = node_feats.reshape(blocks, tile_size, col_count)
-    outgoing = jnp.where(
-        usable[:, :, None, None], own_blocks[safe_ids], jnp.zeros((), jnp.bfloat16)
-    )
+    choosing = (wanted[:, :, None] == jnp.arange(blocks, dtype=jnp.int32)[None, None, :]).astype(
+        jnp.bfloat16
+    )
+    outgoing = jnp.einsum(
+        "psb,bjc->psjc", choosing, own_blocks, preferred_element_type=jnp.float32
+    ).astype(jnp.bfloat16)
     incoming = lax.all_to_all(outgoing, "rows", split_axis=0, concat_axis=0, tiled=True)
-    fetched = incoming.reshape(peer_count * capacity, tile_size, col_count)[slot_ids].reshape(
-        blocks, fanout * tile_size, col_count
-    )
+    picking = (
+        slot_ids[:, None] == jnp.arange(peer_count * capacity, dtype=jnp.int32)[None, :]
+    ).astype(jnp.bfloat16)
+    fetched = jnp.einsum(
+        "ek,kjc->ejc",
+        picking,
+        incoming.reshape(peer_count * capacity, tile_size, col_count),
+        preferred_element_type=jnp.float32,
+    ).astype(jnp.bfloat16).reshape(blocks, fanout * tile_size, col_count)
     far_tiles = far_weights.reshape(blocks, tile_size, fanout * tile_size)
     far_sum = jnp.einsum("bij,bjc->bic", far_tiles, fetched, preferred_element_type=jnp.float32)
     degree = jnp.sum(band_weights.astype(jnp.float32), axis=1) + jnp.sum(

time: 164 us -> 164 us (level)
    convert_element_type x0 -> x1, local copies, waits for them, and re-layouts: none -> 1.67 us  [on_device(): outgoing = jnp.einsum('psb,bjc->psjc', choosing, own_blocks, preferred_el...]
    unnamed x36 -> x35, local copies, waits for them, and re-layouts: 2.51 us -> 4.07 us
where the time goes in v20:
time: 164 us; the launch traced here: 162 us
  waiting for transfers between devices  77.3 us (47%)
  starting transfers between devices  53.8 us (33%)
  local copies, waits for them, and re-layouts  18.7 us (11%)
  matrix products  7.73 us (5%)
  other arithmetic  3.64 us (2%)
    all_to_all x1, waiting for transfers between devices, on_device(): lax.all_to_all(payload, 'rows', split_axis=0, concat_axis=0, tiled=True)  21.6 us
    all_to_all x1, starting transfers between devices, on_device(): lax.all_to_all(request, 'rows', split_axis=0, concat_axis=0, tiled=True)  17.1 us
    all_to_all x1, waiting for transfers between devices, on_device(): lax.all_to_all(jnp.broadcast_to(joined[None], (feat_count,) + joined.shap...  16.7 us
    ppermute x1, waiting for transfers between devices, extended(): lax.ppermute(lax.slice_in_dim(block, block.shape[dim] - width, None, axis...  12.4 us
    all_to_all x1, waiting for transfers between devices, on_device(): lax.all_to_all(request, 'rows', split_axis=0, concat_axis=0, tiled=True)  9.91 us
    all_to_all x1, starting transfers between devices, on_device(): lax.all_to_all(jnp.broadcast_to(joined[None], (feat_count,) + joined.shap...  9.42 us
    all_to_all x1, waiting for transfers between devices, on_device(): lax.all_to_all(jnp.broadcast_to(mine, partials.shape), 'rows', split_axis...  8.41 us
    all_to_all x1, starting transfers between devices, on_device(): lax.all_to_all(jnp.broadcast_to(mine, partials.shape), 'rows', split_axis...  7.89 us
  transfers between devices with their start and end apart: 9, of which 7 were waited for; matrix products, arithmetic and copies ran while one was open for 8% of the time, Pallas kernels for 0%

profile of v20, /device:TPU:1, one launch (start us, length us, event | category | flops | bytes accessed | tf_op | source)
XLA Modules:
  0.0 162.2 jit_solution(8043036993003067824)
XLA Ops:
  3.4 17.1 %all-to-all-start = ((s32[64,1,2]{2,1,0:T(1,128)}), s32[64,1,2]{2,1,0:T(1,128)S(1)}, u32[]{:S(2)}, u32[]{:S(2)}) async-start(s32[64,1,2]{2,1,0:T(1,128)} %bitcast.4), calls=%async_computation | async-start | bytes 65536 | tf_op jit(solution)/shard_map/all_to_all | solution.py:68
  21.4 9.9 %all-to-all-done = s32[64,1,2]{2,1,0:T(1,128)S(1)} async-done(((s32[64,1,2]{2,1,0:T(1,128)}), s32[64,1,2]{2,1,0:T(1,128)S(1)}, u32[]{:S(2)}, u32[]{:S(2)}) %all-to-all-start) | async-done | bytes 544 | tf_op jit(solution)/shard_map/all_to_all | solution.py:68
  31.9 1.7 %copy.157 = bf16[64,2,128,32]{2,3,1,0:T(8,128)(2,1)} copy(bf16[64,2,128,32]{2,0,3,1:T(8,128)(2,1)S(1)} %convolution_convert_fusion.1) | data formatting | bytes 2097152 | tf_op jit(solution)/shard_map/convert_element_type | solution.py:77
  33.6 4.8 %all-to-all-start.1 = ((bf16[64,2,128,32]{2,3,1,0:T(8,128)(2,1)}), bf16[64,2,128,32]{2,3,1,0:T(8,128)(2,1)S(1)}, u32[]{:S(2)}, u32[]{:S(2)}) async-start(bf16[64,2,128,32]{2,3,1,0:T(8,128)(2,1)} %copy.157), calls=%async_computation.1 | async-start | bytes 2097152 | tf_op jit(solution)/shard_map/all_to_all | solution.py:78
  38.4 2.8 %collective-permute-start = (bf16[128,32]{0,1:T(8,128)(2,1)S(1)}, bf16[128,32]{0,1:T(8,128)(2,1)S(1)}, u32[]{:S(2)}, u32[]{:S(2)}) collective-permute-start(bf16[128,32]{0,1:T(8,128)(2,1)S(1)} %get-tuple-element.51), channel_id=1, source_target_pairs={{0,8},{8,16},{16,24},{24,32},{32,40},{40,48},{48,56},{56,64},{64,7... | collective-permute-start | bytes 24584 | tf_op jit(solution)/shard_map/ppermute | solution.py:12
  41.2 1.3 collective-permute-start.1
  43.2 12.4 %collective-permute-done = bf16[128,32]{0,1:T(8,128)(2,1)S(1)} collective-permute-done((bf16[128,32]{0,1:T(8,128)(2,1)S(1)}, bf16[128,32]{0,1:T(8,128)(2,1)S(1)}, u32[]{:S(2)}, u32[]{:S(2)}) %collective-permute-start) | collective-permute-done | bytes 8224 | tf_op jit(solution)/shard_map/ppermute | solution.py:12
  55.6 4.3 %collective-permute-done.1 = bf16[128,32]{0,1:T(8,128)(2,1)S(1)} collective-permute-done((bf16[128,32]{0,1:T(8,128)(2,1)S(1)}, bf16[128,32]{0,1:T(8,128)(2,1)S(1)}, u32[]{:S(2)}, u32[]{:S(2)}) %collective-permute-start.1) | collective-permute-done | bytes 8224 | tf_op jit(solution)/shard_map/ppermute | solution.py:15
  60.3 3.8 %all-to-all-done.1 = bf16[64,2,128,32]{2,3,1,0:T(8,128)(2,1)S(1)} async-done(((bf16[64,2,128,32]{2,3,1,0:T(8,128)(2,1)}), bf16[64,2,128,32]{2,3,1,0:T(8,128)(2,1)S(1)}, u32[]{:S(2)}, u32[]{:S(2)}) %all-to-all-start.1) | async-done | bytes 1048608 | tf_op jit(solution)/shard_map/all_to_all | solution.py:78
  65.6 1.3 broadcast_in_dim.31
  66.9 9.4 %all-to-all-start.2 = ((bf16[8,3088,32]{1,2,0:T(8,128)(2,1)}), bf16[8,3088,32]{1,2,0:T(8,128)(2,1)S(1)}, u32[]{:S(2)}, u32[]{:S(2)}) async-start(bf16[8,3088,32]{1,2,0:T(8,128)(2,1)} %broadcast_in_dim.31), calls=%async_computation.2 | async-start | bytes 3276800 | tf_op jit(solution)/shard_map/all_to_all | solution.py:99
  76.3 1.2 reshape.308
  77.6 2.0 %reshape.309 = bf16[8,32,8,32]{3,2,1,0:T(8,128)(2,1)} reshape(bf16[256,256]{1,0:T(8,128)(2,1)} %param.21) | data formatting | bytes 262144 | tf_op jit(solution)/shard_map/reshape | solution.py:122
  81.0 16.7 %all-to-all-done.2 = bf16[8,3088,32]{1,2,0:T(8,128)(2,1)S(1)} async-done(((bf16[8,3088,32]{1,2,0:T(8,128)(2,1)}), bf16[8,3088,32]{1,2,0:T(8,128)(2,1)S(1)}, u32[]{:S(2)}, u32[]{:S(2)}) %all-to-all-start.2) | async-done | bytes 1581088 | tf_op jit(solution)/shard_map/all_to_all | solution.py:99
  98.8 1.7 %fusion.15 = (bf16[8,1024,32]{1,2,0:T(8,128)(2,1)S(1)}, f32[1024,8,32]{0,2,1:T(8,128)}) fusion(bf16[8,3088,32]{1,2,0:T(8,128)(2,1)S(1)} %all-to-all-done.2, f32[8,32]{1,0:T(8,128)S(1)} %fusion.29, f32[1024,8,32]{0,2,1:T(8,128)S(1)} %convolution_bitcast_fusion.1, bf16[8,32,8,32]{3,2,1,0:T(8,128)(2,1)S(1)} %copy-done.3), kind=kOutput, calls=%fused_computation.30 | convolution fusion | flops 137363456 | bytes 4198400 | tf_op jit(solution)/shard_map/frc,fcgd->grd/dot_general | solution.py:119
  103.8 2.2 %copy.177 = bf16[64,2,128,34]{2,1,3,0:T(2,128)(2,1)} copy(bf16[64,2,128,34]{2,0,3,1:T(8,128)(2,1)S(1)} %maximum_maximum_fusion) | data formatting | bytes 2228224 | tf_op jit(solution)/shard_map/concatenate | solution.py:188
  106.0 6.3 %all-to-all-start.3 = ((bf16[64,2,128,34]{2,1,3,0:T(2,128)(2,1)}), bf16[64,2,128,34]{2,1,3,0:T(2,128)(2,1)S(1)}, u32[]{:S(2)}, u32[]{:S(2)}) async-start(bf16[64,2,128,34]{2,1,3,0:T(2,128)(2,1)} %copy.177), calls=%async_computation.3 | async-start | bytes 2228224 | tf_op jit(solution)/shard_map/all_to_all | solution.py:195
  113.5 2.9 %collective-permute-start.2 = (f32[128,32]{0,1:T(8,128)S(1)}, f32[128,32]{0,1:T(8,128)S(1)}, u32[]{:S(2)}, u32[]{:S(2)}) collective-permute-start(f32[128,32]{0,1:T(8,128)S(1)} %get-tuple-element.41), channel_id=1, source_target_pairs={{0,8},{8,16},{16,24},{24,32},{32,40},{40,48},{48,56},{56,64},{64,7... | collective-permute-start | bytes 49160 | tf_op jit(solution)/shard_map/ppermute | solution.py:23
  116.4 1.3 collective-permute-start.3
  117.7 1.6 fusion.35
  119.3 21.6 %all-to-all-done.3 = bf16[64,2,128,34]{2,1,3,0:T(2,128)(2,1)S(1)} async-done(((bf16[64,2,128,34]{2,1,3,0:T(2,128)(2,1)}), bf16[64,2,128,34]{2,1,3,0:T(2,128)(2,1)S(1)}, u32[]{:S(2)}, u32[]{:S(2)}) %all-to-all-start.3) | async-done | bytes 1114144 | tf_op jit(solution)/shard_map/all_to_all | solution.py:195
  141.9 7.9 %all-to-all-start.4 = ((f32[64,1,256]{2,1,0:T(1,128)}), f32[64,1,256]{2,1,0:T(1,128)S(1)}, u32[]{:S(2)}, u32[]{:S(2)}) async-start(f32[64,1,256]{2,1,0:T(1,128)} %broadcast_in_dim.33), calls=%async_computation.4 | async-start | bytes 131072 | tf_op jit(solution)/shard_map/all_to_all | solution.py:199
  151.0 1.2 fusion.8
  152.5 8.4 %all-to-all-done.4 = f32[64,1,256]{2,1,0:T(1,128)S(1)} async-done(((f32[64,1,256]{2,1,0:T(1,128)}), f32[64,1,256]{2,1,0:T(1,128)S(1)}, u32[]{:S(2)}, u32[]{:S(2)}) %all-to-all-start.4) | async-done | bytes 65568 | tf_op jit(solution)/shard_map/all_to_all | solution.py:199
  (104 shorter events, 17.3 us)
Async XLA Ops:
  2.5 61.7 %copy-start.12 = (s32[16]{0:T(128)}, s32[16]{0:T(128)S(1)}, u32[]{:S(2)}) copy-start(s32[16]{0:T(128)S(1)} %multiply_add_fusion) | copy-start | bytes 196
  3.4 27.9 %all-to-all-start = ((s32[64,1,2]{2,1,0:T(1,128)}), s32[64,1,2]{2,1,0:T(1,128)S(1)}, u32[]{:S(2)}, u32[]{:S(2)}) async-start(s32[64,1,2]{2,1,0:T(1,128)} %bitcast.4), calls=%async_computation | async-start | bytes 65536 | tf_op jit(solution)/shard_map/all_to_all | solution.py:68
  31.4 0.6 copy-start.10
  31.9 6.5 %copy-start.2 = (bf16[1024,32]{0,1:T(8,128)(2,1)S(1)}, bf16[1024,32]{0,1:T(8,128)(2,1)}, u32[]{:S(2)}) copy-start(bf16[1024,32]{0,1:T(8,128)(2,1)} %param.15) | copy-start | bytes 196612
  31.9 10.6 %copy-start.1 = (bf16[1024,256]{1,0:T(8,128)(2,1)S(1)}, bf16[1024,256]{1,0:T(8,128)(2,1)}, u32[]{:S(2)}) copy-start(bf16[1024,256]{1,0:T(8,128)(2,1)} %param.17) | copy-start | bytes 1572868
  33.6 9.2 %copy-start = (bf16[1024,384]{1,0:T(8,128)(2,1)S(1)}, bf16[1024,384]{1,0:T(8,128)(2,1)}, u32[]{:S(2)}) copy-start(bf16[1024,384]{1,0:T(8,128)(2,1)} %param.16) | copy-start | bytes 2359300
  33.6 9.4 %copy-start.14 = (f32[32]{0:T(128)S(1)}, f32[32]{0:T(128)}, u32[]{:S(2)}) copy-start(f32[32]{0:T(128)} %param.22) | copy-start | bytes 388
  33.6 30.6 %all-to-all-start.1 = ((bf16[64,2,128,32]{2,3,1,0:T(8,128)(2,1)}), bf16[64,2,128,32]{2,3,1,0:T(8,128)(2,1)S(1)}, u32[]{:S(2)}, u32[]{:S(2)}) async-start(bf16[64,2,128,32]{2,3,1,0:T(8,128)(2,1)} %copy.157), calls=%async_computation.1 | async-start | bytes 2097152 | tf_op jit(solution)/shard_map/all_to_all | solution.py:78
  38.4 17.2 %collective-permute-start = (bf16[128,32]{0,1:T(8,128)(2,1)S(1)}, bf16[128,32]{0,1:T(8,128)(2,1)S(1)}, u32[]{:S(2)}, u32[]{:S(2)}) collective-permute-start(bf16[128,32]{0,1:T(8,128)(2,1)S(1)} %get-tuple-element.51), channel_id=1, source_target_pairs={{0,8},{8,16},{16,24},{24,32},{32,40},{40,48},{48,56},{56,64},{64,7... | collective-permute-start | bytes 24584 | tf_op jit(solution)/shard_map/ppermute | solution.py:12
  41.2 18.7 %collective-permute-start.1 = (bf16[128,32]{0,1:T(8,128)(2,1)S(1)}, bf16[128,32]{0,1:T(8,128)(2,1)S(1)}, u32[]{:S(2)}, u32[]{:S(2)}) collective-permute-start(bf16[128,32]{0,1:T(8,128)(2,1)S(1)} %get-tuple-element.52), channel_id=1, source_target_pairs={{8,0},{16,8},{24,16},{32,24},{40,32},{48,40},{56,48},{64,56},{72,6... | collective-permute-start | bytes 24584 | tf_op jit(solution)/shard_map/ppermute | solution.py:15
  43.2 21.8 %copy-start.8 = (f32[1024]{0:T(1024)}, f32[1024]{0:T(1024)S(1)}, u32[]{:S(2)}) copy-start(f32[1024]{0:T(1024)S(1)} %add.153) | copy-start | bytes 12292
  60.0 5.6 %copy-start.6 = (bf16[1024,32]{0,1:T(8,128)(2,1)S(1)}, bf16[1024,32]{0,1:T(8,128)(2,1)}, u32[]{:S(2)}) copy-start(bf16[1024,32]{0,1:T(8,128)(2,1)} %param.23) | copy-start | bytes 196612
  64.9 0.7 copy-start.4
  66.9 30.8 %all-to-all-start.2 = ((bf16[8,3088,32]{1,2,0:T(8,128)(2,1)}), bf16[8,3088,32]{1,2,0:T(8,128)(2,1)S(1)}, u32[]{:S(2)}, u32[]{:S(2)}) async-start(bf16[8,3088,32]{1,2,0:T(8,128)(2,1)} %broadcast_in_dim.31), calls=%async_computation.2 | async-start | bytes 3276800 | tf_op jit(solution)/shard_map/all_to_all | solution.py:99
  97.8 1.0 copy-start.3
  98.8 2.0 %copy-start.9 = (f32[1024]{0:T(1024)S(1)}, f32[1024]{0:T(1024)}, u32[]{:S(2)}) copy-start(f32[1024]{0:T(1024)} %copy-done.8) | copy-start | bytes 12292
  100.5 2.1 %copy-start.7 = (bf16[32,8,32]{2,1,0:T(8,128)(2,1)S(1)}, bf16[32,8,32]{2,1,0:T(8,128)(2,1)}, u32[]{:S(2)}) copy-start(bf16[32,8,32]{2,1,0:T(8,128)(2,1)} %reshape.311) | copy-start | bytes 49156
  102.0 1.2 copy-start.13
  106.0 7.1 %copy-start.11 = (s32[64,1,2]{0,2,1:T(2,128)S(1)}, s32[64,1,2]{0,2,1:T(2,128)}, u32[]{:S(2)}) copy-start(s32[64,1,2]{0,2,1:T(2,128)} %copy-done.10) | copy-start | bytes 1540
  106.0 34.9 %all-to-all-start.3 = ((bf16[64,2,128,34]{2,1,3,0:T(2,128)(2,1)}), bf16[64,2,128,34]{2,1,3,0:T(2,128)(2,1)S(1)}, u32[]{:S(2)}, u32[]{:S(2)}) async-start(bf16[64,2,128,34]{2,1,3,0:T(2,128)(2,1)} %copy.177), calls=%async_computation.3 | async-start | bytes 2228224 | tf_op jit(solution)/shard_map/all_to_all | solution.py:195
  113.5 39.0 %collective-permute-start.2 = (f32[128,32]{0,1:T(8,128)S(1)}, f32[128,32]{0,1:T(8,128)S(1)}, u32[]{:S(2)}, u32[]{:S(2)}) collective-permute-start(f32[128,32]{0,1:T(8,128)S(1)} %get-tuple-element.41), channel_id=1, source_target_pairs={{0,8},{8,16},{16,24},{24,32},{32,40},{40,48},{48,56},{56,64},{64,7... | collective-permute-start | bytes 49160 | tf_op jit(solution)/shard_map/ppermute | solution.py:23
  116.4 36.1 %collective-permute-start.3 = (f32[128,32]{0,1:T(8,128)S(1)}, f32[128,32]{0,1:T(8,128)S(1)}, u32[]{:S(2)}, u32[]{:S(2)}) collective-permute-start(f32[128,32]{0,1:T(8,128)S(1)} %get-tuple-element.40), channel_id=1, source_target_pairs={{8,0},{16,8},{24,16},{32,24},{40,32},{48,40},{56,48},{64,56},{72,6... | collective-permute-start | bytes 49160 | tf_op jit(solution)/shard_map/ppermute | solution.py:23
  141.9 19.0 %all-to-all-start.4 = ((f32[64,1,256]{2,1,0:T(1,128)}), f32[64,1,256]{2,1,0:T(1,128)S(1)}, u32[]{:S(2)}, u32[]{:S(2)}) async-start(f32[64,1,256]{2,1,0:T(1,128)} %broadcast_in_dim.33), calls=%async_computation.4 | async-start | bytes 131072 | tf_op jit(solution)/shard_map/all_to_all | solution.py:199
  152.5 9.7 %copy-start.5 = (f32[1024,32]{0,1:T(8,128)}, f32[1024,32]{0,1:T(8,128)S(1)}, u32[]{:S(2)}) copy-start(f32[1024,32]{0,1:T(8,128)S(1)} %fusion.50) | copy-start | bytes 393220
